TPU v7x, 128 devices: a whole 4x4x4 slice. The times are simulated.
128 devices in a mesh: batch: 16 (over y, x), table: 8 (over z, core).
Axes of the slice: x: 4, y: 4, z: 4, core: 2. Of those that a mesh axis runs over, the one named last changes fastest.
Arguments:
- item_table: bfloat16 [262144, 256], P(('batch', 'table'))
- query_table: bfloat16 [8192, 256], replicated, may hold values from -15 to 15
- query_weight: bfloat16 [256, 256], replicated, may hold values from -0.375 to 0.375
- query_ids: int32 [65536, 8], P(('batch', 'table')), may hold values from 0 to 8191
- fetch_rows: int32 [128, 128, 8], P(('batch', 'table')), may hold values from 0 to 2047, as said below
- counts: int32 [128, 128], P(('batch', 'table')), may hold values from 1 to 8, as said below
- example_pos: int32 [65536], P(('batch', 'table')), may hold values from 0 to 1023, as said below
Outputs:
- table_grad: float32 [262144, 256], P(('batch', 'table'))
- weight_grad: float32 [256, 256], replicated
Inputs may be any that keep to these rules, and one draw needn't show every extreme that they name: `fetch_rows`: for each device and owner, the 8 listed rows are distinct; only the first counts of them are live. `counts`: one owner, drawn from the seed, receives 8 live slots from every device; one device, drawn from the seed, has 8 live slots to every owner. `example_pos`: each example's position is below the sum of its device's counts; positions repeat.
All inputs are finite; a program needn't handle non-finite values.
Results may differ from a plain program's by a relative error of at most 0.005.
Values may be sent and summed in bfloat16 or wider, within the bound.
No kernel may reach another device: no remote copies, remote signals or barrier semaphores. Data moves between devices by JAX's collectives and lax.ppermute only.
A program may use at most 128 MiB of HBM per device.

v0:
```python
import jax
import jax.numpy as jnp
from jax import lax
from jax.sharding import PartitionSpec as P


def slot_index(live_slots, positions, slot_cap):
    ending = jnp.cumsum(live_slots)
    holder = jnp.sum((ending[None, :] <= positions[:, None]).astype(jnp.int32), axis=1)
    opening = ending - live_slots
    return holder * slot_cap + positions - jnp.take(opening, holder)


def local(item_table, query_table, query_weight, query_ids, fetch_rows, counts, example_pos):
    table_rows, model_width = item_table.shape
    sources = fetch_rows.shape[1]
    slot_cap = fetch_rows.shape[2]
    scaling = model_width ** (-0.5)
    requests = fetch_rows.reshape(sources, slot_cap)
    wanted = lax.all_to_all(requests, ("batch", "table"), split_axis=0, concat_axis=0, tiled=True)
    found_rows = jnp.take(item_table, wanted, axis=0)
    fetched = lax.all_to_all(
        found_rows, ("batch", "table"), split_axis=0, concat_axis=0, tiled=True
    )
    slot_ids = slot_index(counts.reshape(sources), example_pos, slot_cap)
    item_vectors = jnp.take(fetched.reshape(sources * slot_cap, model_width), slot_ids, axis=0)
    looked = jnp.take(query_table, query_ids, axis=0).astype(jnp.float32)
    hidden = jnp.mean(looked, axis=1).astype(jnp.bfloat16)
    queries = jnp.dot(hidden, query_weight, preferred_element_type=jnp.float32).astype(jnp.bfloat16)
    group_items = lax.all_gather(item_vectors, "batch", axis=0, tiled=True)
    scores = scaling * lax.dot_general(
        queries, group_items, (((1,), (1,)), ((), ())), preferred_element_type=jnp.float32
    )
    highest = jnp.max(scores, axis=1, keepdims=True)
    totals = highest + jnp.log(jnp.sum(jnp.exp(scores - highest), axis=1, keepdims=True))
    soft_weights = jnp.exp(scores - totals).astype(jnp.bfloat16)
    pulled = jnp.dot(soft_weights, group_items, preferred_element_type=jnp.float32)
    query_grad = scaling * (pulled - item_vectors.astype(jnp.float32))
    term_rows = lax.dot_general(
        soft_weights, queries, (((0,), (0,)), ((), ())), preferred_element_type=jnp.float32
    )
    summed = lax.psum_scatter(term_rows, "batch", scatter_dimension=0, tiled=True)
    item_grad = scaling * (summed - queries.astype(jnp.float32))
    slot_grads = jax.ops.segment_sum(item_grad, slot_ids, num_segments=sources * slot_cap)
    slot_grads = slot_grads.reshape(sources, slot_cap, model_width)
    returned = lax.all_to_all(
        slot_grads, ("batch", "table"), split_axis=0, concat_axis=0, tiled=True
    )
    table_grad = (
        jnp.zeros((table_rows, model_width), jnp.float32)
        .at[wanted.reshape(-1)]
        .add(returned.reshape(-1, model_width))
    )
    partial_value = lax.dot_general(
        hidden,
        query_grad.astype(jnp.bfloat16),
        (((0,), (0,)), ((), ())),
        preferred_element_type=jnp.float32,
    )
    weight_grad = lax.psum(partial_value, ("batch", "table"))
    return (table_grad, weight_grad)


def solution(mesh):
    in_specs = (
        P(("batch", "table"), None),
        P(),
        P(),
        P(("batch", "table"), None),
        P(("batch", "table"), None, None),
        P(("batch", "table"), None),
        P(("batch", "table")),
    )
    out_specs = (P(("batch", "table"), None), P())
    return jax.shard_map(local, mesh=mesh, in_specs=in_specs, out_specs=out_specs, check_vma=False)
```

profile of v0, /device:TPU:1, one launch (start us, length us, event | category | flops | bytes accessed | tf_op | source)
XLA Modules:
  0.0 398.5 jit_solution(16462527508807949282)
XLA Ops:
  7.2 0.0 copy-start
  7.2 0.0 copy-start.6
  7.2 0.0 copy-start.5
  7.2 1.5 copy.22
  8.7 11.5 %all-to-all-start = ((s32[128,1,8]{2,1,0:T(1,128)}), s32[128,1,8]{2,1,0:T(1,128)S(1)}, u32[]{:S(2)}, u32[]{:S(2)}) async-start(s32[128,1,8]{2,1,0:T(1,128)} %bitcast), calls=%async_computation | async-start | bytes 131072 | tf_op jit(solution)/shard_map/all_to_all | solution.py:20
  20.2 0.8 copy.23
  21.0 0.2 reduce-window.8
  21.1 0.1 reduce.1
  21.2 0.7 bitcast_subtract_fusion
  21.9 0.9 convert_reduce_fusion.1
  22.8 3.3 gather_fusion
  26.2 3.4 all-to-all-done
  29.6 0.1 reshape.173
  29.7 0.0 copy-done
  29.7 3.9 gather_fusion.2
  33.7 1.0 bitcast_select_fusion.1
  34.7 6.4 %all-to-all-start.1 = ((bf16[128,8,256]{2,1,0:T(8,128)(2,1)}), bf16[128,8,256]{2,1,0:T(8,128)(2,1)S(1)}, u32[]{:S(2)}, u32[]{:S(2)}) async-start(bf16[128,8,256]{2,1,0:T(8,128)(2,1)} %bitcast_select_fusion.1), calls=%async_computation.1 | async-start | bytes 1048576 | tf_op jit(solution)/shard_map/all_to_all | solution.py:22
  41.1 0.0 all-gather.2.cloned.1.call-start
  41.1 0.0 copy-done.6
  41.2 13.4 %all-to-all-done.1 = bf16[128,8,256]{2,1,0:T(8,128)(2,1)S(1)} async-done(((bf16[128,8,256]{2,1,0:T(8,128)(2,1)}), bf16[128,8,256]{2,1,0:T(8,128)(2,1)S(1)}, u32[]{:S(2)}, u32[]{:S(2)}) %all-to-all-start.1) | async-done | bytes 524320 | tf_op jit(solution)/shard_map/all_to_all | solution.py:22
  54.6 1.9 gather_fusion.3
  56.6 0.8 broadcast_select_fusion
  57.4 0.0 all-gather.2.cloned.1.call-update
  57.5 0.0 reduce-scatter.2.cloned.1.call-start
  57.5 0.0 copy-done.5
  57.5 0.2 copy.24
  57.7 0.1 copy.25
  57.9 0.2 reshape.165
  58.0 0.0 copy-start.4
  58.0 15.9 %gather_fusion.1 = bf16[4096,256]{1,0:T(8,128)(2,1)S(1)} fusion(bf16[8192,256]{1,0:T(8,128)(2,1)} %param.8, s32[4096]{0:T(1024)S(1)} %broadcast_clamp_fusion), kind=kCustom, calls=%fused_computation.1 | custom fusion | bytes 4210688 | tf_op jit(solution)/shard_map/jit(_take)/gather | solution.py:27
  74.0 5.6 %convert_reduce_fusion = f32[512,256]{1,0:T(8,128)S(1)} fusion(bf16[4096,256]{1,0:T(8,128)(2,1)S(1)} %gather_fusion.1, pred[512,8]{1,0:T(8,128)(4,1)S(1)} %copy.24), kind=kLoop, calls=%fused_computation.9 | loop fusion | flops 3014656 | bytes 2625536 | tf_op jit(solution)/shard_map/reduce_sum | solution.py:28
  79.5 0.0 copy-start.1
  79.6 0.8 copy-done.1
  80.4 0.0 copy-done.4
  80.4 0.2 convolution_convert_fusion
  80.6 24.4 %all-gather.2.cloned.1.call-done = bf16[8192,256]{1,0:T(8,128)(2,1)} async-done(((bf16[512,256]{1,0:T(8,128)(2,1)}), bf16[8192,256]{1,0:T(8,128)(2,1)}) %all-gather.2.cloned.1.call-update) | async-done | bytes 4194320 | tf_op jit(solution)/shard_map/all_gather | solution.py:30
  105.0 10.3 %multiply_reduce_fusion = (f32[512]{0:T(512)S(1)}, f32[512,8192]{1,0:T(8,128)}) fusion(bf16[512,256]{1,0:T(8,128)(2,1)S(1)} %convolution_convert_fusion, bf16[8192,256]{1,0:T(8,128)(2,1)} %all-gather.2.cloned.1.call-done), kind=kOutput, calls=%fused_computation.8 | convolution fusion | flops 2155871744 | bytes 21235712 | tf_op jit(solution)/shard_map/dot_general | solution.py:31
  115.3 8.6 %exponential_reduce_fusion = f32[512]{0:T(512)S(1)} fusion(f32[512,8192]{1,0:T(8,128)} %get-tuple-element.5, f32[512]{0:T(512)S(1)} %get-tuple-element.4), kind=kLoop, calls=%fused_computation.7 | loop fusion | flops 12582400 | bytes 16781312 | tf_op jit(solution)/shard_map/reduce_sum | solution.py:35
  123.9 12.3 %fusion.17 = f32[8192,256]{1,0:T(8,128)} fusion(bf16[512,256]{1,0:T(8,128)(2,1)S(1)} %convolution_convert_fusion, f32[512,8192]{1,0:T(8,128)} %get-tuple-element.5, f32[512]{0:T(512)S(1)} %log_add_fusion), kind=kOutput, calls=%fused_computation.51 | convolution fusion | flops 2160066560 | bytes 25430016 | tf_op jit(solution)/shard_map/dot_general | solution.py:39
  136.2 0.0 copy-start.2
  136.2 0.0 copy-start.3
  136.2 0.0 reduce-scatter.2.cloned.1.call-update
  136.2 0.5 broadcast.103
  136.7 0.8 reduce.4
  137.6 0.1 reshape.148
  137.7 83.0 %reduce-scatter.2.cloned.1.call-done = f32[512,256]{1,0:T(8,128)} async-done(((f32[8192,256]{1,0:T(8,128)}), f32[512,256]{1,0:T(8,128)}) %reduce-scatter.2.cloned.1.call-update) | async-done | bytes 524304 | tf_op jit(solution)/shard_map/reduce_scatter | solution.py:42
  220.6 5.1 %scatter_custom_fusion = f32[1024,256]{1,0:T(8,128)} fusion(s32[512]{0:T(512)S(1)} %get-tuple-element.3, f32[512,256]{1,0:T(8,128)} %reduce-scatter.2.cloned.1.call-done, bf16[512,256]{1,0:T(8,128)(2,1)S(1)} %convolution_convert_fusion, f32[]{:T(128)} %constant.40.clone.1, f32[]{:T(128)} %constant.77.clone.1), kind=kCustom, calls=%fused_computation.21 | custom fusion | flops 524288 | bytes 1835016 | tf_op jit(solution)/shard_map/scatter-add | solution.py:44
  225.7 9.1 %all-to-all-start.2 = ((f32[128,8,256]{2,1,0:T(8,128)}), f32[128,8,256]{2,1,0:T(8,128)S(1)}, u32[]{:S(2)}, u32[]{:S(2)}) async-start(f32[128,8,256]{2,1,0:T(8,128)} %bitcast.11), calls=%async_computation.3 | async-start | bytes 2097152 | tf_op jit(solution)/shard_map/all_to_all | solution.py:46
  234.8 0.0 all-reduce.2.cloned.1.call-start
  234.9 0.0 copy-done.2
  234.9 0.0 copy-done.3
  234.9 10.6 %fusion.2 = f32[256,256]{1,0:T(8,128)} fusion(bf16[8192,256]{1,0:T(8,128)(2,1)} %all-gather.2.cloned.1.call-done, bf16[512,256]{1,0:T(8,128)(2,1)S(1)} %copy-done.3, f32[512,256]{1,0:T(8,128)S(1)} %copy-done.2, f32[512,8192]{1,0:T(8,128)} %get-tuple-element.5, f32[512]{0:T(512)S(1)} %log_add_fusion), kind=kOutput, calls=%fused_computation.15 | convolution fusion | flops 2227961856 | bytes 22022144 | tf_op jit(solution)/shard_map/dot_general | solution.py:54
  245.4 0.0 all-reduce.2.cloned.1.call-update
  245.5 8.4 %all-to-all-done.2 = f32[128,8,256]{2,1,0:T(8,128)S(1)} async-done(((f32[128,8,256]{2,1,0:T(8,128)}), f32[128,8,256]{2,1,0:T(8,128)S(1)}, u32[]{:S(2)}, u32[]{:S(2)}) %all-to-all-start.2) | async-done | bytes 1048608 | tf_op jit(solution)/shard_map/all_to_all | solution.py:46
  253.8 7.5 %scatter_custom_fusion.1 = f32[2048,256]{1,0:T(8,128)} fusion(s32[1024]{0:T(1024)S(1)} %bitcast.32, f32[128,8,256]{2,1,0:T(8,128)S(1)} %all-to-all-done.2, f32[]{:T(128)} %constant.40.clone.1), kind=kCustom, calls=%fused_computation.16 | custom fusion | flops 262144 | bytes 3145732 | tf_op jit(solution)/shard_map/scatter-add | solution.py:52
  261.4 128.9 %all-reduce.2.cloned.1.call-done = f32[256,256]{1,0:T(8,128)} async-done(((f32[256,256]{1,0:T(8,128)}), f32[256,256]{1,0:T(8,128)}) %all-reduce.2.cloned.1.call-update) | async-done | bytes 262160 | tf_op jit(solution)/shard_map/psum | solution.py:60
  390.3 1.7 copy.27
  (13 shorter events, 0.1 us)
Async XLA Ops:
  7.2 22.5 %copy-start = (bf16[2048,256]{1,0:T(8,128)(2,1)S(1)}, bf16[2048,256]{1,0:T(8,128)(2,1)}, u32[]{:S(2)}) copy-start(bf16[2048,256]{1,0:T(8,128)(2,1)} %param.7) | copy-start | bytes 3145732
  7.2 34.0 %copy-start.6 = (s32[512]{0:T(512)S(1)}, s32[512]{0:T(512)}, u32[]{:S(2)}) copy-start(s32[512]{0:T(512)} %param.13) | copy-start | bytes 6148
  7.2 50.3 %copy-start.5 = (s32[512,8]{0,1:T(8,128)S(1)}, s32[512,8]{0,1:T(8,128)}, u32[]{:S(2)}) copy-start(s32[512,8]{0,1:T(8,128)} %param.10) | copy-start | bytes 49156
  8.7 20.9 %all-to-all-start = ((s32[128,1,8]{2,1,0:T(1,128)}), s32[128,1,8]{2,1,0:T(1,128)S(1)}, u32[]{:S(2)}, u32[]{:S(2)}) async-start(s32[128,1,8]{2,1,0:T(1,128)} %bitcast), calls=%async_computation | async-start | bytes 131072 | tf_op jit(solution)/shard_map/all_to_all | solution.py:20
  34.7 20.0 %all-to-all-start.1 = ((bf16[128,8,256]{2,1,0:T(8,128)(2,1)}), bf16[128,8,256]{2,1,0:T(8,128)(2,1)S(1)}, u32[]{:S(2)}, u32[]{:S(2)}) async-start(bf16[128,8,256]{2,1,0:T(8,128)(2,1)} %bitcast_select_fusion.1), calls=%async_computation.1 | async-start | bytes 1048576 | tf_op jit(solution)/shard_map/all_to_all | solution.py:22
  41.1 63.9 %all-gather.2.cloned.1.call-start = ((), (), s32[]{:S(2)}) async-start(), calls=%async_computation.4 | async-start | bytes 4456448 | tf_op jit(solution)/shard_map/all_gather | solution.py:30
  57.5 163.2 %reduce-scatter.2.cloned.1.call-start = ((), (), s32[]{:S(2)}) async-start(), calls=%async_computation.5 | async-start | bytes 8912896 | tf_op jit(solution)/shard_map/reduce_scatter | solution.py:42
  58.0 22.4 %copy-start.4 = (bf16[256,256]{1,0:T(8,128)(2,1)S(1)}, bf16[256,256]{1,0:T(8,128)(2,1)}, u32[]{:S(2)}) copy-start(bf16[256,256]{1,0:T(8,128)(2,1)} %param.9) | copy-start | bytes 393220
  79.5 0.8 copy-start.1
  136.2 98.7 %copy-start.2 = (f32[512,256]{1,0:T(8,128)S(1)}, f32[512,256]{1,0:T(8,128)}, u32[]{:S(2)}) copy-start(f32[512,256]{1,0:T(8,128)} %copy-done.1) | copy-start | bytes 1572868
  136.2 98.7 %copy-start.3 = (bf16[512,256]{1,0:T(8,128)(2,1)S(1)}, bf16[512,256]{1,0:T(8,128)(2,1)}, u32[]{:S(2)}) copy-start(bf16[512,256]{1,0:T(8,128)(2,1)} %broadcast_select_fusion) | copy-start | bytes 786436
  225.7 28.2 %all-to-all-start.2 = ((f32[128,8,256]{2,1,0:T(8,128)}), f32[128,8,256]{2,1,0:T(8,128)S(1)}, u32[]{:S(2)}, u32[]{:S(2)}) async-start(f32[128,8,256]{2,1,0:T(8,128)} %bitcast.11), calls=%async_computation.3 | async-start | bytes 2097152 | tf_op jit(solution)/shard_map/all_to_all | solution.py:46
  234.8 155.5 %all-reduce.2.cloned.1.call-start = ((), (), s32[]{:S(2)}) async-start(), calls=%async_computation.6 | async-start | bytes 524288 | tf_op jit(solution)/shard_map/psum | solution.py:60
Sparse Core Ops, SparseCore 0:
  57.6 47.3 all-gather.1
  136.3 84.2 reduce-scatter.1
  245.6 144.6 all-reduce.1
where the time goes:
time: 399 us; the launch traced here: 398 us
  waiting for transfers between devices  261 us (65%)
  matrix products  33.4 us (8%)
  other arithmetic  31.4 us (8%)
  local copies, waits for them, and re-layouts  31.1 us (8%)
  starting transfers between devices  27.2 us (7%)
  between operations  14 us (4%)
    psum x1, waiting for transfers between devices, local(): weight_grad = lax.psum(partial_value, ('batch', 'table'))  129 us
    reduce_scatter x1, waiting for transfers between devices, local(): lax.psum_scatter(term_rows, 'batch', scatter_dimension=0, tiled=True)  83 us
    all_gather x1, waiting for transfers between devices, local(): group_items = lax.all_gather(item_vectors, 'batch', axis=0, tiled=True)  24.4 us
    gather x1, local copies, waits for them, and re-layouts, local(): looked = jnp.take(query_table, query_ids, axis=0).astype(jnp.float32)  15.9 us
    all_to_all x1, waiting for transfers between devices, local(): lax.all_to_all(found_rows, ('batch', 'table'), split_axis=0, concat_axis=...  13.4 us
    dot_general x1, matrix products, local(): lax.dot_general(soft_weights, queries, (((0,), (0,)), ((), ())), preferre...  12.3 us
    all_to_all x1, starting transfers between devices, local(): lax.all_to_all(requests, ('batch', 'table'), split_axis=0, concat_axis=0,...  11.5 us
    dot_general x1, matrix products, local(): lax.dot_general(hidden, query_grad.astype(jnp.bfloat16), (((0,), (0,)), (...  10.6 us
  transfers between devices with their start and end apart: 6, of which 6 were waited for; matrix products, arithmetic and copies ran while one was open for 12% of the time, Pallas kernels for 0%

commit v1 on v0

--- a/solution.py
+++ b/solution.py
@@ -9,6 +9,18 @@
     holder = jnp.sum((ending[None, :] <= positions[:, None]).astype(jnp.int32), axis=1)
     opening = ending - live_slots
     return holder * slot_cap + positions - jnp.take(opening, holder)
+
+
+def butterfly_sum(value, axes):
+    total = 1
+    for axis in axes:
+        total *= lax.axis_size(axis)
+    step = 1
+    while step < total:
+        pairs = [(i, i ^ step) for i in range(total)]
+        value = value + lax.ppermute(value, axes, pairs)
+        step *= 2
+    return value
 
 
 def local(item_table, query_table, query_weight, query_ids, fetch_rows, counts, example_pos):
@@ -57,7 +69,7 @@
         (((0,), (0,)), ((), ())),
         preferred_element_type=jnp.float32,
     )
-    weight_grad = lax.psum(partial_value, ("batch", "table"))
+    weight_grad = butterfly_sum(partial_value, ("batch", "table"))
     return (table_grad, weight_grad)
 
 

time: 399 us -> 288 us (0.72)
  waiting for transfers between devices: 261 us -> 136 us
  starting transfers between devices: 27.2 us -> 40.8 us
    psum x1 -> x0, waiting for transfers between devices: 129 us -> none  [local(): weight_grad = lax.psum(partial_value, ('batch', 'table'))]
    ppermute x0 -> x7, waiting for transfers between devices: none -> 38.7 us  [butterfly_sum(): value = value + lax.ppermute(value, axes, pairs)]
    reduce_scatter x1, waiting for transfers between devices: 83 us -> 55.9 us  [local(): lax.psum_scatter(term_rows, 'batch', scatter_dimension=0, tiled=True)]
    ppermute x0 -> x7, starting transfers between devices: none -> 13.7 us  [butterfly_sum(): value = value + lax.ppermute(value, axes, pairs)]
    all_to_all x1, waiting for transfers between devices: 8.36 us -> 0.01 us  [local(): lax.all_to_all(slot_grads, ('batch', 'table'), split_axis=0, concat_axis=...]
  transfers between devices with their start and end apart: 6 -> 12, of which waited for: 6 -> 10; matrix products, arithmetic and copies ran while one was open for 12% -> 16% of each run, Pallas kernels for 0% -> 0%
where the time goes in v1:
time: 288 us; the launch traced here: 286 us
  waiting for transfers between devices  136 us (47%)
  starting transfers between devices  40.8 us (14%)
  matrix products  32.6 us (11%)
  other arithmetic  32.3 us (11%)
  local copies, waits for them, and re-layouts  30.3 us (11%)
  between operations  14.3 us (5%)
    reduce_scatter x1, waiting for transfers between devices, local(): lax.psum_scatter(term_rows, 'batch', scatter_dimension=0, tiled=True)  55.9 us
    ppermute x7, waiting for transfers between devices, butterfly_sum(): value = value + lax.ppermute(value, axes, pairs)  38.7 us
    all_gather x1, waiting for transfers between devices, local(): group_items = lax.all_gather(item_vectors, 'batch', axis=0, tiled=True)  24.4 us
    gather x1, local copies, waits for them, and re-layouts, local(): looked = jnp.take(query_table, query_ids, axis=0).astype(jnp.float32)  15.8 us
    ppermute x7, starting transfers between devices, butterfly_sum(): value = value + lax.ppermute(value, axes, pairs)  13.7 us
    all_to_all x1, waiting for transfers between devices, local(): lax.all_to_all(found_rows, ('batch', 'table'), split_axis=0, concat_axis=...  13.4 us
    dot_general x1, matrix products, local(): lax.dot_general(soft_weights, queries, (((0,), (0,)), ((), ())), preferre...  12.3 us
    all_to_all x1, starting transfers between devices, local(): lax.all_to_all(requests, ('batch', 'table'), split_axis=0, concat_axis=0,...  11.5 us
  transfers between devices with their start and end apart: 12, of which 10 were waited for; matrix products, arithmetic and copies ran while one was open for 16% of the time, Pallas kernels for 0%

profile of v1, /device:TPU:1, one launch (start us, length us, event | category | flops | bytes accessed | tf_op | source)
XLA Modules:
  0.0 286.2 jit_solution(18357552602345560109)
XLA Ops:
  7.2 0.0 copy-start
  7.2 0.0 copy-start.6
  7.2 0.0 copy-start.5
  7.2 1.5 copy.22
  8.7 11.5 %all-to-all-start = ((s32[128,1,8]{2,1,0:T(1,128)}), s32[128,1,8]{2,1,0:T(1,128)S(1)}, u32[]{:S(2)}, u32[]{:S(2)}) async-start(s32[128,1,8]{2,1,0:T(1,128)} %bitcast), calls=%async_computation | async-start | bytes 131072 | tf_op jit(solution)/shard_map/all_to_all | solution.py:32
  20.2 0.8 copy.23
  21.0 0.2 reduce-window.8
  21.1 0.1 reduce.1
  21.2 0.7 bitcast_subtract_fusion
  21.9 0.9 convert_reduce_fusion.1
  22.8 3.3 %gather_fusion = s32[512]{0:T(512)S(1)} fusion(s32[128]{0:T(128)S(1)} %bitcast_subtract_fusion, s32[1024]{0:T(1024)S(1)} %pad_clamp_fusion.1), kind=kCustom, calls=%fused_computation | custom fusion | bytes 6144 | tf_op jit(solution)/shard_map/jit(_take)/gather | solution.py:11
  26.2 3.4 %all-to-all-done = s32[128,1,8]{2,1,0:T(1,128)S(1)} async-done(((s32[128,1,8]{2,1,0:T(1,128)}), s32[128,1,8]{2,1,0:T(1,128)S(1)}, u32[]{:S(2)}, u32[]{:S(2)}) %all-to-all-start) | async-done | bytes 4128 | tf_op jit(solution)/shard_map/all_to_all | solution.py:32
  29.6 0.1 reshape.173
  29.7 3.9 %gather_fusion.2 = bf16[1024,256]{1,0:T(8,128)(2,1)S(1)} fusion(bf16[2048,256]{1,0:T(8,128)(2,1)S(1)} %copy-done, s32[1024]{0:T(1024)S(1)} %broadcast_clamp_fusion.1), kind=kCustom, calls=%fused_computation.2 | custom fusion | bytes 1052672 | tf_op jit(solution)/shard_map/jit(_take)/gather | solution.py:33
  33.7 1.0 bitcast_select_fusion.1
  34.7 6.4 %all-to-all-start.1 = ((bf16[128,8,256]{2,1,0:T(8,128)(2,1)}), bf16[128,8,256]{2,1,0:T(8,128)(2,1)S(1)}, u32[]{:S(2)}, u32[]{:S(2)}) async-start(bf16[128,8,256]{2,1,0:T(8,128)(2,1)} %bitcast_select_fusion.1), calls=%async_computation.1 | async-start | bytes 1048576 | tf_op jit(solution)/shard_map/all_to_all | solution.py:34
  41.1 0.0 all-gather.2.cloned.1.call-start
  41.1 0.0 copy-done.6
  41.2 13.4 %all-to-all-done.1 = bf16[128,8,256]{2,1,0:T(8,128)(2,1)S(1)} async-done(((bf16[128,8,256]{2,1,0:T(8,128)(2,1)}), bf16[128,8,256]{2,1,0:T(8,128)(2,1)S(1)}, u32[]{:S(2)}, u32[]{:S(2)}) %all-to-all-start.1) | async-done | bytes 524320 | tf_op jit(solution)/shard_map/all_to_all | solution.py:34
  54.6 1.9 gather_fusion.3
  56.6 0.8 broadcast_select_fusion
  57.4 0.0 all-gather.2.cloned.1.call-update
  57.5 0.0 reduce-scatter.2.cloned.1.call-start
  57.5 0.0 copy-done.5
  57.5 0.2 copy.24
  57.7 0.1 copy.25
  57.9 0.2 reshape.165
  58.0 0.0 copy-start.4
  58.0 15.8 %gather_fusion.1 = bf16[4096,256]{1,0:T(8,128)(2,1)S(1)} fusion(bf16[8192,256]{1,0:T(8,128)(2,1)} %param.8, s32[4096]{0:T(1024)S(1)} %broadcast_clamp_fusion), kind=kCustom, calls=%fused_computation.1 | custom fusion | bytes 4210688 | tf_op jit(solution)/shard_map/jit(_take)/gather | solution.py:39
  73.8 5.7 %convert_reduce_fusion = f32[512,256]{1,0:T(8,128)S(1)} fusion(bf16[4096,256]{1,0:T(8,128)(2,1)S(1)} %gather_fusion.1, pred[512,8]{1,0:T(8,128)(4,1)S(1)} %copy.24), kind=kLoop, calls=%fused_computation.9 | loop fusion | flops 3014656 | bytes 2625536 | tf_op jit(solution)/shard_map/reduce_sum | solution.py:40
  79.5 0.0 copy-start.1
  79.6 0.8 copy-done.1
  80.3 0.2 convolution_convert_fusion
  80.6 24.4 %all-gather.2.cloned.1.call-done = bf16[8192,256]{1,0:T(8,128)(2,1)} async-done(((bf16[512,256]{1,0:T(8,128)(2,1)}), bf16[8192,256]{1,0:T(8,128)(2,1)}) %all-gather.2.cloned.1.call-update) | async-done | bytes 4194320 | tf_op jit(solution)/shard_map/all_gather | solution.py:42
  105.0 10.3 %multiply_reduce_fusion = (f32[512]{0:T(512)S(1)}, f32[512,8192]{1,0:T(8,128)}) fusion(bf16[512,256]{1,0:T(8,128)(2,1)S(1)} %convolution_convert_fusion, bf16[8192,256]{1,0:T(8,128)(2,1)} %all-gather.2.cloned.1.call-done), kind=kOutput, calls=%fused_computation.8 | convolution fusion | flops 2155871744 | bytes 21235712 | tf_op jit(solution)/shard_map/dot_general | solution.py:43
  115.3 8.6 %exponential_reduce_fusion = f32[512]{0:T(512)S(1)} fusion(f32[512,8192]{1,0:T(8,128)} %get-tuple-element.5, f32[512]{0:T(512)S(1)} %get-tuple-element.4), kind=kLoop, calls=%fused_computation.7 | loop fusion | flops 12582400 | bytes 16781312 | tf_op jit(solution)/shard_map/reduce_sum | solution.py:47
  123.9 12.3 %fusion.17 = f32[8192,256]{1,0:T(8,128)} fusion(bf16[512,256]{1,0:T(8,128)(2,1)S(1)} %convolution_convert_fusion, f32[512,8192]{1,0:T(8,128)} %get-tuple-element.5, f32[512]{0:T(512)S(1)} %log_add_fusion), kind=kOutput, calls=%fused_computation.51 | convolution fusion | flops 2160066560 | bytes 25430016 | tf_op jit(solution)/shard_map/dot_general | solution.py:51
  136.2 0.0 reduce-scatter.2.cloned.1.call-update
  136.2 1.0 copy-done.2
  137.2 0.1 copy-done.3
  137.3 9.8 %fusion.2 = f32[256,256]{1,0:T(8,128)S(1)} fusion(bf16[8192,256]{1,0:T(8,128)(2,1)} %all-gather.2.cloned.1.call-done, bf16[512,256]{1,0:T(8,128)(2,1)S(1)} %copy-done.3, f32[512,256]{1,0:T(8,128)S(1)} %copy-done.2, f32[512,8192]{1,0:T(8,128)} %get-tuple-element.5, f32[512]{0:T(512)S(1)} %log_add_fusion), kind=kOutput, calls=%fused_computation.15 | convolution fusion | flops 2227961856 | bytes 22022144 | tf_op jit(solution)/shard_map/dot_general | solution.py:66
  147.2 1.1 collective-permute-start
  148.3 1.2 collective-permute-done
  149.5 1.4 collective-permute-start.1
  150.8 6.3 %collective-permute-done.1 = f32[256,256]{1,0:T(8,128)S(1)} collective-permute-done((f32[256,256]{1,0:T(8,128)S(1)}, f32[256,256]{1,0:T(8,128)S(1)}, u32[]{:S(2)}, u32[]{:S(2)}) %collective-permute-start.1) | collective-permute-done | bytes 262176 | tf_op jit(solution)/shard_map/ppermute | solution.py:21
  157.2 2.9 %collective-permute-start.2 = (f32[256,256]{1,0:T(8,128)S(1)}, f32[256,256]{1,0:T(8,128)S(1)}, u32[]{:S(2)}, u32[]{:S(2)}) collective-permute-start(f32[256,256]{1,0:T(8,128)S(1)} %add.126), channel_id=1, source_target_pairs={{0,4},{1,5},{2,6},{3,7},{4,0},{5,1},{6,2},{7,3},{8,12},{9,13},{10,... | collective-permute-start | bytes 786440 | tf_op jit(solution)/shard_map/ppermute | solution.py:21
  160.2 5.4 %collective-permute-done.2 = f32[256,256]{1,0:T(8,128)S(1)} collective-permute-done((f32[256,256]{1,0:T(8,128)S(1)}, f32[256,256]{1,0:T(8,128)S(1)}, u32[]{:S(2)}, u32[]{:S(2)}) %collective-permute-start.2) | collective-permute-done | bytes 262176 | tf_op jit(solution)/shard_map/ppermute | solution.py:21
  165.6 1.3 collective-permute-start.3
  166.8 55.9 %reduce-scatter.2.cloned.1.call-done = f32[512,256]{1,0:T(8,128)} async-done(((f32[8192,256]{1,0:T(8,128)}), f32[512,256]{1,0:T(8,128)}) %reduce-scatter.2.cloned.1.call-update) | async-done | bytes 524304 | tf_op jit(solution)/shard_map/reduce_scatter | solution.py:54
  222.7 4.8 %scatter_custom_fusion = f32[1024,256]{1,0:T(8,128)} fusion(s32[512]{0:T(512)S(1)} %get-tuple-element.3, f32[512,256]{1,0:T(8,128)} %reduce-scatter.2.cloned.1.call-done, bf16[512,256]{1,0:T(8,128)(2,1)S(1)} %convolution_convert_fusion, f32[]{:T(128)} %constant.40.clone.1, f32[]{:T(128)} %constant.77.clone.1), kind=kCustom, calls=%fused_computation.21 | custom fusion | flops 524288 | bytes 1835016 | tf_op jit(solution)/shard_map/scatter-add | solution.py:56
  227.5 9.1 %all-to-all-start.2 = ((f32[128,8,256]{2,1,0:T(8,128)}), f32[128,8,256]{2,1,0:T(8,128)S(1)}, u32[]{:S(2)}, u32[]{:S(2)}) async-start(f32[128,8,256]{2,1,0:T(8,128)} %bitcast.11), calls=%async_computation.3 | async-start | bytes 2097152 | tf_op jit(solution)/shard_map/all_to_all | solution.py:58
  236.7 0.0 collective-permute-done.3
  236.7 2.9 %collective-permute-start.4 = (f32[256,256]{1,0:T(8,128)S(1)}, f32[256,256]{1,0:T(8,128)S(1)}, u32[]{:S(2)}, u32[]{:S(2)}) collective-permute-start(f32[256,256]{1,0:T(8,128)S(1)} %add.128), channel_id=1, source_target_pairs={{0,16},{1,17},{2,18},{3,19},{4,20},{5,21},{6,22},{7,23},{8,24},{9,... | collective-permute-start | bytes 786440 | tf_op jit(solution)/shard_map/ppermute | solution.py:21
  239.7 16.7 %collective-permute-done.4 = f32[256,256]{1,0:T(8,128)S(1)} collective-permute-done((f32[256,256]{1,0:T(8,128)S(1)}, f32[256,256]{1,0:T(8,128)S(1)}, u32[]{:S(2)}, u32[]{:S(2)}) %collective-permute-start.4) | collective-permute-done | bytes 262176 | tf_op jit(solution)/shard_map/ppermute | solution.py:21
  256.4 1.3 collective-permute-start.5
  257.7 5.7 %collective-permute-done.5 = f32[256,256]{1,0:T(8,128)S(1)} collective-permute-done((f32[256,256]{1,0:T(8,128)S(1)}, f32[256,256]{1,0:T(8,128)S(1)}, u32[]{:S(2)}, u32[]{:S(2)}) %collective-permute-start.5) | collective-permute-done | bytes 262176 | tf_op jit(solution)/shard_map/ppermute | solution.py:21
  263.5 2.8 collective-permute-start.6
  266.3 0.5 broadcast.103
  266.8 0.8 reduce.4
  267.6 0.1 reshape.148
  267.7 3.4 %collective-permute-done.6 = f32[256,256]{1,0:T(8,128)S(1)} collective-permute-done((f32[256,256]{1,0:T(8,128)S(1)}, f32[256,256]{1,0:T(8,128)S(1)}, u32[]{:S(2)}, u32[]{:S(2)}) %collective-permute-start.6) | collective-permute-done | bytes 262176 | tf_op jit(solution)/shard_map/ppermute | solution.py:21
  271.1 0.7 add.131
  271.8 0.0 all-to-all-done.2
  271.8 7.5 %scatter_custom_fusion.1 = f32[2048,256]{1,0:T(8,128)} fusion(s32[1024]{0:T(1024)S(1)} %bitcast.32, f32[128,8,256]{2,1,0:T(8,128)S(1)} %all-to-all-done.2, f32[]{:T(128)} %constant.40.clone.1), kind=kCustom, calls=%fused_computation.16 | custom fusion | flops 262144 | bytes 3145732 | tf_op jit(solution)/shard_map/scatter-add | solution.py:64
  (23 shorter events, 0.3 us)
Async XLA Ops:
  7.2 22.5 %copy-start = (bf16[2048,256]{1,0:T(8,128)(2,1)S(1)}, bf16[2048,256]{1,0:T(8,128)(2,1)}, u32[]{:S(2)}) copy-start(bf16[2048,256]{1,0:T(8,128)(2,1)} %param.7) | copy-start | bytes 3145732
  7.2 34.0 %copy-start.6 = (s32[512]{0:T(512)S(1)}, s32[512]{0:T(512)}, u32[]{:S(2)}) copy-start(s32[512]{0:T(512)} %param.13) | copy-start | bytes 6148
  7.2 50.3 %copy-start.5 = (s32[512,8]{0,1:T(8,128)S(1)}, s32[512,8]{0,1:T(8,128)}, u32[]{:S(2)}) copy-start(s32[512,8]{0,1:T(8,128)} %param.10) | copy-start | bytes 49156
  8.7 20.9 %all-to-all-start = ((s32[128,1,8]{2,1,0:T(1,128)}), s32[128,1,8]{2,1,0:T(1,128)S(1)}, u32[]{:S(2)}, u32[]{:S(2)}) async-start(s32[128,1,8]{2,1,0:T(1,128)} %bitcast), calls=%async_computation | async-start | bytes 131072 | tf_op jit(solution)/shard_map/all_to_all | solution.py:32
  34.7 20.0 %all-to-all-start.1 = ((bf16[128,8,256]{2,1,0:T(8,128)(2,1)}), bf16[128,8,256]{2,1,0:T(8,128)(2,1)S(1)}, u32[]{:S(2)}, u32[]{:S(2)}) async-start(bf16[128,8,256]{2,1,0:T(8,128)(2,1)} %bitcast_select_fusion.1), calls=%async_computation.1 | async-start | bytes 1048576 | tf_op jit(solution)/shard_map/all_to_all | solution.py:34
  41.1 63.9 %all-gather.2.cloned.1.call-start = ((), (), s32[]{:S(2)}) async-start(), calls=%async_computation.4 | async-start | bytes 4456448 | tf_op jit(solution)/shard_map/all_gather | solution.py:42
  57.5 165.3 %reduce-scatter.2.cloned.1.call-start = ((), (), s32[]{:S(2)}) async-start(), calls=%async_computation.5 | async-start | bytes 8912896 | tf_op jit(solution)/shard_map/reduce_scatter | solution.py:54
  58.0 22.3 %copy-start.4 = (bf16[256,256]{1,0:T(8,128)(2,1)S(1)}, bf16[256,256]{1,0:T(8,128)(2,1)}, u32[]{:S(2)}) copy-start(bf16[256,256]{1,0:T(8,128)(2,1)} %param.9) | copy-start | bytes 393220
  79.5 0.8 copy-start.1
  136.2 1.0 copy-start.2
  136.2 1.1 copy-start.3
  147.2 2.3 collective-permute-start
  149.5 7.7 %collective-permute-start.1 = (f32[256,256]{1,0:T(8,128)S(1)}, f32[256,256]{1,0:T(8,128)S(1)}, u32[]{:S(2)}, u32[]{:S(2)}) collective-permute-start(f32[256,256]{1,0:T(8,128)S(1)} %add.125), channel_id=1, source_target_pairs={{0,2},{1,3},{2,0},{3,1},{4,6},{5,7},{6,4},{7,5},{8,10},{9,11},{10,... | collective-permute-start | bytes 786440 | tf_op jit(solution)/shard_map/ppermute | solution.py:21
  157.2 8.3 %collective-permute-start.2 = (f32[256,256]{1,0:T(8,128)S(1)}, f32[256,256]{1,0:T(8,128)S(1)}, u32[]{:S(2)}, u32[]{:S(2)}) collective-permute-start(f32[256,256]{1,0:T(8,128)S(1)} %add.126), channel_id=1, source_target_pairs={{0,4},{1,5},{2,6},{3,7},{4,0},{5,1},{6,2},{7,3},{8,12},{9,13},{10,... | collective-permute-start | bytes 786440 | tf_op jit(solution)/shard_map/ppermute | solution.py:21
  165.6 71.1 %collective-permute-start.3 = (f32[256,256]{1,0:T(8,128)S(1)}, f32[256,256]{1,0:T(8,128)S(1)}, u32[]{:S(2)}, u32[]{:S(2)}) collective-permute-start(f32[256,256]{1,0:T(8,128)S(1)} %add.127), channel_id=1, source_target_pairs={{0,8},{1,9},{2,10},{3,11},{4,12},{5,13},{6,14},{7,15},{8,0},{9,1},... | collective-permute-start | bytes 786440 | tf_op jit(solution)/shard_map/ppermute | solution.py:21
  227.5 44.3 %all-to-all-start.2 = ((f32[128,8,256]{2,1,0:T(8,128)}), f32[128,8,256]{2,1,0:T(8,128)S(1)}, u32[]{:S(2)}, u32[]{:S(2)}) async-start(f32[128,8,256]{2,1,0:T(8,128)} %bitcast.11), calls=%async_computation.3 | async-start | bytes 2097152 | tf_op jit(solution)/shard_map/all_to_all | solution.py:58
  236.7 19.7 %collective-permute-start.4 = (f32[256,256]{1,0:T(8,128)S(1)}, f32[256,256]{1,0:T(8,128)S(1)}, u32[]{:S(2)}, u32[]{:S(2)}) collective-permute-start(f32[256,256]{1,0:T(8,128)S(1)} %add.128), channel_id=1, source_target_pairs={{0,16},{1,17},{2,18},{3,19},{4,20},{5,21},{6,22},{7,23},{8,24},{9,... | collective-permute-start | bytes 786440 | tf_op jit(solution)/shard_map/ppermute | solution.py:21
  256.4 7.0 %collective-permute-start.5 = (f32[256,256]{1,0:T(8,128)S(1)}, f32[256,256]{1,0:T(8,128)S(1)}, u32[]{:S(2)}, u32[]{:S(2)}) collective-permute-start(f32[256,256]{1,0:T(8,128)S(1)} %add.129), channel_id=1, source_target_pairs={{0,32},{1,33},{2,34},{3,35},{4,36},{5,37},{6,38},{7,39},{8,40},{9,... | collective-permute-start | bytes 786440 | tf_op jit(solution)/shard_map/ppermute | solution.py:21
  263.5 7.6 %collective-permute-start.6 = (f32[256,256]{1,0:T(8,128)S(1)}, f32[256,256]{1,0:T(8,128)S(1)}, u32[]{:S(2)}, u32[]{:S(2)}) collective-permute-start(f32[256,256]{1,0:T(8,128)S(1)} %add.130), channel_id=1, source_target_pairs={{0,64},{1,65},{2,66},{3,67},{4,68},{5,69},{6,70},{7,71},{8,72},{9,... | collective-permute-start | bytes 786440 | tf_op jit(solution)/shard_map/ppermute | solution.py:21
Sparse Core Ops, SparseCore 0:
  57.6 47.3 all-gather.1
  136.3 86.3 reduce-scatter.1

commit v2 on v1

--- a/solution.py
+++ b/solution.py
@@ -39,6 +39,7 @@
     looked = jnp.take(query_table, query_ids, axis=0).astype(jnp.float32)
     hidden = jnp.mean(looked, axis=1).astype(jnp.bfloat16)
     queries = jnp.dot(hidden, query_weight, preferred_element_type=jnp.float32).astype(jnp.bfloat16)
+    group_queries = lax.all_gather(queries, "batch", axis=0, tiled=True)
     group_items = lax.all_gather(item_vectors, "batch", axis=0, tiled=True)
     scores = scaling * lax.dot_general(
         queries, group_items, (((1,), (1,)), ((), ())), preferred_element_type=jnp.float32
@@ -48,10 +49,12 @@
     soft_weights = jnp.exp(scores - totals).astype(jnp.bfloat16)
     pulled = jnp.dot(soft_weights, group_items, preferred_element_type=jnp.float32)
     query_grad = scaling * (pulled - item_vectors.astype(jnp.float32))
-    term_rows = lax.dot_general(
-        soft_weights, queries, (((0,), (0,)), ((), ())), preferred_element_type=jnp.float32
+    group_totals = lax.all_gather(totals.reshape(1, -1), "batch", axis=1, tiled=True)
+    scores_back = scaling * lax.dot_general(
+        item_vectors, group_queries, (((1,), (1,)), ((), ())), preferred_element_type=jnp.float32
     )
-    summed = lax.psum_scatter(term_rows, "batch", scatter_dimension=0, tiled=True)
+    soft_back = jnp.exp(scores_back - group_totals).astype(jnp.bfloat16)
+    summed = jnp.dot(soft_back, group_queries, preferred_element_type=jnp.float32)
     item_grad = scaling * (summed - queries.astype(jnp.float32))
     slot_grads = jax.ops.segment_sum(item_grad, slot_ids, num_segments=sources * slot_cap)
     slot_grads = slot_grads.reshape(sources, slot_cap, model_width)

time: 288 us -> 238 us (0.83)
  waiting for transfers between devices: 136 us -> 70.4 us
  blocking collectives: 0 us -> 19 us
  matrix products: 32.6 us -> 29.5 us
    reduce_scatter x1 -> x0, waiting for transfers between devices: 55.9 us -> none  [local(): lax.psum_scatter(term_rows, 'batch', scatter_dimension=0, tiled=True)]
    all_gather x0 -> x1, blocking collectives: none -> 19 us  [local(): lax.all_gather(totals.reshape(1, -1), 'batch', axis=1, tiled=True)]
    ppermute x7, waiting for transfers between devices: 38.7 us -> 29.9 us  [butterfly_sum(): value = value + lax.ppermute(value, axes, pairs)]
    dot_general x1, matrix products: 12.3 us -> 8.15 us  [local(): jnp.dot(soft_back, group_queries, preferred_element_type=jnp.float32)]
  transfers between devices with their start and end apart: 12 -> 12, of which waited for: 10 -> 7; matrix products, arithmetic and copies ran while one was open for 16% -> 34% of each run, Pallas kernels for 0% -> 0%
where the time goes in v2:
time: 238 us; the launch traced here: 237 us
  waiting for transfers between devices  70.4 us (30%)
  starting transfers between devices  42.3 us (18%)
  other arithmetic  31.9 us (13%)
  matrix products  29.5 us (12%)
  local copies, waits for them, and re-layouts  29.2 us (12%)
  blocking collectives  19 us (8%)
  between operations  14.4 us (6%)
    ppermute x7, waiting for transfers between devices, butterfly_sum(): value = value + lax.ppermute(value, axes, pairs)  29.9 us
    all_gather x1, waiting for transfers between devices, local(): group_items = lax.all_gather(item_vectors, 'batch', axis=0, tiled=True)  23.7 us
    all_gather x1, blocking collectives, local(): lax.all_gather(totals.reshape(1, -1), 'batch', axis=1, tiled=True)  19 us
    gather x1, local copies, waits for them, and re-layouts, local(): looked = jnp.take(query_table, query_ids, axis=0).astype(jnp.float32)  15.8 us
    all_to_all x1, waiting for transfers between devices, local(): lax.all_to_all(found_rows, ('batch', 'table'), split_axis=0, concat_axis=...  13.4 us
    ppermute x7, starting transfers between devices, butterfly_sum(): value = value + lax.ppermute(value, axes, pairs)  13 us
    all_to_all x1, starting transfers between devices, local(): lax.all_to_all(requests, ('batch', 'table'), split_axis=0, concat_axis=0,...  11.5 us
    all_to_all x1, starting transfers between devices, local(): lax.all_to_all(slot_grads, ('batch', 'table'), split_axis=0, concat_axis=...  11 us
  transfers between devices with their start and end apart: 12, of which 7 were waited for; matrix products, arithmetic and copies ran while one was open for 34% of the time, Pallas kernels for 0%

profile of v2, /device:TPU:1, one launch (start us, length us, event | category | flops | bytes accessed | tf_op | source)
XLA Modules:
  0.0 236.7 jit_solution(15056156169078863793)
XLA Ops:
  7.2 0.0 copy-start
  7.2 1.5 copy.22
  8.7 11.5 %all-to-all-start = ((s32[128,1,8]{2,1,0:T(1,128)}), s32[128,1,8]{2,1,0:T(1,128)S(1)}, u32[]{:S(2)}, u32[]{:S(2)}) async-start(s32[128,1,8]{2,1,0:T(1,128)} %bitcast), calls=%async_computation | async-start | bytes 131072 | tf_op jit(solution)/shard_map/all_to_all | solution.py:32
  20.2 0.8 copy.23
  20.9 0.2 reduce-window.8
  21.1 0.1 reduce.1
  21.2 0.7 bitcast_subtract_fusion
  21.9 0.9 convert_reduce_fusion.1
  22.8 0.0 copy-start.7
  22.8 3.3 %gather_fusion = s32[512]{0:T(512)S(1)} fusion(s32[128]{0:T(128)S(1)} %bitcast_subtract_fusion, s32[1024]{0:T(1024)S(1)} %pad_clamp_fusion.1), kind=kCustom, calls=%fused_computation | custom fusion | bytes 6144 | tf_op jit(solution)/shard_map/jit(_take)/gather | solution.py:11
  26.2 3.3 %all-to-all-done = s32[128,1,8]{2,1,0:T(1,128)S(1)} async-done(((s32[128,1,8]{2,1,0:T(1,128)}), s32[128,1,8]{2,1,0:T(1,128)S(1)}, u32[]{:S(2)}, u32[]{:S(2)}) %all-to-all-start) | async-done | bytes 4128 | tf_op jit(solution)/shard_map/all_to_all | solution.py:32
  29.5 0.1 reshape.182
  29.7 0.0 copy-start.6
  29.7 3.9 %gather_fusion.1 = bf16[1024,256]{1,0:T(8,128)(2,1)S(1)} fusion(bf16[2048,256]{1,0:T(8,128)(2,1)S(1)} %copy-done, s32[1024]{0:T(1024)S(1)} %broadcast_clamp_fusion.1), kind=kCustom, calls=%fused_computation.1 | custom fusion | bytes 1052672 | tf_op jit(solution)/shard_map/jit(_take)/gather | solution.py:33
  33.7 1.0 bitcast_select_fusion.1
  34.7 6.4 %all-to-all-start.1 = ((bf16[128,8,256]{2,1,0:T(8,128)(2,1)}), bf16[128,8,256]{2,1,0:T(8,128)(2,1)S(1)}, u32[]{:S(2)}, u32[]{:S(2)}) async-start(bf16[128,8,256]{2,1,0:T(8,128)(2,1)} %bitcast_select_fusion.1), calls=%async_computation.1 | async-start | bytes 1048576 | tf_op jit(solution)/shard_map/all_to_all | solution.py:34
  41.1 0.0 all-gather.7.cloned.1.call-start
  41.2 13.4 %all-to-all-done.1 = bf16[128,8,256]{2,1,0:T(8,128)(2,1)S(1)} async-done(((bf16[128,8,256]{2,1,0:T(8,128)(2,1)}), bf16[128,8,256]{2,1,0:T(8,128)(2,1)S(1)}, u32[]{:S(2)}, u32[]{:S(2)}) %all-to-all-start.1) | async-done | bytes 524320 | tf_op jit(solution)/shard_map/all_to_all | solution.py:34
  54.6 1.9 gather_fusion.2
  56.6 0.9 broadcast_select_fusion
  57.5 0.0 all-gather.7.cloned.1.call-update
  57.5 0.2 all-gather.5.cloned.1.call-start
  57.7 0.0 copy-done.6
  57.7 0.1 copy.25
  57.9 0.2 reshape.198
  58.0 0.2 copy.24
  58.2 0.0 copy-start.5
  58.2 15.8 %gather_fusion.3 = bf16[4096,256]{1,0:T(8,128)(2,1)S(1)} fusion(bf16[8192,256]{1,0:T(8,128)(2,1)} %param.8, s32[4096]{0:T(1024)S(1)} %broadcast_clamp_fusion), kind=kCustom, calls=%fused_computation.3 | custom fusion | bytes 4210688 | tf_op jit(solution)/shard_map/jit(_take)/gather | solution.py:39
  74.0 5.6 %convert_reduce_fusion = f32[512,256]{1,0:T(8,128)S(1)} fusion(bf16[4096,256]{1,0:T(8,128)(2,1)S(1)} %gather_fusion.3, pred[512,8]{1,0:T(8,128)(4,1)S(1)} %copy.24), kind=kLoop, calls=%fused_computation.13 | loop fusion | flops 3014656 | bytes 2625536 | tf_op jit(solution)/shard_map/reduce_sum | solution.py:40
  79.6 0.0 copy-start.2
  79.6 0.8 copy-done.2
  80.4 0.9 convolution_convert_fusion
  81.3 0.0 all-gather.5.cloned.1.call-update
  81.3 23.7 %all-gather.7.cloned.1.call-done = bf16[8192,256]{1,0:T(8,128)(2,1)} async-done(((bf16[512,256]{1,0:T(8,128)(2,1)}), bf16[8192,256]{1,0:T(8,128)(2,1)}) %all-gather.7.cloned.1.call-update) | async-done | bytes 4194320 | tf_op jit(solution)/shard_map/all_gather | solution.py:43
  105.0 10.4 %multiply_reduce_fusion = (f32[512]{0:T(512)S(1)}, f32[512,8192]{1,0:T(8,128)}) fusion(bf16[512,256]{1,0:T(8,128)(2,1)} %convolution_convert_fusion, bf16[8192,256]{1,0:T(8,128)(2,1)} %all-gather.7.cloned.1.call-done), kind=kOutput, calls=%fused_computation.9 | convolution fusion | flops 2155871744 | bytes 21235712 | tf_op jit(solution)/shard_map/dot_general | solution.py:44
  115.4 9.0 %exponential_reduce_fusion = f32[512]{0:T(512)S(1)} fusion(f32[512,8192]{1,0:T(8,128)} %get-tuple-element.5, f32[512]{0:T(512)S(1)} %get-tuple-element.4), kind=kLoop, calls=%fused_computation.8 | loop fusion | flops 12582400 | bytes 16781312 | tf_op jit(solution)/shard_map/reduce_sum | solution.py:48
  124.4 0.0 copy-done.3
  124.4 0.0 copy-done.4
  124.4 0.0 copy-start.1
  124.4 10.0 %fusion.7 = f32[256,256]{1,0:T(8,128)S(1)} fusion(bf16[8192,256]{1,0:T(8,128)(2,1)} %all-gather.7.cloned.1.call-done, f32[512,8192]{1,0:T(8,128)} %get-tuple-element.5, f32[512]{0:T(512)S(1)} %log_add_fusion, bf16[512,256]{1,0:T(8,128)(2,1)S(1)} %copy-done.4, f32[512,256]{1,0:T(8,128)S(1)} %copy-done.3), kind=kOutput, calls=%fused_computation.21 | convolution fusion | flops 2227961856 | bytes 22022144 | tf_op jit(solution)/shard_map/dot_general | solution.py:69
  134.4 0.9 collective-permute-start
  135.4 1.2 collective-permute-done
  136.6 1.6 collective-permute-start.1
  138.1 6.3 %collective-permute-done.1 = f32[256,256]{1,0:T(8,128)S(1)} collective-permute-done((f32[256,256]{1,0:T(8,128)S(1)}, f32[256,256]{1,0:T(8,128)S(1)}, u32[]{:S(2)}, u32[]{:S(2)}) %collective-permute-start.1) | collective-permute-done | bytes 262176 | tf_op jit(solution)/shard_map/ppermute | solution.py:21
  144.5 2.9 %collective-permute-start.2 = (f32[256,256]{1,0:T(8,128)S(1)}, f32[256,256]{1,0:T(8,128)S(1)}, u32[]{:S(2)}, u32[]{:S(2)}) collective-permute-start(f32[256,256]{1,0:T(8,128)S(1)} %add.135), channel_id=1, source_target_pairs={{0,4},{1,5},{2,6},{3,7},{4,0},{5,1},{6,2},{7,3},{8,12},{9,13},{10,... | collective-permute-start | bytes 786440 | tf_op jit(solution)/shard_map/ppermute | solution.py:21
  147.5 19.0 %all-gather.1 = f32[16,1,512]{2,1,0:T(1,128)S(1)} all-gather(f32[1,1,512]{2,1,0:T(1,128)S(1)} %bitcast.45), channel_id=2, replica_groups=mesh['batch'=16,'table'=8] {'batch'}, dimensions={0}, use_global_device_ids=true | all-gather | bytes 34816 | tf_op jit(solution)/shard_map/all_gather | solution.py:52
  166.5 0.0 collective-permute-done.2
  166.5 0.3 collective-permute-start.3
  166.9 8.1 %fusion.5 = f32[512,256]{1,0:T(8,128)S(1)} fusion(bf16[8192,256]{1,0:T(8,128)(2,1)} %all-gather.5.cloned.1.call-done, bf16[512,256]{1,0:T(8,128)(2,1)S(1)} %copy-done.1, bf16[512,256]{1,0:T(8,128)(2,1)S(1)} %copy-done.4, f32[8192]{0:T(1024)S(1)} %bitcast.43), kind=kOutput, calls=%fused_computation.18 | convolution fusion | flops 4307943424 | bytes 5275648 | tf_op jit(solution)/shard_map/dot_general | solution.py:57
  175.0 4.3 %scatter_custom_fusion = f32[1024,256]{1,0:T(8,128)} fusion(s32[512]{0:T(512)S(1)} %get-tuple-element.3, f32[512,256]{1,0:T(8,128)S(1)} %fusion.5, f32[]{:T(128)} %constant.40.clone.1), kind=kCustom, calls=%fused_computation.28 | custom fusion | flops 131072 | bytes 1048580 | tf_op jit(solution)/shard_map/scatter-add | solution.py:59
  179.3 11.0 %all-to-all-start.2 = ((f32[128,8,256]{2,1,0:T(8,128)}), f32[128,8,256]{2,1,0:T(8,128)S(1)}, u32[]{:S(2)}, u32[]{:S(2)}) async-start(f32[128,8,256]{2,1,0:T(8,128)} %bitcast.13), calls=%async_computation.2 | async-start | bytes 2097152 | tf_op jit(solution)/shard_map/all_to_all | solution.py:61
  190.4 0.0 collective-permute-done.3
  190.4 2.9 %collective-permute-start.4 = (f32[256,256]{1,0:T(8,128)S(1)}, f32[256,256]{1,0:T(8,128)S(1)}, u32[]{:S(2)}, u32[]{:S(2)}) collective-permute-start(f32[256,256]{1,0:T(8,128)S(1)} %add.137), channel_id=1, source_target_pairs={{0,16},{1,17},{2,18},{3,19},{4,20},{5,21},{6,22},{7,23},{8,24},{9,... | collective-permute-start | bytes 786440 | tf_op jit(solution)/shard_map/ppermute | solution.py:21
  193.3 16.7 %collective-permute-done.4 = f32[256,256]{1,0:T(8,128)S(1)} collective-permute-done((f32[256,256]{1,0:T(8,128)S(1)}, f32[256,256]{1,0:T(8,128)S(1)}, u32[]{:S(2)}, u32[]{:S(2)}) %collective-permute-start.4) | collective-permute-done | bytes 262176 | tf_op jit(solution)/shard_map/ppermute | solution.py:21
  210.1 1.3 collective-permute-start.5
  211.4 5.7 %collective-permute-done.5 = f32[256,256]{1,0:T(8,128)S(1)} collective-permute-done((f32[256,256]{1,0:T(8,128)S(1)}, f32[256,256]{1,0:T(8,128)S(1)}, u32[]{:S(2)}, u32[]{:S(2)}) %collective-permute-start.5) | collective-permute-done | bytes 262176 | tf_op jit(solution)/shard_map/ppermute | solution.py:21
  217.1 3.1 %collective-permute-start.6 = (f32[256,256]{1,0:T(8,128)S(1)}, f32[256,256]{1,0:T(8,128)S(1)}, u32[]{:S(2)}, u32[]{:S(2)}) collective-permute-start(f32[256,256]{1,0:T(8,128)S(1)} %add.139), channel_id=1, source_target_pairs={{0,64},{1,65},{2,66},{3,67},{4,68},{5,69},{6,70},{7,71},{8,72},{9,... | collective-permute-start | bytes 786440 | tf_op jit(solution)/shard_map/ppermute | solution.py:21
  220.2 0.5 broadcast.120
  220.7 0.8 reduce.4
  221.5 0.1 reshape.165
  221.6 0.0 all-to-all-done.2
  221.6 7.5 %scatter_custom_fusion.1 = f32[2048,256]{1,0:T(8,128)} fusion(s32[1024]{0:T(1024)S(1)} %bitcast.47, f32[128,8,256]{2,1,0:T(8,128)S(1)} %all-to-all-done.2, f32[]{:T(128)} %constant.40.clone.1), kind=kCustom, calls=%fused_computation.22 | custom fusion | flops 262144 | bytes 3145732 | tf_op jit(solution)/shard_map/scatter-add | solution.py:67
  229.1 0.0 collective-permute-done.6
  229.2 0.7 add.140
  (26 shorter events, 0.3 us)
Async XLA Ops:
  7.2 22.5 %copy-start = (bf16[2048,256]{1,0:T(8,128)(2,1)S(1)}, bf16[2048,256]{1,0:T(8,128)(2,1)}, u32[]{:S(2)}) copy-start(bf16[2048,256]{1,0:T(8,128)(2,1)} %param.7) | copy-start | bytes 3145732
  8.7 20.9 %all-to-all-start = ((s32[128,1,8]{2,1,0:T(1,128)}), s32[128,1,8]{2,1,0:T(1,128)S(1)}, u32[]{:S(2)}, u32[]{:S(2)}) async-start(s32[128,1,8]{2,1,0:T(1,128)} %bitcast), calls=%async_computation | async-start | bytes 131072 | tf_op jit(solution)/shard_map/all_to_all | solution.py:32
  22.8 18.3 %copy-start.7 = (s32[512]{0:T(512)S(1)}, s32[512]{0:T(512)}, u32[]{:S(2)}) copy-start(s32[512]{0:T(512)} %param.13) | copy-start | bytes 6148
  29.7 28.0 %copy-start.6 = (s32[512,8]{0,1:T(8,128)S(1)}, s32[512,8]{0,1:T(8,128)}, u32[]{:S(2)}) copy-start(s32[512,8]{0,1:T(8,128)} %param.10) | copy-start | bytes 49156
  34.7 20.0 %all-to-all-start.1 = ((bf16[128,8,256]{2,1,0:T(8,128)(2,1)}), bf16[128,8,256]{2,1,0:T(8,128)(2,1)S(1)}, u32[]{:S(2)}, u32[]{:S(2)}) async-start(bf16[128,8,256]{2,1,0:T(8,128)(2,1)} %bitcast_select_fusion.1), calls=%async_computation.1 | async-start | bytes 1048576 | tf_op jit(solution)/shard_map/all_to_all | solution.py:34
  41.1 63.9 %all-gather.7.cloned.1.call-start = ((), (), s32[]{:S(2)}) async-start(), calls=%async_computation.4 | async-start | bytes 4456448 | tf_op jit(solution)/shard_map/all_gather | solution.py:43
  57.5 109.4 %all-gather.5.cloned.1.call-start = ((), (), s32[]{:S(2)}) async-start(), calls=%async_computation.3 | async-start | bytes 4456448 | tf_op jit(solution)/shard_map/all_gather | solution.py:42
  58.2 22.1 %copy-start.5 = (bf16[256,256]{1,0:T(8,128)(2,1)S(1)}, bf16[256,256]{1,0:T(8,128)(2,1)}, u32[]{:S(2)}) copy-start(bf16[256,256]{1,0:T(8,128)(2,1)} %param.9) | copy-start | bytes 393220
  79.6 0.8 copy-start.2
  115.4 9.0 %copy-start.3 = (f32[512,256]{1,0:T(8,128)S(1)}, f32[512,256]{1,0:T(8,128)}, u32[]{:S(2)}) copy-start(f32[512,256]{1,0:T(8,128)} %copy-done.2) | copy-start | bytes 1572868
  115.4 9.0 %copy-start.4 = (bf16[512,256]{1,0:T(8,128)(2,1)S(1)}, bf16[512,256]{1,0:T(8,128)(2,1)}, u32[]{:S(2)}) copy-start(bf16[512,256]{1,0:T(8,128)(2,1)} %broadcast_select_fusion) | copy-start | bytes 786436
  124.4 42.4 %copy-start.1 = (bf16[512,256]{1,0:T(8,128)(2,1)S(1)}, bf16[512,256]{1,0:T(8,128)(2,1)}, u32[]{:S(2)}) copy-start(bf16[512,256]{1,0:T(8,128)(2,1)} %convolution_convert_fusion) | copy-start | bytes 786436
  134.4 2.1 collective-permute-start
  136.6 7.9 %collective-permute-start.1 = (f32[256,256]{1,0:T(8,128)S(1)}, f32[256,256]{1,0:T(8,128)S(1)}, u32[]{:S(2)}, u32[]{:S(2)}) collective-permute-start(f32[256,256]{1,0:T(8,128)S(1)} %add.134), channel_id=1, source_target_pairs={{0,2},{1,3},{2,0},{3,1},{4,6},{5,7},{6,4},{7,5},{8,10},{9,11},{10,... | collective-permute-start | bytes 786440 | tf_op jit(solution)/shard_map/ppermute | solution.py:21
  144.5 22.0 %collective-permute-start.2 = (f32[256,256]{1,0:T(8,128)S(1)}, f32[256,256]{1,0:T(8,128)S(1)}, u32[]{:S(2)}, u32[]{:S(2)}) collective-permute-start(f32[256,256]{1,0:T(8,128)S(1)} %add.135), channel_id=1, source_target_pairs={{0,4},{1,5},{2,6},{3,7},{4,0},{5,1},{6,2},{7,3},{8,12},{9,13},{10,... | collective-permute-start | bytes 786440 | tf_op jit(solution)/shard_map/ppermute | solution.py:21
  166.5 23.8 %collective-permute-start.3 = (f32[256,256]{1,0:T(8,128)S(1)}, f32[256,256]{1,0:T(8,128)S(1)}, u32[]{:S(2)}, u32[]{:S(2)}) collective-permute-start(f32[256,256]{1,0:T(8,128)S(1)} %add.136), channel_id=1, source_target_pairs={{0,8},{1,9},{2,10},{3,11},{4,12},{5,13},{6,14},{7,15},{8,0},{9,1},... | collective-permute-start | bytes 786440 | tf_op jit(solution)/shard_map/ppermute | solution.py:21
  179.3 42.3 %all-to-all-start.2 = ((f32[128,8,256]{2,1,0:T(8,128)}), f32[128,8,256]{2,1,0:T(8,128)S(1)}, u32[]{:S(2)}, u32[]{:S(2)}) async-start(f32[128,8,256]{2,1,0:T(8,128)} %bitcast.13), calls=%async_computation.2 | async-start | bytes 2097152 | tf_op jit(solution)/shard_map/all_to_all | solution.py:61
  190.4 19.7 %collective-permute-start.4 = (f32[256,256]{1,0:T(8,128)S(1)}, f32[256,256]{1,0:T(8,128)S(1)}, u32[]{:S(2)}, u32[]{:S(2)}) collective-permute-start(f32[256,256]{1,0:T(8,128)S(1)} %add.137), channel_id=1, source_target_pairs={{0,16},{1,17},{2,18},{3,19},{4,20},{5,21},{6,22},{7,23},{8,24},{9,... | collective-permute-start | bytes 786440 | tf_op jit(solution)/shard_map/ppermute | solution.py:21
  210.1 7.0 %collective-permute-start.5 = (f32[256,256]{1,0:T(8,128)S(1)}, f32[256,256]{1,0:T(8,128)S(1)}, u32[]{:S(2)}, u32[]{:S(2)}) collective-permute-start(f32[256,256]{1,0:T(8,128)S(1)} %add.138), channel_id=1, source_target_pairs={{0,32},{1,33},{2,34},{3,35},{4,36},{5,37},{6,38},{7,39},{8,40},{9,... | collective-permute-start | bytes 786440 | tf_op jit(solution)/shard_map/ppermute | solution.py:21
  217.1 12.0 %collective-permute-start.6 = (f32[256,256]{1,0:T(8,128)S(1)}, f32[256,256]{1,0:T(8,128)S(1)}, u32[]{:S(2)}, u32[]{:S(2)}) collective-permute-start(f32[256,256]{1,0:T(8,128)S(1)} %add.139), channel_id=1, source_target_pairs={{0,64},{1,65},{2,66},{3,67},{4,68},{5,69},{6,70},{7,71},{8,72},{9,... | collective-permute-start | bytes 786440 | tf_op jit(solution)/shard_map/ppermute | solution.py:21
Sparse Core Ops, SparseCore 0:
  57.6 47.3 all-gather.6
  107.7 50.9 all-gather.4

commit v3 on v2

--- a/solution.py
+++ b/solution.py
@@ -1,7 +1,69 @@
+import functools
+
 import jax
 import jax.numpy as jnp
 from jax import lax
+from jax.experimental import pallas as pl
+from jax.experimental.pallas import tpu as pltpu
 from jax.sharding import PartitionSpec as P
+
+
+def forward_block(q_ref, items_ref, own_ref, grad_ref, totals_ref, *, scaling):
+    scores = scaling * lax.dot_general(
+        q_ref[...], items_ref[...], (((1,), (1,)), ((), ())), preferred_element_type=jnp.float32
+    )
+    highest = jnp.max(scores, axis=1, keepdims=True)
+    totals = highest + jnp.log(jnp.sum(jnp.exp(scores - highest), axis=1, keepdims=True))
+    soft_weights = jnp.exp(scores - totals).astype(jnp.bfloat16)
+    pulled = jnp.dot(soft_weights, items_ref[...], preferred_element_type=jnp.float32)
+    grad_ref[...] = scaling * (pulled - own_ref[...].astype(jnp.float32))
+    totals_ref[...] = jnp.broadcast_to(totals, totals_ref.shape)
+
+
+def forward(queries, group_items, item_vectors, tile=256):
+    rows, width = queries.shape
+    group = group_items.shape[0]
+    return pl.pallas_call(
+        functools.partial(forward_block, scaling=width ** (-0.5)),
+        grid=(rows // tile,),
+        in_specs=[
+            pl.BlockSpec((tile, width), lambda i: (i, 0)),
+            pl.BlockSpec((group, width), lambda i: (0, 0)),
+            pl.BlockSpec((tile, width), lambda i: (i, 0)),
+        ],
+        out_specs=[
+            pl.BlockSpec((tile, width), lambda i: (i, 0)),
+            pl.BlockSpec((tile, 128), lambda i: (i, 0)),
+        ],
+        out_shape=[
+            jax.ShapeDtypeStruct((rows, width), jnp.float32),
+            jax.ShapeDtypeStruct((rows, 128), jnp.float32),
+        ],
+        compiler_params=pltpu.CompilerParams(vmem_limit_bytes=48 * 1024 * 1024),
+    )(queries, group_items, item_vectors)
+
+
+def plane_gather(value, axis, side):
+    size = side * side
+    index = lax.axis_index(axis)
+    column = index % side
+    line = index // side
+
+    def shift(piece, step, along_row):
+        pairs = []
+        for source in range(size):
+            high, low = divmod(source, side)
+            if along_row:
+                target = high * side + (low + step) % side
+            else:
+                target = ((high + step) % side) * side + low
+            pairs.append((source, target))
+        return lax.ppermute(piece, axis, pairs)
+
+    pieces = jnp.stack([value] + [shift(value, step, True) for step in range(1, side)])
+    row = jnp.concatenate([jnp.take(pieces, (column - c) % side, axis=0) for c in range(side)], axis=1)
+    rows = jnp.stack([row] + [shift(row, step, False) for step in range(1, side)])
+    return jnp.concatenate([jnp.take(rows, (line - r) % side, axis=0) for r in range(side)], axis=1)
 
 
 def slot_index(live_slots, positions, slot_cap):
@@ -41,15 +103,12 @@
     queries = jnp.dot(hidden, query_weight, preferred_element_type=jnp.float32).astype(jnp.bfloat16)
     group_queries = lax.all_gather(queries, "batch", axis=0, tiled=True)
     group_items = lax.all_gather(item_vectors, "batch", axis=0, tiled=True)
-    scores = scaling * lax.dot_general(
-        queries, group_items, (((1,), (1,)), ((), ())), preferred_element_type=jnp.float32
-    )
-    highest = jnp.max(scores, axis=1, keepdims=True)
-    totals = highest + jnp.log(jnp.sum(jnp.exp(scores - highest), axis=1, keepdims=True))
-    soft_weights = jnp.exp(scores - totals).astype(jnp.bfloat16)
-    pulled = jnp.dot(soft_weights, group_items, preferred_element_type=jnp.float32)
-    query_grad = scaling * (pulled - item_vectors.astype(jnp.float32))
-    group_totals = lax.all_gather(totals.reshape(1, -1), "batch", axis=1, tiled=True)
+    query_grad, totals = forward(queries, group_items, item_vectors)
+    side = int(round(lax.axis_size("batch") ** 0.5))
+    if side * side == lax.axis_size("batch"):
+        group_totals = plane_gather(totals[:, :1].reshape(1, -1), "batch", side)
+    else:
+        group_totals = lax.all_gather(totals[:, :1].reshape(1, -1), "batch", axis=1, tiled=True)
     scores_back = scaling * lax.dot_general(
         item_vectors, group_queries, (((1,), (1,)), ((), ())), preferred_element_type=jnp.float32
     )

time: 238 us -> 233 us (0.979)
  matrix products: 29.5 us -> 10.2 us
  blocking collectives: 19 us -> 0 us
  waiting for transfers between devices: 70.4 us -> 86.1 us
  Pallas kernels: 0 us -> 14.2 us
  other arithmetic: 31.9 us -> 23.1 us
  starting transfers between devices: 42.3 us -> 50.6 us
  local copies, waits for them, and re-layouts: 29.2 us -> 32.5 us
    all_gather x1 -> x0, blocking collectives: 19 us -> none  [local(): lax.all_gather(totals.reshape(1, -1), 'batch', axis=1, tiled=True)]
    pallas_call x0 -> x1, Pallas kernels: none -> 14.2 us  [forward(): pl.pallas_call(functools.partial(forward_block, scaling=width ** (-0.5)),...]
    all_gather x1, waiting for transfers between devices: 0.01 us -> 13.4 us  [local(): group_queries = lax.all_gather(queries, 'batch', axis=0, tiled=True)]
    dot_general x1 -> x0, matrix products: 10.4 us -> none  [local(): lax.dot_general(queries, group_items, (((1,), (1,)), ((), ())), preferred...]
    dot_general x1, matrix products: 9.99 us -> 0.27 us  [local(): lax.dot_general(hidden, query_grad.astype(jnp.bfloat16), (((0,), (0,)), (...]
    reduce_sum x1 -> x0, other arithmetic: 8.97 us -> none  [local(): jnp.sum(jnp.exp(scores - highest), axis=1, keepdims=True)]
    ppermute x0 -> x6, starting transfers between devices: none -> 8.01 us  [shift(): return lax.ppermute(piece, axis, pairs)]
    unnamed x17 -> x19, local copies, waits for them, and re-layouts: 2.33 us -> 5.46 us
  transfers between devices with their start and end apart: 12 -> 18, of which waited for: 7 -> 10; matrix products, arithmetic and copies ran while one was open for 34% -> 22% of each run, Pallas kernels for 0% -> 6%
where the time goes in v3:
time: 233 us; the launch traced here: 231 us
  waiting for transfers between devices  86.1 us (37%)
  starting transfers between devices  50.6 us (22%)
  local copies, waits for them, and re-layouts  32.5 us (14%)
  other arithmetic  23.1 us (10%)
  between operations  14.6 us (6%)
  Pallas kernels  14.2 us (6%)
  matrix products  10.2 us (4%)
    ppermute x7, waiting for transfers between devices, butterfly_sum(): value = value + lax.ppermute(value, axes, pairs)  32.2 us
    all_gather x1, waiting for transfers between devices, local(): group_items = lax.all_gather(item_vectors, 'batch', axis=0, tiled=True)  22.6 us
    gather x1, local copies, waits for them, and re-layouts, local(): looked = jnp.take(query_table, query_ids, axis=0).astype(jnp.float32)  15.7 us
    pallas_call x1, Pallas kernels, forward(): pl.pallas_call(functools.partial(forward_block, scaling=width ** (-0.5)),...  14.2 us
    all_to_all x1, waiting for transfers between devices, local(): lax.all_to_all(found_rows, ('batch', 'table'), split_axis=0, concat_axis=...  13.4 us
    ppermute x7, starting transfers between devices, butterfly_sum(): value = value + lax.ppermute(value, axes, pairs)  13.4 us
    all_gather x1, waiting for transfers between devices, local(): group_queries = lax.all_gather(queries, 'batch', axis=0, tiled=True)  13.4 us
    all_to_all x1, starting transfers between devices, local(): lax.all_to_all(requests, ('batch', 'table'), split_axis=0, concat_axis=0,...  11.5 us
  transfers between devices with their start and end apart: 18, of which 10 were waited for; matrix products, arithmetic and copies ran while one was open for 22% of the time, Pallas kernels for 6%

profile of v3, /device:TPU:1, one launch (start us, length us, event | category | flops | bytes accessed | tf_op | source)
XLA Modules:
  0.0 231.4 jit_solution(2663617069437215297)
XLA Ops:
  7.2 0.0 copy-start
  7.2 1.5 copy.22
  8.7 11.5 %all-to-all-start = ((s32[128,1,8]{2,1,0:T(1,128)}), s32[128,1,8]{2,1,0:T(1,128)S(1)}, u32[]{:S(2)}, u32[]{:S(2)}) async-start(s32[128,1,8]{2,1,0:T(1,128)} %bitcast), calls=%async_computation | async-start | bytes 131072 | tf_op jit(solution)/shard_map/all_to_all | solution.py:94
  20.2 0.8 copy.23
  20.9 0.2 reduce-window.8
  21.1 0.1 reduce.1
  21.2 0.7 bitcast_subtract_fusion
  21.9 0.9 convert_reduce_fusion.1
  22.8 3.3 %gather_fusion = s32[512]{0:T(512)S(1)} fusion(s32[128]{0:T(128)S(1)} %bitcast_subtract_fusion, s32[1024]{0:T(1024)S(1)} %pad_clamp_fusion.1), kind=kCustom, calls=%fused_computation | custom fusion | bytes 6144 | tf_op jit(solution)/shard_map/jit(_take)/gather | solution.py:73
  26.2 3.3 %all-to-all-done = s32[128,1,8]{2,1,0:T(1,128)S(1)} async-done(((s32[128,1,8]{2,1,0:T(1,128)}), s32[128,1,8]{2,1,0:T(1,128)S(1)}, u32[]{:S(2)}, u32[]{:S(2)}) %all-to-all-start) | async-done | bytes 4128 | tf_op jit(solution)/shard_map/all_to_all | solution.py:94
  29.6 0.1 reshape.320
  29.7 0.0 copy-start.7
  29.7 3.9 %gather_fusion.1 = bf16[1024,256]{1,0:T(8,128)(2,1)S(1)} fusion(bf16[2048,256]{1,0:T(8,128)(2,1)S(1)} %copy-done, s32[1024]{0:T(1024)S(1)} %broadcast_clamp_fusion.1), kind=kCustom, calls=%fused_computation.1 | custom fusion | bytes 1052672 | tf_op jit(solution)/shard_map/jit(_take)/gather | solution.py:95
  33.7 1.0 bitcast_select_fusion.1
  34.7 6.4 %all-to-all-start.1 = ((bf16[128,8,256]{2,1,0:T(8,128)(2,1)}), bf16[128,8,256]{2,1,0:T(8,128)(2,1)S(1)}, u32[]{:S(2)}, u32[]{:S(2)}) async-start(bf16[128,8,256]{2,1,0:T(8,128)(2,1)} %bitcast_select_fusion.1), calls=%async_computation.1 | async-start | bytes 1048576 | tf_op jit(solution)/shard_map/all_to_all | solution.py:96
  41.1 0.0 all-gather.5.cloned.1.call-start
  41.2 13.4 %all-to-all-done.1 = bf16[128,8,256]{2,1,0:T(8,128)(2,1)S(1)} async-done(((bf16[128,8,256]{2,1,0:T(8,128)(2,1)}), bf16[128,8,256]{2,1,0:T(8,128)(2,1)S(1)}, u32[]{:S(2)}, u32[]{:S(2)}) %all-to-all-start.1) | async-done | bytes 524320 | tf_op jit(solution)/shard_map/all_to_all | solution.py:96
  54.6 1.9 gather_fusion.2
  56.6 0.9 broadcast_select_fusion.own_ref
  57.5 0.0 all-gather.5.cloned.1.call-update
  57.5 0.2 all-gather.3.cloned.1.call-start
  57.7 0.2 copy.24
  57.9 0.1 copy.25
  58.1 0.2 reshape.336
  58.2 15.7 %gather_fusion.3 = bf16[4096,256]{1,0:T(8,128)(2,1)S(1)} fusion(bf16[8192,256]{1,0:T(8,128)(2,1)} %param.12, s32[4096]{0:T(1024)S(1)} %broadcast_clamp_fusion), kind=kCustom, calls=%fused_computation.3 | custom fusion | bytes 4210688 | tf_op jit(solution)/shard_map/jit(_take)/gather | solution.py:101
  74.0 5.6 %convert_reduce_fusion = f32[512,256]{1,0:T(8,128)S(1)} fusion(bf16[4096,256]{1,0:T(8,128)(2,1)S(1)} %gather_fusion.3, pred[512,8]{1,0:T(8,128)(4,1)S(1)} %copy.24), kind=kLoop, calls=%fused_computation.7 | loop fusion | flops 3014656 | bytes 2625536 | tf_op jit(solution)/shard_map/reduce_sum | solution.py:102
  79.5 0.0 copy-start.5
  79.6 0.8 copy-done.5
  80.3 1.8 convolution_convert_fusion.q_ref
  82.2 0.0 all-gather.3.cloned.1.call-update
  82.4 22.6 %all-gather.5.cloned.1.call-done.items_ref = bf16[8192,256]{1,0:T(8,128)(2,1)} async-done(((bf16[512,256]{1,0:T(8,128)(2,1)}), bf16[8192,256]{1,0:T(8,128)(2,1)}) %all-gather.5.cloned.1.call-update) | async-done | bytes 4194320 | tf_op jit(solution)/shard_map/all_gather | solution.py:105
  105.0 2.2 copy-done.1
  107.2 0.9 copy-done.2
  108.2 14.2 %shard_map.86 = (f32[512,256]{1,0:T(8,128)S(1)}, f32[512,128]{1,0:T(8,128)S(1)}) custom-call(bf16[512,256]{1,0:T(8,128)(2,1)S(1)} %copy-done.2, bf16[8192,256]{1,0:T(8,128)(2,1)S(1)} %copy-done.1, bf16[512,256]{1,0:T(8,128)(2,1)S(1)} %copy-done.4), custom_call_target="tpu_custom_call" | custom-call | tf_op jit(solution)/shard_map/pallas_call | solution.py:26
  122.4 0.1 slice_reduce_fusion
  122.6 2.5 %collective-permute-start.2 = (f32[1,512]{1,0:T(1,128)S(1)}, f32[1,512]{1,0:T(1,128)S(1)}, u32[]{:S(2)}, u32[]{:S(2)}) collective-permute-start(f32[1,512]{1,0:T(1,128)S(1)} %bitcast.67), channel_id=1, source_target_pairs={{0,24},{8,0},{16,8},{24,16},{32,56},{40,32},{48,40},{56,48},{64,88... | collective-permute-start | bytes 6152 | tf_op jit(solution)/shard_map/ppermute | solution.py:61
  125.0 0.6 collective-permute-start.1
  125.6 0.6 collective-permute-start
  126.2 0.3 fusion.6
  126.5 1.8 collective-permute-start.6
  128.2 0.8 collective-permute-done.1
  129.0 0.3 collective-permute-done
  129.3 1.7 collective-permute-start.4
  131.0 0.3 collective-permute-start.3
  131.3 2.4 %collective-permute-start.5 = (f32[1,2048]{1,0:T(1,128)S(1)}, f32[1,2048]{1,0:T(1,128)S(1)}, u32[]{:S(2)}, u32[]{:S(2)}) collective-permute-start(f32[1,2048]{1,0:T(1,128)S(1)} %pad_maximum_fusion.3), channel_id=1, source_target_pairs={{0,96},{8,104},{16,112},{24,120},{32,0},{40,8},{48,16},{56,24},{64... | collective-permute-start | bytes 24584 | tf_op jit(solution)/shard_map/ppermute | solution.py:61
  133.8 1.4 collective-permute-start.7
  135.2 3.8 %collective-permute-done.7 = f32[256,256]{1,0:T(8,128)S(1)} collective-permute-done((f32[256,256]{1,0:T(8,128)S(1)}, f32[256,256]{1,0:T(8,128)S(1)}, u32[]{:S(2)}, u32[]{:S(2)}) %collective-permute-start.7) | collective-permute-done | bytes 262176 | tf_op jit(solution)/shard_map/ppermute | solution.py:83
  139.1 3.0 %collective-permute-start.8 = (f32[256,256]{1,0:T(8,128)S(1)}, f32[256,256]{1,0:T(8,128)S(1)}, u32[]{:S(2)}, u32[]{:S(2)}) collective-permute-start(f32[256,256]{1,0:T(8,128)S(1)} %add.165), channel_id=1, source_target_pairs={{0,4},{1,5},{2,6},{3,7},{4,0},{5,1},{6,2},{7,3},{8,12},{9,13},{10,... | collective-permute-start | bytes 786440 | tf_op jit(solution)/shard_map/ppermute | solution.py:83
  142.1 5.9 %collective-permute-done.8 = f32[256,256]{1,0:T(8,128)S(1)} collective-permute-done((f32[256,256]{1,0:T(8,128)S(1)}, f32[256,256]{1,0:T(8,128)S(1)}, u32[]{:S(2)}, u32[]{:S(2)}) %collective-permute-start.8) | collective-permute-done | bytes 262176 | tf_op jit(solution)/shard_map/ppermute | solution.py:83
  148.0 0.1 collective-permute-start.9
  148.1 13.4 %all-gather.3.cloned.1.call-done = bf16[8192,256]{1,0:T(8,128)(2,1)} async-done(((bf16[512,256]{1,0:T(8,128)(2,1)}), bf16[8192,256]{1,0:T(8,128)(2,1)}) %all-gather.3.cloned.1.call-update) | async-done | bytes 4194320 | tf_op jit(solution)/shard_map/all_gather | solution.py:104
  161.5 8.1 %fusion = f32[512,256]{1,0:T(8,128)S(1)} fusion(bf16[8192,256]{1,0:T(8,128)(2,1)} %all-gather.3.cloned.1.call-done, bf16[512,256]{1,0:T(8,128)(2,1)S(1)} %copy-done.3, bf16[512,256]{1,0:T(8,128)(2,1)S(1)} %copy-done.4, f32[8192]{0:T(1024)S(1)} %bitcast.65), kind=kOutput, calls=%fused_computation.10 | convolution fusion | flops 4307943424 | bytes 5275648 | tf_op jit(solution)/shard_map/dot_general | solution.py:116
  169.7 4.3 %scatter_custom_fusion = f32[1024,256]{1,0:T(8,128)} fusion(s32[512]{0:T(512)S(1)} %get-tuple-element.31, f32[512,256]{1,0:T(8,128)S(1)} %fusion, f32[]{:T(128)} %constant.149.clone.1), kind=kCustom, calls=%fused_computation.17 | custom fusion | flops 131072 | bytes 1048580 | tf_op jit(solution)/shard_map/scatter-add | solution.py:118
  174.0 11.0 %all-to-all-start.2 = ((f32[128,8,256]{2,1,0:T(8,128)}), f32[128,8,256]{2,1,0:T(8,128)S(1)}, u32[]{:S(2)}, u32[]{:S(2)}) async-start(f32[128,8,256]{2,1,0:T(8,128)} %bitcast.27), calls=%async_computation.2 | async-start | bytes 2097152 | tf_op jit(solution)/shard_map/all_to_all | solution.py:120
  185.0 2.9 %collective-permute-start.10 = (f32[256,256]{1,0:T(8,128)S(1)}, f32[256,256]{1,0:T(8,128)S(1)}, u32[]{:S(2)}, u32[]{:S(2)}) collective-permute-start(f32[256,256]{1,0:T(8,128)S(1)} %add.167), channel_id=1, source_target_pairs={{0,16},{1,17},{2,18},{3,19},{4,20},{5,21},{6,22},{7,23},{8,24},{9,... | collective-permute-start | bytes 786440 | tf_op jit(solution)/shard_map/ppermute | solution.py:83
  188.0 16.7 %collective-permute-done.10 = f32[256,256]{1,0:T(8,128)S(1)} collective-permute-done((f32[256,256]{1,0:T(8,128)S(1)}, f32[256,256]{1,0:T(8,128)S(1)}, u32[]{:S(2)}, u32[]{:S(2)}) %collective-permute-start.10) | collective-permute-done | bytes 262176 | tf_op jit(solution)/shard_map/ppermute | solution.py:83
  204.7 1.3 collective-permute-start.11
  206.0 5.7 %collective-permute-done.11 = f32[256,256]{1,0:T(8,128)S(1)} collective-permute-done((f32[256,256]{1,0:T(8,128)S(1)}, f32[256,256]{1,0:T(8,128)S(1)}, u32[]{:S(2)}, u32[]{:S(2)}) %collective-permute-start.11) | collective-permute-done | bytes 262176 | tf_op jit(solution)/shard_map/ppermute | solution.py:83
  211.8 3.1 %collective-permute-start.12 = (f32[256,256]{1,0:T(8,128)S(1)}, f32[256,256]{1,0:T(8,128)S(1)}, u32[]{:S(2)}, u32[]{:S(2)}) collective-permute-start(f32[256,256]{1,0:T(8,128)S(1)} %add.169), channel_id=1, source_target_pairs={{0,64},{1,65},{2,66},{3,67},{4,68},{5,69},{6,70},{7,71},{8,72},{9,... | collective-permute-start | bytes 786440 | tf_op jit(solution)/shard_map/ppermute | solution.py:83
  214.8 0.5 broadcast.252
  215.3 0.8 reduce.7
  216.1 0.1 reshape.160
  216.3 7.5 %scatter_custom_fusion.1 = f32[2048,256]{1,0:T(8,128)} fusion(s32[1024]{0:T(1024)S(1)} %bitcast.75, f32[128,8,256]{2,1,0:T(8,128)S(1)} %all-to-all-done.2, f32[]{:T(128)} %constant.149.clone.1), kind=kCustom, calls=%fused_computation.12 | custom fusion | flops 262144 | bytes 3145732 | tf_op jit(solution)/shard_map/scatter-add | solution.py:126
  223.8 0.7 add.170
  (45 shorter events, 0.5 us)
Async XLA Ops:
  7.2 22.5 %copy-start = (bf16[2048,256]{1,0:T(8,128)(2,1)S(1)}, bf16[2048,256]{1,0:T(8,128)(2,1)}, u32[]{:S(2)}) copy-start(bf16[2048,256]{1,0:T(8,128)(2,1)} %param.11) | copy-start | bytes 3145732
  8.7 20.9 %all-to-all-start = ((s32[128,1,8]{2,1,0:T(1,128)}), s32[128,1,8]{2,1,0:T(1,128)S(1)}, u32[]{:S(2)}, u32[]{:S(2)}) async-start(s32[128,1,8]{2,1,0:T(1,128)} %bitcast), calls=%async_computation | async-start | bytes 131072 | tf_op jit(solution)/shard_map/all_to_all | solution.py:94
  22.8 18.3 %copy-start.8 = (s32[512]{0:T(512)S(1)}, s32[512]{0:T(512)}, u32[]{:S(2)}) copy-start(s32[512]{0:T(512)} %param.17) | copy-start | bytes 6148
  29.7 28.0 %copy-start.7 = (s32[512,8]{0,1:T(8,128)S(1)}, s32[512,8]{0,1:T(8,128)}, u32[]{:S(2)}) copy-start(s32[512,8]{0,1:T(8,128)} %param.14) | copy-start | bytes 49156
  34.7 20.0 %all-to-all-start.1 = ((bf16[128,8,256]{2,1,0:T(8,128)(2,1)}), bf16[128,8,256]{2,1,0:T(8,128)(2,1)S(1)}, u32[]{:S(2)}, u32[]{:S(2)}) async-start(bf16[128,8,256]{2,1,0:T(8,128)(2,1)} %bitcast_select_fusion.1), calls=%async_computation.1 | async-start | bytes 1048576 | tf_op jit(solution)/shard_map/all_to_all | solution.py:96
  41.1 63.9 %all-gather.5.cloned.1.call-start = ((), (), s32[]{:S(2)}) async-start(), calls=%async_computation.4 | async-start | bytes 4456448 | tf_op jit(solution)/shard_map/all_gather | solution.py:105
  57.5 104.0 %all-gather.3.cloned.1.call-start = ((), (), s32[]{:S(2)}) async-start(), calls=%async_computation.3 | async-start | bytes 4456448 | tf_op jit(solution)/shard_map/all_gather | solution.py:104
  74.0 31.1 %copy-start.4 = (bf16[512,256]{1,0:T(8,128)(2,1)S(1)}, bf16[512,256]{1,0:T(8,128)(2,1)}, u32[]{:S(2)}) copy-start(bf16[512,256]{1,0:T(8,128)(2,1)} %broadcast_select_fusion.own_ref) | copy-start | bytes 786436
  79.5 0.8 copy-start.5
  82.2 44.0 %copy-start.6 = (f32[512,256]{1,0:T(8,128)S(1)}, f32[512,256]{1,0:T(8,128)}, u32[]{:S(2)}) copy-start(f32[512,256]{1,0:T(8,128)} %copy-done.5) | copy-start | bytes 1572868
  105.0 2.2 copy-start.1
  107.2 0.9 copy-start.2
  108.2 53.4 %copy-start.3 = (bf16[512,256]{1,0:T(8,128)(2,1)S(1)}, bf16[512,256]{1,0:T(8,128)(2,1)}, u32[]{:S(2)}) copy-start(bf16[512,256]{1,0:T(8,128)(2,1)} %convolution_convert_fusion.q_ref) | copy-start | bytes 786436
  122.6 5.7 %collective-permute-start.2 = (f32[1,512]{1,0:T(1,128)S(1)}, f32[1,512]{1,0:T(1,128)S(1)}, u32[]{:S(2)}, u32[]{:S(2)}) collective-permute-start(f32[1,512]{1,0:T(1,128)S(1)} %bitcast.67), channel_id=1, source_target_pairs={{0,24},{8,0},{16,8},{24,16},{32,56},{40,32},{48,40},{56,48},{64,88... | collective-permute-start | bytes 6152 | tf_op jit(solution)/shard_map/ppermute | solution.py:61
  125.0 3.9 %collective-permute-start.1 = (f32[1,512]{1,0:T(1,128)S(1)}, f32[1,512]{1,0:T(1,128)S(1)}, u32[]{:S(2)}, u32[]{:S(2)}) collective-permute-start(f32[1,512]{1,0:T(1,128)S(1)} %bitcast.68), channel_id=1, source_target_pairs={{0,16},{8,24},{16,0},{24,8},{32,48},{40,56},{48,32},{56,40},{64,80... | collective-permute-start | bytes 6152 | tf_op jit(solution)/shard_map/ppermute | solution.py:61
  125.6 3.6 %collective-permute-start = (f32[1,512]{1,0:T(1,128)S(1)}, f32[1,512]{1,0:T(1,128)S(1)}, u32[]{:S(2)}, u32[]{:S(2)}) collective-permute-start(f32[1,512]{1,0:T(1,128)S(1)} %bitcast.69), channel_id=1, source_target_pairs={{0,8},{8,16},{16,24},{24,0},{32,40},{40,48},{48,56},{56,32},{64,72... | collective-permute-start | bytes 6152 | tf_op jit(solution)/shard_map/ppermute | solution.py:61
  126.5 7.2 %collective-permute-start.6 = (f32[256,256]{1,0:T(8,128)S(1)}, f32[256,256]{1,0:T(8,128)S(1)}, u32[]{:S(2)}, u32[]{:S(2)}) collective-permute-start(f32[256,256]{1,0:T(8,128)S(1)} %fusion.6), channel_id=1, source_target_pairs={{0,1},{1,0},{2,3},{3,2},{4,5},{5,4},{6,7},{7,6},{8,9},{9,8},{10,11... | collective-permute-start | bytes 786440 | tf_op jit(solution)/shard_map/ppermute | solution.py:83
  129.3 5.8 %collective-permute-start.4 = (f32[1,2048]{1,0:T(1,128)S(1)}, f32[1,2048]{1,0:T(1,128)S(1)}, u32[]{:S(2)}, u32[]{:S(2)}) collective-permute-start(f32[1,2048]{1,0:T(1,128)S(1)} %pad_maximum_fusion.3), channel_id=1, source_target_pairs={{0,64},{8,72},{16,80},{24,88},{32,96},{40,104},{48,112},{56,120},{... | collective-permute-start | bytes 24584 | tf_op jit(solution)/shard_map/ppermute | solution.py:61
  131.0 4.1 %collective-permute-start.3 = (f32[1,2048]{1,0:T(1,128)S(1)}, f32[1,2048]{1,0:T(1,128)S(1)}, u32[]{:S(2)}, u32[]{:S(2)}) collective-permute-start(f32[1,2048]{1,0:T(1,128)S(1)} %pad_maximum_fusion.3), channel_id=1, source_target_pairs={{0,32},{8,40},{16,48},{24,56},{32,64},{40,72},{48,80},{56,88},{64,... | collective-permute-start | bytes 24584 | tf_op jit(solution)/shard_map/ppermute | solution.py:61
  131.3 3.8 %collective-permute-start.5 = (f32[1,2048]{1,0:T(1,128)S(1)}, f32[1,2048]{1,0:T(1,128)S(1)}, u32[]{:S(2)}, u32[]{:S(2)}) collective-permute-start(f32[1,2048]{1,0:T(1,128)S(1)} %pad_maximum_fusion.3), channel_id=1, source_target_pairs={{0,96},{8,104},{16,112},{24,120},{32,0},{40,8},{48,16},{56,24},{64... | collective-permute-start | bytes 24584 | tf_op jit(solution)/shard_map/ppermute | solution.py:61
  133.8 5.3 %collective-permute-start.7 = (f32[256,256]{1,0:T(8,128)S(1)}, f32[256,256]{1,0:T(8,128)S(1)}, u32[]{:S(2)}, u32[]{:S(2)}) collective-permute-start(f32[256,256]{1,0:T(8,128)S(1)} %add.164), channel_id=1, source_target_pairs={{0,2},{1,3},{2,0},{3,1},{4,6},{5,7},{6,4},{7,5},{8,10},{9,11},{10,... | collective-permute-start | bytes 786440 | tf_op jit(solution)/shard_map/ppermute | solution.py:83
  139.1 8.9 %collective-permute-start.8 = (f32[256,256]{1,0:T(8,128)S(1)}, f32[256,256]{1,0:T(8,128)S(1)}, u32[]{:S(2)}, u32[]{:S(2)}) collective-permute-start(f32[256,256]{1,0:T(8,128)S(1)} %add.165), channel_id=1, source_target_pairs={{0,4},{1,5},{2,6},{3,7},{4,0},{5,1},{6,2},{7,3},{8,12},{9,13},{10,... | collective-permute-start | bytes 786440 | tf_op jit(solution)/shard_map/ppermute | solution.py:83
  148.0 36.9 %collective-permute-start.9 = (f32[256,256]{1,0:T(8,128)S(1)}, f32[256,256]{1,0:T(8,128)S(1)}, u32[]{:S(2)}, u32[]{:S(2)}) collective-permute-start(f32[256,256]{1,0:T(8,128)S(1)} %add.166), channel_id=1, source_target_pairs={{0,8},{1,9},{2,10},{3,11},{4,12},{5,13},{6,14},{7,15},{8,0},{9,1},... | collective-permute-start | bytes 786440 | tf_op jit(solution)/shard_map/ppermute | solution.py:83
  174.0 42.3 %all-to-all-start.2 = ((f32[128,8,256]{2,1,0:T(8,128)}), f32[128,8,256]{2,1,0:T(8,128)S(1)}, u32[]{:S(2)}, u32[]{:S(2)}) async-start(f32[128,8,256]{2,1,0:T(8,128)} %bitcast.27), calls=%async_computation.2 | async-start | bytes 2097152 | tf_op jit(solution)/shard_map/all_to_all | solution.py:120
  185.0 19.7 %collective-permute-start.10 = (f32[256,256]{1,0:T(8,128)S(1)}, f32[256,256]{1,0:T(8,128)S(1)}, u32[]{:S(2)}, u32[]{:S(2)}) collective-permute-start(f32[256,256]{1,0:T(8,128)S(1)} %add.167), channel_id=1, source_target_pairs={{0,16},{1,17},{2,18},{3,19},{4,20},{5,21},{6,22},{7,23},{8,24},{9,... | collective-permute-start | bytes 786440 | tf_op jit(solution)/shard_map/ppermute | solution.py:83
  204.7 7.0 %collective-permute-start.11 = (f32[256,256]{1,0:T(8,128)S(1)}, f32[256,256]{1,0:T(8,128)S(1)}, u32[]{:S(2)}, u32[]{:S(2)}) collective-permute-start(f32[256,256]{1,0:T(8,128)S(1)} %add.168), channel_id=1, source_target_pairs={{0,32},{1,33},{2,34},{3,35},{4,36},{5,37},{6,38},{7,39},{8,40},{9,... | collective-permute-start | bytes 786440 | tf_op jit(solution)/shard_map/ppermute | solution.py:83
  211.8 12.0 %collective-permute-start.12 = (f32[256,256]{1,0:T(8,128)S(1)}, f32[256,256]{1,0:T(8,128)S(1)}, u32[]{:S(2)}, u32[]{:S(2)}) collective-permute-start(f32[256,256]{1,0:T(8,128)S(1)} %add.169), channel_id=1, source_target_pairs={{0,64},{1,65},{2,66},{3,67},{4,68},{5,69},{6,70},{7,71},{8,72},{9,... | collective-permute-start | bytes 786440 | tf_op jit(solution)/shard_map/ppermute | solution.py:83
Sparse Core Ops, SparseCore 0:
  57.6 47.3 all-gather.4
  107.7 53.7 all-gather.2

commit v4 on v3

--- a/solution.py
+++ b/solution.py
@@ -85,6 +85,64 @@
     return value
 
 
+def plane_shift(value, axis, side, step, along_row):
+    pairs = []
+    for source in range(side * side):
+        high, low = divmod(source, side)
+        if along_row:
+            target = high * side + (low + step) % side
+        else:
+            target = ((high + step) % side) * side + low
+        pairs.append((source, target))
+    return lax.ppermute(value, axis, pairs)
+
+
+def plane_gather_rows(value, axis, side, along_row):
+    pieces = [value] + [plane_shift(value, axis, side, step, along_row) for step in range(1, side)]
+    return jnp.concatenate(pieces, axis=0)
+
+
+def plane_reduce_rows(value, axis, side, along_row):
+    block = value.shape[0] // side
+    total = value[:block]
+    for step in range(1, side):
+        part = value[((side - step) % side) * block:((side - step) % side + 1) * block]
+        total = total + plane_shift(part, axis, side, step, along_row)
+    return total
+
+
+def block_grads(queries, item_vectors, axis, side, scaling):
+    row_queries = plane_gather_rows(queries, axis, side, True)
+    column_items = plane_gather_rows(item_vectors, axis, side, False)
+    scores = scaling * lax.dot_general(
+        row_queries, column_items, (((1,), (1,)), ((), ())), preferred_element_type=jnp.float32
+    )
+    local_max = jnp.max(scores, axis=1)
+    local_sum = jnp.sum(jnp.exp(scores - local_max[:, None]), axis=1)
+    stats = jnp.stack([local_max, local_sum])
+    block = queries.shape[0]
+    gathered = [stats] + [
+        jnp.roll(plane_shift(stats, axis, side, step, True), step * block, axis=1) for step in range(1, side)
+    ]
+    highest = gathered[0][0]
+    for other in gathered[1:]:
+        highest = jnp.maximum(highest, other[0])
+    mass = gathered[0][1] * jnp.exp(gathered[0][0] - highest)
+    for other in gathered[1:]:
+        mass = mass + other[1] * jnp.exp(other[0] - highest)
+    totals = highest + jnp.log(mass)
+    soft_weights = jnp.exp(scores - totals[:, None]).astype(jnp.bfloat16)
+    pulled = jnp.dot(soft_weights, column_items, preferred_element_type=jnp.float32)
+    pushed = lax.dot_general(
+        soft_weights, row_queries, (((0,), (0,)), ((), ())), preferred_element_type=jnp.float32
+    )
+    pulled = plane_reduce_rows(pulled, axis, side, True)
+    pushed = plane_reduce_rows(pushed, axis, side, False)
+    query_grad = scaling * (pulled - item_vectors.astype(jnp.float32))
+    item_grad = scaling * (pushed - queries.astype(jnp.float32))
+    return query_grad, item_grad
+
+
 def local(item_table, query_table, query_weight, query_ids, fetch_rows, counts, example_pos):
     table_rows, model_width = item_table.shape
     sources = fetch_rows.shape[1]
@@ -101,20 +159,24 @@
     looked = jnp.take(query_table, query_ids, axis=0).astype(jnp.float32)
     hidden = jnp.mean(looked, axis=1).astype(jnp.bfloat16)
     queries = jnp.dot(hidden, query_weight, preferred_element_type=jnp.float32).astype(jnp.bfloat16)
-    group_queries = lax.all_gather(queries, "batch", axis=0, tiled=True)
-    group_items = lax.all_gather(item_vectors, "batch", axis=0, tiled=True)
-    query_grad, totals = forward(queries, group_items, item_vectors)
     side = int(round(lax.axis_size("batch") ** 0.5))
-    if side * side == lax.axis_size("batch"):
-        group_totals = plane_gather(totals[:, :1].reshape(1, -1), "batch", side)
+    if side * side == lax.axis_size("batch") and side > 1:
+        query_grad, item_grad = block_grads(queries, item_vectors, "batch", side, scaling)
     else:
-        group_totals = lax.all_gather(totals[:, :1].reshape(1, -1), "batch", axis=1, tiled=True)
-    scores_back = scaling * lax.dot_general(
-        item_vectors, group_queries, (((1,), (1,)), ((), ())), preferred_element_type=jnp.float32
-    )
-    soft_back = jnp.exp(scores_back - group_totals).astype(jnp.bfloat16)
-    summed = jnp.dot(soft_back, group_queries, preferred_element_type=jnp.float32)
-    item_grad = scaling * (summed - queries.astype(jnp.float32))
+        group_queries = lax.all_gather(queries, "batch", axis=0, tiled=True)
+        group_items = lax.all_gather(item_vectors, "batch", axis=0, tiled=True)
+        query_grad, totals = forward(queries, group_items, item_vectors)
+        side = int(round(lax.axis_size("batch") ** 0.5))
+        if side * side == lax.axis_size("batch"):
+            group_totals = plane_gather(totals[:, :1].reshape(1, -1), "batch", side)
+        else:
+            group_totals = lax.all_gather(totals[:, :1].reshape(1, -1), "batch", axis=1, tiled=True)
+        scores_back = scaling * lax.dot_general(
+            item_vectors, group_queries, (((1,), (1,)), ((), ())), preferred_element_type=jnp.float32
+        )
+        soft_back = jnp.exp(scores_back - group_totals).astype(jnp.bfloat16)
+        summed = jnp.dot(soft_back, group_queries, preferred_element_type=jnp.float32)
+        item_grad = scaling * (summed - queries.astype(jnp.float32))
     slot_grads = jax.ops.segment_sum(item_grad, slot_ids, num_segments=sources * slot_cap)
     slot_grads = slot_grads.reshape(sources, slot_cap, model_width)
     returned = lax.all_to_all(

time: 233 us -> 234 us (level)
  Pallas kernels: 14.2 us -> 0 us
  waiting for transfers between devices: 86.1 us -> 100 us
  between operations: 14.6 us -> 1.17 us
  other arithmetic: 23.1 us -> 33.7 us
  matrix products: 10.2 us -> 19.1 us
  local copies, waits for them, and re-layouts: 32.5 us -> 28.1 us
    ppermute x6 -> x15, waiting for transfers between devices: 1.04 us -> 46.9 us  [plane_shift(): return lax.ppermute(value, axis, pairs)]
    all_gather x2 -> x0, waiting for transfers between devices: 36 us -> none  [the longest x1 22.6 us: local(): group_items = lax.all_gather(item_vectors, 'batch', axis=0, tiled=True)]
    pallas_call x1 -> x0, Pallas kernels: 14.2 us -> none  [forward(): pl.pallas_call(functools.partial(forward_block, scaling=width ** (-0.5)),...]
    dot_general x1 -> x3, matrix products: 8.14 us -> 18.5 us  [the longest x1 8.21 us: block_grads(): lax.dot_general(row_queries, column_items, (((1,), (1,)), ((), ())), pref...]
    reduce_sum x0 -> x1, other arithmetic: none -> 8.55 us  [block_grads(): local_sum = jnp.sum(jnp.exp(scores - local_max[:, None]), axis=1)]
    ppermute x6 -> x15, starting transfers between devices: 8.01 us -> 14.4 us  [plane_shift(): return lax.ppermute(value, axis, pairs)]
    unnamed x19 -> x35, local copies, waits for them, and re-layouts: 5.46 us -> 1.64 us
    all_to_all x1, starting transfers between devices: 11 us -> 8.53 us  [local(): lax.all_to_all(slot_grads, ('batch', 'table'), split_axis=0, concat_axis=...]
  transfers between devices with their start and end apart: 18 -> 25, of which waited for: 10 -> 15; matrix products, arithmetic and copies ran while one was open for 22% -> 13% of each run, Pallas kernels for 6% -> 0%
where the time goes in v4:
time: 234 us; the launch traced here: 233 us
  waiting for transfers between devices  100 us (43%)
  starting transfers between devices  50.9 us (22%)
  other arithmetic  33.7 us (14%)
  local copies, waits for them, and re-layouts  28.1 us (12%)
  matrix products  19.1 us (8%)
    ppermute x15, waiting for transfers between devices, plane_shift(): return lax.ppermute(value, axis, pairs)  46.9 us
    ppermute x7, waiting for transfers between devices, butterfly_sum(): value = value + lax.ppermute(value, axes, pairs)  34.3 us
    gather x1, local copies, waits for them, and re-layouts, local(): looked = jnp.take(query_table, query_ids, axis=0).astype(jnp.float32)  15.7 us
    ppermute x15, starting transfers between devices, plane_shift(): return lax.ppermute(value, axis, pairs)  14.4 us
    all_to_all x1, waiting for transfers between devices, local(): lax.all_to_all(found_rows, ('batch', 'table'), split_axis=0, concat_axis=...  13.6 us
    ppermute x7, starting transfers between devices, butterfly_sum(): value = value + lax.ppermute(value, axes, pairs)  12.4 us
    all_to_all x1, starting transfers between devices, local(): lax.all_to_all(requests, ('batch', 'table'), split_axis=0, concat_axis=0,...  10.8 us
    reduce_sum x1, other arithmetic, block_grads(): local_sum = jnp.sum(jnp.exp(scores - local_max[:, None]), axis=1)  8.55 us
  transfers between devices with their start and end apart: 25, of which 15 were waited for; matrix products, arithmetic and copies ran while one was open for 13% of the time, Pallas kernels for 0%

profile of v4, /device:TPU:1, one launch (start us, length us, event | category | flops | bytes accessed | tf_op | source)
XLA Modules:
  0.0 233.0 jit_solution(7563539521938401883)
XLA Ops:
  0.6 0.8 compare_and_fusion.1
  1.5 0.7 compare_select_fusion.2
  2.2 0.2 copy.24
  2.4 0.1 copy.25
  2.5 0.2 reshape.214
  2.6 15.7 %gather_fusion.1 = bf16[4096,256]{1,0:T(8,128)(2,1)S(1)} fusion(bf16[8192,256]{1,0:T(8,128)(2,1)} %param.8, s32[4096]{0:T(1024)S(1)} %broadcast_clamp_fusion), kind=kCustom, calls=%fused_computation.1 | custom fusion | bytes 4210688 | tf_op jit(solution)/shard_map/jit(_take)/gather | solution.py:159
  18.4 5.6 %convert_reduce_fusion = f32[512,256]{1,0:T(8,128)S(1)} fusion(bf16[4096,256]{1,0:T(8,128)(2,1)S(1)} %gather_fusion.1, pred[512,8]{1,0:T(8,128)(4,1)S(1)} %copy.24), kind=kLoop, calls=%fused_computation.9 | loop fusion | flops 3014656 | bytes 2625536 | tf_op jit(solution)/shard_map/reduce_sum | solution.py:160
  24.0 0.8 copy-done.1
  24.8 0.2 convolution_convert_fusion
  25.1 3.4 %collective-permute-start.2 = (bf16[512,256]{1,0:T(8,128)(2,1)S(1)}, bf16[512,256]{1,0:T(8,128)(2,1)S(1)}, u32[]{:S(2)}, u32[]{:S(2)}) collective-permute-start(bf16[512,256]{1,0:T(8,128)(2,1)S(1)} %convolution_convert_fusion), channel_id=1, source_target_pairs={{0,24},{8,0},{16,8},{24,16},{32,56},{40,32},{48,40},{56,48},{64,88... | collective-permute-start | bytes 786440 | tf_op jit(solution)/shard_map/ppermute | solution.py:97
  28.4 0.5 collective-permute-start.1
  28.9 0.6 collective-permute-start
  29.6 0.7 copy.22
  30.3 10.8 %all-to-all-start = ((s32[128,1,8]{2,1,0:T(1,128)}), s32[128,1,8]{2,1,0:T(1,128)S(1)}, u32[]{:S(2)}, u32[]{:S(2)}) async-start(s32[128,1,8]{2,1,0:T(1,128)} %bitcast), calls=%async_computation | async-start | bytes 131072 | tf_op jit(solution)/shard_map/all_to_all | solution.py:152
  41.1 0.1 copy.23
  41.3 0.2 reduce-window.8
  41.6 0.2 convert_reduce_fusion.1
  41.8 3.3 %gather_fusion = s32[512]{0:T(512)S(1)} fusion(s32[128]{0:T(128)S(1)} %bitcast_subtract_fusion, s32[1024]{0:T(1024)S(1)} %pad_clamp_fusion.1), kind=kCustom, calls=%fused_computation | custom fusion | bytes 6144 | tf_op jit(solution)/shard_map/jit(_take)/gather | solution.py:73
  45.2 5.3 %all-to-all-done = s32[128,1,8]{2,1,0:T(1,128)S(1)} async-done(((s32[128,1,8]{2,1,0:T(1,128)}), s32[128,1,8]{2,1,0:T(1,128)S(1)}, u32[]{:S(2)}, u32[]{:S(2)}) %all-to-all-start) | async-done | bytes 4128 | tf_op jit(solution)/shard_map/all_to_all | solution.py:152
  50.6 3.9 %gather_fusion.2 = bf16[1024,256]{1,0:T(8,128)(2,1)S(1)} fusion(bf16[2048,256]{1,0:T(8,128)(2,1)S(1)} %copy-done, s32[1024]{0:T(1024)S(1)} %broadcast_clamp_fusion.1), kind=kCustom, calls=%fused_computation.2 | custom fusion | bytes 1052672 | tf_op jit(solution)/shard_map/jit(_take)/gather | solution.py:153
  54.6 1.0 bitcast_select_fusion.1
  55.6 4.6 %all-to-all-start.1 = ((bf16[128,8,256]{2,1,0:T(8,128)(2,1)}), bf16[128,8,256]{2,1,0:T(8,128)(2,1)S(1)}, u32[]{:S(2)}, u32[]{:S(2)}) async-start(bf16[128,8,256]{2,1,0:T(8,128)(2,1)} %bitcast_select_fusion.1), calls=%async_computation.1 | async-start | bytes 1048576 | tf_op jit(solution)/shard_map/all_to_all | solution.py:154
  60.3 13.6 %all-to-all-done.1 = bf16[128,8,256]{2,1,0:T(8,128)(2,1)S(1)} async-done(((bf16[128,8,256]{2,1,0:T(8,128)(2,1)}), bf16[128,8,256]{2,1,0:T(8,128)(2,1)S(1)}, u32[]{:S(2)}, u32[]{:S(2)}) %all-to-all-start.1) | async-done | bytes 524320 | tf_op jit(solution)/shard_map/all_to_all | solution.py:154
  73.9 1.9 gather_fusion.3
  75.8 0.1 broadcast_select_fusion
  76.0 0.8 collective-permute-start.5
  76.8 1.3 collective-permute-start.4
  78.1 4.6 %collective-permute-done.5 = bf16[512,256]{1,0:T(8,128)(2,1)S(1)} collective-permute-done((bf16[512,256]{1,0:T(8,128)(2,1)S(1)}, bf16[512,256]{1,0:T(8,128)(2,1)S(1)}, u32[]{:S(2)}, u32[]{:S(2)}) %collective-permute-start.5) | collective-permute-done | bytes 262176 | tf_op jit(solution)/shard_map/ppermute | solution.py:97
  82.7 1.9 collective-permute-done.4
  84.6 7.5 %collective-permute-done.3 = bf16[512,256]{1,0:T(8,128)(2,1)S(1)} collective-permute-done((bf16[512,256]{1,0:T(8,128)(2,1)S(1)}, bf16[512,256]{1,0:T(8,128)(2,1)S(1)}, u32[]{:S(2)}, u32[]{:S(2)}) %collective-permute-start.3) | collective-permute-done | bytes 262176 | tf_op jit(solution)/shard_map/ppermute | solution.py:97
  92.1 8.2 %multiply_reduce_fusion = (f32[2048]{0:T(1024)S(1)}, f32[2048,2048]{0,1:T(8,128)}) fusion(bf16[512,256]{1,0:T(8,128)(2,1)S(1)} %collective-permute-done.5, bf16[512,256]{1,0:T(8,128)(2,1)S(1)} %collective-permute-done.4, bf16[512,256]{1,0:T(8,128)(2,1)S(1)} %collective-permute-done.3, bf16[512,256]{1,0:T(8,128)(2,1)S(1)} %broadcast_select_fusion, ...), kind=kOutput, calls=%fused_computation.8 | convolution fusion | flops 2164258816 | bytes 18882560 | tf_op jit(solution)/shard_map/dot_general | solution.py:117
  100.3 8.6 %exponential_reduce_fusion = f32[2048]{0:T(1024)S(1)} fusion(f32[2048,2048]{0,1:T(8,128)} %get-tuple-element.19, f32[2048]{0:T(1024)S(1)} %get-tuple-element.18), kind=kLoop, calls=%fused_computation.7 | loop fusion | flops 12580864 | bytes 16793600 | tf_op jit(solution)/shard_map/reduce_sum | solution.py:121
  108.9 0.9 collective-permute-start.8
  109.8 1.3 collective-permute-start.7
  111.2 0.4 collective-permute-done.8
  111.6 2.3 collective-permute-done.7
  113.9 1.3 collective-permute-done.6
  115.4 7.4 %fusion = f32[2048,256]{1,0:T(8,128)S(1)} fusion(f32[2048,2048]{0,1:T(8,128)} %get-tuple-element.19, f32[2048]{0:T(1024)S(1)} %log_add_fusion, bf16[512,256]{1,0:T(8,128)(2,1)S(1)} %collective-permute-done.5, bf16[512,256]{1,0:T(8,128)(2,1)S(1)} %collective-permute-done.4, bf16[512,256]{1,0:T(8,128)(2,1)S(1)} %collective-permute-done.3, ...), kind=kOutput, calls=%fused_computation.11 | convolution fusion | flops 2164260864 | bytes 19931136 | tf_op jit(solution)/shard_map/dot_general | solution.py:135
  123.0 2.7 %collective-permute-start.14 = (f32[512,256]{1,0:T(8,128)S(1)}, f32[512,256]{1,0:T(8,128)S(1)}, u32[]{:S(2)}, u32[]{:S(2)}) collective-permute-start(f32[512,256]{1,0:T(8,128)S(1)} %get-tuple-element.5), channel_id=1, source_target_pairs={{0,24},{8,0},{16,8},{24,16},{32,56},{40,32},{48,40},{56,48},{64,88... | collective-permute-start | bytes 1572872 | tf_op jit(solution)/shard_map/ppermute | solution.py:97
  125.7 10.8 %collective-permute-done.12 = f32[512,256]{1,0:T(8,128)S(1)} collective-permute-done((f32[512,256]{1,0:T(8,128)S(1)}, f32[512,256]{1,0:T(8,128)S(1)}, u32[]{:S(2)}, u32[]{:S(2)}) %collective-permute-start.12) | collective-permute-done | bytes 524320 | tf_op jit(solution)/shard_map/ppermute | solution.py:97
  136.4 9.9 %collective-permute-done.13 = f32[512,256]{1,0:T(8,128)S(1)} collective-permute-done((f32[512,256]{1,0:T(8,128)S(1)}, f32[512,256]{1,0:T(8,128)S(1)}, u32[]{:S(2)}, u32[]{:S(2)}) %collective-permute-start.13) | collective-permute-done | bytes 524320 | tf_op jit(solution)/shard_map/ppermute | solution.py:97
  146.4 0.3 fusion.18
  146.7 3.7 %collective-permute-start.15 = (f32[256,256]{1,0:T(8,128)S(1)}, f32[256,256]{1,0:T(8,128)S(1)}, u32[]{:S(2)}, u32[]{:S(2)}) collective-permute-start(f32[256,256]{1,0:T(8,128)S(1)} %fusion.18), channel_id=1, source_target_pairs={{0,1},{1,0},{2,3},{3,2},{4,5},{5,4},{6,7},{7,6},{8,9},{9,8},{10,11... | collective-permute-start | bytes 786440 | tf_op jit(solution)/shard_map/ppermute | solution.py:83
  150.5 2.9 %fusion.1 = f32[2048,256]{1,0:T(8,128)S(1)} fusion(f32[2048,2048]{0,1:T(8,128)S(1)} %bitcast.32, f32[2048]{0:T(1024)S(1)} %log_add_fusion, bf16[512,256]{1,0:T(8,128)(2,1)S(1)} %copy-done.8, bf16[512,256]{1,0:T(8,128)(2,1)S(1)} %copy-done.10, bf16[512,256]{1,0:T(8,128)(2,1)S(1)} %copy-done.12, bf16[512,256]{1,0:T(8,128)(2,1)S(1)} %convolution_convert_fusion), kind=kOutput, calls=%fused_computation.12 | convolution fusion | flops 2164260864 | bytes 19931136 | tf_op jit(solution)/shard_map/dot_general | solution.py:136
  153.7 2.7 %collective-permute-start.11 = (f32[512,256]{1,0:T(8,128)S(1)}, f32[512,256]{1,0:T(8,128)}, u32[]{:S(2)}, u32[]{:S(2)}) collective-permute-start(f32[512,256]{1,0:T(8,128)S(1)} %get-tuple-element.8), channel_id=1, source_target_pairs={{0,96},{8,104},{16,112},{24,120},{32,0},{40,8},{48,16},{56,24},{64... | collective-permute-start | bytes 1572872 | tf_op jit(solution)/shard_map/ppermute | solution.py:97
  156.4 0.1 collective-permute-start.10
  156.5 4.9 %collective-permute-done.16 = f32[256,256]{1,0:T(8,128)S(1)} collective-permute-done((f32[256,256]{1,0:T(8,128)S(1)}, f32[256,256]{1,0:T(8,128)S(1)}, u32[]{:S(2)}, u32[]{:S(2)}) %collective-permute-start.16) | collective-permute-done | bytes 262176 | tf_op jit(solution)/shard_map/ppermute | solution.py:83
  161.5 0.8 collective-permute-start.17
  162.3 7.9 %collective-permute-done.17 = f32[256,256]{1,0:T(8,128)S(1)} collective-permute-done((f32[256,256]{1,0:T(8,128)S(1)}, f32[256,256]{1,0:T(8,128)S(1)}, u32[]{:S(2)}, u32[]{:S(2)}) %collective-permute-start.17) | collective-permute-done | bytes 262176 | tf_op jit(solution)/shard_map/ppermute | solution.py:83
  170.3 0.7 add.172
  171.0 0.6 collective-permute-start.18
  171.6 8.2 %collective-permute-done.9 = f32[512,256]{1,0:T(8,128)} collective-permute-done((f32[512,256]{1,0:T(8,128)S(1)}, f32[512,256]{1,0:T(8,128)}, u32[]{:S(2)}, u32[]{:S(2)}) %collective-permute-start.9) | collective-permute-done | bytes 524320 | tf_op jit(solution)/shard_map/ppermute | solution.py:97
  179.7 5.2 %scatter_custom_fusion = f32[1024,256]{1,0:T(8,128)} fusion(s32[512]{0:T(512)S(1)} %get-tuple-element.3, f32[512,256]{1,0:T(8,128)} %collective-permute-done.11, f32[512,256]{1,0:T(8,128)} %collective-permute-done.10, f32[512,256]{1,0:T(8,128)} %collective-permute-done.9, f32[2048,256]{1,0:T(8,128)S(1)} %fusion.1, ...), kind=kCustom, calls=%fused_computation.30 | custom fusion | flops 917504 | bytes 3407880 | tf_op jit(solution)/shard_map/scatter-add | solution.py:180
  184.9 8.5 %all-to-all-start.2 = ((f32[128,8,256]{2,1,0:T(8,128)}), f32[128,8,256]{2,1,0:T(8,128)S(1)}, u32[]{:S(2)}, u32[]{:S(2)}) async-start(f32[128,8,256]{2,1,0:T(8,128)} %bitcast.19), calls=%async_computation.2 | async-start | bytes 2097152 | tf_op jit(solution)/shard_map/all_to_all | solution.py:182
  193.5 1.1 add.173
  194.6 2.9 %collective-permute-start.19 = (f32[256,256]{1,0:T(8,128)S(1)}, f32[256,256]{1,0:T(8,128)S(1)}, u32[]{:S(2)}, u32[]{:S(2)}) collective-permute-start(f32[256,256]{1,0:T(8,128)S(1)} %add.173), channel_id=1, source_target_pairs={{0,16},{1,17},{2,18},{3,19},{4,20},{5,21},{6,22},{7,23},{8,24},{9,... | collective-permute-start | bytes 786440 | tf_op jit(solution)/shard_map/ppermute | solution.py:83
  197.5 15.7 %collective-permute-done.19 = f32[256,256]{1,0:T(8,128)S(1)} collective-permute-done((f32[256,256]{1,0:T(8,128)S(1)}, f32[256,256]{1,0:T(8,128)S(1)}, u32[]{:S(2)}, u32[]{:S(2)}) %collective-permute-start.19) | collective-permute-done | bytes 262176 | tf_op jit(solution)/shard_map/ppermute | solution.py:83
  213.2 1.3 collective-permute-start.20
  214.5 5.7 %collective-permute-done.20 = f32[256,256]{1,0:T(8,128)S(1)} collective-permute-done((f32[256,256]{1,0:T(8,128)S(1)}, f32[256,256]{1,0:T(8,128)S(1)}, u32[]{:S(2)}, u32[]{:S(2)}) %collective-permute-start.20) | collective-permute-done | bytes 262176 | tf_op jit(solution)/shard_map/ppermute | solution.py:83
  220.2 3.1 %collective-permute-start.21 = (f32[256,256]{1,0:T(8,128)S(1)}, f32[256,256]{1,0:T(8,128)S(1)}, u32[]{:S(2)}, u32[]{:S(2)}) collective-permute-start(f32[256,256]{1,0:T(8,128)S(1)} %add.175), channel_id=1, source_target_pairs={{0,64},{1,65},{2,66},{3,67},{4,68},{5,69},{6,70},{7,71},{8,72},{9,... | collective-permute-start | bytes 786440 | tf_op jit(solution)/shard_map/ppermute | solution.py:83
  223.3 0.5 broadcast.103
  223.8 0.8 reduce.4
  224.8 7.5 %scatter_custom_fusion.1 = f32[2048,256]{1,0:T(8,128)} fusion(s32[1024]{0:T(1024)S(1)} %bitcast.46, f32[128,8,256]{2,1,0:T(8,128)S(1)} %all-to-all-done.2, f32[]{:T(128)} %constant.40.clone.1), kind=kCustom, calls=%fused_computation.16 | custom fusion | flops 262144 | bytes 3145732 | tf_op jit(solution)/shard_map/scatter-add | solution.py:188
  232.3 0.7 add.176
  (80 shorter events, 1.2 us)
Async XLA Ops:
  0.6 50.0 %copy-start = (bf16[2048,256]{1,0:T(8,128)(2,1)S(1)}, bf16[2048,256]{1,0:T(8,128)(2,1)}, u32[]{:S(2)}) copy-start(bf16[2048,256]{1,0:T(8,128)(2,1)} %param.7) | copy-start | bytes 3145732
  18.4 6.5 %copy-start.3 = (bf16[256,256]{1,0:T(8,128)(2,1)S(1)}, bf16[256,256]{1,0:T(8,128)(2,1)}, u32[]{:S(2)}) copy-start(bf16[256,256]{1,0:T(8,128)(2,1)} %param.9) | copy-start | bytes 393220
  18.4 11.2 %copy-start.5 = (s32[1,128,8]{1,2,0:T(8,128)S(1)}, s32[1,128,8]{1,2,0:T(8,128)}, u32[]{:S(2)}) copy-start(s32[1,128,8]{1,2,0:T(8,128)} %param.11) | copy-start | bytes 12292
  18.4 22.7 %copy-start.6 = (s32[1,128]{1,0:T(1,128)S(1)}, s32[1,128]{1,0:T(1,128)}, u32[]{:S(2)}) copy-start(s32[1,128]{1,0:T(1,128)} %param.12) | copy-start | bytes 1540
  18.4 23.1 %copy-start.4 = (s32[512]{0:T(512)S(1)}, s32[512]{0:T(512)}, u32[]{:S(2)}) copy-start(s32[512]{0:T(512)} %param.13) | copy-start | bytes 6148
  24.0 0.8 copy-start.1
  25.1 53.0 %collective-permute-start.2 = (bf16[512,256]{1,0:T(8,128)(2,1)S(1)}, bf16[512,256]{1,0:T(8,128)(2,1)S(1)}, u32[]{:S(2)}, u32[]{:S(2)}) collective-permute-start(bf16[512,256]{1,0:T(8,128)(2,1)S(1)} %convolution_convert_fusion), channel_id=1, source_target_pairs={{0,24},{8,0},{16,8},{24,16},{32,56},{40,32},{48,40},{56,48},{64,88... | collective-permute-start | bytes 786440 | tf_op jit(solution)/shard_map/ppermute | solution.py:97
  28.4 49.7 %collective-permute-start.1 = (bf16[512,256]{1,0:T(8,128)(2,1)S(1)}, bf16[512,256]{1,0:T(8,128)(2,1)S(1)}, u32[]{:S(2)}, u32[]{:S(2)}) collective-permute-start(bf16[512,256]{1,0:T(8,128)(2,1)S(1)} %convolution_convert_fusion), channel_id=1, source_target_pairs={{0,16},{8,24},{16,0},{24,8},{32,48},{40,56},{48,32},{56,40},{64,80... | collective-permute-start | bytes 786440 | tf_op jit(solution)/shard_map/ppermute | solution.py:97
  28.9 49.2 %collective-permute-start = (bf16[512,256]{1,0:T(8,128)(2,1)S(1)}, bf16[512,256]{1,0:T(8,128)(2,1)S(1)}, u32[]{:S(2)}, u32[]{:S(2)}) collective-permute-start(bf16[512,256]{1,0:T(8,128)(2,1)S(1)} %convolution_convert_fusion), channel_id=1, source_target_pairs={{0,8},{8,16},{16,24},{24,0},{32,40},{40,48},{48,56},{56,32},{64,72... | collective-permute-start | bytes 786440 | tf_op jit(solution)/shard_map/ppermute | solution.py:97
  30.3 20.2 %all-to-all-start = ((s32[128,1,8]{2,1,0:T(1,128)}), s32[128,1,8]{2,1,0:T(1,128)S(1)}, u32[]{:S(2)}, u32[]{:S(2)}) async-start(s32[128,1,8]{2,1,0:T(1,128)} %bitcast), calls=%async_computation | async-start | bytes 131072 | tf_op jit(solution)/shard_map/all_to_all | solution.py:152
  55.6 18.3 %all-to-all-start.1 = ((bf16[128,8,256]{2,1,0:T(8,128)(2,1)}), bf16[128,8,256]{2,1,0:T(8,128)(2,1)S(1)}, u32[]{:S(2)}, u32[]{:S(2)}) async-start(bf16[128,8,256]{2,1,0:T(8,128)(2,1)} %bitcast_select_fusion.1), calls=%async_computation.1 | async-start | bytes 1048576 | tf_op jit(solution)/shard_map/all_to_all | solution.py:154
  76.0 6.7 %collective-permute-start.5 = (bf16[512,256]{1,0:T(8,128)(2,1)S(1)}, bf16[512,256]{1,0:T(8,128)(2,1)S(1)}, u32[]{:S(2)}, u32[]{:S(2)}) collective-permute-start(bf16[512,256]{1,0:T(8,128)(2,1)S(1)} %broadcast_select_fusion), channel_id=1, source_target_pairs={{0,96},{8,104},{16,112},{24,120},{32,0},{40,8},{48,16},{56,24},{64... | collective-permute-start | bytes 786440 | tf_op jit(solution)/shard_map/ppermute | solution.py:97
  76.8 7.8 %collective-permute-start.4 = (bf16[512,256]{1,0:T(8,128)(2,1)S(1)}, bf16[512,256]{1,0:T(8,128)(2,1)S(1)}, u32[]{:S(2)}, u32[]{:S(2)}) collective-permute-start(bf16[512,256]{1,0:T(8,128)(2,1)S(1)} %broadcast_select_fusion), channel_id=1, source_target_pairs={{0,64},{8,72},{16,80},{24,88},{32,96},{40,104},{48,112},{56,120},{... | collective-permute-start | bytes 786440 | tf_op jit(solution)/shard_map/ppermute | solution.py:97
  78.1 22.2 %copy-start.7 = (bf16[512,256]{1,0:T(8,128)(2,1)}, bf16[512,256]{1,0:T(8,128)(2,1)S(1)}, u32[]{:S(2)}) copy-start(bf16[512,256]{1,0:T(8,128)(2,1)S(1)} %collective-permute-done.2) | copy-start | bytes 786436
  78.1 14.0 %collective-permute-start.3 = (bf16[512,256]{1,0:T(8,128)(2,1)S(1)}, bf16[512,256]{1,0:T(8,128)(2,1)S(1)}, u32[]{:S(2)}, u32[]{:S(2)}) collective-permute-start(bf16[512,256]{1,0:T(8,128)(2,1)S(1)} %broadcast_select_fusion), channel_id=1, source_target_pairs={{0,32},{8,40},{16,48},{24,56},{32,64},{40,72},{48,80},{56,88},{64,... | collective-permute-start | bytes 786440 | tf_op jit(solution)/shard_map/ppermute | solution.py:97
  78.1 22.2 %copy-start.9 = (bf16[512,256]{1,0:T(8,128)(2,1)}, bf16[512,256]{1,0:T(8,128)(2,1)S(1)}, u32[]{:S(2)}) copy-start(bf16[512,256]{1,0:T(8,128)(2,1)S(1)} %collective-permute-done.1) | copy-start | bytes 786436
  78.1 22.2 %copy-start.11 = (bf16[512,256]{1,0:T(8,128)(2,1)}, bf16[512,256]{1,0:T(8,128)(2,1)S(1)}, u32[]{:S(2)}) copy-start(bf16[512,256]{1,0:T(8,128)(2,1)S(1)} %collective-permute-done) | copy-start | bytes 786436
  108.9 2.7 %collective-permute-start.8 = (f32[2,2048]{1,0:T(2,128)S(1)}, f32[2,2048]{1,0:T(2,128)S(1)}, u32[]{:S(2)}, u32[]{:S(2)}) collective-permute-start(f32[2,2048]{1,0:T(2,128)S(1)} %pad_maximum_fusion.6), channel_id=1, source_target_pairs={{0,24},{8,0},{16,8},{24,16},{32,56},{40,32},{48,40},{56,48},{64,88... | collective-permute-start | bytes 49160 | tf_op jit(solution)/shard_map/ppermute | solution.py:97
  109.8 4.1 %collective-permute-start.7 = (f32[2,2048]{1,0:T(2,128)S(1)}, f32[2,2048]{1,0:T(2,128)S(1)}, u32[]{:S(2)}, u32[]{:S(2)}) collective-permute-start(f32[2,2048]{1,0:T(2,128)S(1)} %pad_maximum_fusion.6), channel_id=1, source_target_pairs={{0,16},{8,24},{16,0},{24,8},{32,48},{40,56},{48,32},{56,40},{64,80... | collective-permute-start | bytes 49160 | tf_op jit(solution)/shard_map/ppermute | solution.py:97
  111.2 4.1 %collective-permute-start.6 = (f32[2,2048]{1,0:T(2,128)S(1)}, f32[2,2048]{1,0:T(2,128)S(1)}, u32[]{:S(2)}, u32[]{:S(2)}) collective-permute-start(f32[2,2048]{1,0:T(2,128)S(1)} %pad_maximum_fusion.6), channel_id=1, source_target_pairs={{0,8},{8,16},{16,24},{24,0},{32,40},{40,48},{48,56},{56,32},{64,72... | collective-permute-start | bytes 49160 | tf_op jit(solution)/shard_map/ppermute | solution.py:97
  115.3 35.1 %slice-start = ((s8[16777216]{0:T(1024)(128)(4,1)}), s8[4194304]{0:T(1024)(128)(4,1)S(1)}, s32[]{:S(2)}) async-start(s8[16777216]{0:T(1024)(128)(4,1)} %bitcast.31), calls=%async_computation.3 | async-start | bytes 8388608
  115.3 35.1 %slice-start.1 = ((s8[16777216]{0:T(1024)(128)(4,1)}), s8[4194304]{0:T(1024)(128)(4,1)S(1)}, s32[]{:S(2)}) async-start(s8[16777216]{0:T(1024)(128)(4,1)} %bitcast.31), calls=%async_computation.4 | async-start | bytes 8388608
  115.3 35.1 %slice-start.2 = ((s8[16777216]{0:T(1024)(128)(4,1)}), s8[4194304]{0:T(1024)(128)(4,1)S(1)}, s32[]{:S(2)}) async-start(s8[16777216]{0:T(1024)(128)(4,1)} %bitcast.31), calls=%async_computation.5 | async-start | bytes 8388608
  115.3 35.1 %slice-start.3 = ((s8[16777216]{0:T(1024)(128)(4,1)}), s8[4194304]{0:T(1024)(128)(4,1)S(1)}, s32[]{:S(2)}) async-start(s8[16777216]{0:T(1024)(128)(4,1)} %bitcast.31), calls=%async_computation.6 | async-start | bytes 8388608
  122.8 23.6 %copy-start.2 = (f32[512,256]{1,0:T(8,128)S(1)}, f32[512,256]{1,0:T(8,128)}, u32[]{:S(2)}) copy-start(f32[512,256]{1,0:T(8,128)} %copy-done.1) | copy-start | bytes 1572868
  122.9 27.6 %copy-start.8 = (bf16[512,256]{1,0:T(8,128)(2,1)S(1)}, bf16[512,256]{1,0:T(8,128)(2,1)}, u32[]{:S(2)}) copy-start(bf16[512,256]{1,0:T(8,128)(2,1)} %copy-done.7) | copy-start | bytes 786436
  122.9 27.6 %copy-start.10 = (bf16[512,256]{1,0:T(8,128)(2,1)S(1)}, bf16[512,256]{1,0:T(8,128)(2,1)}, u32[]{:S(2)}) copy-start(bf16[512,256]{1,0:T(8,128)(2,1)} %copy-done.9) | copy-start | bytes 786436
  122.9 27.5 %copy-start.12 = (bf16[512,256]{1,0:T(8,128)(2,1)S(1)}, bf16[512,256]{1,0:T(8,128)(2,1)}, u32[]{:S(2)}) copy-start(bf16[512,256]{1,0:T(8,128)(2,1)} %copy-done.11) | copy-start | bytes 786436
  122.9 13.5 %collective-permute-start.12 = (f32[512,256]{1,0:T(8,128)S(1)}, f32[512,256]{1,0:T(8,128)S(1)}, u32[]{:S(2)}, u32[]{:S(2)}) collective-permute-start(f32[512,256]{1,0:T(8,128)S(1)} %get-tuple-element.4), channel_id=1, source_target_pairs={{0,8},{8,16},{16,24},{24,0},{32,40},{40,48},{48,56},{56,32},{64,72... | collective-permute-start | bytes 1572872 | tf_op jit(solution)/shard_map/ppermute | solution.py:97
  123.0 13.4 %collective-permute-start.14 = (f32[512,256]{1,0:T(8,128)S(1)}, f32[512,256]{1,0:T(8,128)S(1)}, u32[]{:S(2)}, u32[]{:S(2)}) collective-permute-start(f32[512,256]{1,0:T(8,128)S(1)} %get-tuple-element.5), channel_id=1, source_target_pairs={{0,24},{8,0},{16,8},{24,16},{32,56},{40,32},{48,40},{56,48},{64,88... | collective-permute-start | bytes 1572872 | tf_op jit(solution)/shard_map/ppermute | solution.py:97
  125.7 20.7 %collective-permute-start.13 = (f32[512,256]{1,0:T(8,128)S(1)}, f32[512,256]{1,0:T(8,128)S(1)}, u32[]{:S(2)}, u32[]{:S(2)}) collective-permute-start(f32[512,256]{1,0:T(8,128)S(1)} %get-tuple-element.6), channel_id=1, source_target_pairs={{0,16},{8,24},{16,0},{24,8},{32,48},{40,56},{48,32},{56,40},{64,80... | collective-permute-start | bytes 1572872 | tf_op jit(solution)/shard_map/ppermute | solution.py:97
  146.7 6.7 %collective-permute-start.15 = (f32[256,256]{1,0:T(8,128)S(1)}, f32[256,256]{1,0:T(8,128)S(1)}, u32[]{:S(2)}, u32[]{:S(2)}) collective-permute-start(f32[256,256]{1,0:T(8,128)S(1)} %fusion.18), channel_id=1, source_target_pairs={{0,1},{1,0},{2,3},{3,2},{4,5},{5,4},{6,7},{7,6},{8,9},{9,8},{10,11... | collective-permute-start | bytes 786440 | tf_op jit(solution)/shard_map/ppermute | solution.py:83
  153.5 8.0 %collective-permute-start.16 = (f32[256,256]{1,0:T(8,128)S(1)}, f32[256,256]{1,0:T(8,128)S(1)}, u32[]{:S(2)}, u32[]{:S(2)}) collective-permute-start(f32[256,256]{1,0:T(8,128)S(1)} %add.170), channel_id=1, source_target_pairs={{0,2},{1,3},{2,0},{3,1},{4,6},{5,7},{6,4},{7,5},{8,10},{9,11},{10,... | collective-permute-start | bytes 786440 | tf_op jit(solution)/shard_map/ppermute | solution.py:83
  153.7 26.1 %collective-permute-start.9 = (f32[512,256]{1,0:T(8,128)S(1)}, f32[512,256]{1,0:T(8,128)}, u32[]{:S(2)}, u32[]{:S(2)}) collective-permute-start(f32[512,256]{1,0:T(8,128)S(1)} %get-tuple-element.7), channel_id=1, source_target_pairs={{0,32},{8,40},{16,48},{24,56},{32,64},{40,72},{48,80},{56,88},{64,... | collective-permute-start | bytes 1572872 | tf_op jit(solution)/shard_map/ppermute | solution.py:97
  153.7 26.0 %collective-permute-start.11 = (f32[512,256]{1,0:T(8,128)S(1)}, f32[512,256]{1,0:T(8,128)}, u32[]{:S(2)}, u32[]{:S(2)}) collective-permute-start(f32[512,256]{1,0:T(8,128)S(1)} %get-tuple-element.8), channel_id=1, source_target_pairs={{0,96},{8,104},{16,112},{24,120},{32,0},{40,8},{48,16},{56,24},{64... | collective-permute-start | bytes 1572872 | tf_op jit(solution)/shard_map/ppermute | solution.py:97
  156.4 23.3 %collective-permute-start.10 = (f32[512,256]{1,0:T(8,128)S(1)}, f32[512,256]{1,0:T(8,128)}, u32[]{:S(2)}, u32[]{:S(2)}) collective-permute-start(f32[512,256]{1,0:T(8,128)S(1)} %get-tuple-element.9), channel_id=1, source_target_pairs={{0,64},{8,72},{16,80},{24,88},{32,96},{40,104},{48,112},{56,120},{... | collective-permute-start | bytes 1572872 | tf_op jit(solution)/shard_map/ppermute | solution.py:97
  161.5 8.8 %collective-permute-start.17 = (f32[256,256]{1,0:T(8,128)S(1)}, f32[256,256]{1,0:T(8,128)S(1)}, u32[]{:S(2)}, u32[]{:S(2)}) collective-permute-start(f32[256,256]{1,0:T(8,128)S(1)} %add.171), channel_id=1, source_target_pairs={{0,4},{1,5},{2,6},{3,7},{4,0},{5,1},{6,2},{7,3},{8,12},{9,13},{10,... | collective-permute-start | bytes 786440 | tf_op jit(solution)/shard_map/ppermute | solution.py:83
  171.0 22.5 %collective-permute-start.18 = (f32[256,256]{1,0:T(8,128)}, f32[256,256]{1,0:T(8,128)}, u32[]{:S(2)}, u32[]{:S(2)}) collective-permute-start(f32[256,256]{1,0:T(8,128)} %add.172), channel_id=1, source_target_pairs={{0,8},{1,9},{2,10},{3,11},{4,12},{5,13},{6,14},{7,15},{8,0},{9,1},... | collective-permute-start | bytes 786440 | tf_op jit(solution)/shard_map/ppermute | solution.py:83
  184.9 39.8 %all-to-all-start.2 = ((f32[128,8,256]{2,1,0:T(8,128)}), f32[128,8,256]{2,1,0:T(8,128)S(1)}, u32[]{:S(2)}, u32[]{:S(2)}) async-start(f32[128,8,256]{2,1,0:T(8,128)} %bitcast.19), calls=%async_computation.2 | async-start | bytes 2097152 | tf_op jit(solution)/shard_map/all_to_all | solution.py:182
  194.6 18.6 %collective-permute-start.19 = (f32[256,256]{1,0:T(8,128)S(1)}, f32[256,256]{1,0:T(8,128)S(1)}, u32[]{:S(2)}, u32[]{:S(2)}) collective-permute-start(f32[256,256]{1,0:T(8,128)S(1)} %add.173), channel_id=1, source_target_pairs={{0,16},{1,17},{2,18},{3,19},{4,20},{5,21},{6,22},{7,23},{8,24},{9,... | collective-permute-start | bytes 786440 | tf_op jit(solution)/shard_map/ppermute | solution.py:83
  213.2 7.0 %collective-permute-start.20 = (f32[256,256]{1,0:T(8,128)S(1)}, f32[256,256]{1,0:T(8,128)S(1)}, u32[]{:S(2)}, u32[]{:S(2)}) collective-permute-start(f32[256,256]{1,0:T(8,128)S(1)} %add.174), channel_id=1, source_target_pairs={{0,32},{1,33},{2,34},{3,35},{4,36},{5,37},{6,38},{7,39},{8,40},{9,... | collective-permute-start | bytes 786440 | tf_op jit(solution)/shard_map/ppermute | solution.py:83
  220.2 12.0 %collective-permute-start.21 = (f32[256,256]{1,0:T(8,128)S(1)}, f32[256,256]{1,0:T(8,128)S(1)}, u32[]{:S(2)}, u32[]{:S(2)}) collective-permute-start(f32[256,256]{1,0:T(8,128)S(1)} %add.175), channel_id=1, source_target_pairs={{0,64},{1,65},{2,66},{3,67},{4,68},{5,69},{6,70},{7,71},{8,72},{9,... | collective-permute-start | bytes 786440 | tf_op jit(solution)/shard_map/ppermute | solution.py:83

commit v5 on v4

--- a/solution.py
+++ b/solution.py
@@ -151,6 +151,7 @@
     requests = fetch_rows.reshape(sources, slot_cap)
     wanted = lax.all_to_all(requests, ("batch", "table"), split_axis=0, concat_axis=0, tiled=True)
     found_rows = jnp.take(item_table, wanted, axis=0)
+    found_rows, query_ids = lax.optimization_barrier((found_rows, query_ids))
     fetched = lax.all_to_all(
         found_rows, ("batch", "table"), split_axis=0, concat_axis=0, tiled=True
     )

time: 234 us -> 230 us (0.983)
  waiting for transfers between devices: 100 us -> 80.6 us
  starting transfers between devices: 50.9 us -> 61.8 us
  local copies, waits for them, and re-layouts: 28.1 us -> 31.6 us
    all_to_all x1, waiting for transfers between devices: 13.6 us -> 0.01 us  [local(): lax.all_to_all(found_rows, ('batch', 'table'), split_axis=0, concat_axis=...]
    ppermute x7, starting transfers between devices: 12.4 us -> 17.8 us  [butterfly_sum(): value = value + lax.ppermute(value, axes, pairs)]
    ppermute x7, waiting for transfers between devices: 34.3 us -> 31 us  [butterfly_sum(): value = value + lax.ppermute(value, axes, pairs)]
    gather x1, local copies, waits for them, and re-layouts: 15.7 us -> 18.7 us  [local(): looked = jnp.take(query_table, query_ids, axis=0).astype(jnp.float32)]
  transfers between devices with their start and end apart: 25 -> 25, of which waited for: 15 -> 13; matrix products, arithmetic and copies ran while one was open for 13% -> 23% of each run, Pallas kernels for 0% -> 0%
where the time goes in v5:
time: 230 us; the launch traced here: 228 us
  waiting for transfers between devices  80.6 us (35%)
  starting transfers between devices  61.8 us (27%)
  other arithmetic  32 us (14%)
  local copies, waits for them, and re-layouts  31.6 us (14%)
  matrix products  21.2 us (9%)
    ppermute x15, waiting for transfers between devices, plane_shift(): return lax.ppermute(value, axis, pairs)  46.3 us
    ppermute x7, waiting for transfers between devices, butterfly_sum(): value = value + lax.ppermute(value, axes, pairs)  31 us
    gather x1, local copies, waits for them, and re-layouts, local(): looked = jnp.take(query_table, query_ids, axis=0).astype(jnp.float32)  18.7 us
    ppermute x7, starting transfers between devices, butterfly_sum(): value = value + lax.ppermute(value, axes, pairs)  17.8 us
    ppermute x15, starting transfers between devices, plane_shift(): return lax.ppermute(value, axis, pairs)  16 us
    all_to_all x1, starting transfers between devices, local(): lax.all_to_all(requests, ('batch', 'table'), split_axis=0, concat_axis=0,...  11.5 us
    all_to_all x1, starting transfers between devices, local(): lax.all_to_all(slot_grads, ('batch', 'table'), split_axis=0, concat_axis=...  10 us
    dot_general x1, matrix products, block_grads(): lax.dot_general(row_queries, column_items, (((1,), (1,)), ((), ())), pref...  9.25 us
  transfers between devices with their start and end apart: 25, of which 13 were waited for; matrix products, arithmetic and copies ran while one was open for 23% of the time, Pallas kernels for 0%

profile of v5, /device:TPU:1, one launch (start us, length us, event | category | flops | bytes accessed | tf_op | source)
XLA Modules:
  0.0 228.3 jit_solution(5182093347811872893)
XLA Ops:
  0.7 1.5 copy.22
  2.2 11.5 %all-to-all-start = ((s32[128,1,8]{2,1,0:T(1,128)}), s32[128,1,8]{2,1,0:T(1,128)S(1)}, u32[]{:S(2)}, u32[]{:S(2)}) async-start(s32[128,1,8]{2,1,0:T(1,128)} %bitcast), calls=%async_computation | async-start | bytes 131072 | tf_op jit(solution)/shard_map/all_to_all | solution.py:152
  13.7 0.8 copy.23
  14.4 0.2 reduce-window.8
  14.6 0.1 reduce.1
  14.7 0.7 bitcast_subtract_fusion
  15.4 0.9 convert_reduce_fusion.1
  16.3 3.3 %gather_fusion = s32[512]{0:T(512)S(1)} fusion(s32[128]{0:T(128)S(1)} %bitcast_subtract_fusion, s32[1024]{0:T(1024)S(1)} %pad_clamp_fusion.1), kind=kCustom, calls=%fused_computation | custom fusion | bytes 6144 | tf_op jit(solution)/shard_map/jit(_take)/gather | solution.py:73
  19.7 3.3 %all-to-all-done = s32[128,1,8]{2,1,0:T(1,128)S(1)} async-done(((s32[128,1,8]{2,1,0:T(1,128)}), s32[128,1,8]{2,1,0:T(1,128)S(1)}, u32[]{:S(2)}, u32[]{:S(2)}) %all-to-all-start) | async-done | bytes 4128 | tf_op jit(solution)/shard_map/all_to_all | solution.py:152
  23.2 3.9 %gather_fusion.1 = bf16[1024,256]{1,0:T(8,128)(2,1)S(1)} fusion(bf16[2048,256]{1,0:T(8,128)(2,1)S(1)} %copy-done, s32[1024]{0:T(1024)S(1)} %broadcast_clamp_fusion.1), kind=kCustom, calls=%fused_computation.1 | custom fusion | bytes 1052672 | tf_op jit(solution)/shard_map/jit(_take)/gather | solution.py:153
  27.1 1.0 bitcast_select_fusion.1
  28.2 6.5 %all-to-all-start.1 = ((bf16[128,8,256]{2,1,0:T(8,128)(2,1)}), bf16[128,8,256]{2,1,0:T(8,128)(2,1)S(1)}, u32[]{:S(2)}, u32[]{:S(2)}) async-start(bf16[128,8,256]{2,1,0:T(8,128)(2,1)} %bitcast_select_fusion.1), calls=%async_computation.1 | async-start | bytes 1048576 | tf_op jit(solution)/shard_map/all_to_all | solution.py:155
  34.6 0.2 copy.24
  34.8 0.1 copy.25
  35.0 0.2 reshape.222
  35.1 18.7 %gather_fusion.2 = bf16[4096,256]{1,0:T(8,128)(2,1)} fusion(bf16[8192,256]{1,0:T(8,128)(2,1)} %param.8, s32[4096]{0:T(1024)S(1)} %broadcast_clamp_fusion), kind=kCustom, calls=%fused_computation.2 | custom fusion | bytes 4210688 | tf_op jit(solution)/shard_map/jit(_take)/gather | solution.py:160
  53.8 4.1 %convert_reduce_fusion = f32[512,256]{1,0:T(8,128)S(1)} fusion(bf16[4096,256]{1,0:T(8,128)(2,1)} %gather_fusion.2, pred[512,8]{1,0:T(8,128)(4,1)S(1)} %copy.24), kind=kLoop, calls=%fused_computation.9 | loop fusion | flops 3014656 | bytes 2625536 | tf_op jit(solution)/shard_map/reduce_sum | solution.py:161
  57.9 0.2 convolution_convert_fusion
  58.1 2.6 %collective-permute-start.2 = (bf16[512,256]{1,0:T(8,128)(2,1)S(1)}, bf16[512,256]{1,0:T(8,128)(2,1)S(1)}, u32[]{:S(2)}, u32[]{:S(2)}) collective-permute-start(bf16[512,256]{1,0:T(8,128)(2,1)S(1)} %convolution_convert_fusion), channel_id=1, source_target_pairs={{0,24},{8,0},{16,8},{24,16},{32,56},{40,32},{48,40},{56,48},{64,88... | collective-permute-start | bytes 786440 | tf_op jit(solution)/shard_map/ppermute | solution.py:97
  60.8 0.6 collective-permute-start.1
  61.4 0.6 collective-permute-start
  61.9 1.9 gather_fusion.3
  63.9 0.1 broadcast_select_fusion
  64.0 2.6 %collective-permute-start.5 = (bf16[512,256]{1,0:T(8,128)(2,1)S(1)}, bf16[512,256]{1,0:T(8,128)(2,1)S(1)}, u32[]{:S(2)}, u32[]{:S(2)}) collective-permute-start(bf16[512,256]{1,0:T(8,128)(2,1)S(1)} %broadcast_select_fusion), channel_id=1, source_target_pairs={{0,96},{8,104},{16,112},{24,120},{32,0},{40,8},{48,16},{56,24},{64... | collective-permute-start | bytes 786440 | tf_op jit(solution)/shard_map/ppermute | solution.py:97
  66.6 0.5 collective-permute-start.4
  67.1 4.5 %collective-permute-done.2 = bf16[512,256]{1,0:T(8,128)(2,1)S(1)} collective-permute-done((bf16[512,256]{1,0:T(8,128)(2,1)S(1)}, bf16[512,256]{1,0:T(8,128)(2,1)S(1)}, u32[]{:S(2)}, u32[]{:S(2)}) %collective-permute-start.2) | collective-permute-done | bytes 262176 | tf_op jit(solution)/shard_map/ppermute | solution.py:97
  71.5 4.7 %collective-permute-done = bf16[512,256]{1,0:T(8,128)(2,1)} collective-permute-done((bf16[512,256]{1,0:T(8,128)(2,1)S(1)}, bf16[512,256]{1,0:T(8,128)(2,1)}, u32[]{:S(2)}, u32[]{:S(2)}) %collective-permute-start) | collective-permute-done | bytes 262176 | tf_op jit(solution)/shard_map/ppermute | solution.py:97
  76.3 5.4 %collective-permute-done.3 = bf16[512,256]{1,0:T(8,128)(2,1)S(1)} collective-permute-done((bf16[512,256]{1,0:T(8,128)(2,1)S(1)}, bf16[512,256]{1,0:T(8,128)(2,1)S(1)}, u32[]{:S(2)}, u32[]{:S(2)}) %collective-permute-start.3) | collective-permute-done | bytes 262176 | tf_op jit(solution)/shard_map/ppermute | solution.py:97
  81.6 9.3 %multiply_reduce_fusion = (f32[2048]{0:T(1024)S(1)}, f32[2048,2048]{0,1:T(8,128)}) fusion(bf16[512,256]{1,0:T(8,128)(2,1)S(1)} %collective-permute-done.5, bf16[512,256]{1,0:T(8,128)(2,1)S(1)} %collective-permute-done.4, bf16[512,256]{1,0:T(8,128)(2,1)S(1)} %collective-permute-done.3, bf16[512,256]{1,0:T(8,128)(2,1)S(1)} %broadcast_select_fusion, ...), kind=kOutput, calls=%fused_computation.8 | convolution fusion | flops 2164258816 | bytes 18882560 | tf_op jit(solution)/shard_map/dot_general | solution.py:117
  90.9 8.5 %exponential_reduce_fusion = f32[2048]{0:T(1024)S(1)} fusion(f32[2048,2048]{0,1:T(8,128)} %get-tuple-element.23, f32[2048]{0:T(1024)S(1)} %get-tuple-element.22), kind=kLoop, calls=%fused_computation.7 | loop fusion | flops 12580864 | bytes 16793600 | tf_op jit(solution)/shard_map/reduce_sum | solution.py:121
  99.4 1.4 collective-permute-start.8
  100.8 2.3 %collective-permute-start.7 = (f32[2,2048]{1,0:T(2,128)S(1)}, f32[2,2048]{1,0:T(2,128)S(1)}, u32[]{:S(2)}, u32[]{:S(2)}) collective-permute-start(f32[2,2048]{1,0:T(2,128)S(1)} %pad_maximum_fusion.6), channel_id=1, source_target_pairs={{0,16},{8,24},{16,0},{24,8},{32,48},{40,56},{48,32},{56,40},{64,80... | collective-permute-start | bytes 49160 | tf_op jit(solution)/shard_map/ppermute | solution.py:97
  103.2 1.7 collective-permute-done.7
  104.9 2.0 collective-permute-done.6
  107.0 7.4 %fusion = f32[2048,256]{1,0:T(8,128)S(1)} fusion(f32[2048,2048]{0,1:T(8,128)} %get-tuple-element.23, f32[2048]{0:T(1024)S(1)} %log_add_fusion, bf16[512,256]{1,0:T(8,128)(2,1)S(1)} %collective-permute-done.5, bf16[512,256]{1,0:T(8,128)(2,1)S(1)} %collective-permute-done.4, bf16[512,256]{1,0:T(8,128)(2,1)S(1)} %collective-permute-done.3, ...), kind=kOutput, calls=%fused_computation.11 | convolution fusion | flops 2164260864 | bytes 19931136 | tf_op jit(solution)/shard_map/dot_general | solution.py:135
  114.5 0.1 fusion.34
  114.7 2.7 %collective-permute-start.14 = (f32[512,256]{1,0:T(8,128)S(1)}, f32[512,256]{1,0:T(8,128)S(1)}, u32[]{:S(2)}, u32[]{:S(2)}) collective-permute-start(f32[512,256]{1,0:T(8,128)S(1)} %get-tuple-element.9), channel_id=1, source_target_pairs={{0,24},{8,0},{16,8},{24,16},{32,56},{40,32},{48,40},{56,48},{64,88... | collective-permute-start | bytes 1572872 | tf_op jit(solution)/shard_map/ppermute | solution.py:97
  117.4 11.6 %collective-permute-done.12 = f32[512,256]{1,0:T(8,128)S(1)} collective-permute-done((f32[512,256]{1,0:T(8,128)S(1)}, f32[512,256]{1,0:T(8,128)S(1)}, u32[]{:S(2)}, u32[]{:S(2)}) %collective-permute-start.12) | collective-permute-done | bytes 524320 | tf_op jit(solution)/shard_map/ppermute | solution.py:97
  129.0 7.6 %collective-permute-done.13 = f32[512,256]{1,0:T(8,128)S(1)} collective-permute-done((f32[512,256]{1,0:T(8,128)S(1)}, f32[512,256]{1,0:T(8,128)S(1)}, u32[]{:S(2)}, u32[]{:S(2)}) %collective-permute-start.13) | collective-permute-done | bytes 524320 | tf_op jit(solution)/shard_map/ppermute | solution.py:97
  136.6 0.3 fusion.18
  136.9 5.2 %collective-permute-start.15 = (f32[256,256]{1,0:T(8,128)S(1)}, f32[256,256]{1,0:T(8,128)S(1)}, u32[]{:S(2)}, u32[]{:S(2)}) collective-permute-start(f32[256,256]{1,0:T(8,128)S(1)} %fusion.18), channel_id=1, source_target_pairs={{0,1},{1,0},{2,3},{3,2},{4,5},{5,4},{6,7},{7,6},{8,9},{9,8},{10,11... | collective-permute-start | bytes 786440 | tf_op jit(solution)/shard_map/ppermute | solution.py:83
  142.1 3.9 %fusion.1 = f32[2048,256]{1,0:T(8,128)S(1)} fusion(f32[2048,2048]{0,1:T(8,128)S(1)} %bitcast.32, f32[2048]{0:T(1024)S(1)} %log_add_fusion, bf16[512,256]{1,0:T(8,128)(2,1)S(1)} %copy-done.5, bf16[512,256]{1,0:T(8,128)(2,1)} %collective-permute-done.1, bf16[512,256]{1,0:T(8,128)(2,1)} %collective-permute-done, bf16[512,256]{1,0:T(8,128)(2,1)S(1)} %convolution_convert_fusion), kind=kOutput, calls=%fused_computation.12 | convolution fusion | flops 2164260864 | bytes 19931136 | tf_op jit(solution)/shard_map/dot_general | solution.py:136
  146.1 1.5 collective-permute-start.16
  147.7 0.1 fusion.35
  147.9 2.7 %collective-permute-start.11 = (f32[512,256]{1,0:T(8,128)S(1)}, f32[512,256]{1,0:T(8,128)}, u32[]{:S(2)}, u32[]{:S(2)}) collective-permute-start(f32[512,256]{1,0:T(8,128)S(1)} %get-tuple-element.12), channel_id=1, source_target_pairs={{0,96},{8,104},{16,112},{24,120},{32,0},{40,8},{48,16},{56,24},{64... | collective-permute-start | bytes 1572872 | tf_op jit(solution)/shard_map/ppermute | solution.py:97
  150.5 3.6 %collective-permute-done.16 = f32[256,256]{1,0:T(8,128)S(1)} collective-permute-done((f32[256,256]{1,0:T(8,128)S(1)}, f32[256,256]{1,0:T(8,128)S(1)}, u32[]{:S(2)}, u32[]{:S(2)}) %collective-permute-start.16) | collective-permute-done | bytes 262176 | tf_op jit(solution)/shard_map/ppermute | solution.py:83
  154.2 3.3 %collective-permute-start.17 = (f32[256,256]{1,0:T(8,128)S(1)}, f32[256,256]{1,0:T(8,128)S(1)}, u32[]{:S(2)}, u32[]{:S(2)}) collective-permute-start(f32[256,256]{1,0:T(8,128)S(1)} %add.171), channel_id=1, source_target_pairs={{0,4},{1,5},{2,6},{3,7},{4,0},{5,1},{6,2},{7,3},{8,12},{9,13},{10,... | collective-permute-start | bytes 786440 | tf_op jit(solution)/shard_map/ppermute | solution.py:83
  157.5 6.0 %collective-permute-done.17 = f32[256,256]{1,0:T(8,128)S(1)} collective-permute-done((f32[256,256]{1,0:T(8,128)S(1)}, f32[256,256]{1,0:T(8,128)S(1)}, u32[]{:S(2)}, u32[]{:S(2)}) %collective-permute-start.17) | collective-permute-done | bytes 262176 | tf_op jit(solution)/shard_map/ppermute | solution.py:83
  163.5 0.7 add.172
  164.2 0.6 collective-permute-start.18
  164.8 8.8 %collective-permute-done.9 = f32[512,256]{1,0:T(8,128)} collective-permute-done((f32[512,256]{1,0:T(8,128)S(1)}, f32[512,256]{1,0:T(8,128)}, u32[]{:S(2)}, u32[]{:S(2)}) %collective-permute-start.9) | collective-permute-done | bytes 524320 | tf_op jit(solution)/shard_map/ppermute | solution.py:97
  173.6 5.2 %scatter_custom_fusion = f32[1024,256]{1,0:T(8,128)} fusion(s32[512]{0:T(512)S(1)} %get-tuple-element.7, f32[512,256]{1,0:T(8,128)} %collective-permute-done.11, f32[512,256]{1,0:T(8,128)} %collective-permute-done.10, f32[512,256]{1,0:T(8,128)} %collective-permute-done.9, f32[2048,256]{1,0:T(8,128)S(1)} %fusion.1, ...), kind=kCustom, calls=%fused_computation.30 | custom fusion | flops 917504 | bytes 3407880 | tf_op jit(solution)/shard_map/scatter-add | solution.py:181
  178.8 10.0 %all-to-all-start.2 = ((f32[128,8,256]{2,1,0:T(8,128)}), f32[128,8,256]{2,1,0:T(8,128)S(1)}, u32[]{:S(2)}, u32[]{:S(2)}) async-start(f32[128,8,256]{2,1,0:T(8,128)} %bitcast.19), calls=%async_computation.2 | async-start | bytes 2097152 | tf_op jit(solution)/shard_map/all_to_all | solution.py:183
  188.8 1.1 add.173
  189.9 2.9 %collective-permute-start.19 = (f32[256,256]{1,0:T(8,128)S(1)}, f32[256,256]{1,0:T(8,128)S(1)}, u32[]{:S(2)}, u32[]{:S(2)}) collective-permute-start(f32[256,256]{1,0:T(8,128)S(1)} %add.173), channel_id=1, source_target_pairs={{0,16},{1,17},{2,18},{3,19},{4,20},{5,21},{6,22},{7,23},{8,24},{9,... | collective-permute-start | bytes 786440 | tf_op jit(solution)/shard_map/ppermute | solution.py:83
  192.8 15.7 %collective-permute-done.19 = f32[256,256]{1,0:T(8,128)S(1)} collective-permute-done((f32[256,256]{1,0:T(8,128)S(1)}, f32[256,256]{1,0:T(8,128)S(1)}, u32[]{:S(2)}, u32[]{:S(2)}) %collective-permute-start.19) | collective-permute-done | bytes 262176 | tf_op jit(solution)/shard_map/ppermute | solution.py:83
  208.6 1.3 collective-permute-start.20
  209.8 5.7 %collective-permute-done.20 = f32[256,256]{1,0:T(8,128)S(1)} collective-permute-done((f32[256,256]{1,0:T(8,128)S(1)}, f32[256,256]{1,0:T(8,128)S(1)}, u32[]{:S(2)}, u32[]{:S(2)}) %collective-permute-start.20) | collective-permute-done | bytes 262176 | tf_op jit(solution)/shard_map/ppermute | solution.py:83
  215.6 3.1 %collective-permute-start.21 = (f32[256,256]{1,0:T(8,128)S(1)}, f32[256,256]{1,0:T(8,128)S(1)}, u32[]{:S(2)}, u32[]{:S(2)}) collective-permute-start(f32[256,256]{1,0:T(8,128)S(1)} %add.175), channel_id=1, source_target_pairs={{0,64},{1,65},{2,66},{3,67},{4,68},{5,69},{6,70},{7,71},{8,72},{9,... | collective-permute-start | bytes 786440 | tf_op jit(solution)/shard_map/ppermute | solution.py:83
  218.6 0.5 broadcast.103
  219.1 0.8 reduce.4
  220.0 0.1 reshape.197
  220.1 7.5 %scatter_custom_fusion.1 = f32[2048,256]{1,0:T(8,128)} fusion(s32[1024]{0:T(1024)S(1)} %bitcast.46, f32[128,8,256]{2,1,0:T(8,128)S(1)} %all-to-all-done.2, f32[]{:T(128)} %constant.40.clone.1), kind=kCustom, calls=%fused_computation.16 | custom fusion | flops 262144 | bytes 3145732 | tf_op jit(solution)/shard_map/scatter-add | solution.py:189
  227.6 0.7 add.176
  (66 shorter events, 0.7 us)
Async XLA Ops:
  0.6 22.5 %copy-start = (bf16[2048,256]{1,0:T(8,128)(2,1)S(1)}, bf16[2048,256]{1,0:T(8,128)(2,1)}, u32[]{:S(2)}) copy-start(bf16[2048,256]{1,0:T(8,128)(2,1)} %param.7) | copy-start | bytes 3145732
  0.6 19.0 %copy-start.3 = (s32[512]{0:T(512)S(1)}, s32[512]{0:T(512)}, u32[]{:S(2)}) copy-start(s32[512]{0:T(512)} %param.13) | copy-start | bytes 6148
  2.2 20.9 %all-to-all-start = ((s32[128,1,8]{2,1,0:T(1,128)}), s32[128,1,8]{2,1,0:T(1,128)S(1)}, u32[]{:S(2)}, u32[]{:S(2)}) async-start(s32[128,1,8]{2,1,0:T(1,128)} %bitcast), calls=%async_computation | async-start | bytes 131072 | tf_op jit(solution)/shard_map/all_to_all | solution.py:152
  23.2 5.0 %copy-start.2 = (s32[512,8]{0,1:T(8,128)S(1)}, s32[512,8]{0,1:T(8,128)}, u32[]{:S(2)}) copy-start(s32[512,8]{0,1:T(8,128)} %param.10) | copy-start | bytes 49156
  28.2 33.8 %all-to-all-start.1 = ((bf16[128,8,256]{2,1,0:T(8,128)(2,1)}), bf16[128,8,256]{2,1,0:T(8,128)(2,1)S(1)}, u32[]{:S(2)}, u32[]{:S(2)}) async-start(bf16[128,8,256]{2,1,0:T(8,128)(2,1)} %bitcast_select_fusion.1), calls=%async_computation.1 | async-start | bytes 1048576 | tf_op jit(solution)/shard_map/all_to_all | solution.py:155
  53.8 4.1 %copy-start.1 = (bf16[256,256]{1,0:T(8,128)(2,1)S(1)}, bf16[256,256]{1,0:T(8,128)(2,1)}, u32[]{:S(2)}) copy-start(bf16[256,256]{1,0:T(8,128)(2,1)} %param.9) | copy-start | bytes 393220
  58.1 13.4 %collective-permute-start.2 = (bf16[512,256]{1,0:T(8,128)(2,1)S(1)}, bf16[512,256]{1,0:T(8,128)(2,1)S(1)}, u32[]{:S(2)}, u32[]{:S(2)}) collective-permute-start(bf16[512,256]{1,0:T(8,128)(2,1)S(1)} %convolution_convert_fusion), channel_id=1, source_target_pairs={{0,24},{8,0},{16,8},{24,16},{32,56},{40,32},{48,40},{56,48},{64,88... | collective-permute-start | bytes 786440 | tf_op jit(solution)/shard_map/ppermute | solution.py:97
  60.8 10.8 %collective-permute-start.1 = (bf16[512,256]{1,0:T(8,128)(2,1)S(1)}, bf16[512,256]{1,0:T(8,128)(2,1)}, u32[]{:S(2)}, u32[]{:S(2)}) collective-permute-start(bf16[512,256]{1,0:T(8,128)(2,1)S(1)} %convolution_convert_fusion), channel_id=1, source_target_pairs={{0,16},{8,24},{16,0},{24,8},{32,48},{40,56},{48,32},{56,40},{64,80... | collective-permute-start | bytes 786440 | tf_op jit(solution)/shard_map/ppermute | solution.py:97
  61.4 14.9 %collective-permute-start = (bf16[512,256]{1,0:T(8,128)(2,1)S(1)}, bf16[512,256]{1,0:T(8,128)(2,1)}, u32[]{:S(2)}, u32[]{:S(2)}) collective-permute-start(bf16[512,256]{1,0:T(8,128)(2,1)S(1)} %convolution_convert_fusion), channel_id=1, source_target_pairs={{0,8},{8,16},{16,24},{24,0},{32,40},{40,48},{48,56},{56,32},{64,72... | collective-permute-start | bytes 786440 | tf_op jit(solution)/shard_map/ppermute | solution.py:97
  64.0 12.2 %collective-permute-start.5 = (bf16[512,256]{1,0:T(8,128)(2,1)S(1)}, bf16[512,256]{1,0:T(8,128)(2,1)S(1)}, u32[]{:S(2)}, u32[]{:S(2)}) collective-permute-start(bf16[512,256]{1,0:T(8,128)(2,1)S(1)} %broadcast_select_fusion), channel_id=1, source_target_pairs={{0,96},{8,104},{16,112},{24,120},{32,0},{40,8},{48,16},{56,24},{64... | collective-permute-start | bytes 786440 | tf_op jit(solution)/shard_map/ppermute | solution.py:97
  66.6 9.7 %collective-permute-start.4 = (bf16[512,256]{1,0:T(8,128)(2,1)S(1)}, bf16[512,256]{1,0:T(8,128)(2,1)S(1)}, u32[]{:S(2)}, u32[]{:S(2)}) collective-permute-start(bf16[512,256]{1,0:T(8,128)(2,1)S(1)} %broadcast_select_fusion), channel_id=1, source_target_pairs={{0,64},{8,72},{16,80},{24,88},{32,96},{40,104},{48,112},{56,120},{... | collective-permute-start | bytes 786440 | tf_op jit(solution)/shard_map/ppermute | solution.py:97
  71.5 19.3 %copy-start.4 = (bf16[512,256]{1,0:T(8,128)(2,1)}, bf16[512,256]{1,0:T(8,128)(2,1)S(1)}, u32[]{:S(2)}) copy-start(bf16[512,256]{1,0:T(8,128)(2,1)S(1)} %collective-permute-done.2) | copy-start | bytes 786436
  71.5 10.1 %collective-permute-start.3 = (bf16[512,256]{1,0:T(8,128)(2,1)S(1)}, bf16[512,256]{1,0:T(8,128)(2,1)S(1)}, u32[]{:S(2)}, u32[]{:S(2)}) collective-permute-start(bf16[512,256]{1,0:T(8,128)(2,1)S(1)} %broadcast_select_fusion), channel_id=1, source_target_pairs={{0,32},{8,40},{16,48},{24,56},{32,64},{40,72},{48,80},{56,88},{64,... | collective-permute-start | bytes 786440 | tf_op jit(solution)/shard_map/ppermute | solution.py:97
  99.4 3.7 %collective-permute-start.8 = (f32[2,2048]{1,0:T(2,128)S(1)}, f32[2,2048]{1,0:T(2,128)S(1)}, u32[]{:S(2)}, u32[]{:S(2)}) collective-permute-start(f32[2,2048]{1,0:T(2,128)S(1)} %pad_maximum_fusion.6), channel_id=1, source_target_pairs={{0,24},{8,0},{16,8},{24,16},{32,56},{40,32},{48,40},{56,48},{64,88... | collective-permute-start | bytes 49160 | tf_op jit(solution)/shard_map/ppermute | solution.py:97
  100.8 4.1 %collective-permute-start.7 = (f32[2,2048]{1,0:T(2,128)S(1)}, f32[2,2048]{1,0:T(2,128)S(1)}, u32[]{:S(2)}, u32[]{:S(2)}) collective-permute-start(f32[2,2048]{1,0:T(2,128)S(1)} %pad_maximum_fusion.6), channel_id=1, source_target_pairs={{0,16},{8,24},{16,0},{24,8},{32,48},{40,56},{48,32},{56,40},{64,80... | collective-permute-start | bytes 49160 | tf_op jit(solution)/shard_map/ppermute | solution.py:97
  103.1 3.8 %collective-permute-start.6 = (f32[2,2048]{1,0:T(2,128)S(1)}, f32[2,2048]{1,0:T(2,128)S(1)}, u32[]{:S(2)}, u32[]{:S(2)}) collective-permute-start(f32[2,2048]{1,0:T(2,128)S(1)} %pad_maximum_fusion.6), channel_id=1, source_target_pairs={{0,8},{8,16},{16,24},{24,0},{32,40},{40,48},{48,56},{56,32},{64,72... | collective-permute-start | bytes 49160 | tf_op jit(solution)/shard_map/ppermute | solution.py:97
  107.0 35.1 %slice-start = ((s8[16777216]{0:T(1024)(128)(4,1)}), s8[4194304]{0:T(1024)(128)(4,1)S(1)}, s32[]{:S(2)}) async-start(s8[16777216]{0:T(1024)(128)(4,1)} %bitcast.31), calls=%async_computation.3 | async-start | bytes 8388608
  107.0 35.1 %slice-start.1 = ((s8[16777216]{0:T(1024)(128)(4,1)}), s8[4194304]{0:T(1024)(128)(4,1)S(1)}, s32[]{:S(2)}) async-start(s8[16777216]{0:T(1024)(128)(4,1)} %bitcast.31), calls=%async_computation.4 | async-start | bytes 8388608
  107.0 35.1 %slice-start.2 = ((s8[16777216]{0:T(1024)(128)(4,1)}), s8[4194304]{0:T(1024)(128)(4,1)S(1)}, s32[]{:S(2)}) async-start(s8[16777216]{0:T(1024)(128)(4,1)} %bitcast.31), calls=%async_computation.5 | async-start | bytes 8388608
  107.0 35.1 %slice-start.3 = ((s8[16777216]{0:T(1024)(128)(4,1)}), s8[4194304]{0:T(1024)(128)(4,1)S(1)}, s32[]{:S(2)}) async-start(s8[16777216]{0:T(1024)(128)(4,1)} %bitcast.31), calls=%async_computation.6 | async-start | bytes 8388608
  114.6 27.5 %copy-start.5 = (bf16[512,256]{1,0:T(8,128)(2,1)S(1)}, bf16[512,256]{1,0:T(8,128)(2,1)}, u32[]{:S(2)}) copy-start(bf16[512,256]{1,0:T(8,128)(2,1)} %copy-done.4) | copy-start | bytes 786436
  114.6 14.4 %collective-permute-start.12 = (f32[512,256]{1,0:T(8,128)S(1)}, f32[512,256]{1,0:T(8,128)S(1)}, u32[]{:S(2)}, u32[]{:S(2)}) collective-permute-start(f32[512,256]{1,0:T(8,128)S(1)} %get-tuple-element.8), channel_id=1, source_target_pairs={{0,8},{8,16},{16,24},{24,0},{32,40},{40,48},{48,56},{56,32},{64,72... | collective-permute-start | bytes 1572872 | tf_op jit(solution)/shard_map/ppermute | solution.py:97
  114.7 14.3 %collective-permute-start.14 = (f32[512,256]{1,0:T(8,128)S(1)}, f32[512,256]{1,0:T(8,128)S(1)}, u32[]{:S(2)}, u32[]{:S(2)}) collective-permute-start(f32[512,256]{1,0:T(8,128)S(1)} %get-tuple-element.9), channel_id=1, source_target_pairs={{0,24},{8,0},{16,8},{24,16},{32,56},{40,32},{48,40},{56,48},{64,88... | collective-permute-start | bytes 1572872 | tf_op jit(solution)/shard_map/ppermute | solution.py:97
  117.4 19.2 %collective-permute-start.13 = (f32[512,256]{1,0:T(8,128)S(1)}, f32[512,256]{1,0:T(8,128)S(1)}, u32[]{:S(2)}, u32[]{:S(2)}) collective-permute-start(f32[512,256]{1,0:T(8,128)S(1)} %get-tuple-element.10), channel_id=1, source_target_pairs={{0,16},{8,24},{16,0},{24,8},{32,48},{40,56},{48,32},{56,40},{64,80... | collective-permute-start | bytes 1572872 | tf_op jit(solution)/shard_map/ppermute | solution.py:97
  136.9 9.2 %collective-permute-start.15 = (f32[256,256]{1,0:T(8,128)S(1)}, f32[256,256]{1,0:T(8,128)S(1)}, u32[]{:S(2)}, u32[]{:S(2)}) collective-permute-start(f32[256,256]{1,0:T(8,128)S(1)} %fusion.18), channel_id=1, source_target_pairs={{0,1},{1,0},{2,3},{3,2},{4,5},{5,4},{6,7},{7,6},{8,9},{9,8},{10,11... | collective-permute-start | bytes 786440 | tf_op jit(solution)/shard_map/ppermute | solution.py:83
  146.1 8.0 %collective-permute-start.16 = (f32[256,256]{1,0:T(8,128)S(1)}, f32[256,256]{1,0:T(8,128)S(1)}, u32[]{:S(2)}, u32[]{:S(2)}) collective-permute-start(f32[256,256]{1,0:T(8,128)S(1)} %add.170), channel_id=1, source_target_pairs={{0,2},{1,3},{2,0},{3,1},{4,6},{5,7},{6,4},{7,5},{8,10},{9,11},{10,... | collective-permute-start | bytes 786440 | tf_op jit(solution)/shard_map/ppermute | solution.py:83
  147.8 25.8 %collective-permute-start.9 = (f32[512,256]{1,0:T(8,128)S(1)}, f32[512,256]{1,0:T(8,128)}, u32[]{:S(2)}, u32[]{:S(2)}) collective-permute-start(f32[512,256]{1,0:T(8,128)S(1)} %get-tuple-element.11), channel_id=1, source_target_pairs={{0,32},{8,40},{16,48},{24,56},{32,64},{40,72},{48,80},{56,88},{64,... | collective-permute-start | bytes 1572872 | tf_op jit(solution)/shard_map/ppermute | solution.py:97
  147.9 25.7 %collective-permute-start.11 = (f32[512,256]{1,0:T(8,128)S(1)}, f32[512,256]{1,0:T(8,128)}, u32[]{:S(2)}, u32[]{:S(2)}) collective-permute-start(f32[512,256]{1,0:T(8,128)S(1)} %get-tuple-element.12), channel_id=1, source_target_pairs={{0,96},{8,104},{16,112},{24,120},{32,0},{40,8},{48,16},{56,24},{64... | collective-permute-start | bytes 1572872 | tf_op jit(solution)/shard_map/ppermute | solution.py:97
  150.5 23.0 %collective-permute-start.10 = (f32[512,256]{1,0:T(8,128)S(1)}, f32[512,256]{1,0:T(8,128)}, u32[]{:S(2)}, u32[]{:S(2)}) collective-permute-start(f32[512,256]{1,0:T(8,128)S(1)} %get-tuple-element.13), channel_id=1, source_target_pairs={{0,64},{8,72},{16,80},{24,88},{32,96},{40,104},{48,112},{56,120},{... | collective-permute-start | bytes 1572872 | tf_op jit(solution)/shard_map/ppermute | solution.py:97
  154.2 9.3 %collective-permute-start.17 = (f32[256,256]{1,0:T(8,128)S(1)}, f32[256,256]{1,0:T(8,128)S(1)}, u32[]{:S(2)}, u32[]{:S(2)}) collective-permute-start(f32[256,256]{1,0:T(8,128)S(1)} %add.171), channel_id=1, source_target_pairs={{0,4},{1,5},{2,6},{3,7},{4,0},{5,1},{6,2},{7,3},{8,12},{9,13},{10,... | collective-permute-start | bytes 786440 | tf_op jit(solution)/shard_map/ppermute | solution.py:83
  164.2 24.6 %collective-permute-start.18 = (f32[256,256]{1,0:T(8,128)}, f32[256,256]{1,0:T(8,128)}, u32[]{:S(2)}, u32[]{:S(2)}) collective-permute-start(f32[256,256]{1,0:T(8,128)} %add.172), channel_id=1, source_target_pairs={{0,8},{1,9},{2,10},{3,11},{4,12},{5,13},{6,14},{7,15},{8,0},{9,1},... | collective-permute-start | bytes 786440 | tf_op jit(solution)/shard_map/ppermute | solution.py:83
  178.8 41.3 %all-to-all-start.2 = ((f32[128,8,256]{2,1,0:T(8,128)}), f32[128,8,256]{2,1,0:T(8,128)S(1)}, u32[]{:S(2)}, u32[]{:S(2)}) async-start(f32[128,8,256]{2,1,0:T(8,128)} %bitcast.19), calls=%async_computation.2 | async-start | bytes 2097152 | tf_op jit(solution)/shard_map/all_to_all | solution.py:183
  189.9 18.6 %collective-permute-start.19 = (f32[256,256]{1,0:T(8,128)S(1)}, f32[256,256]{1,0:T(8,128)S(1)}, u32[]{:S(2)}, u32[]{:S(2)}) collective-permute-start(f32[256,256]{1,0:T(8,128)S(1)} %add.173), channel_id=1, source_target_pairs={{0,16},{1,17},{2,18},{3,19},{4,20},{5,21},{6,22},{7,23},{8,24},{9,... | collective-permute-start | bytes 786440 | tf_op jit(solution)/shard_map/ppermute | solution.py:83
  208.6 7.0 %collective-permute-start.20 = (f32[256,256]{1,0:T(8,128)S(1)}, f32[256,256]{1,0:T(8,128)S(1)}, u32[]{:S(2)}, u32[]{:S(2)}) collective-permute-start(f32[256,256]{1,0:T(8,128)S(1)} %add.174), channel_id=1, source_target_pairs={{0,32},{1,33},{2,34},{3,35},{4,36},{5,37},{6,38},{7,39},{8,40},{9,... | collective-permute-start | bytes 786440 | tf_op jit(solution)/shard_map/ppermute | solution.py:83
  215.6 12.0 %collective-permute-start.21 = (f32[256,256]{1,0:T(8,128)S(1)}, f32[256,256]{1,0:T(8,128)S(1)}, u32[]{:S(2)}, u32[]{:S(2)}) collective-permute-start(f32[256,256]{1,0:T(8,128)S(1)} %add.175), channel_id=1, source_target_pairs={{0,64},{1,65},{2,66},{3,67},{4,68},{5,69},{6,70},{7,71},{8,72},{9,... | collective-permute-start | bytes 786440 | tf_op jit(solution)/shard_map/ppermute | solution.py:83

commit v6 on v5

--- a/solution.py
+++ b/solution.py
@@ -73,6 +73,34 @@
     return holder * slot_cap + positions - jnp.take(opening, holder)
 
 
+def tree_sum(value, axes, inner):
+    total = 1
+    for axis in axes:
+        total *= lax.axis_size(axis)
+    index = 0
+    for axis in axes:
+        index = index * lax.axis_size(axis) + lax.axis_index(axis)
+    step = 1
+    while step < inner and step < total and value.shape[0] % 2 == 0:
+        half = value.shape[0] // 2
+        upper = (index & step) != 0
+        keep = jnp.where(upper, value[half:], value[:half])
+        send = jnp.where(upper, value[:half], value[half:])
+        value = keep + lax.ppermute(send, axes, [(i, i ^ step) for i in range(total)])
+        step *= 2
+    halved = step
+    while step < total:
+        value = value + lax.ppermute(value, axes, [(i, i ^ step) for i in range(total)])
+        step *= 2
+    step = halved // 2
+    while step >= 1:
+        got = lax.ppermute(value, axes, [(i, i ^ step) for i in range(total)])
+        upper = (index & step) != 0
+        value = jnp.where(upper, jnp.concatenate([got, value]), jnp.concatenate([value, got]))
+        step //= 2
+    return value
+
+
 def butterfly_sum(value, axes):
     total = 1
     for axis in axes:
@@ -136,6 +164,7 @@
     pushed = lax.dot_general(
         soft_weights, row_queries, (((0,), (0,)), ((), ())), preferred_element_type=jnp.float32
     )
+    pulled, pushed = lax.optimization_barrier((pulled, pushed))
     pulled = plane_reduce_rows(pulled, axis, side, True)
     pushed = plane_reduce_rows(pushed, axis, side, False)
     query_grad = scaling * (pulled - item_vectors.astype(jnp.float32))
@@ -194,7 +223,11 @@
         (((0,), (0,)), ((), ())),
         preferred_element_type=jnp.float32,
     )
-    weight_grad = butterfly_sum(partial_value, ("batch", "table"))
+    total = lax.axis_size("batch") * lax.axis_size("table")
+    if total & (total - 1) == 0:
+        weight_grad = tree_sum(partial_value, ("batch", "table"), min(8, lax.axis_size("table")))
+    else:
+        weight_grad = lax.psum(partial_value, ("batch", "table"))
     return (table_grad, weight_grad)
 
 

time: 230 us -> 242 us (1.052)
  waiting for transfers between devices: 80.6 us -> 89.6 us
  local copies, waits for them, and re-layouts: 31.6 us -> 38.2 us
    ppermute x15, waiting for transfers between devices: 46.3 us -> 65.5 us  [plane_shift(): return lax.ppermute(value, axis, pairs)]
    ppermute x7 -> x10, waiting for transfers between devices: 31 us -> 20.8 us  [the longest x4 16.8 us: tree_sum(): lax.ppermute(value, axes, [(i, i ^ step) for i in range(total)])]
    ppermute x7 -> x10, starting transfers between devices: 17.8 us -> 22.8 us  [the longest x3 10.3 us: tree_sum(): got = lax.ppermute(value, axes, [(i, i ^ step) for i in range(total)])]
    all_to_all x1, starting transfers between devices: 10 us -> 5.67 us  [local(): lax.all_to_all(slot_grads, ('batch', 'table'), split_axis=0, concat_axis=...]
    slice x2, local copies, waits for them, and re-layouts: 0.21 us -> 3.77 us  [plane_reduce_rows(): value[(side - step) % side * block:((side - step) % side + 1) * block]]
    unnamed x21 -> x13, local copies, waits for them, and re-layouts: 1.56 us -> 4.65 us
    ppermute x15, starting transfers between devices: 16 us -> 13.5 us  [plane_shift(): return lax.ppermute(value, axis, pairs)]
  transfers between devices with their start and end apart: 25 -> 28, of which waited for: 13 -> 20; matrix products, arithmetic and copies ran while one was open for 23% -> 17% of each run, Pallas kernels for 0% -> 0%
where the time goes in v6:
time: 242 us
  waiting for transfers between devices  89.6 us (37%)
  starting transfers between devices  59.9 us (25%)
  local copies, waits for them, and re-layouts  38.2 us (16%)
  other arithmetic  31.3 us (13%)
  matrix products  21.6 us (9%)
    ppermute x15, waiting for transfers between devices, plane_shift(): return lax.ppermute(value, axis, pairs)  65.5 us
    gather x1, local copies, waits for them, and re-layouts, local(): looked = jnp.take(query_table, query_ids, axis=0).astype(jnp.float32)  18.7 us
    ppermute x4, waiting for transfers between devices, tree_sum(): lax.ppermute(value, axes, [(i, i ^ step) for i in range(total)])  16.8 us
    ppermute x15, starting transfers between devices, plane_shift(): return lax.ppermute(value, axis, pairs)  13.5 us
    all_to_all x1, starting transfers between devices, local(): lax.all_to_all(requests, ('batch', 'table'), split_axis=0, concat_axis=0,...  11.5 us
    ppermute x3, starting transfers between devices, tree_sum(): got = lax.ppermute(value, axes, [(i, i ^ step) for i in range(total)])  10.3 us
    reduce_sum x1, other arithmetic, block_grads(): local_sum = jnp.sum(jnp.exp(scores - local_max[:, None]), axis=1)  8.54 us
    dot_general x1, matrix products, block_grads(): lax.dot_general(row_queries, column_items, (((1,), (1,)), ((), ())), pref...  8.23 us
  transfers between devices with their start and end apart: 28, of which 20 were waited for; matrix products, arithmetic and copies ran while one was open for 17% of the time, Pallas kernels for 0%

profile of v6, /device:TPU:1, one launch (start us, length us, event | category | flops | bytes accessed | tf_op | source)
XLA Modules:
  0.0 241.7 jit_solution(115011696913426103)
XLA Ops:
  0.7 1.5 copy.22
  2.2 11.5 %all-to-all-start = ((s32[128,1,8]{2,1,0:T(1,128)}), s32[128,1,8]{2,1,0:T(1,128)S(1)}, u32[]{:S(2)}, u32[]{:S(2)}) async-start(s32[128,1,8]{2,1,0:T(1,128)} %bitcast), calls=%async_computation | async-start | bytes 131072 | tf_op jit(solution)/shard_map/all_to_all | solution.py:181
  13.7 0.8 copy.23
  14.7 0.7 bitcast_subtract_fusion
  15.4 0.9 convert_reduce_fusion.1
  16.3 3.3 %gather_fusion = s32[512]{0:T(512)S(1)} fusion(s32[128]{0:T(128)S(1)} %bitcast_subtract_fusion, s32[1024]{0:T(1024)S(1)} %pad_clamp_fusion.1), kind=kCustom, calls=%fused_computation | custom fusion | bytes 6144 | tf_op jit(solution)/shard_map/jit(_take)/gather | solution.py:73
  19.7 3.3 %all-to-all-done = s32[128,1,8]{2,1,0:T(1,128)S(1)} async-done(((s32[128,1,8]{2,1,0:T(1,128)}), s32[128,1,8]{2,1,0:T(1,128)S(1)}, u32[]{:S(2)}, u32[]{:S(2)}) %all-to-all-start) | async-done | bytes 4128 | tf_op jit(solution)/shard_map/all_to_all | solution.py:181
  23.2 3.9 %gather_fusion.1 = bf16[1024,256]{1,0:T(8,128)(2,1)S(1)} fusion(bf16[2048,256]{1,0:T(8,128)(2,1)S(1)} %copy-done, s32[1024]{0:T(1024)S(1)} %broadcast_clamp_fusion.1), kind=kCustom, calls=%fused_computation.1 | custom fusion | bytes 1052672 | tf_op jit(solution)/shard_map/jit(_take)/gather | solution.py:182
  27.1 1.0 bitcast_select_fusion.1
  28.6 6.5 %all-to-all-start.1 = ((bf16[128,8,256]{2,1,0:T(8,128)(2,1)}), bf16[128,8,256]{2,1,0:T(8,128)(2,1)S(1)}, u32[]{:S(2)}, u32[]{:S(2)}) async-start(bf16[128,8,256]{2,1,0:T(8,128)(2,1)} %bitcast_select_fusion.1), calls=%async_computation.1 | async-start | bytes 1048576 | tf_op jit(solution)/shard_map/all_to_all | solution.py:184
  35.1 18.7 %gather_fusion.2 = bf16[4096,256]{1,0:T(8,128)(2,1)} fusion(bf16[8192,256]{1,0:T(8,128)(2,1)} %param.8, s32[4096]{0:T(1024)S(1)} %broadcast_clamp_fusion), kind=kCustom, calls=%fused_computation.2 | custom fusion | bytes 4210688 | tf_op jit(solution)/shard_map/jit(_take)/gather | solution.py:189
  53.8 4.1 %convert_reduce_fusion = f32[512,256]{1,0:T(8,128)S(1)} fusion(bf16[4096,256]{1,0:T(8,128)(2,1)} %gather_fusion.2, pred[512,8]{1,0:T(8,128)(4,1)S(1)} %copy.24), kind=kLoop, calls=%fused_computation.9 | loop fusion | flops 3014656 | bytes 2625536 | tf_op jit(solution)/shard_map/reduce_sum | solution.py:190
  58.1 2.6 %collective-permute-start.2 = (bf16[512,256]{1,0:T(8,128)(2,1)S(1)}, bf16[512,256]{1,0:T(8,128)(2,1)S(1)}, u32[]{:S(2)}, u32[]{:S(2)}) collective-permute-start(bf16[512,256]{1,0:T(8,128)(2,1)S(1)} %convolution_convert_fusion), channel_id=1, source_target_pairs={{0,24},{8,0},{16,8},{24,16},{32,56},{40,32},{48,40},{56,48},{64,88... | collective-permute-start | bytes 786440 | tf_op jit(solution)/shard_map/ppermute | solution.py:125
  60.8 0.6 collective-permute-start.1
  61.4 0.6 collective-permute-start
  61.9 1.9 gather_fusion.3
  64.0 2.6 %collective-permute-start.5 = (bf16[512,256]{1,0:T(8,128)(2,1)S(1)}, bf16[512,256]{1,0:T(8,128)(2,1)S(1)}, u32[]{:S(2)}, u32[]{:S(2)}) collective-permute-start(bf16[512,256]{1,0:T(8,128)(2,1)S(1)} %broadcast_select_fusion), channel_id=1, source_target_pairs={{0,96},{8,104},{16,112},{24,120},{32,0},{40,8},{48,16},{56,24},{64... | collective-permute-start | bytes 786440 | tf_op jit(solution)/shard_map/ppermute | solution.py:125
  67.1 4.5 %collective-permute-done.2 = bf16[512,256]{1,0:T(8,128)(2,1)S(1)} collective-permute-done((bf16[512,256]{1,0:T(8,128)(2,1)S(1)}, bf16[512,256]{1,0:T(8,128)(2,1)S(1)}, u32[]{:S(2)}, u32[]{:S(2)}) %collective-permute-start.2) | collective-permute-done | bytes 262176 | tf_op jit(solution)/shard_map/ppermute | solution.py:125
  71.5 4.6 %collective-permute-done = bf16[512,256]{1,0:T(8,128)(2,1)S(1)} collective-permute-done((bf16[512,256]{1,0:T(8,128)(2,1)S(1)}, bf16[512,256]{1,0:T(8,128)(2,1)S(1)}, u32[]{:S(2)}, u32[]{:S(2)}) %collective-permute-start) | collective-permute-done | bytes 262176 | tf_op jit(solution)/shard_map/ppermute | solution.py:125
  76.1 5.5 %collective-permute-done.3 = bf16[512,256]{1,0:T(8,128)(2,1)S(1)} collective-permute-done((bf16[512,256]{1,0:T(8,128)(2,1)S(1)}, bf16[512,256]{1,0:T(8,128)(2,1)S(1)}, u32[]{:S(2)}, u32[]{:S(2)}) %collective-permute-start.3) | collective-permute-done | bytes 262176 | tf_op jit(solution)/shard_map/ppermute | solution.py:125
  81.6 8.2 %multiply_reduce_fusion = (f32[2048]{0:T(1024)S(1)}, f32[2048,2048]{0,1:T(8,128)}) fusion(bf16[512,256]{1,0:T(8,128)(2,1)S(1)} %collective-permute-done.5, bf16[512,256]{1,0:T(8,128)(2,1)S(1)} %collective-permute-done.4, bf16[512,256]{1,0:T(8,128)(2,1)S(1)} %collective-permute-done.3, bf16[512,256]{1,0:T(8,128)(2,1)S(1)} %broadcast_select_fusion, ...), kind=kOutput, calls=%fused_computation.8 | convolution fusion | flops 2164258816 | bytes 18882560 | tf_op jit(solution)/shard_map/dot_general | solution.py:145
  89.8 8.5 %exponential_reduce_fusion = f32[2048]{0:T(1024)S(1)} fusion(f32[2048,2048]{0,1:T(8,128)} %get-tuple-element.27, f32[2048]{0:T(1024)S(1)} %get-tuple-element.26), kind=kLoop, calls=%fused_computation.7 | loop fusion | flops 12580864 | bytes 16793600 | tf_op jit(solution)/shard_map/reduce_sum | solution.py:149
  98.4 1.4 collective-permute-start.8
  99.8 2.3 collective-permute-start.7
  102.2 1.7 collective-permute-done.7
  103.9 2.0 collective-permute-done.6
  106.0 7.4 %fusion.1 = f32[2048,256]{1,0:T(8,128)S(1)} fusion(f32[2048,2048]{0,1:T(8,128)} %get-tuple-element.27, f32[2048]{0:T(1024)S(1)} %log_add_fusion, bf16[512,256]{1,0:T(8,128)(2,1)S(1)} %collective-permute-done.5, bf16[512,256]{1,0:T(8,128)(2,1)S(1)} %collective-permute-done.4, bf16[512,256]{1,0:T(8,128)(2,1)S(1)} %collective-permute-done.3, ...), kind=kOutput, calls=%fused_computation.12 | convolution fusion | flops 2164260864 | bytes 19931136 | tf_op jit(solution)/shard_map/dot_general | solution.py:163
  113.4 3.1 %copy-done.1 = f32[2048,2048]{0,1:T(8,128)S(1)} copy-done((f32[2048,2048]{0,1:T(8,128)S(1)}, f32[2048,2048]{0,1:T(8,128)}, u32[]{:S(2)}) %copy-start.1) | copy-done | bytes 16777240
  116.5 4.2 %fusion = f32[2048,256]{1,0:T(8,128)} fusion(f32[2048,2048]{0,1:T(8,128)S(1)} %copy-done.1, f32[2048]{0:T(1024)S(1)} %log_add_fusion, bf16[512,256]{1,0:T(8,128)(2,1)S(1)} %collective-permute-done.2, bf16[512,256]{1,0:T(8,128)(2,1)S(1)} %collective-permute-done.1, bf16[512,256]{1,0:T(8,128)(2,1)S(1)} %collective-permute-done, ...), kind=kOutput, calls=%fused_computation.11 | convolution fusion | flops 2164260864 | bytes 19931136 | tf_op jit(solution)/shard_map/dot_general | solution.py:164
  120.8 1.2 fusion.29
  122.0 0.8 collective-permute-start.13
  122.7 0.7 collective-permute-start.12
  123.4 10.0 %collective-permute-done.14 = f32[512,256]{1,0:T(8,128)S(1)} collective-permute-done((f32[512,256]{1,0:T(8,128)}, f32[512,256]{1,0:T(8,128)S(1)}, u32[]{:S(2)}, u32[]{:S(2)}) %collective-permute-start.14) | collective-permute-done | bytes 524320 | tf_op jit(solution)/shard_map/ppermute | solution.py:125
  133.5 1.5 collective-permute-done.13
  134.9 13.9 %collective-permute-done.12 = f32[512,256]{1,0:T(8,128)} collective-permute-done((f32[512,256]{1,0:T(8,128)}, f32[512,256]{1,0:T(8,128)}, u32[]{:S(2)}, u32[]{:S(2)}) %collective-permute-start.12) | collective-permute-done | bytes 524320 | tf_op jit(solution)/shard_map/ppermute | solution.py:125
  148.9 1.5 fusion.14
  151.0 1.0 collective-permute-done.15
  152.0 1.5 collective-permute-start.16
  153.6 2.6 %fusion.30 = (f32[512,256]{1,0:T(8,128)}, f32[512,256]{1,0:T(8,128)}, f32[512,256]{1,0:T(8,128)}) fusion(f32[2048,256]{1,0:T(8,128)} %fusion), kind=kLoop, calls=%fused_computation.85 | loop fusion | bytes 3145728 | tf_op jit(solution)/shard_map/slice | solution.py:137
  156.6 1.0 collective-permute-start.9
  157.6 0.6 slice_select_fusion.2
  158.2 2.9 %collective-permute-start.17 = (f32[32,256]{1,0:T(8,128)}, f32[32,256]{1,0:T(8,128)}, u32[]{:S(2)}, u32[]{:S(2)}) collective-permute-start(f32[32,256]{1,0:T(8,128)} %slice_select_fusion.2), channel_id=1, source_target_pairs={{0,4},{1,5},{2,6},{3,7},{4,0},{5,1},{6,2},{7,3},{8,12},{9,13},{10,... | collective-permute-start | bytes 98312 | tf_op jit(solution)/shard_map/ppermute | solution.py:89
  161.2 8.0 %collective-permute-done.11 = f32[512,256]{1,0:T(8,128)S(1)} collective-permute-done((f32[512,256]{1,0:T(8,128)}, f32[512,256]{1,0:T(8,128)S(1)}, u32[]{:S(2)}, u32[]{:S(2)}) %collective-permute-start.11) | collective-permute-done | bytes 524320 | tf_op jit(solution)/shard_map/ppermute | solution.py:125
  169.2 1.6 collective-permute-done.10
  170.7 12.2 %collective-permute-done.9 = f32[512,256]{1,0:T(8,128)S(1)} collective-permute-done((f32[512,256]{1,0:T(8,128)}, f32[512,256]{1,0:T(8,128)S(1)}, u32[]{:S(2)}, u32[]{:S(2)}) %collective-permute-start.9) | collective-permute-done | bytes 524320 | tf_op jit(solution)/shard_map/ppermute | solution.py:125
  182.9 4.9 %scatter_custom_fusion = f32[1024,256]{1,0:T(8,128)} fusion(s32[512]{0:T(512)S(1)} %get-tuple-element.11, bf16[512,256]{1,0:T(8,128)(2,1)S(1)} %convolution_convert_fusion, f32[512,256]{1,0:T(8,128)S(1)} %collective-permute-done.11, f32[512,256]{1,0:T(8,128)S(1)} %collective-permute-done.10, f32[512,256]{1,0:T(8,128)S(1)} %collective-permute-done.9, ...), kind=kCustom, calls=%fused_computation.21 | custom fusion | flops 917504 | bytes 3408896 | tf_op jit(solution)/shard_map/scatter-add | solution.py:210
  187.8 5.7 %all-to-all-start.2 = ((f32[128,8,256]{2,1,0:T(8,128)}), f32[128,8,256]{2,1,0:T(8,128)S(1)}, u32[]{:S(2)}, u32[]{:S(2)}) async-start(f32[128,8,256]{2,1,0:T(8,128)} %bitcast.19), calls=%async_computation.2 | async-start | bytes 2097152 | tf_op jit(solution)/shard_map/all_to_all | solution.py:212
  193.5 0.8 select_add_fusion.2
  194.3 1.4 collective-permute-start.18
  195.6 11.2 %collective-permute-done.18 = f32[32,256]{1,0:T(8,128)S(1)} collective-permute-done((f32[32,256]{1,0:T(8,128)S(1)}, f32[32,256]{1,0:T(8,128)S(1)}, u32[]{:S(2)}, u32[]{:S(2)}) %collective-permute-start.18) | collective-permute-done | bytes 32800 | tf_op jit(solution)/shard_map/ppermute | solution.py:93
  206.8 2.4 collective-permute-start.19
  209.2 2.2 collective-permute-done.19
  211.4 1.2 collective-permute-start.20
  212.6 1.6 collective-permute-done.20
  214.1 2.6 %collective-permute-start.21 = (f32[32,256]{1,0:T(8,128)S(1)}, f32[32,256]{1,0:T(8,128)S(1)}, u32[]{:S(2)}, u32[]{:S(2)}) collective-permute-start(f32[32,256]{1,0:T(8,128)S(1)} %add.179), channel_id=1, source_target_pairs={{0,64},{1,65},{2,66},{3,67},{4,68},{5,69},{6,70},{7,71},{8,72},{9,... | collective-permute-start | bytes 98312 | tf_op jit(solution)/shard_map/ppermute | solution.py:93
  216.7 1.8 collective-permute-done.21
  218.6 2.7 %collective-permute-start.22 = (f32[32,256]{1,0:T(8,128)S(1)}, f32[32,256]{1,0:T(8,128)S(1)}, u32[]{:S(2)}, u32[]{:S(2)}) collective-permute-start(f32[32,256]{1,0:T(8,128)S(1)} %add.180), channel_id=1, source_target_pairs={{0,4},{1,5},{2,6},{3,7},{4,0},{5,1},{6,2},{7,3},{8,12},{9,13},{10,... | collective-permute-start | bytes 98312 | tf_op jit(solution)/shard_map/ppermute | solution.py:97
  221.2 1.6 collective-permute-done.22
  222.9 1.3 collective-permute-start.23
  224.7 0.8 reduce.4
  226.1 6.4 %collective-permute-start.24 = (f32[128,256]{1,0:T(8,128)S(1)}, f32[128,256]{1,0:T(8,128)S(1)}, u32[]{:S(2)}, u32[]{:S(2)}) collective-permute-start(f32[128,256]{1,0:T(8,128)S(1)} %maximum_select_fusion.1), channel_id=1, source_target_pairs={{0,1},{1,0},{2,3},{3,2},{4,5},{5,4},{6,7},{7,6},{8,9},{9,8},{10,11... | collective-permute-start | bytes 393224 | tf_op jit(solution)/shard_map/ppermute | solution.py:97
  232.4 1.0 collective-permute-done.24
  233.4 0.7 maximum_select_fusion
  234.1 7.5 %scatter_custom_fusion.1 = f32[2048,256]{1,0:T(8,128)} fusion(s32[1024]{0:T(1024)S(1)} %bitcast.44, f32[128,8,256]{2,1,0:T(8,128)S(1)} %all-to-all-done.2, f32[]{:T(128)} %constant.37.clone.1), kind=kCustom, calls=%fused_computation.16 | custom fusion | flops 262144 | bytes 3145732 | tf_op jit(solution)/shard_map/scatter-add | solution.py:218
  (69 shorter events, 4.1 us)
Async XLA Ops:
  0.6 22.5 %copy-start = (bf16[2048,256]{1,0:T(8,128)(2,1)S(1)}, bf16[2048,256]{1,0:T(8,128)(2,1)}, u32[]{:S(2)}) copy-start(bf16[2048,256]{1,0:T(8,128)(2,1)} %param.7) | copy-start | bytes 3145732
  0.6 19.0 %copy-start.5 = (s32[512]{0:T(512)S(1)}, s32[512]{0:T(512)}, u32[]{:S(2)}) copy-start(s32[512]{0:T(512)} %param.13) | copy-start | bytes 6148
  2.2 20.9 %all-to-all-start = ((s32[128,1,8]{2,1,0:T(1,128)}), s32[128,1,8]{2,1,0:T(1,128)S(1)}, u32[]{:S(2)}, u32[]{:S(2)}) async-start(s32[128,1,8]{2,1,0:T(1,128)} %bitcast), calls=%async_computation | async-start | bytes 131072 | tf_op jit(solution)/shard_map/all_to_all | solution.py:181
  23.2 5.0 %copy-start.4 = (s32[512,8]{0,1:T(8,128)S(1)}, s32[512,8]{0,1:T(8,128)}, u32[]{:S(2)}) copy-start(s32[512,8]{0,1:T(8,128)} %param.10) | copy-start | bytes 49156
  28.6 33.3 %all-to-all-start.1 = ((bf16[128,8,256]{2,1,0:T(8,128)(2,1)}), bf16[128,8,256]{2,1,0:T(8,128)(2,1)S(1)}, u32[]{:S(2)}, u32[]{:S(2)}) async-start(bf16[128,8,256]{2,1,0:T(8,128)(2,1)} %bitcast_select_fusion.1), calls=%async_computation.1 | async-start | bytes 1048576 | tf_op jit(solution)/shard_map/all_to_all | solution.py:184
  53.8 4.1 %copy-start.3 = (bf16[256,256]{1,0:T(8,128)(2,1)S(1)}, bf16[256,256]{1,0:T(8,128)(2,1)}, u32[]{:S(2)}) copy-start(bf16[256,256]{1,0:T(8,128)(2,1)} %param.9) | copy-start | bytes 393220
  58.1 13.4 %collective-permute-start.2 = (bf16[512,256]{1,0:T(8,128)(2,1)S(1)}, bf16[512,256]{1,0:T(8,128)(2,1)S(1)}, u32[]{:S(2)}, u32[]{:S(2)}) collective-permute-start(bf16[512,256]{1,0:T(8,128)(2,1)S(1)} %convolution_convert_fusion), channel_id=1, source_target_pairs={{0,24},{8,0},{16,8},{24,16},{32,56},{40,32},{48,40},{56,48},{64,88... | collective-permute-start | bytes 786440 | tf_op jit(solution)/shard_map/ppermute | solution.py:125
  60.8 10.8 %collective-permute-start.1 = (bf16[512,256]{1,0:T(8,128)(2,1)S(1)}, bf16[512,256]{1,0:T(8,128)(2,1)S(1)}, u32[]{:S(2)}, u32[]{:S(2)}) collective-permute-start(bf16[512,256]{1,0:T(8,128)(2,1)S(1)} %convolution_convert_fusion), channel_id=1, source_target_pairs={{0,16},{8,24},{16,0},{24,8},{32,48},{40,56},{48,32},{56,40},{64,80... | collective-permute-start | bytes 786440 | tf_op jit(solution)/shard_map/ppermute | solution.py:125
  61.4 14.8 %collective-permute-start = (bf16[512,256]{1,0:T(8,128)(2,1)S(1)}, bf16[512,256]{1,0:T(8,128)(2,1)S(1)}, u32[]{:S(2)}, u32[]{:S(2)}) collective-permute-start(bf16[512,256]{1,0:T(8,128)(2,1)S(1)} %convolution_convert_fusion), channel_id=1, source_target_pairs={{0,8},{8,16},{16,24},{24,0},{32,40},{40,48},{48,56},{56,32},{64,72... | collective-permute-start | bytes 786440 | tf_op jit(solution)/shard_map/ppermute | solution.py:125
  64.0 12.1 %collective-permute-start.5 = (bf16[512,256]{1,0:T(8,128)(2,1)S(1)}, bf16[512,256]{1,0:T(8,128)(2,1)S(1)}, u32[]{:S(2)}, u32[]{:S(2)}) collective-permute-start(bf16[512,256]{1,0:T(8,128)(2,1)S(1)} %broadcast_select_fusion), channel_id=1, source_target_pairs={{0,96},{8,104},{16,112},{24,120},{32,0},{40,8},{48,16},{56,24},{64... | collective-permute-start | bytes 786440 | tf_op jit(solution)/shard_map/ppermute | solution.py:125
  66.6 9.5 %collective-permute-start.4 = (bf16[512,256]{1,0:T(8,128)(2,1)S(1)}, bf16[512,256]{1,0:T(8,128)(2,1)S(1)}, u32[]{:S(2)}, u32[]{:S(2)}) collective-permute-start(bf16[512,256]{1,0:T(8,128)(2,1)S(1)} %broadcast_select_fusion), channel_id=1, source_target_pairs={{0,64},{8,72},{16,80},{24,88},{32,96},{40,104},{48,112},{56,120},{... | collective-permute-start | bytes 786440 | tf_op jit(solution)/shard_map/ppermute | solution.py:125
  71.5 10.1 %collective-permute-start.3 = (bf16[512,256]{1,0:T(8,128)(2,1)S(1)}, bf16[512,256]{1,0:T(8,128)(2,1)S(1)}, u32[]{:S(2)}, u32[]{:S(2)}) collective-permute-start(bf16[512,256]{1,0:T(8,128)(2,1)S(1)} %broadcast_select_fusion), channel_id=1, source_target_pairs={{0,32},{8,40},{16,48},{24,56},{32,64},{40,72},{48,80},{56,88},{64,... | collective-permute-start | bytes 786440 | tf_op jit(solution)/shard_map/ppermute | solution.py:125
  98.4 3.7 %collective-permute-start.8 = (f32[2,2048]{1,0:T(2,128)S(1)}, f32[2,2048]{1,0:T(2,128)S(1)}, u32[]{:S(2)}, u32[]{:S(2)}) collective-permute-start(f32[2,2048]{1,0:T(2,128)S(1)} %pad_maximum_fusion.6), channel_id=1, source_target_pairs={{0,24},{8,0},{16,8},{24,16},{32,56},{40,32},{48,40},{56,48},{64,88... | collective-permute-start | bytes 49160 | tf_op jit(solution)/shard_map/ppermute | solution.py:125
  99.8 4.1 %collective-permute-start.7 = (f32[2,2048]{1,0:T(2,128)S(1)}, f32[2,2048]{1,0:T(2,128)S(1)}, u32[]{:S(2)}, u32[]{:S(2)}) collective-permute-start(f32[2,2048]{1,0:T(2,128)S(1)} %pad_maximum_fusion.6), channel_id=1, source_target_pairs={{0,16},{8,24},{16,0},{24,8},{32,48},{40,56},{48,32},{56,40},{64,80... | collective-permute-start | bytes 49160 | tf_op jit(solution)/shard_map/ppermute | solution.py:125
  102.1 3.8 %collective-permute-start.6 = (f32[2,2048]{1,0:T(2,128)S(1)}, f32[2,2048]{1,0:T(2,128)S(1)}, u32[]{:S(2)}, u32[]{:S(2)}) collective-permute-start(f32[2,2048]{1,0:T(2,128)S(1)} %pad_maximum_fusion.6), channel_id=1, source_target_pairs={{0,8},{8,16},{16,24},{24,0},{32,40},{40,48},{48,56},{56,32},{64,72... | collective-permute-start | bytes 49160 | tf_op jit(solution)/shard_map/ppermute | solution.py:125
  106.0 10.5 %copy-start.1 = (f32[2048,2048]{0,1:T(8,128)S(1)}, f32[2048,2048]{0,1:T(8,128)}, u32[]{:S(2)}) copy-start(f32[2048,2048]{0,1:T(8,128)} %get-tuple-element.27) | copy-start | bytes 50331652
  116.5 4.2 %copy-start.2 = (f32[2048,256]{1,0:T(8,128)}, f32[2048,256]{1,0:T(8,128)S(1)}, u32[]{:S(2)}) copy-start(f32[2048,256]{1,0:T(8,128)S(1)} %fusion.1) | copy-start | bytes 6291460
  122.0 11.5 %collective-permute-start.14 = (f32[512,256]{1,0:T(8,128)}, f32[512,256]{1,0:T(8,128)S(1)}, u32[]{:S(2)}, u32[]{:S(2)}) collective-permute-start(f32[512,256]{1,0:T(8,128)} %get-tuple-element.13), channel_id=1, source_target_pairs={{0,24},{8,0},{16,8},{24,16},{32,56},{40,32},{48,40},{56,48},{64,88... | collective-permute-start | bytes 1572872 | tf_op jit(solution)/shard_map/ppermute | solution.py:125
  122.0 13.0 %collective-permute-start.13 = (f32[512,256]{1,0:T(8,128)}, f32[512,256]{1,0:T(8,128)S(1)}, u32[]{:S(2)}, u32[]{:S(2)}) collective-permute-start(f32[512,256]{1,0:T(8,128)} %get-tuple-element.14), channel_id=1, source_target_pairs={{0,16},{8,24},{16,0},{24,8},{32,48},{40,56},{48,32},{56,40},{64,80... | collective-permute-start | bytes 1572872 | tf_op jit(solution)/shard_map/ppermute | solution.py:125
  122.7 26.1 %collective-permute-start.12 = (f32[512,256]{1,0:T(8,128)}, f32[512,256]{1,0:T(8,128)}, u32[]{:S(2)}, u32[]{:S(2)}) collective-permute-start(f32[512,256]{1,0:T(8,128)} %get-tuple-element.12), channel_id=1, source_target_pairs={{0,8},{8,16},{16,24},{24,0},{32,40},{40,48},{48,56},{56,32},{64,72... | collective-permute-start | bytes 1572872 | tf_op jit(solution)/shard_map/ppermute | solution.py:125
  150.4 1.6 collective-permute-start.15
  152.0 5.6 %collective-permute-start.16 = (f32[64,256]{1,0:T(8,128)S(1)}, f32[64,256]{1,0:T(8,128)S(1)}, u32[]{:S(2)}, u32[]{:S(2)}) collective-permute-start(f32[64,256]{1,0:T(8,128)S(1)} %slice_select_fusion.1), channel_id=1, source_target_pairs={{0,2},{1,3},{2,0},{3,1},{4,6},{5,7},{6,4},{7,5},{8,10},{9,11},{10,... | collective-permute-start | bytes 196616 | tf_op jit(solution)/shard_map/ppermute | solution.py:89
  156.1 13.1 %collective-permute-start.11 = (f32[512,256]{1,0:T(8,128)}, f32[512,256]{1,0:T(8,128)S(1)}, u32[]{:S(2)}, u32[]{:S(2)}) collective-permute-start(f32[512,256]{1,0:T(8,128)} %get-tuple-element.16), channel_id=1, source_target_pairs={{0,96},{8,104},{16,112},{24,120},{32,0},{40,8},{48,16},{56,24},{64... | collective-permute-start | bytes 1572872 | tf_op jit(solution)/shard_map/ppermute | solution.py:125
  156.1 14.6 %collective-permute-start.10 = (f32[512,256]{1,0:T(8,128)}, f32[512,256]{1,0:T(8,128)S(1)}, u32[]{:S(2)}, u32[]{:S(2)}) collective-permute-start(f32[512,256]{1,0:T(8,128)} %get-tuple-element.17), channel_id=1, source_target_pairs={{0,64},{8,72},{16,80},{24,88},{32,96},{40,104},{48,112},{56,120},{... | collective-permute-start | bytes 1572872 | tf_op jit(solution)/shard_map/ppermute | solution.py:125
  156.6 26.4 %collective-permute-start.9 = (f32[512,256]{1,0:T(8,128)}, f32[512,256]{1,0:T(8,128)S(1)}, u32[]{:S(2)}, u32[]{:S(2)}) collective-permute-start(f32[512,256]{1,0:T(8,128)} %get-tuple-element.15), channel_id=1, source_target_pairs={{0,32},{8,40},{16,48},{24,56},{32,64},{40,72},{48,80},{56,88},{64,... | collective-permute-start | bytes 1572872 | tf_op jit(solution)/shard_map/ppermute | solution.py:125
  158.2 35.3 %collective-permute-start.17 = (f32[32,256]{1,0:T(8,128)}, f32[32,256]{1,0:T(8,128)}, u32[]{:S(2)}, u32[]{:S(2)}) collective-permute-start(f32[32,256]{1,0:T(8,128)} %slice_select_fusion.2), channel_id=1, source_target_pairs={{0,4},{1,5},{2,6},{3,7},{4,0},{5,1},{6,2},{7,3},{8,12},{9,13},{10,... | collective-permute-start | bytes 98312 | tf_op jit(solution)/shard_map/ppermute | solution.py:89
  187.8 46.3 %all-to-all-start.2 = ((f32[128,8,256]{2,1,0:T(8,128)}), f32[128,8,256]{2,1,0:T(8,128)S(1)}, u32[]{:S(2)}, u32[]{:S(2)}) async-start(f32[128,8,256]{2,1,0:T(8,128)} %bitcast.19), calls=%async_computation.2 | async-start | bytes 2097152 | tf_op jit(solution)/shard_map/all_to_all | solution.py:212
  194.3 12.5 %collective-permute-start.18 = (f32[32,256]{1,0:T(8,128)S(1)}, f32[32,256]{1,0:T(8,128)S(1)}, u32[]{:S(2)}, u32[]{:S(2)}) collective-permute-start(f32[32,256]{1,0:T(8,128)S(1)} %select_add_fusion.2), channel_id=1, source_target_pairs={{0,8},{1,9},{2,10},{3,11},{4,12},{5,13},{6,14},{7,15},{8,0},{9,1},... | collective-permute-start | bytes 98312 | tf_op jit(solution)/shard_map/ppermute | solution.py:93
  206.8 4.6 %collective-permute-start.19 = (f32[32,256]{1,0:T(8,128)S(1)}, f32[32,256]{1,0:T(8,128)S(1)}, u32[]{:S(2)}, u32[]{:S(2)}) collective-permute-start(f32[32,256]{1,0:T(8,128)S(1)} %add.177), channel_id=1, source_target_pairs={{0,16},{1,17},{2,18},{3,19},{4,20},{5,21},{6,22},{7,23},{8,24},{9,... | collective-permute-start | bytes 98312 | tf_op jit(solution)/shard_map/ppermute | solution.py:93
  211.4 2.8 %collective-permute-start.20 = (f32[32,256]{1,0:T(8,128)S(1)}, f32[32,256]{1,0:T(8,128)S(1)}, u32[]{:S(2)}, u32[]{:S(2)}) collective-permute-start(f32[32,256]{1,0:T(8,128)S(1)} %add.178), channel_id=1, source_target_pairs={{0,32},{1,33},{2,34},{3,35},{4,36},{5,37},{6,38},{7,39},{8,40},{9,... | collective-permute-start | bytes 98312 | tf_op jit(solution)/shard_map/ppermute | solution.py:93
  214.1 4.4 %collective-permute-start.21 = (f32[32,256]{1,0:T(8,128)S(1)}, f32[32,256]{1,0:T(8,128)S(1)}, u32[]{:S(2)}, u32[]{:S(2)}) collective-permute-start(f32[32,256]{1,0:T(8,128)S(1)} %add.179), channel_id=1, source_target_pairs={{0,64},{1,65},{2,66},{3,67},{4,68},{5,69},{6,70},{7,71},{8,72},{9,... | collective-permute-start | bytes 98312 | tf_op jit(solution)/shard_map/ppermute | solution.py:93
  218.6 4.3 %collective-permute-start.22 = (f32[32,256]{1,0:T(8,128)S(1)}, f32[32,256]{1,0:T(8,128)S(1)}, u32[]{:S(2)}, u32[]{:S(2)}) collective-permute-start(f32[32,256]{1,0:T(8,128)S(1)} %add.180), channel_id=1, source_target_pairs={{0,4},{1,5},{2,6},{3,7},{4,0},{5,1},{6,2},{7,3},{8,12},{9,13},{10,... | collective-permute-start | bytes 98312 | tf_op jit(solution)/shard_map/ppermute | solution.py:97
  222.9 3.2 %collective-permute-start.23 = (f32[64,256]{1,0:T(8,128)S(1)}, f32[64,256]{1,0:T(8,128)S(1)}, u32[]{:S(2)}, u32[]{:S(2)}) collective-permute-start(f32[64,256]{1,0:T(8,128)S(1)} %maximum_select_fusion.2), channel_id=1, source_target_pairs={{0,2},{1,3},{2,0},{3,1},{4,6},{5,7},{6,4},{7,5},{8,10},{9,11},{10,... | collective-permute-start | bytes 196616 | tf_op jit(solution)/shard_map/ppermute | solution.py:97
  226.1 7.3 %collective-permute-start.24 = (f32[128,256]{1,0:T(8,128)S(1)}, f32[128,256]{1,0:T(8,128)S(1)}, u32[]{:S(2)}, u32[]{:S(2)}) collective-permute-start(f32[128,256]{1,0:T(8,128)S(1)} %maximum_select_fusion.1), channel_id=1, source_target_pairs={{0,1},{1,0},{2,3},{3,2},{4,5},{5,4},{6,7},{7,6},{8,9},{9,8},{10,11... | collective-permute-start | bytes 393224 | tf_op jit(solution)/shard_map/ppermute | solution.py:97

commit v7 on v6

--- a/solution.py
+++ b/solution.py
@@ -139,16 +139,17 @@
     return total
 
 
-def block_grads(queries, item_vectors, axis, side, scaling):
-    row_queries = plane_gather_rows(queries, axis, side, True)
+def block_grads(hidden, query_weight, item_vectors, axis, side, scaling):
+    row_hidden = plane_gather_rows(hidden, axis, side, True)
     column_items = plane_gather_rows(item_vectors, axis, side, False)
+    row_queries = jnp.dot(row_hidden, query_weight, preferred_element_type=jnp.float32).astype(jnp.bfloat16)
     scores = scaling * lax.dot_general(
         row_queries, column_items, (((1,), (1,)), ((), ())), preferred_element_type=jnp.float32
     )
     local_max = jnp.max(scores, axis=1)
     local_sum = jnp.sum(jnp.exp(scores - local_max[:, None]), axis=1)
     stats = jnp.stack([local_max, local_sum])
-    block = queries.shape[0]
+    block = hidden.shape[0]
     gathered = [stats] + [
         jnp.roll(plane_shift(stats, axis, side, step, True), step * block, axis=1) for step in range(1, side)
     ]
@@ -164,12 +165,15 @@
     pushed = lax.dot_general(
         soft_weights, row_queries, (((0,), (0,)), ((), ())), preferred_element_type=jnp.float32
     )
-    pulled, pushed = lax.optimization_barrier((pulled, pushed))
-    pulled = plane_reduce_rows(pulled, axis, side, True)
+    weight_part = lax.dot_general(
+        row_hidden, pulled, (((0,), (0,)), ((), ())),
+        preferred_element_type=jnp.float32, precision=lax.Precision.HIGHEST,
+    ) - lax.dot_general(
+        hidden, item_vectors, (((0,), (0,)), ((), ())), preferred_element_type=jnp.float32
+    )
     pushed = plane_reduce_rows(pushed, axis, side, False)
-    query_grad = scaling * (pulled - item_vectors.astype(jnp.float32))
-    item_grad = scaling * (pushed - queries.astype(jnp.float32))
-    return query_grad, item_grad
+    item_grad = scaling * (pushed - row_queries[:block].astype(jnp.float32))
+    return item_grad, scaling * weight_part
 
 
 def local(item_table, query_table, query_weight, query_ids, fetch_rows, counts, example_pos):
@@ -191,7 +195,7 @@
     queries = jnp.dot(hidden, query_weight, preferred_element_type=jnp.float32).astype(jnp.bfloat16)
     side = int(round(lax.axis_size("batch") ** 0.5))
     if side * side == lax.axis_size("batch") and side > 1:
-        query_grad, item_grad = block_grads(queries, item_vectors, "batch", side, scaling)
+        item_grad, partial_value = block_grads(hidden, query_weight, item_vectors, "batch", side, scaling)
     else:
         group_queries = lax.all_gather(queries, "batch", axis=0, tiled=True)
         group_items = lax.all_gather(item_vectors, "batch", axis=0, tiled=True)
@@ -207,6 +211,12 @@
         soft_back = jnp.exp(scores_back - group_totals).astype(jnp.bfloat16)
         summed = jnp.dot(soft_back, group_queries, preferred_element_type=jnp.float32)
         item_grad = scaling * (summed - queries.astype(jnp.float32))
+        partial_value = lax.dot_general(
+            hidden,
+            query_grad.astype(jnp.bfloat16),
+            (((0,), (0,)), ((), ())),
+            preferred_element_type=jnp.float32,
+        )
     slot_grads = jax.ops.segment_sum(item_grad, slot_ids, num_segments=sources * slot_cap)
     slot_grads = slot_grads.reshape(sources, slot_cap, model_width)
     returned = lax.all_to_all(
@@ -216,12 +226,6 @@
         jnp.zeros((table_rows, model_width), jnp.float32)
         .at[wanted.reshape(-1)]
         .add(returned.reshape(-1, model_width))
-    )
-    partial_value = lax.dot_general(
-        hidden,
-        query_grad.astype(jnp.bfloat16),
-        (((0,), (0,)), ((), ())),
-        preferred_element_type=jnp.float32,
     )
     total = lax.axis_size("batch") * lax.axis_size("table")
     if total & (total - 1) == 0:

time: 242 us -> 211 us (0.87)
  waiting for transfers between devices: 89.6 us -> 53.7 us
  starting transfers between devices: 59.9 us -> 69.6 us
  local copies, waits for them, and re-layouts: 38.2 us -> 32.6 us
    ppermute x15 -> x12, waiting for transfers between devices: 65.5 us -> 29.9 us  [plane_shift(): return lax.ppermute(value, axis, pairs)]
    dot_general x2 -> x3, matrix products: 1.75 us -> 5.19 us  [the longest x1 3.36 us: block_grads(): lax.dot_general(row_hidden, pulled, (((0,), (0,)), ((), ())), preferred_e...]
    ppermute x3, starting transfers between devices: 5.02 us -> 8.35 us  [tree_sum(): lax.ppermute(send, axes, [(i, i ^ step) for i in range(total)])]
    unnamed x13 -> x17, local copies, waits for them, and re-layouts: 4.65 us -> 1.55 us
    ppermute x15 -> x12, starting transfers between devices: 13.5 us -> 16.6 us  [plane_shift(): return lax.ppermute(value, axis, pairs)]
    all_to_all x1, starting transfers between devices: 5.67 us -> 8.61 us  [local(): lax.all_to_all(slot_grads, ('batch', 'table'), split_axis=0, concat_axis=...]
    slice x2 -> x1, local copies, waits for them, and re-layouts: 3.77 us -> 1.2 us  [plane_reduce_rows(): value[(side - step) % side * block:((side - step) % side + 1) * block]]
  transfers between devices with their start and end apart: 28 -> 25, of which waited for: 20 -> 16; matrix products, arithmetic and copies ran while one was open for 17% -> 21% of each run, Pallas kernels for 0% -> 0%
where the time goes in v7:
time: 211 us
  starting transfers between devices  69.6 us (33%)
  waiting for transfers between devices  53.7 us (25%)
  local copies, waits for them, and re-layouts  32.6 us (15%)
  other arithmetic  30.2 us (14%)
  matrix products  23.7 us (11%)
    ppermute x12, waiting for transfers between devices, plane_shift(): return lax.ppermute(value, axis, pairs)  29.9 us
    gather x1, local copies, waits for them, and re-layouts, local(): looked = jnp.take(query_table, query_ids, axis=0).astype(jnp.float32)  18.7 us
    ppermute x4, waiting for transfers between devices, tree_sum(): lax.ppermute(value, axes, [(i, i ^ step) for i in range(total)])  17.4 us
    ppermute x12, starting transfers between devices, plane_shift(): return lax.ppermute(value, axis, pairs)  16.6 us
    all_to_all x1, starting transfers between devices, local(): lax.all_to_all(requests, ('batch', 'table'), split_axis=0, concat_axis=0,...  11.5 us
    ppermute x3, starting transfers between devices, tree_sum(): got = lax.ppermute(value, axes, [(i, i ^ step) for i in range(total)])  10.6 us
    all_to_all x1, starting transfers between devices, local(): lax.all_to_all(slot_grads, ('batch', 'table'), split_axis=0, concat_axis=...  8.61 us
    reduce_sum x1, other arithmetic, block_grads(): local_sum = jnp.sum(jnp.exp(scores - local_max[:, None]), axis=1)  8.55 us
  transfers between devices with their start and end apart: 25, of which 16 were waited for; matrix products, arithmetic and copies ran while one was open for 21% of the time, Pallas kernels for 0%

profile of v7, /device:TPU:1, one launch (start us, length us, event | category | flops | bytes accessed | tf_op | source)
XLA Modules:
  0.0 210.9 jit_solution(4787201470763536537)
XLA Ops:
  0.7 1.5 copy.22
  2.2 11.5 %all-to-all-start = ((s32[128,1,8]{2,1,0:T(1,128)}), s32[128,1,8]{2,1,0:T(1,128)S(1)}, u32[]{:S(2)}, u32[]{:S(2)}) async-start(s32[128,1,8]{2,1,0:T(1,128)} %bitcast), calls=%async_computation | async-start | bytes 131072 | tf_op jit(solution)/shard_map/all_to_all | solution.py:185
  13.7 0.8 copy.23
  14.4 0.2 reduce-window.8
  14.7 0.7 bitcast_subtract_fusion
  15.4 0.9 convert_reduce_fusion.1
  16.3 3.3 %gather_fusion = s32[512]{0:T(512)S(1)} fusion(s32[128]{0:T(128)S(1)} %bitcast_subtract_fusion, s32[1024]{0:T(1024)S(1)} %pad_clamp_fusion.1), kind=kCustom, calls=%fused_computation | custom fusion | bytes 6144 | tf_op jit(solution)/shard_map/jit(_take)/gather | solution.py:73
  19.7 3.3 %all-to-all-done = s32[128,1,8]{2,1,0:T(1,128)S(1)} async-done(((s32[128,1,8]{2,1,0:T(1,128)}), s32[128,1,8]{2,1,0:T(1,128)S(1)}, u32[]{:S(2)}, u32[]{:S(2)}) %all-to-all-start) | async-done | bytes 4128 | tf_op jit(solution)/shard_map/all_to_all | solution.py:185
  23.2 3.9 %gather_fusion.1 = bf16[1024,256]{1,0:T(8,128)(2,1)S(1)} fusion(bf16[2048,256]{1,0:T(8,128)(2,1)S(1)} %copy-done, s32[1024]{0:T(1024)S(1)} %broadcast_clamp_fusion.1), kind=kCustom, calls=%fused_computation.1 | custom fusion | bytes 1052672 | tf_op jit(solution)/shard_map/jit(_take)/gather | solution.py:186
  27.1 1.0 bitcast_select_fusion.1
  28.6 6.5 %all-to-all-start.1 = ((bf16[128,8,256]{2,1,0:T(8,128)(2,1)}), bf16[128,8,256]{2,1,0:T(8,128)(2,1)S(1)}, u32[]{:S(2)}, u32[]{:S(2)}) async-start(bf16[128,8,256]{2,1,0:T(8,128)(2,1)} %bitcast_select_fusion.1), calls=%async_computation.1 | async-start | bytes 1048576 | tf_op jit(solution)/shard_map/all_to_all | solution.py:188
  35.1 18.7 %gather_fusion.2 = bf16[4096,256]{1,0:T(8,128)(2,1)} fusion(bf16[8192,256]{1,0:T(8,128)(2,1)} %param.8, s32[4096]{0:T(1024)S(1)} %broadcast_clamp_fusion), kind=kCustom, calls=%fused_computation.2 | custom fusion | bytes 4210688 | tf_op jit(solution)/shard_map/jit(_take)/gather | solution.py:193
  53.8 4.1 %convert_reduce_fusion = f32[512,256]{1,0:T(8,128)S(1)} fusion(bf16[4096,256]{1,0:T(8,128)(2,1)} %gather_fusion.2, pred[512,8]{1,0:T(8,128)(4,1)S(1)} %copy.24), kind=kLoop, calls=%fused_computation.9 | loop fusion | flops 3014656 | bytes 2625536 | tf_op jit(solution)/shard_map/reduce_sum | solution.py:194
  57.9 1.4 collective-permute-start
  59.3 2.4 %collective-permute-start.1 = (bf16[512,256]{1,0:T(8,128)(2,1)S(1)}, bf16[512,256]{1,0:T(8,128)(2,1)}, u32[]{:S(2)}, u32[]{:S(2)}) collective-permute-start(bf16[512,256]{1,0:T(8,128)(2,1)S(1)} %multiply_convert_fusion), channel_id=1, source_target_pairs={{0,16},{8,24},{16,0},{24,8},{32,48},{40,56},{48,32},{56,40},{64,80... | collective-permute-start | bytes 786440 | tf_op jit(solution)/shard_map/ppermute | solution.py:125
  61.7 1.2 collective-permute-start.2
  62.9 2.0 gather_fusion.3
  65.0 1.3 collective-permute-start.3
  66.3 2.5 %collective-permute-start.4 = (bf16[512,256]{1,0:T(8,128)(2,1)S(1)}, bf16[512,256]{1,0:T(8,128)(2,1)S(1)}, u32[]{:S(2)}, u32[]{:S(2)}) collective-permute-start(bf16[512,256]{1,0:T(8,128)(2,1)S(1)} %broadcast_select_fusion), channel_id=1, source_target_pairs={{0,64},{8,72},{16,80},{24,88},{32,96},{40,104},{48,112},{56,120},{... | collective-permute-start | bytes 786440 | tf_op jit(solution)/shard_map/ppermute | solution.py:125
  68.8 1.1 collective-permute-start.5
  69.9 3.6 %collective-permute-done.1 = bf16[512,256]{1,0:T(8,128)(2,1)} collective-permute-done((bf16[512,256]{1,0:T(8,128)(2,1)S(1)}, bf16[512,256]{1,0:T(8,128)(2,1)}, u32[]{:S(2)}, u32[]{:S(2)}) %collective-permute-start.1) | collective-permute-done | bytes 262176 | tf_op jit(solution)/shard_map/ppermute | solution.py:125
  73.4 1.6 convolution_convert_fusion
  75.0 4.5 %collective-permute-done.4 = bf16[512,256]{1,0:T(8,128)(2,1)S(1)} collective-permute-done((bf16[512,256]{1,0:T(8,128)(2,1)S(1)}, bf16[512,256]{1,0:T(8,128)(2,1)S(1)}, u32[]{:S(2)}, u32[]{:S(2)}) %collective-permute-start.4) | collective-permute-done | bytes 262176 | tf_op jit(solution)/shard_map/ppermute | solution.py:125
  79.6 8.2 %multiply_reduce_fusion = (f32[2048]{0:T(1024)S(1)}, f32[2048,2048]{0,1:T(8,128)}) fusion(bf16[2048,256]{1,0:T(8,128)(2,1)S(1)} %convolution_convert_fusion, bf16[512,256]{1,0:T(8,128)(2,1)S(1)} %collective-permute-done.5, bf16[512,256]{1,0:T(8,128)(2,1)S(1)} %collective-permute-done.4, bf16[512,256]{1,0:T(8,128)(2,1)S(1)} %collective-permute-done.3, ...), kind=kOutput, calls=%fused_computation.8 | convolution fusion | flops 2160064512 | bytes 18882560 | tf_op jit(solution)/shard_map/dot_general | solution.py:146
  87.8 8.6 %exponential_reduce_fusion = f32[2048]{0:T(1024)S(1)} fusion(f32[2048,2048]{0,1:T(8,128)} %get-tuple-element.20, f32[2048]{0:T(1024)S(1)} %get-tuple-element.19), kind=kLoop, calls=%fused_computation.7 | loop fusion | flops 12580864 | bytes 16793600 | tf_op jit(solution)/shard_map/reduce_sum | solution.py:150
  96.4 0.4 collective-permute-start.6
  96.7 0.3 fusion.28
  97.0 1.3 collective-permute-start.7
  98.2 1.3 collective-permute-start.8
  99.5 0.7 collective-permute-done.6
  100.3 1.0 collective-permute-done.7
  101.4 7.4 %fusion = f32[2048,256]{1,0:T(8,128)S(1)} fusion(f32[2048,2048]{0,1:T(8,128)} %get-tuple-element.20, f32[2048]{0:T(1024)S(1)} %log_add_fusion, bf16[512,256]{1,0:T(8,128)(2,1)S(1)} %collective-permute-done.5, bf16[512,256]{1,0:T(8,128)(2,1)S(1)} %collective-permute-done.4, bf16[512,256]{1,0:T(8,128)(2,1)S(1)} %collective-permute-done.3, ...), kind=kOutput, calls=%fused_computation.12 | convolution fusion | flops 2164260864 | bytes 19931136 | tf_op jit(solution)/shard_map/dot_general | solution.py:164
  108.8 3.4 %fusion.2 = f32[256,256]{1,0:T(8,128)S(1)} fusion(f32[256,256]{1,0:T(8,128)S(1)} %fusion.28, f32[2048,256]{1,0:T(8,128)S(1)} %fusion, bf16[512,256]{1,0:T(8,128)(2,1)} %collective-permute-done.2, bf16[512,256]{1,0:T(8,128)(2,1)} %collective-permute-done.1, bf16[512,256]{1,0:T(8,128)(2,1)} %collective-permute-done, bf16[512,256]{1,0:T(8,128)(2,1)S(1)} %multiply_convert_fusion), kind=kOutput, calls=%fused_computation.15 | convolution fusion | flops 1614938112 | bytes 3670016 | tf_op jit(solution)/shard_map/dot_general | solution.py:168
  112.2 3.8 %collective-permute-start.12 = (f32[128,256]{1,0:T(8,128)S(1)}, f32[128,256]{1,0:T(8,128)S(1)}, u32[]{:S(2)}, u32[]{:S(2)}) collective-permute-start(f32[128,256]{1,0:T(8,128)S(1)} %slice_select_fusion), channel_id=1, source_target_pairs={{0,1},{1,0},{2,3},{3,2},{4,5},{5,4},{6,7},{7,6},{8,9},{9,8},{10,11... | collective-permute-start | bytes 393224 | tf_op jit(solution)/shard_map/ppermute | solution.py:89
  116.0 2.9 %fusion.1 = f32[2048,256]{1,0:T(8,128)S(1)} fusion(bf16[2048,256]{1,0:T(8,128)(2,1)S(1)} %convolution_convert_fusion, f32[2048,2048]{0,1:T(8,128)S(1)} %bitcast.37, f32[2048]{0:T(1024)S(1)} %log_add_fusion), kind=kOutput, calls=%fused_computation.13 | convolution fusion | flops 2160066560 | bytes 19931136 | tf_op jit(solution)/shard_map/dot_general | solution.py:165
  119.0 1.5 collective-permute-start.13
  120.6 1.2 fusion.26
  121.8 2.3 %collective-permute-start.10 = (f32[512,256]{1,0:T(8,128)}, f32[512,256]{1,0:T(8,128)S(1)}, u32[]{:S(2)}, u32[]{:S(2)}) collective-permute-start(f32[512,256]{1,0:T(8,128)} %get-tuple-element.10), channel_id=1, source_target_pairs={{0,64},{8,72},{16,80},{24,88},{32,96},{40,104},{48,112},{56,120},{... | collective-permute-start | bytes 1572872 | tf_op jit(solution)/shard_map/ppermute | solution.py:125
  124.1 1.3 collective-permute-start.11
  125.3 0.2 collective-permute-start.9
  125.6 3.0 %collective-permute-start.14 = (f32[32,256]{1,0:T(8,128)S(1)}, f32[32,256]{1,0:T(8,128)S(1)}, u32[]{:S(2)}, u32[]{:S(2)}) collective-permute-start(f32[32,256]{1,0:T(8,128)S(1)} %slice_select_fusion.2), channel_id=1, source_target_pairs={{0,4},{1,5},{2,6},{3,7},{4,0},{5,1},{6,2},{7,3},{8,12},{9,13},{10,... | collective-permute-start | bytes 98312 | tf_op jit(solution)/shard_map/ppermute | solution.py:89
  128.6 8.1 %collective-permute-done.10 = f32[512,256]{1,0:T(8,128)S(1)} collective-permute-done((f32[512,256]{1,0:T(8,128)}, f32[512,256]{1,0:T(8,128)S(1)}, u32[]{:S(2)}, u32[]{:S(2)}) %collective-permute-start.10) | collective-permute-done | bytes 524320 | tf_op jit(solution)/shard_map/ppermute | solution.py:125
  136.7 10.8 %collective-permute-done.11 = f32[512,256]{1,0:T(8,128)} collective-permute-done((f32[512,256]{1,0:T(8,128)}, f32[512,256]{1,0:T(8,128)}, u32[]{:S(2)}, u32[]{:S(2)}) %collective-permute-start.11) | collective-permute-done | bytes 524320 | tf_op jit(solution)/shard_map/ppermute | solution.py:125
  147.5 1.2 collective-permute-done.9
  148.7 5.2 %scatter_custom_fusion = f32[1024,256]{1,0:T(8,128)} fusion(s32[512]{0:T(512)S(1)} %get-tuple-element.7, f32[512,256]{1,0:T(8,128)} %collective-permute-done.11, f32[512,256]{1,0:T(8,128)S(1)} %collective-permute-done.10, f32[512,256]{1,0:T(8,128)} %collective-permute-done.9, f32[2048,256]{1,0:T(8,128)} %copy-done.1, f32[]{:T(128)} %constant.37.clone.1, ...), kind=kCustom, calls=%fused_computation.26 | custom fusion | flops 917504 | bytes 3408896 | tf_op jit(solution)/shard_map/scatter-add | solution.py:220
  153.9 8.6 %all-to-all-start.2 = ((f32[128,8,256]{2,1,0:T(8,128)}), f32[128,8,256]{2,1,0:T(8,128)S(1)}, u32[]{:S(2)}, u32[]{:S(2)}) async-start(f32[128,8,256]{2,1,0:T(8,128)} %bitcast.19), calls=%async_computation.2 | async-start | bytes 2097152 | tf_op jit(solution)/shard_map/all_to_all | solution.py:222
  162.5 1.4 collective-permute-start.15
  164.0 11.8 %collective-permute-done.15 = f32[32,256]{1,0:T(8,128)S(1)} collective-permute-done((f32[32,256]{1,0:T(8,128)S(1)}, f32[32,256]{1,0:T(8,128)S(1)}, u32[]{:S(2)}, u32[]{:S(2)}) %collective-permute-start.15) | collective-permute-done | bytes 32800 | tf_op jit(solution)/shard_map/ppermute | solution.py:93
  175.8 2.4 %collective-permute-start.16 = (f32[32,256]{1,0:T(8,128)S(1)}, f32[32,256]{1,0:T(8,128)S(1)}, u32[]{:S(2)}, u32[]{:S(2)}) collective-permute-start(f32[32,256]{1,0:T(8,128)S(1)} %add.165), channel_id=1, source_target_pairs={{0,16},{1,17},{2,18},{3,19},{4,20},{5,21},{6,22},{7,23},{8,24},{9,... | collective-permute-start | bytes 98312 | tf_op jit(solution)/shard_map/ppermute | solution.py:93
  178.2 2.2 %collective-permute-done.16 = f32[32,256]{1,0:T(8,128)S(1)} collective-permute-done((f32[32,256]{1,0:T(8,128)S(1)}, f32[32,256]{1,0:T(8,128)S(1)}, u32[]{:S(2)}, u32[]{:S(2)}) %collective-permute-start.16) | collective-permute-done | bytes 32800 | tf_op jit(solution)/shard_map/ppermute | solution.py:93
  180.4 1.2 collective-permute-start.17
  181.6 1.6 collective-permute-done.17
  183.1 2.6 %collective-permute-start.18 = (f32[32,256]{1,0:T(8,128)S(1)}, f32[32,256]{1,0:T(8,128)S(1)}, u32[]{:S(2)}, u32[]{:S(2)}) collective-permute-start(f32[32,256]{1,0:T(8,128)S(1)} %add.167), channel_id=1, source_target_pairs={{0,64},{1,65},{2,66},{3,67},{4,68},{5,69},{6,70},{7,71},{8,72},{9,... | collective-permute-start | bytes 98312 | tf_op jit(solution)/shard_map/ppermute | solution.py:93
  185.7 1.8 collective-permute-done.18
  187.6 2.7 %collective-permute-start.19 = (f32[32,256]{1,0:T(8,128)S(1)}, f32[32,256]{1,0:T(8,128)S(1)}, u32[]{:S(2)}, u32[]{:S(2)}) collective-permute-start(f32[32,256]{1,0:T(8,128)S(1)} %add.168), channel_id=1, source_target_pairs={{0,4},{1,5},{2,6},{3,7},{4,0},{5,1},{6,2},{7,3},{8,12},{9,13},{10,... | collective-permute-start | bytes 98312 | tf_op jit(solution)/shard_map/ppermute | solution.py:97
  190.2 1.6 collective-permute-done.19
  191.8 1.3 collective-permute-start.20
  193.1 0.5 broadcast.91
  193.7 0.8 reduce.4
  194.6 0.5 collective-permute-done.20
  195.1 6.6 %collective-permute-start.21 = (f32[128,256]{1,0:T(8,128)S(1)}, f32[128,256]{1,0:T(8,128)S(1)}, u32[]{:S(2)}, u32[]{:S(2)}) collective-permute-start(f32[128,256]{1,0:T(8,128)S(1)} %maximum_select_fusion.1), channel_id=1, source_target_pairs={{0,1},{1,0},{2,3},{3,2},{4,5},{5,4},{6,7},{7,6},{8,9},{9,8},{10,11... | collective-permute-start | bytes 393224 | tf_op jit(solution)/shard_map/ppermute | solution.py:97
  201.7 1.0 collective-permute-done.21
  202.7 0.7 maximum_select_fusion
  203.4 7.5 %scatter_custom_fusion.1 = f32[2048,256]{1,0:T(8,128)} fusion(s32[1024]{0:T(1024)S(1)} %bitcast.51, f32[128,8,256]{2,1,0:T(8,128)S(1)} %all-to-all-done.2, f32[]{:T(128)} %constant.37.clone.1), kind=kCustom, calls=%fused_computation.18 | custom fusion | flops 262144 | bytes 3145732 | tf_op jit(solution)/shard_map/scatter-add | solution.py:228
  (69 shorter events, 1.4 us)
Async XLA Ops:
  0.6 22.5 %copy-start = (bf16[2048,256]{1,0:T(8,128)(2,1)S(1)}, bf16[2048,256]{1,0:T(8,128)(2,1)}, u32[]{:S(2)}) copy-start(bf16[2048,256]{1,0:T(8,128)(2,1)} %param.7) | copy-start | bytes 3145732
  0.6 19.0 %copy-start.3 = (s32[512]{0:T(512)S(1)}, s32[512]{0:T(512)}, u32[]{:S(2)}) copy-start(s32[512]{0:T(512)} %param.13) | copy-start | bytes 6148
  2.2 20.9 %all-to-all-start = ((s32[128,1,8]{2,1,0:T(1,128)}), s32[128,1,8]{2,1,0:T(1,128)S(1)}, u32[]{:S(2)}, u32[]{:S(2)}) async-start(s32[128,1,8]{2,1,0:T(1,128)} %bitcast), calls=%async_computation | async-start | bytes 131072 | tf_op jit(solution)/shard_map/all_to_all | solution.py:185
  23.2 5.0 %copy-start.2 = (s32[512,8]{0,1:T(8,128)S(1)}, s32[512,8]{0,1:T(8,128)}, u32[]{:S(2)}) copy-start(s32[512,8]{0,1:T(8,128)} %param.10) | copy-start | bytes 49156
  28.6 34.3 %all-to-all-start.1 = ((bf16[128,8,256]{2,1,0:T(8,128)(2,1)}), bf16[128,8,256]{2,1,0:T(8,128)(2,1)S(1)}, u32[]{:S(2)}, u32[]{:S(2)}) async-start(bf16[128,8,256]{2,1,0:T(8,128)(2,1)} %bitcast_select_fusion.1), calls=%async_computation.1 | async-start | bytes 1048576 | tf_op jit(solution)/shard_map/all_to_all | solution.py:188
  57.9 10.9 %collective-permute-start = (bf16[512,256]{1,0:T(8,128)(2,1)S(1)}, bf16[512,256]{1,0:T(8,128)(2,1)}, u32[]{:S(2)}, u32[]{:S(2)}) collective-permute-start(bf16[512,256]{1,0:T(8,128)(2,1)S(1)} %multiply_convert_fusion), channel_id=1, source_target_pairs={{0,8},{8,16},{16,24},{24,0},{32,40},{40,48},{48,56},{56,32},{64,72... | collective-permute-start | bytes 786440 | tf_op jit(solution)/shard_map/ppermute | solution.py:125
  59.3 14.1 %collective-permute-start.1 = (bf16[512,256]{1,0:T(8,128)(2,1)S(1)}, bf16[512,256]{1,0:T(8,128)(2,1)}, u32[]{:S(2)}, u32[]{:S(2)}) collective-permute-start(bf16[512,256]{1,0:T(8,128)(2,1)S(1)} %multiply_convert_fusion), channel_id=1, source_target_pairs={{0,16},{8,24},{16,0},{24,8},{32,48},{40,56},{48,32},{56,40},{64,80... | collective-permute-start | bytes 786440 | tf_op jit(solution)/shard_map/ppermute | solution.py:125
  61.7 11.7 %collective-permute-start.2 = (bf16[512,256]{1,0:T(8,128)(2,1)S(1)}, bf16[512,256]{1,0:T(8,128)(2,1)}, u32[]{:S(2)}, u32[]{:S(2)}) collective-permute-start(bf16[512,256]{1,0:T(8,128)(2,1)S(1)} %multiply_convert_fusion), channel_id=1, source_target_pairs={{0,24},{8,0},{16,8},{24,16},{32,56},{40,32},{48,40},{56,48},{64,88... | collective-permute-start | bytes 786440 | tf_op jit(solution)/shard_map/ppermute | solution.py:125
  65.0 10.0 %collective-permute-start.3 = (bf16[512,256]{1,0:T(8,128)(2,1)S(1)}, bf16[512,256]{1,0:T(8,128)(2,1)S(1)}, u32[]{:S(2)}, u32[]{:S(2)}) collective-permute-start(bf16[512,256]{1,0:T(8,128)(2,1)S(1)} %broadcast_select_fusion), channel_id=1, source_target_pairs={{0,32},{8,40},{16,48},{24,56},{32,64},{40,72},{48,80},{56,88},{64,... | collective-permute-start | bytes 786440 | tf_op jit(solution)/shard_map/ppermute | solution.py:125
  66.3 13.3 %collective-permute-start.4 = (bf16[512,256]{1,0:T(8,128)(2,1)S(1)}, bf16[512,256]{1,0:T(8,128)(2,1)S(1)}, u32[]{:S(2)}, u32[]{:S(2)}) collective-permute-start(bf16[512,256]{1,0:T(8,128)(2,1)S(1)} %broadcast_select_fusion), channel_id=1, source_target_pairs={{0,64},{8,72},{16,80},{24,88},{32,96},{40,104},{48,112},{56,120},{... | collective-permute-start | bytes 786440 | tf_op jit(solution)/shard_map/ppermute | solution.py:125
  68.8 10.8 %collective-permute-start.5 = (bf16[512,256]{1,0:T(8,128)(2,1)S(1)}, bf16[512,256]{1,0:T(8,128)(2,1)S(1)}, u32[]{:S(2)}, u32[]{:S(2)}) collective-permute-start(bf16[512,256]{1,0:T(8,128)(2,1)S(1)} %broadcast_select_fusion), channel_id=1, source_target_pairs={{0,96},{8,104},{16,112},{24,120},{32,0},{40,8},{48,16},{56,24},{64... | collective-permute-start | bytes 786440 | tf_op jit(solution)/shard_map/ppermute | solution.py:125
  96.4 3.9 %collective-permute-start.6 = (f32[2,2048]{1,0:T(2,128)S(1)}, f32[2,2048]{1,0:T(2,128)S(1)}, u32[]{:S(2)}, u32[]{:S(2)}) collective-permute-start(f32[2,2048]{1,0:T(2,128)S(1)} %pad_maximum_fusion.6), channel_id=1, source_target_pairs={{0,8},{8,16},{16,24},{24,0},{32,40},{40,48},{48,56},{56,32},{64,72... | collective-permute-start | bytes 49160 | tf_op jit(solution)/shard_map/ppermute | solution.py:125
  96.7 19.3 %slice-start = ((s8[16777216]{0:T(1024)(128)(4,1)}), s8[4194304]{0:T(1024)(128)(4,1)S(1)}, s32[]{:S(2)}) async-start(s8[16777216]{0:T(1024)(128)(4,1)} %bitcast.36), calls=%async_computation.3 | async-start | bytes 8388608
  97.0 4.2 %collective-permute-start.7 = (f32[2,2048]{1,0:T(2,128)S(1)}, f32[2,2048]{1,0:T(2,128)S(1)}, u32[]{:S(2)}, u32[]{:S(2)}) collective-permute-start(f32[2,2048]{1,0:T(2,128)S(1)} %pad_maximum_fusion.6), channel_id=1, source_target_pairs={{0,16},{8,24},{16,0},{24,8},{32,48},{40,56},{48,32},{56,40},{64,80... | collective-permute-start | bytes 49160 | tf_op jit(solution)/shard_map/ppermute | solution.py:125
  98.2 3.1 %collective-permute-start.8 = (f32[2,2048]{1,0:T(2,128)S(1)}, f32[2,2048]{1,0:T(2,128)S(1)}, u32[]{:S(2)}, u32[]{:S(2)}) collective-permute-start(f32[2,2048]{1,0:T(2,128)S(1)} %pad_maximum_fusion.6), channel_id=1, source_target_pairs={{0,24},{8,0},{16,8},{24,16},{32,56},{40,32},{48,40},{56,48},{64,88... | collective-permute-start | bytes 49160 | tf_op jit(solution)/shard_map/ppermute | solution.py:125
  101.4 14.6 %slice-start.1 = ((s8[16777216]{0:T(1024)(128)(4,1)}), s8[4194304]{0:T(1024)(128)(4,1)S(1)}, s32[]{:S(2)}) async-start(s8[16777216]{0:T(1024)(128)(4,1)} %bitcast.36), calls=%async_computation.4 | async-start | bytes 8388608
  101.4 14.6 %slice-start.2 = ((s8[16777216]{0:T(1024)(128)(4,1)}), s8[4194304]{0:T(1024)(128)(4,1)S(1)}, s32[]{:S(2)}) async-start(s8[16777216]{0:T(1024)(128)(4,1)} %bitcast.36), calls=%async_computation.5 | async-start | bytes 8388608
  101.4 14.6 %slice-start.3 = ((s8[16777216]{0:T(1024)(128)(4,1)}), s8[4194304]{0:T(1024)(128)(4,1)S(1)}, s32[]{:S(2)}) async-start(s8[16777216]{0:T(1024)(128)(4,1)} %bitcast.36), calls=%async_computation.6 | async-start | bytes 8388608
  112.2 6.7 %collective-permute-start.12 = (f32[128,256]{1,0:T(8,128)S(1)}, f32[128,256]{1,0:T(8,128)S(1)}, u32[]{:S(2)}, u32[]{:S(2)}) collective-permute-start(f32[128,256]{1,0:T(8,128)S(1)} %slice_select_fusion), channel_id=1, source_target_pairs={{0,1},{1,0},{2,3},{3,2},{4,5},{5,4},{6,7},{7,6},{8,9},{9,8},{10,11... | collective-permute-start | bytes 393224 | tf_op jit(solution)/shard_map/ppermute | solution.py:89
  118.9 1.6 copy-start.1
  119.0 6.5 %collective-permute-start.13 = (f32[64,256]{1,0:T(8,128)S(1)}, f32[64,256]{1,0:T(8,128)S(1)}, u32[]{:S(2)}, u32[]{:S(2)}) collective-permute-start(f32[64,256]{1,0:T(8,128)S(1)} %slice_select_fusion.1), channel_id=1, source_target_pairs={{0,2},{1,3},{2,0},{3,1},{4,6},{5,7},{6,4},{7,5},{8,10},{9,11},{10,... | collective-permute-start | bytes 196616 | tf_op jit(solution)/shard_map/ppermute | solution.py:89
  121.8 14.9 %collective-permute-start.10 = (f32[512,256]{1,0:T(8,128)}, f32[512,256]{1,0:T(8,128)S(1)}, u32[]{:S(2)}, u32[]{:S(2)}) collective-permute-start(f32[512,256]{1,0:T(8,128)} %get-tuple-element.10), channel_id=1, source_target_pairs={{0,64},{8,72},{16,80},{24,88},{32,96},{40,104},{48,112},{56,120},{... | collective-permute-start | bytes 1572872 | tf_op jit(solution)/shard_map/ppermute | solution.py:125
  124.1 23.4 %collective-permute-start.11 = (f32[512,256]{1,0:T(8,128)}, f32[512,256]{1,0:T(8,128)}, u32[]{:S(2)}, u32[]{:S(2)}) collective-permute-start(f32[512,256]{1,0:T(8,128)} %get-tuple-element.9), channel_id=1, source_target_pairs={{0,96},{8,104},{16,112},{24,120},{32,0},{40,8},{48,16},{56,24},{64... | collective-permute-start | bytes 1572872 | tf_op jit(solution)/shard_map/ppermute | solution.py:125
  125.3 23.3 %collective-permute-start.9 = (f32[512,256]{1,0:T(8,128)}, f32[512,256]{1,0:T(8,128)}, u32[]{:S(2)}, u32[]{:S(2)}) collective-permute-start(f32[512,256]{1,0:T(8,128)} %get-tuple-element.8), channel_id=1, source_target_pairs={{0,32},{8,40},{16,48},{24,56},{32,64},{40,72},{48,80},{56,88},{64,... | collective-permute-start | bytes 1572872 | tf_op jit(solution)/shard_map/ppermute | solution.py:125
  125.6 36.9 %collective-permute-start.14 = (f32[32,256]{1,0:T(8,128)S(1)}, f32[32,256]{1,0:T(8,128)S(1)}, u32[]{:S(2)}, u32[]{:S(2)}) collective-permute-start(f32[32,256]{1,0:T(8,128)S(1)} %slice_select_fusion.2), channel_id=1, source_target_pairs={{0,4},{1,5},{2,6},{3,7},{4,0},{5,1},{6,2},{7,3},{8,12},{9,13},{10,... | collective-permute-start | bytes 98312 | tf_op jit(solution)/shard_map/ppermute | solution.py:89
  153.9 49.5 %all-to-all-start.2 = ((f32[128,8,256]{2,1,0:T(8,128)}), f32[128,8,256]{2,1,0:T(8,128)S(1)}, u32[]{:S(2)}, u32[]{:S(2)}) async-start(f32[128,8,256]{2,1,0:T(8,128)} %bitcast.19), calls=%async_computation.2 | async-start | bytes 2097152 | tf_op jit(solution)/shard_map/all_to_all | solution.py:222
  162.5 13.3 %collective-permute-start.15 = (f32[32,256]{1,0:T(8,128)S(1)}, f32[32,256]{1,0:T(8,128)S(1)}, u32[]{:S(2)}, u32[]{:S(2)}) collective-permute-start(f32[32,256]{1,0:T(8,128)S(1)} %select_add_fusion.2), channel_id=1, source_target_pairs={{0,8},{1,9},{2,10},{3,11},{4,12},{5,13},{6,14},{7,15},{8,0},{9,1},... | collective-permute-start | bytes 98312 | tf_op jit(solution)/shard_map/ppermute | solution.py:93
  175.8 4.6 %collective-permute-start.16 = (f32[32,256]{1,0:T(8,128)S(1)}, f32[32,256]{1,0:T(8,128)S(1)}, u32[]{:S(2)}, u32[]{:S(2)}) collective-permute-start(f32[32,256]{1,0:T(8,128)S(1)} %add.165), channel_id=1, source_target_pairs={{0,16},{1,17},{2,18},{3,19},{4,20},{5,21},{6,22},{7,23},{8,24},{9,... | collective-permute-start | bytes 98312 | tf_op jit(solution)/shard_map/ppermute | solution.py:93
  180.4 2.8 %collective-permute-start.17 = (f32[32,256]{1,0:T(8,128)S(1)}, f32[32,256]{1,0:T(8,128)S(1)}, u32[]{:S(2)}, u32[]{:S(2)}) collective-permute-start(f32[32,256]{1,0:T(8,128)S(1)} %add.166), channel_id=1, source_target_pairs={{0,32},{1,33},{2,34},{3,35},{4,36},{5,37},{6,38},{7,39},{8,40},{9,... | collective-permute-start | bytes 98312 | tf_op jit(solution)/shard_map/ppermute | solution.py:93
  183.1 4.4 %collective-permute-start.18 = (f32[32,256]{1,0:T(8,128)S(1)}, f32[32,256]{1,0:T(8,128)S(1)}, u32[]{:S(2)}, u32[]{:S(2)}) collective-permute-start(f32[32,256]{1,0:T(8,128)S(1)} %add.167), channel_id=1, source_target_pairs={{0,64},{1,65},{2,66},{3,67},{4,68},{5,69},{6,70},{7,71},{8,72},{9,... | collective-permute-start | bytes 98312 | tf_op jit(solution)/shard_map/ppermute | solution.py:93
  187.6 4.3 %collective-permute-start.19 = (f32[32,256]{1,0:T(8,128)S(1)}, f32[32,256]{1,0:T(8,128)S(1)}, u32[]{:S(2)}, u32[]{:S(2)}) collective-permute-start(f32[32,256]{1,0:T(8,128)S(1)} %add.168), channel_id=1, source_target_pairs={{0,4},{1,5},{2,6},{3,7},{4,0},{5,1},{6,2},{7,3},{8,12},{9,13},{10,... | collective-permute-start | bytes 98312 | tf_op jit(solution)/shard_map/ppermute | solution.py:97
  191.8 3.2 %collective-permute-start.20 = (f32[64,256]{1,0:T(8,128)S(1)}, f32[64,256]{1,0:T(8,128)S(1)}, u32[]{:S(2)}, u32[]{:S(2)}) collective-permute-start(f32[64,256]{1,0:T(8,128)S(1)} %maximum_select_fusion.2), channel_id=1, source_target_pairs={{0,2},{1,3},{2,0},{3,1},{4,6},{5,7},{6,4},{7,5},{8,10},{9,11},{10,... | collective-permute-start | bytes 196616 | tf_op jit(solution)/shard_map/ppermute | solution.py:97
  195.1 7.6 %collective-permute-start.21 = (f32[128,256]{1,0:T(8,128)S(1)}, f32[128,256]{1,0:T(8,128)S(1)}, u32[]{:S(2)}, u32[]{:S(2)}) collective-permute-start(f32[128,256]{1,0:T(8,128)S(1)} %maximum_select_fusion.1), channel_id=1, source_target_pairs={{0,1},{1,0},{2,3},{3,2},{4,5},{5,4},{6,7},{7,6},{8,9},{9,8},{10,11... | collective-permute-start | bytes 393224 | tf_op jit(solution)/shard_map/ppermute | solution.py:97

commit v8 on v7

--- a/solution.py
+++ b/solution.py
@@ -217,21 +217,22 @@
             (((0,), (0,)), ((), ())),
             preferred_element_type=jnp.float32,
         )
-    slot_grads = jax.ops.segment_sum(item_grad, slot_ids, num_segments=sources * slot_cap)
-    slot_grads = slot_grads.reshape(sources, slot_cap, model_width)
-    returned = lax.all_to_all(
-        slot_grads, ("batch", "table"), split_axis=0, concat_axis=0, tiled=True
-    )
-    table_grad = (
-        jnp.zeros((table_rows, model_width), jnp.float32)
-        .at[wanted.reshape(-1)]
-        .add(returned.reshape(-1, model_width))
-    )
     total = lax.axis_size("batch") * lax.axis_size("table")
     if total & (total - 1) == 0:
         weight_grad = tree_sum(partial_value, ("batch", "table"), min(8, lax.axis_size("table")))
     else:
         weight_grad = lax.psum(partial_value, ("batch", "table"))
+    item_grad, weight_grad = lax.optimization_barrier((item_grad, weight_grad))
+    slot_grads = jax.ops.segment_sum(item_grad, slot_ids, num_segments=sources * slot_cap)
+    slot_grads = slot_grads.reshape(sources, slot_cap, model_width)
+    returned = lax.all_to_all(
+        slot_grads, ("batch", "table"), split_axis=0, concat_axis=0, tiled=True
+    )
+    table_grad = (
+        jnp.zeros((table_rows, model_width), jnp.float32)
+        .at[wanted.reshape(-1)]
+        .add(returned.reshape(-1, model_width))
+    )
     return (table_grad, weight_grad)
 
 

time: 211 us -> 210 us (level)
  starting transfers between devices: 69.6 us -> 59.8 us
  waiting for transfers between devices: 53.7 us -> 60.2 us
  matrix products: 23.7 us -> 27.2 us
    ppermute x12, waiting for transfers between devices: 29.9 us -> 9.87 us  [plane_shift(): return lax.ppermute(value, axis, pairs)]
    all_to_all x1, waiting for transfers between devices: 0.01 us -> 17.5 us  [local(): lax.all_to_all(slot_grads, ('batch', 'table'), split_axis=0, concat_axis=...]
    ppermute x3, starting transfers between devices: 10.6 us -> 5.12 us  [tree_sum(): got = lax.ppermute(value, axes, [(i, i ^ step) for i in range(total)])]
    ppermute x3, waiting for transfers between devices: 3.06 us -> 8.45 us  [tree_sum(): got = lax.ppermute(value, axes, [(i, i ^ step) for i in range(total)])]
    dot_general x1, matrix products: 2.9 us -> 7.22 us  [block_grads(): lax.dot_general(soft_weights, row_queries, (((0,), (0,)), ((), ())), pref...]
    all_to_all x1, starting transfers between devices: 8.61 us -> 5.88 us  [local(): lax.all_to_all(slot_grads, ('batch', 'table'), split_axis=0, concat_axis=...]
    ppermute x4, waiting for transfers between devices: 17.4 us -> 20.1 us  [tree_sum(): lax.ppermute(value, axes, [(i, i ^ step) for i in range(total)])]
  transfers between devices with their start and end apart: 25 -> 25, of which waited for: 16 -> 15; matrix products, arithmetic and copies ran while one was open for 21% -> 20% of each run, Pallas kernels for 0% -> 0%
where the time goes in v8:
time: 210 us; the launch traced here: 209 us
  waiting for transfers between devices  60.2 us (29%)
  starting transfers between devices  59.8 us (28%)
  local copies, waits for them, and re-layouts  31.5 us (15%)
  other arithmetic  29.4 us (14%)
  matrix products  27.2 us (13%)
    ppermute x4, waiting for transfers between devices, tree_sum(): lax.ppermute(value, axes, [(i, i ^ step) for i in range(total)])  20.1 us
    gather x1, local copies, waits for them, and re-layouts, local(): looked = jnp.take(query_table, query_ids, axis=0).astype(jnp.float32)  18.7 us
    all_to_all x1, waiting for transfers between devices, local(): lax.all_to_all(slot_grads, ('batch', 'table'), split_axis=0, concat_axis=...  17.5 us
    ppermute x12, starting transfers between devices, plane_shift(): return lax.ppermute(value, axis, pairs)  16.7 us
    all_to_all x1, starting transfers between devices, local(): lax.all_to_all(requests, ('batch', 'table'), split_axis=0, concat_axis=0,...  11.5 us
    ppermute x12, waiting for transfers between devices, plane_shift(): return lax.ppermute(value, axis, pairs)  9.87 us
    reduce_sum x1, other arithmetic, block_grads(): local_sum = jnp.sum(jnp.exp(scores - local_max[:, None]), axis=1)  8.55 us
    ppermute x3, waiting for transfers between devices, tree_sum(): got = lax.ppermute(value, axes, [(i, i ^ step) for i in range(total)])  8.45 us
  transfers between devices with their start and end apart: 25, of which 15 were waited for; matrix products, arithmetic and copies ran while one was open for 20% of the time, Pallas kernels for 0%

profile of v8, /device:TPU:1, one launch (start us, length us, event | category | flops | bytes accessed | tf_op | source)
XLA Modules:
  0.0 209.2 jit_solution(9896147682847142400)
XLA Ops:
  0.7 1.5 copy.22
  2.2 11.5 %all-to-all-start = ((s32[128,1,8]{2,1,0:T(1,128)}), s32[128,1,8]{2,1,0:T(1,128)S(1)}, u32[]{:S(2)}, u32[]{:S(2)}) async-start(s32[128,1,8]{2,1,0:T(1,128)} %bitcast), calls=%async_computation | async-start | bytes 131072 | tf_op jit(solution)/shard_map/all_to_all | solution.py:185
  13.7 0.8 copy.23
  14.4 0.2 reduce-window.8
  14.7 0.7 bitcast_subtract_fusion
  15.4 0.9 convert_reduce_fusion.1
  16.3 3.3 %gather_fusion = s32[512]{0:T(512)S(1)} fusion(s32[128]{0:T(128)S(1)} %bitcast_subtract_fusion, s32[1024]{0:T(1024)S(1)} %pad_clamp_fusion.1), kind=kCustom, calls=%fused_computation | custom fusion | bytes 6144 | tf_op jit(solution)/shard_map/jit(_take)/gather | solution.py:73
  19.7 3.3 %all-to-all-done = s32[128,1,8]{2,1,0:T(1,128)S(1)} async-done(((s32[128,1,8]{2,1,0:T(1,128)}), s32[128,1,8]{2,1,0:T(1,128)S(1)}, u32[]{:S(2)}, u32[]{:S(2)}) %all-to-all-start) | async-done | bytes 4128 | tf_op jit(solution)/shard_map/all_to_all | solution.py:185
  23.2 3.9 %gather_fusion.1 = bf16[1024,256]{1,0:T(8,128)(2,1)S(1)} fusion(bf16[2048,256]{1,0:T(8,128)(2,1)S(1)} %copy-done, s32[1024]{0:T(1024)S(1)} %broadcast_clamp_fusion.1), kind=kCustom, calls=%fused_computation.1 | custom fusion | bytes 1052672 | tf_op jit(solution)/shard_map/jit(_take)/gather | solution.py:186
  27.1 1.0 bitcast_select_fusion.1
  28.2 0.1 copy.25
  28.3 0.2 reshape.222
  28.4 0.2 copy.24
  28.6 6.5 %all-to-all-start.1 = ((bf16[128,8,256]{2,1,0:T(8,128)(2,1)}), bf16[128,8,256]{2,1,0:T(8,128)(2,1)S(1)}, u32[]{:S(2)}, u32[]{:S(2)}) async-start(bf16[128,8,256]{2,1,0:T(8,128)(2,1)} %bitcast_select_fusion.1), calls=%async_computation.1 | async-start | bytes 1048576 | tf_op jit(solution)/shard_map/all_to_all | solution.py:188
  35.1 18.7 %gather_fusion.2 = bf16[4096,256]{1,0:T(8,128)(2,1)} fusion(bf16[8192,256]{1,0:T(8,128)(2,1)} %param.8, s32[4096]{0:T(1024)S(1)} %broadcast_clamp_fusion), kind=kCustom, calls=%fused_computation.2 | custom fusion | bytes 4210688 | tf_op jit(solution)/shard_map/jit(_take)/gather | solution.py:193
  53.8 4.1 %convert_reduce_fusion = f32[512,256]{1,0:T(8,128)S(1)} fusion(bf16[4096,256]{1,0:T(8,128)(2,1)} %gather_fusion.2, pred[512,8]{1,0:T(8,128)(4,1)S(1)} %copy.24), kind=kLoop, calls=%fused_computation.9 | loop fusion | flops 3014656 | bytes 2625536 | tf_op jit(solution)/shard_map/reduce_sum | solution.py:194
  57.9 1.4 collective-permute-start
  59.3 2.4 %collective-permute-start.1 = (bf16[512,256]{1,0:T(8,128)(2,1)S(1)}, bf16[512,256]{1,0:T(8,128)(2,1)}, u32[]{:S(2)}, u32[]{:S(2)}) collective-permute-start(bf16[512,256]{1,0:T(8,128)(2,1)S(1)} %multiply_convert_fusion), channel_id=1, source_target_pairs={{0,16},{8,24},{16,0},{24,8},{32,48},{40,56},{48,32},{56,40},{64,80... | collective-permute-start | bytes 786440 | tf_op jit(solution)/shard_map/ppermute | solution.py:125
  61.7 1.2 collective-permute-start.2
  62.9 2.0 gather_fusion.3
  64.9 0.1 broadcast_select_fusion
  65.0 1.3 collective-permute-start.3
  66.3 2.5 %collective-permute-start.4 = (bf16[512,256]{1,0:T(8,128)(2,1)S(1)}, bf16[512,256]{1,0:T(8,128)(2,1)S(1)}, u32[]{:S(2)}, u32[]{:S(2)}) collective-permute-start(bf16[512,256]{1,0:T(8,128)(2,1)S(1)} %broadcast_select_fusion), channel_id=1, source_target_pairs={{0,64},{8,72},{16,80},{24,88},{32,96},{40,104},{48,112},{56,120},{... | collective-permute-start | bytes 786440 | tf_op jit(solution)/shard_map/ppermute | solution.py:125
  68.8 1.1 collective-permute-start.5
  69.9 3.6 %collective-permute-done.1 = bf16[512,256]{1,0:T(8,128)(2,1)} collective-permute-done((bf16[512,256]{1,0:T(8,128)(2,1)S(1)}, bf16[512,256]{1,0:T(8,128)(2,1)}, u32[]{:S(2)}, u32[]{:S(2)}) %collective-permute-start.1) | collective-permute-done | bytes 262176 | tf_op jit(solution)/shard_map/ppermute | solution.py:125
  73.4 1.6 convolution_convert_fusion
  75.0 4.5 %collective-permute-done.4 = bf16[512,256]{1,0:T(8,128)(2,1)S(1)} collective-permute-done((bf16[512,256]{1,0:T(8,128)(2,1)S(1)}, bf16[512,256]{1,0:T(8,128)(2,1)S(1)}, u32[]{:S(2)}, u32[]{:S(2)}) %collective-permute-start.4) | collective-permute-done | bytes 262176 | tf_op jit(solution)/shard_map/ppermute | solution.py:125
  79.6 8.2 %multiply_reduce_fusion = (f32[2048]{0:T(1024)S(1)}, f32[2048,2048]{0,1:T(8,128)}) fusion(bf16[2048,256]{1,0:T(8,128)(2,1)S(1)} %convolution_convert_fusion, bf16[512,256]{1,0:T(8,128)(2,1)S(1)} %collective-permute-done.5, bf16[512,256]{1,0:T(8,128)(2,1)S(1)} %collective-permute-done.4, bf16[512,256]{1,0:T(8,128)(2,1)S(1)} %collective-permute-done.3, ...), kind=kOutput, calls=%fused_computation.8 | convolution fusion | flops 2160064512 | bytes 18882560 | tf_op jit(solution)/shard_map/dot_general | solution.py:146
  87.8 8.5 %exponential_reduce_fusion = f32[2048]{0:T(1024)S(1)} fusion(f32[2048,2048]{0,1:T(8,128)} %get-tuple-element.24, f32[2048]{0:T(1024)S(1)} %get-tuple-element.23), kind=kLoop, calls=%fused_computation.7 | loop fusion | flops 12580864 | bytes 16793600 | tf_op jit(solution)/shard_map/reduce_sum | solution.py:150
  96.4 0.4 collective-permute-start.6
  96.7 0.3 fusion.24
  97.0 1.3 collective-permute-start.7
  98.2 1.3 collective-permute-start.8
  99.5 0.7 collective-permute-done.6
  100.3 1.0 collective-permute-done.7
  101.4 7.3 %fusion = f32[2048,256]{1,0:T(8,128)S(1)} fusion(f32[2048,2048]{0,1:T(8,128)} %get-tuple-element.24, f32[2048]{0:T(1024)S(1)} %log_add_fusion, bf16[512,256]{1,0:T(8,128)(2,1)S(1)} %collective-permute-done.5, bf16[512,256]{1,0:T(8,128)(2,1)S(1)} %collective-permute-done.4, bf16[512,256]{1,0:T(8,128)(2,1)S(1)} %collective-permute-done.3, ...), kind=kOutput, calls=%fused_computation.12 | convolution fusion | flops 2164260864 | bytes 19931136 | tf_op jit(solution)/shard_map/dot_general | solution.py:164
  108.7 2.6 %fusion.2 = f32[256,256]{1,0:T(8,128)S(1)} fusion(f32[256,256]{1,0:T(8,128)S(1)} %fusion.24, f32[2048,256]{1,0:T(8,128)S(1)} %fusion, bf16[512,256]{1,0:T(8,128)(2,1)} %collective-permute-done.2, bf16[512,256]{1,0:T(8,128)(2,1)} %collective-permute-done.1, bf16[512,256]{1,0:T(8,128)(2,1)} %collective-permute-done, bf16[512,256]{1,0:T(8,128)(2,1)S(1)} %multiply_convert_fusion), kind=kOutput, calls=%fused_computation.15 | convolution fusion | flops 1614938112 | bytes 3670016 | tf_op jit(solution)/shard_map/dot_general | solution.py:168
  111.3 3.6 %collective-permute-start.12 = (f32[128,256]{1,0:T(8,128)S(1)}, f32[128,256]{1,0:T(8,128)S(1)}, u32[]{:S(2)}, u32[]{:S(2)}) collective-permute-start(f32[128,256]{1,0:T(8,128)S(1)} %slice_select_fusion), channel_id=1, source_target_pairs={{0,1},{1,0},{2,3},{3,2},{4,5},{5,4},{6,7},{7,6},{8,9},{9,8},{10,11... | collective-permute-start | bytes 393224 | tf_op jit(solution)/shard_map/ppermute | solution.py:89
  114.9 1.0 collective-permute-done.12
  115.9 1.7 collective-permute-start.13
  117.7 7.2 %fusion.1 = f32[2048,256]{1,0:T(8,128)S(1)} fusion(bf16[2048,256]{1,0:T(8,128)(2,1)S(1)} %convolution_convert_fusion, f32[2048,2048]{0,1:T(8,128)} %get-tuple-element.24, f32[2048]{0:T(1024)S(1)} %log_add_fusion), kind=kOutput, calls=%fused_computation.13 | convolution fusion | flops 2160066560 | bytes 19931136 | tf_op jit(solution)/shard_map/dot_general | solution.py:165
  125.0 3.0 %collective-permute-start.14 = (f32[32,256]{1,0:T(8,128)S(1)}, f32[32,256]{1,0:T(8,128)S(1)}, u32[]{:S(2)}, u32[]{:S(2)}) collective-permute-start(f32[32,256]{1,0:T(8,128)S(1)} %slice_select_fusion.2), channel_id=1, source_target_pairs={{0,4},{1,5},{2,6},{3,7},{4,0},{5,1},{6,2},{7,3},{8,12},{9,13},{10,... | collective-permute-start | bytes 98312 | tf_op jit(solution)/shard_map/ppermute | solution.py:89
  128.1 2.4 %collective-permute-start.10 = (f32[512,256]{1,0:T(8,128)S(1)}, f32[512,256]{1,0:T(8,128)S(1)}, u32[]{:S(2)}, u32[]{:S(2)}) collective-permute-start(f32[512,256]{1,0:T(8,128)S(1)} %get-tuple-element.14), channel_id=1, source_target_pairs={{0,64},{8,72},{16,80},{24,88},{32,96},{40,104},{48,112},{56,120},{... | collective-permute-start | bytes 1572872 | tf_op jit(solution)/shard_map/ppermute | solution.py:125
  130.5 1.2 collective-permute-start.11
  131.7 0.2 collective-permute-start.9
  132.0 1.6 collective-permute-start.15
  133.6 1.6 collective-permute-done.15
  135.2 1.9 collective-permute-start.16
  137.1 2.7 %collective-permute-done.16 = f32[32,256]{1,0:T(8,128)S(1)} collective-permute-done((f32[32,256]{1,0:T(8,128)S(1)}, f32[32,256]{1,0:T(8,128)S(1)}, u32[]{:S(2)}, u32[]{:S(2)}) %collective-permute-start.16) | collective-permute-done | bytes 32800 | tf_op jit(solution)/shard_map/ppermute | solution.py:93
  139.8 13.9 %collective-permute-done.17 = f32[32,256]{1,0:T(8,128)S(1)} collective-permute-done((f32[32,256]{1,0:T(8,128)S(1)}, f32[32,256]{1,0:T(8,128)S(1)}, u32[]{:S(2)}, u32[]{:S(2)}) %collective-permute-start.17) | collective-permute-done | bytes 32800 | tf_op jit(solution)/shard_map/ppermute | solution.py:93
  153.7 2.4 %collective-permute-start.18 = (f32[32,256]{1,0:T(8,128)S(1)}, f32[32,256]{1,0:T(8,128)S(1)}, u32[]{:S(2)}, u32[]{:S(2)}) collective-permute-start(f32[32,256]{1,0:T(8,128)S(1)} %add.167), channel_id=1, source_target_pairs={{0,64},{1,65},{2,66},{3,67},{4,68},{5,69},{6,70},{7,71},{8,72},{9,... | collective-permute-start | bytes 98312 | tf_op jit(solution)/shard_map/ppermute | solution.py:93
  156.1 1.9 collective-permute-done.18
  158.0 4.2 %collective-permute-done.19 = f32[32,256]{1,0:T(8,128)S(1)} collective-permute-done((f32[32,256]{1,0:T(8,128)S(1)}, f32[32,256]{1,0:T(8,128)S(1)}, u32[]{:S(2)}, u32[]{:S(2)}) %collective-permute-start.19) | collective-permute-done | bytes 32800 | tf_op jit(solution)/shard_map/ppermute | solution.py:97
  162.3 3.4 %collective-permute-done.20 = f32[64,256]{1,0:T(8,128)S(1)} collective-permute-done((f32[64,256]{1,0:T(8,128)S(1)}, f32[64,256]{1,0:T(8,128)S(1)}, u32[]{:S(2)}, u32[]{:S(2)}) %collective-permute-start.20) | collective-permute-done | bytes 65568 | tf_op jit(solution)/shard_map/ppermute | solution.py:97
  165.8 5.0 %collective-permute-start.21 = (f32[128,256]{1,0:T(8,128)S(1)}, f32[128,256]{1,0:T(8,128)S(1)}, u32[]{:S(2)}, u32[]{:S(2)}) collective-permute-start(f32[128,256]{1,0:T(8,128)S(1)} %maximum_select_fusion.1), channel_id=1, source_target_pairs={{0,1},{1,0},{2,3},{3,2},{4,5},{5,4},{6,7},{7,6},{8,9},{9,8},{10,11... | collective-permute-start | bytes 393224 | tf_op jit(solution)/shard_map/ppermute | solution.py:97
  170.8 0.2 fusion.9
  170.9 0.8 collective-permute-done.21
  171.7 0.7 maximum_select_fusion
  172.5 4.3 %scatter_custom_fusion = f32[1024,256]{1,0:T(8,128)} fusion(s32[512]{0:T(512)S(1)} %get-tuple-element.11, f32[512,256]{1,0:T(8,128)S(1)} %fusion.9, f32[]{:T(128)} %constant.37.clone.1), kind=kCustom, calls=%fused_computation.28 | custom fusion | flops 131072 | bytes 1048580 | tf_op jit(solution)/shard_map/scatter-add | solution.py:226
  176.8 5.9 %all-to-all-start.2 = ((f32[128,8,256]{2,1,0:T(8,128)}), f32[128,8,256]{2,1,0:T(8,128)S(1)}, u32[]{:S(2)}, u32[]{:S(2)}) async-start(f32[128,8,256]{2,1,0:T(8,128)} %bitcast.19), calls=%async_computation.2 | async-start | bytes 2097152 | tf_op jit(solution)/shard_map/all_to_all | solution.py:228
  182.7 0.6 broadcast.91
  183.2 0.8 reduce.4
  184.1 17.5 %all-to-all-done.2 = f32[128,8,256]{2,1,0:T(8,128)S(1)} async-done(((f32[128,8,256]{2,1,0:T(8,128)}), f32[128,8,256]{2,1,0:T(8,128)S(1)}, u32[]{:S(2)}, u32[]{:S(2)}) %all-to-all-start.2) | async-done | bytes 1048608 | tf_op jit(solution)/shard_map/all_to_all | solution.py:228
  201.7 7.5 %scatter_custom_fusion.1 = f32[2048,256]{1,0:T(8,128)} fusion(s32[1024]{0:T(1024)S(1)} %bitcast.49, f32[128,8,256]{2,1,0:T(8,128)S(1)} %all-to-all-done.2, f32[]{:T(128)} %constant.37.clone.1), kind=kCustom, calls=%fused_computation.18 | custom fusion | flops 262144 | bytes 3145732 | tf_op jit(solution)/shard_map/scatter-add | solution.py:234
  (59 shorter events, 1.1 us)
Async XLA Ops:
  0.6 22.5 %copy-start = (bf16[2048,256]{1,0:T(8,128)(2,1)S(1)}, bf16[2048,256]{1,0:T(8,128)(2,1)}, u32[]{:S(2)}) copy-start(bf16[2048,256]{1,0:T(8,128)(2,1)} %param.7) | copy-start | bytes 3145732
  0.6 19.0 %copy-start.2 = (s32[512]{0:T(512)S(1)}, s32[512]{0:T(512)}, u32[]{:S(2)}) copy-start(s32[512]{0:T(512)} %param.13) | copy-start | bytes 6148
  2.2 20.9 %all-to-all-start = ((s32[128,1,8]{2,1,0:T(1,128)}), s32[128,1,8]{2,1,0:T(1,128)S(1)}, u32[]{:S(2)}, u32[]{:S(2)}) async-start(s32[128,1,8]{2,1,0:T(1,128)} %bitcast), calls=%async_computation | async-start | bytes 131072 | tf_op jit(solution)/shard_map/all_to_all | solution.py:185
  23.2 5.0 %copy-start.1 = (s32[512,8]{0,1:T(8,128)S(1)}, s32[512,8]{0,1:T(8,128)}, u32[]{:S(2)}) copy-start(s32[512,8]{0,1:T(8,128)} %param.10) | copy-start | bytes 49156
  28.6 34.3 %all-to-all-start.1 = ((bf16[128,8,256]{2,1,0:T(8,128)(2,1)}), bf16[128,8,256]{2,1,0:T(8,128)(2,1)S(1)}, u32[]{:S(2)}, u32[]{:S(2)}) async-start(bf16[128,8,256]{2,1,0:T(8,128)(2,1)} %bitcast_select_fusion.1), calls=%async_computation.1 | async-start | bytes 1048576 | tf_op jit(solution)/shard_map/all_to_all | solution.py:188
  57.9 10.9 %collective-permute-start = (bf16[512,256]{1,0:T(8,128)(2,1)S(1)}, bf16[512,256]{1,0:T(8,128)(2,1)}, u32[]{:S(2)}, u32[]{:S(2)}) collective-permute-start(bf16[512,256]{1,0:T(8,128)(2,1)S(1)} %multiply_convert_fusion), channel_id=1, source_target_pairs={{0,8},{8,16},{16,24},{24,0},{32,40},{40,48},{48,56},{56,32},{64,72... | collective-permute-start | bytes 786440 | tf_op jit(solution)/shard_map/ppermute | solution.py:125
  59.3 14.1 %collective-permute-start.1 = (bf16[512,256]{1,0:T(8,128)(2,1)S(1)}, bf16[512,256]{1,0:T(8,128)(2,1)}, u32[]{:S(2)}, u32[]{:S(2)}) collective-permute-start(bf16[512,256]{1,0:T(8,128)(2,1)S(1)} %multiply_convert_fusion), channel_id=1, source_target_pairs={{0,16},{8,24},{16,0},{24,8},{32,48},{40,56},{48,32},{56,40},{64,80... | collective-permute-start | bytes 786440 | tf_op jit(solution)/shard_map/ppermute | solution.py:125
  61.7 11.7 %collective-permute-start.2 = (bf16[512,256]{1,0:T(8,128)(2,1)S(1)}, bf16[512,256]{1,0:T(8,128)(2,1)}, u32[]{:S(2)}, u32[]{:S(2)}) collective-permute-start(bf16[512,256]{1,0:T(8,128)(2,1)S(1)} %multiply_convert_fusion), channel_id=1, source_target_pairs={{0,24},{8,0},{16,8},{24,16},{32,56},{40,32},{48,40},{56,48},{64,88... | collective-permute-start | bytes 786440 | tf_op jit(solution)/shard_map/ppermute | solution.py:125
  65.0 10.0 %collective-permute-start.3 = (bf16[512,256]{1,0:T(8,128)(2,1)S(1)}, bf16[512,256]{1,0:T(8,128)(2,1)S(1)}, u32[]{:S(2)}, u32[]{:S(2)}) collective-permute-start(bf16[512,256]{1,0:T(8,128)(2,1)S(1)} %broadcast_select_fusion), channel_id=1, source_target_pairs={{0,32},{8,40},{16,48},{24,56},{32,64},{40,72},{48,80},{56,88},{64,... | collective-permute-start | bytes 786440 | tf_op jit(solution)/shard_map/ppermute | solution.py:125
  66.3 13.3 %collective-permute-start.4 = (bf16[512,256]{1,0:T(8,128)(2,1)S(1)}, bf16[512,256]{1,0:T(8,128)(2,1)S(1)}, u32[]{:S(2)}, u32[]{:S(2)}) collective-permute-start(bf16[512,256]{1,0:T(8,128)(2,1)S(1)} %broadcast_select_fusion), channel_id=1, source_target_pairs={{0,64},{8,72},{16,80},{24,88},{32,96},{40,104},{48,112},{56,120},{... | collective-permute-start | bytes 786440 | tf_op jit(solution)/shard_map/ppermute | solution.py:125
  68.8 10.8 %collective-permute-start.5 = (bf16[512,256]{1,0:T(8,128)(2,1)S(1)}, bf16[512,256]{1,0:T(8,128)(2,1)S(1)}, u32[]{:S(2)}, u32[]{:S(2)}) collective-permute-start(bf16[512,256]{1,0:T(8,128)(2,1)S(1)} %broadcast_select_fusion), channel_id=1, source_target_pairs={{0,96},{8,104},{16,112},{24,120},{32,0},{40,8},{48,16},{56,24},{64... | collective-permute-start | bytes 786440 | tf_op jit(solution)/shard_map/ppermute | solution.py:125
  96.4 3.9 %collective-permute-start.6 = (f32[2,2048]{1,0:T(2,128)S(1)}, f32[2,2048]{1,0:T(2,128)S(1)}, u32[]{:S(2)}, u32[]{:S(2)}) collective-permute-start(f32[2,2048]{1,0:T(2,128)S(1)} %pad_maximum_fusion.6), channel_id=1, source_target_pairs={{0,8},{8,16},{16,24},{24,0},{32,40},{40,48},{48,56},{56,32},{64,72... | collective-permute-start | bytes 49160 | tf_op jit(solution)/shard_map/ppermute | solution.py:125
  97.0 4.2 %collective-permute-start.7 = (f32[2,2048]{1,0:T(2,128)S(1)}, f32[2,2048]{1,0:T(2,128)S(1)}, u32[]{:S(2)}, u32[]{:S(2)}) collective-permute-start(f32[2,2048]{1,0:T(2,128)S(1)} %pad_maximum_fusion.6), channel_id=1, source_target_pairs={{0,16},{8,24},{16,0},{24,8},{32,48},{40,56},{48,32},{56,40},{64,80... | collective-permute-start | bytes 49160 | tf_op jit(solution)/shard_map/ppermute | solution.py:125
  98.2 3.1 %collective-permute-start.8 = (f32[2,2048]{1,0:T(2,128)S(1)}, f32[2,2048]{1,0:T(2,128)S(1)}, u32[]{:S(2)}, u32[]{:S(2)}) collective-permute-start(f32[2,2048]{1,0:T(2,128)S(1)} %pad_maximum_fusion.6), channel_id=1, source_target_pairs={{0,24},{8,0},{16,8},{24,16},{32,56},{40,32},{48,40},{56,48},{64,88... | collective-permute-start | bytes 49160 | tf_op jit(solution)/shard_map/ppermute | solution.py:125
  111.3 4.6 %collective-permute-start.12 = (f32[128,256]{1,0:T(8,128)S(1)}, f32[128,256]{1,0:T(8,128)S(1)}, u32[]{:S(2)}, u32[]{:S(2)}) collective-permute-start(f32[128,256]{1,0:T(8,128)S(1)} %slice_select_fusion), channel_id=1, source_target_pairs={{0,1},{1,0},{2,3},{3,2},{4,5},{5,4},{6,7},{7,6},{8,9},{9,8},{10,11... | collective-permute-start | bytes 393224 | tf_op jit(solution)/shard_map/ppermute | solution.py:89
  115.9 9.0 %collective-permute-start.13 = (f32[64,256]{1,0:T(8,128)S(1)}, f32[64,256]{1,0:T(8,128)S(1)}, u32[]{:S(2)}, u32[]{:S(2)}) collective-permute-start(f32[64,256]{1,0:T(8,128)S(1)} %slice_select_fusion.1), channel_id=1, source_target_pairs={{0,2},{1,3},{2,0},{3,1},{4,6},{5,7},{6,4},{7,5},{8,10},{9,11},{10,... | collective-permute-start | bytes 196616 | tf_op jit(solution)/shard_map/ppermute | solution.py:89
  125.0 7.0 %collective-permute-start.14 = (f32[32,256]{1,0:T(8,128)S(1)}, f32[32,256]{1,0:T(8,128)S(1)}, u32[]{:S(2)}, u32[]{:S(2)}) collective-permute-start(f32[32,256]{1,0:T(8,128)S(1)} %slice_select_fusion.2), channel_id=1, source_target_pairs={{0,4},{1,5},{2,6},{3,7},{4,0},{5,1},{6,2},{7,3},{8,12},{9,13},{10,... | collective-permute-start | bytes 98312 | tf_op jit(solution)/shard_map/ppermute | solution.py:89
  128.1 42.7 %collective-permute-start.10 = (f32[512,256]{1,0:T(8,128)S(1)}, f32[512,256]{1,0:T(8,128)S(1)}, u32[]{:S(2)}, u32[]{:S(2)}) collective-permute-start(f32[512,256]{1,0:T(8,128)S(1)} %get-tuple-element.14), channel_id=1, source_target_pairs={{0,64},{8,72},{16,80},{24,88},{32,96},{40,104},{48,112},{56,120},{... | collective-permute-start | bytes 1572872 | tf_op jit(solution)/shard_map/ppermute | solution.py:125
  130.5 40.3 %collective-permute-start.11 = (f32[512,256]{1,0:T(8,128)S(1)}, f32[512,256]{1,0:T(8,128)S(1)}, u32[]{:S(2)}, u32[]{:S(2)}) collective-permute-start(f32[512,256]{1,0:T(8,128)S(1)} %get-tuple-element.13), channel_id=1, source_target_pairs={{0,96},{8,104},{16,112},{24,120},{32,0},{40,8},{48,16},{56,24},{64... | collective-permute-start | bytes 1572872 | tf_op jit(solution)/shard_map/ppermute | solution.py:125
  131.7 39.0 %collective-permute-start.9 = (f32[512,256]{1,0:T(8,128)S(1)}, f32[512,256]{1,0:T(8,128)S(1)}, u32[]{:S(2)}, u32[]{:S(2)}) collective-permute-start(f32[512,256]{1,0:T(8,128)S(1)} %get-tuple-element.12), channel_id=1, source_target_pairs={{0,32},{8,40},{16,48},{24,56},{32,64},{40,72},{48,80},{56,88},{64,... | collective-permute-start | bytes 1572872 | tf_op jit(solution)/shard_map/ppermute | solution.py:125
  132.0 3.2 %collective-permute-start.15 = (f32[32,256]{1,0:T(8,128)S(1)}, f32[32,256]{1,0:T(8,128)S(1)}, u32[]{:S(2)}, u32[]{:S(2)}) collective-permute-start(f32[32,256]{1,0:T(8,128)S(1)} %select_add_fusion.2), channel_id=1, source_target_pairs={{0,8},{1,9},{2,10},{3,11},{4,12},{5,13},{6,14},{7,15},{8,0},{9,1},... | collective-permute-start | bytes 98312 | tf_op jit(solution)/shard_map/ppermute | solution.py:93
  135.2 4.6 %collective-permute-start.16 = (f32[32,256]{1,0:T(8,128)S(1)}, f32[32,256]{1,0:T(8,128)S(1)}, u32[]{:S(2)}, u32[]{:S(2)}) collective-permute-start(f32[32,256]{1,0:T(8,128)S(1)} %add.165), channel_id=1, source_target_pairs={{0,16},{1,17},{2,18},{3,19},{4,20},{5,21},{6,22},{7,23},{8,24},{9,... | collective-permute-start | bytes 98312 | tf_op jit(solution)/shard_map/ppermute | solution.py:93
  139.8 13.9 %collective-permute-start.17 = (f32[32,256]{1,0:T(8,128)S(1)}, f32[32,256]{1,0:T(8,128)S(1)}, u32[]{:S(2)}, u32[]{:S(2)}) collective-permute-start(f32[32,256]{1,0:T(8,128)S(1)} %add.166), channel_id=1, source_target_pairs={{0,32},{1,33},{2,34},{3,35},{4,36},{5,37},{6,38},{7,39},{8,40},{9,... | collective-permute-start | bytes 98312 | tf_op jit(solution)/shard_map/ppermute | solution.py:93
  153.7 4.3 %collective-permute-start.18 = (f32[32,256]{1,0:T(8,128)S(1)}, f32[32,256]{1,0:T(8,128)S(1)}, u32[]{:S(2)}, u32[]{:S(2)}) collective-permute-start(f32[32,256]{1,0:T(8,128)S(1)} %add.167), channel_id=1, source_target_pairs={{0,64},{1,65},{2,66},{3,67},{4,68},{5,69},{6,70},{7,71},{8,72},{9,... | collective-permute-start | bytes 98312 | tf_op jit(solution)/shard_map/ppermute | solution.py:93
  158.0 4.3 %collective-permute-start.19 = (f32[32,256]{1,0:T(8,128)S(1)}, f32[32,256]{1,0:T(8,128)S(1)}, u32[]{:S(2)}, u32[]{:S(2)}) collective-permute-start(f32[32,256]{1,0:T(8,128)S(1)} %add.168), channel_id=1, source_target_pairs={{0,4},{1,5},{2,6},{3,7},{4,0},{5,1},{6,2},{7,3},{8,12},{9,13},{10,... | collective-permute-start | bytes 98312 | tf_op jit(solution)/shard_map/ppermute | solution.py:97
  162.2 3.5 %collective-permute-start.20 = (f32[64,256]{1,0:T(8,128)S(1)}, f32[64,256]{1,0:T(8,128)S(1)}, u32[]{:S(2)}, u32[]{:S(2)}) collective-permute-start(f32[64,256]{1,0:T(8,128)S(1)} %maximum_select_fusion.2), channel_id=1, source_target_pairs={{0,2},{1,3},{2,0},{3,1},{4,6},{5,7},{6,4},{7,5},{8,10},{9,11},{10,... | collective-permute-start | bytes 196616 | tf_op jit(solution)/shard_map/ppermute | solution.py:97
  165.8 6.0 %collective-permute-start.21 = (f32[128,256]{1,0:T(8,128)S(1)}, f32[128,256]{1,0:T(8,128)S(1)}, u32[]{:S(2)}, u32[]{:S(2)}) collective-permute-start(f32[128,256]{1,0:T(8,128)S(1)} %maximum_select_fusion.1), channel_id=1, source_target_pairs={{0,1},{1,0},{2,3},{3,2},{4,5},{5,4},{6,7},{7,6},{8,9},{9,8},{10,11... | collective-permute-start | bytes 393224 | tf_op jit(solution)/shard_map/ppermute | solution.py:97
  176.8 24.9 %all-to-all-start.2 = ((f32[128,8,256]{2,1,0:T(8,128)}), f32[128,8,256]{2,1,0:T(8,128)S(1)}, u32[]{:S(2)}, u32[]{:S(2)}) async-start(f32[128,8,256]{2,1,0:T(8,128)} %bitcast.19), calls=%async_computation.2 | async-start | bytes 2097152 | tf_op jit(solution)/shard_map/all_to_all | solution.py:228

commit v9 on v8

--- a/solution.py
+++ b/solution.py
@@ -42,6 +42,48 @@
         compiler_params=pltpu.CompilerParams(vmem_limit_bytes=48 * 1024 * 1024),
     )(queries, group_items, item_vectors)
 
+
+def stats_block(q_ref, items_ref, stats_ref, *, scaling):
+    scores = scaling * lax.dot_general(q_ref[...], items_ref[...], (((1,), (1,)), ((), ())), preferred_element_type=jnp.float32)
+    highest = jnp.max(scores, axis=1, keepdims=True)
+    mass = jnp.sum(jnp.exp(scores - highest), axis=1, keepdims=True)
+    lane = lax.broadcasted_iota(jnp.int32, stats_ref.shape, 1)
+    stats_ref[...] = jnp.where(lane == 0, highest, mass)
+
+def block_stats(queries, items, scaling, tile=256):
+    rows, width = queries.shape
+    return pl.pallas_call(
+        functools.partial(stats_block, scaling=scaling),
+        grid=(rows // tile,),
+        in_specs=[pl.BlockSpec((tile, width), lambda i: (i, 0)), pl.BlockSpec(items.shape, lambda i: (0, 0))],
+        out_specs=pl.BlockSpec((tile, 128), lambda i: (i, 0)),
+        out_shape=jax.ShapeDtypeStruct((rows, 128), jnp.float32),
+        compiler_params=pltpu.CompilerParams(vmem_limit_bytes=48 * 1024 * 1024),
+    )(queries, items)
+
+def grads_block(q_ref, items_ref, totals_ref, pulled_ref, pushed_ref, *, scaling):
+    scores = scaling * lax.dot_general(q_ref[...], items_ref[...], (((1,), (1,)), ((), ())), preferred_element_type=jnp.float32)
+    soft = jnp.exp(scores - totals_ref[:, :1]).astype(jnp.bfloat16)
+    pulled_ref[...] = jnp.dot(soft, items_ref[...], preferred_element_type=jnp.float32)
+    part = lax.dot_general(soft, q_ref[...], (((0,), (0,)), ((), ())), preferred_element_type=jnp.float32)
+    @pl.when(pl.program_id(0) == 0)
+    def _():
+        pushed_ref[...] = part
+    @pl.when(pl.program_id(0) != 0)
+    def _():
+        pushed_ref[...] += part
+
+def block_grads_k(queries, items, totals, scaling, tile=256):
+    rows, width = queries.shape
+    return pl.pallas_call(
+        functools.partial(grads_block, scaling=scaling),
+        grid=(rows // tile,),
+        in_specs=[pl.BlockSpec((tile, width), lambda i: (i, 0)), pl.BlockSpec(items.shape, lambda i: (0, 0)),
+                  pl.BlockSpec((tile, 128), lambda i: (i, 0))],
+        out_specs=[pl.BlockSpec((tile, width), lambda i: (i, 0)), pl.BlockSpec((items.shape[0], width), lambda i: (0, 0))],
+        out_shape=[jax.ShapeDtypeStruct((rows, width), jnp.float32), jax.ShapeDtypeStruct((items.shape[0], width), jnp.float32)],
+        compiler_params=pltpu.CompilerParams(vmem_limit_bytes=48 * 1024 * 1024, dimension_semantics=("arbitrary",)),
+    )(queries, items, totals)
 
 def plane_gather(value, axis, side):
     size = side * side
@@ -143,11 +185,9 @@
     row_hidden = plane_gather_rows(hidden, axis, side, True)
     column_items = plane_gather_rows(item_vectors, axis, side, False)
     row_queries = jnp.dot(row_hidden, query_weight, preferred_element_type=jnp.float32).astype(jnp.bfloat16)
-    scores = scaling * lax.dot_general(
-        row_queries, column_items, (((1,), (1,)), ((), ())), preferred_element_type=jnp.float32
-    )
-    local_max = jnp.max(scores, axis=1)
-    local_sum = jnp.sum(jnp.exp(scores - local_max[:, None]), axis=1)
+    stats = block_stats(row_queries, column_items, scaling)
+    local_max = stats[:, 0]
+    local_sum = stats[:, 1]
     stats = jnp.stack([local_max, local_sum])
     block = hidden.shape[0]
     gathered = [stats] + [
@@ -160,11 +200,8 @@
     for other in gathered[1:]:
         mass = mass + other[1] * jnp.exp(other[0] - highest)
     totals = highest + jnp.log(mass)
-    soft_weights = jnp.exp(scores - totals[:, None]).astype(jnp.bfloat16)
-    pulled = jnp.dot(soft_weights, column_items, preferred_element_type=jnp.float32)
-    pushed = lax.dot_general(
-        soft_weights, row_queries, (((0,), (0,)), ((), ())), preferred_element_type=jnp.float32
-    )
+    lanes = jnp.broadcast_to(totals[:, None], (totals.shape[0], 128))
+    pulled, pushed = block_grads_k(row_queries, column_items, lanes, scaling)
     weight_part = lax.dot_general(
         row_hidden, pulled, (((0,), (0,)), ((), ())),
         preferred_element_type=jnp.float32, precision=lax.Precision.HIGHEST,

time: 210 us -> 217 us (1.033)
  matrix products: 27.2 us -> 5.14 us
  Pallas kernels: 0 us -> 18.8 us
  local copies, waits for them, and re-layouts: 31.5 us -> 41.4 us
  waiting for transfers between devices: 60.2 us -> 68 us
  starting transfers between devices: 59.8 us -> 54.7 us
    dot_general x3 -> x0, matrix products: 22.7 us -> none  [the longest x1 8.23 us: block_grads(): lax.dot_general(row_queries, column_items, (((1,), (1,)), ((), ())), pref...]
    pallas_call x0 -> x2, Pallas kernels: none -> 18.8 us  [the longest x1 11.5 us: block_grads_k(): pl.pallas_call(functools.partial(grads_block, scaling=scaling), grid=(row...]
    reduce_sum x1 -> x0, other arithmetic: 8.55 us -> none  [block_grads(): local_sum = jnp.sum(jnp.exp(scores - local_max[:, None]), axis=1)]
    squeeze x0 -> x6, local copies, waits for them, and re-layouts: none -> 8.16 us  [the longest x3 4.1 us: block_grads(): highest = jnp.maximum(highest, other[0])]
    ppermute x12, waiting for transfers between devices: 9.87 us -> 14.7 us  [plane_shift(): return lax.ppermute(value, axis, pairs)]
    add x1, other arithmetic: 0.03 us -> 3.97 us  [block_grads(): totals = highest + jnp.log(mass)]
    ppermute x12, starting transfers between devices: 16.7 us -> 13.1 us  [plane_shift(): return lax.ppermute(value, axis, pairs)]
    ppermute x4, starting transfers between devices: 5.91 us -> 3.28 us  [tree_sum(): lax.ppermute(value, axes, [(i, i ^ step) for i in range(total)])]
  transfers between devices with their start and end apart: 25 -> 25, of which waited for: 15 -> 14; matrix products, arithmetic and copies ran while one was open for 20% -> 19% of each run, Pallas kernels for 0% -> 0%
where the time goes in v9:
time: 217 us
  waiting for transfers between devices  68 us (31%)
  starting transfers between devices  54.7 us (25%)
  local copies, waits for them, and re-layouts  41.4 us (19%)
  other arithmetic  28 us (13%)
  Pallas kernels  18.8 us (9%)
  matrix products  5.14 us (2%)
    ppermute x4, waiting for transfers between devices, tree_sum(): lax.ppermute(value, axes, [(i, i ^ step) for i in range(total)])  22.5 us
    gather x1, local copies, waits for them, and re-layouts, local(): looked = jnp.take(query_table, query_ids, axis=0).astype(jnp.float32)  18.7 us
    all_to_all x1, waiting for transfers between devices, local(): lax.all_to_all(slot_grads, ('batch', 'table'), split_axis=0, concat_axis=...  17.7 us
    ppermute x12, waiting for transfers between devices, plane_shift(): return lax.ppermute(value, axis, pairs)  14.7 us
    ppermute x12, starting transfers between devices, plane_shift(): return lax.ppermute(value, axis, pairs)  13.1 us
    all_to_all x1, starting transfers between devices, local(): lax.all_to_all(requests, ('batch', 'table'), split_axis=0, concat_axis=0,...  11.5 us
    pallas_call x1, Pallas kernels, block_grads_k(): pl.pallas_call(functools.partial(grads_block, scaling=scaling), grid=(row...  11.5 us
    ppermute x3, starting transfers between devices, tree_sum(): lax.ppermute(send, axes, [(i, i ^ step) for i in range(total)])  8.28 us
  transfers between devices with their start and end apart: 25, of which 14 were waited for; matrix products, arithmetic and copies ran while one was open for 19% of the time, Pallas kernels for 0%

profile of v9, /device:TPU:1, one launch (start us, length us, event | category | flops | bytes accessed | tf_op | source)
XLA Modules:
  0.0 217.0 jit_solution(6554938500268384233)
XLA Ops:
  0.7 1.5 copy.53
  2.2 11.5 %all-to-all-start = ((s32[128,1,8]{2,1,0:T(1,128)}), s32[128,1,8]{2,1,0:T(1,128)S(1)}, u32[]{:S(2)}, u32[]{:S(2)}) async-start(s32[128,1,8]{2,1,0:T(1,128)} %bitcast), calls=%async_computation | async-start | bytes 131072 | tf_op jit(solution)/shard_map/all_to_all | solution.py:222
  13.7 0.8 copy.54
  14.7 0.7 bitcast_subtract_fusion
  15.4 0.9 convert_reduce_fusion.1
  16.3 3.3 %gather_fusion = s32[512]{0:T(512)S(1)} fusion(s32[128]{0:T(128)S(1)} %bitcast_subtract_fusion, s32[1024]{0:T(1024)S(1)} %pad_clamp_fusion.1), kind=kCustom, calls=%fused_computation | custom fusion | bytes 6144 | tf_op jit(solution)/shard_map/jit(_take)/gather | solution.py:115
  19.7 3.3 %all-to-all-done = s32[128,1,8]{2,1,0:T(1,128)S(1)} async-done(((s32[128,1,8]{2,1,0:T(1,128)}), s32[128,1,8]{2,1,0:T(1,128)S(1)}, u32[]{:S(2)}, u32[]{:S(2)}) %all-to-all-start) | async-done | bytes 4128 | tf_op jit(solution)/shard_map/all_to_all | solution.py:222
  23.1 0.5 copy-done.7
  23.7 3.9 %gather_fusion.1 = bf16[1024,256]{1,0:T(8,128)(2,1)S(1)} fusion(bf16[2048,256]{1,0:T(8,128)(2,1)S(1)} %copy-done, s32[1024]{0:T(1024)S(1)} %broadcast_clamp_fusion.1), kind=kCustom, calls=%fused_computation.1 | custom fusion | bytes 1052672 | tf_op jit(solution)/shard_map/jit(_take)/gather | solution.py:223
  27.6 1.0 bitcast_select_fusion.1
  29.1 6.5 %all-to-all-start.1 = ((bf16[128,8,256]{2,1,0:T(8,128)(2,1)}), bf16[128,8,256]{2,1,0:T(8,128)(2,1)S(1)}, u32[]{:S(2)}, u32[]{:S(2)}) async-start(bf16[128,8,256]{2,1,0:T(8,128)(2,1)} %bitcast_select_fusion.1), calls=%async_computation.1 | async-start | bytes 1048576 | tf_op jit(solution)/shard_map/all_to_all | solution.py:225
  35.6 18.7 %gather_fusion.2 = bf16[4096,256]{1,0:T(8,128)(2,1)} fusion(bf16[8192,256]{1,0:T(8,128)(2,1)} %param.8, s32[4096]{0:T(1024)S(1)} %broadcast_clamp_fusion), kind=kCustom, calls=%fused_computation.2 | custom fusion | bytes 4210688 | tf_op jit(solution)/shard_map/jit(_take)/gather | solution.py:230
  54.3 4.1 %convert_reduce_fusion = f32[512,256]{1,0:T(8,128)S(1)} fusion(bf16[4096,256]{1,0:T(8,128)(2,1)} %gather_fusion.2, pred[512,8]{1,0:T(8,128)(4,1)S(1)} %copy.55), kind=kLoop, calls=%fused_computation.6 | loop fusion | flops 3014656 | bytes 2625536 | tf_op jit(solution)/shard_map/reduce_sum | solution.py:231
  58.4 2.6 %collective-permute-start.2 = (bf16[512,256]{1,0:T(8,128)(2,1)S(1)}, bf16[512,256]{1,0:T(8,128)(2,1)S(1)}, u32[]{:S(2)}, u32[]{:S(2)}) collective-permute-start(bf16[512,256]{1,0:T(8,128)(2,1)S(1)} %multiply_convert_fusion), channel_id=1, source_target_pairs={{0,24},{8,0},{16,8},{24,16},{32,56},{40,32},{48,40},{56,48},{64,88... | collective-permute-start | bytes 786440 | tf_op jit(solution)/shard_map/ppermute | solution.py:167
  61.1 0.6 collective-permute-start.1
  61.6 0.6 collective-permute-start
  62.2 2.0 gather_fusion.3
  64.3 2.6 %collective-permute-start.5 = (bf16[512,256]{1,0:T(8,128)(2,1)S(1)}, bf16[512,256]{1,0:T(8,128)(2,1)S(1)}, u32[]{:S(2)}, u32[]{:S(2)}) collective-permute-start(bf16[512,256]{1,0:T(8,128)(2,1)S(1)} %broadcast_select_fusion), channel_id=1, source_target_pairs={{0,96},{8,104},{16,112},{24,120},{32,0},{40,8},{48,16},{56,24},{64... | collective-permute-start | bytes 786440 | tf_op jit(solution)/shard_map/ppermute | solution.py:167
  66.9 0.5 collective-permute-start.4
  67.4 4.4 %collective-permute-done.2 = bf16[512,256]{1,0:T(8,128)(2,1)S(1)} collective-permute-done((bf16[512,256]{1,0:T(8,128)(2,1)S(1)}, bf16[512,256]{1,0:T(8,128)(2,1)S(1)}, u32[]{:S(2)}, u32[]{:S(2)}) %collective-permute-start.2) | collective-permute-done | bytes 262176 | tf_op jit(solution)/shard_map/ppermute | solution.py:167
  71.8 4.7 %collective-permute-done = bf16[512,256]{1,0:T(8,128)(2,1)} collective-permute-done((bf16[512,256]{1,0:T(8,128)(2,1)S(1)}, bf16[512,256]{1,0:T(8,128)(2,1)}, u32[]{:S(2)}, u32[]{:S(2)}) %collective-permute-start) | collective-permute-done | bytes 262176 | tf_op jit(solution)/shard_map/ppermute | solution.py:167
  76.5 1.5 convolution_convert_fusion.q_ref
  78.1 3.8 %collective-permute-done.3 = bf16[512,256]{1,0:T(8,128)(2,1)S(1)} collective-permute-done((bf16[512,256]{1,0:T(8,128)(2,1)S(1)}, bf16[512,256]{1,0:T(8,128)(2,1)S(1)}, u32[]{:S(2)}, u32[]{:S(2)}) %collective-permute-start.3) | collective-permute-done | bytes 262176 | tf_op jit(solution)/shard_map/ppermute | solution.py:167
  82.0 7.3 %shard_map.86 = f32[2048,128]{1,0:T(8,128)S(1)} custom-call(bf16[2048,256]{1,0:T(8,128)(2,1)S(1)} %convolution_convert_fusion.q_ref, bf16[2048,256]{1,0:T(8,128)(2,1)S(1)} %pad_maximum_fusion.1.items_ref), custom_call_target="tpu_custom_call" | custom-call | tf_op jit(solution)/shard_map/pallas_call | solution.py:55
  89.3 0.9 slice_reduce_fusion.1
  90.2 1.4 collective-permute-start.8
  91.6 1.0 fusion.19
  92.5 2.4 %collective-permute-start.7 = (f32[2,2048]{1,0:T(2,128)S(1)}, f32[2,2048]{1,0:T(2,128)S(1)}, u32[]{:S(2)}, u32[]{:S(2)}) collective-permute-start(f32[2,2048]{1,0:T(2,128)S(1)} %pad_maximum_fusion.4), channel_id=1, source_target_pairs={{0,16},{8,24},{16,0},{24,8},{32,48},{40,56},{48,32},{56,40},{64,80... | collective-permute-start | bytes 49160 | tf_op jit(solution)/shard_map/ppermute | solution.py:167
  94.9 1.7 collective-permute-done.7
  96.7 1.3 copy.65
  98.0 1.4 copy.59
  99.4 1.4 copy.63
  100.7 1.4 copy.58
  102.1 1.4 copy.61
  103.5 1.4 copy.57
  104.8 4.0 %add_reduce_fusion = f32[2048]{0:T(1024)S(1)} fusion(f32[2048,1]{1,0:T(8,128)} %copy.65, f32[2048,1]{1,0:T(8,128)} %copy.59, f32[2048,1]{1,0:T(8,128)} %copy.63, f32[2048,1]{1,0:T(8,128)} %copy.58, f32[2048,1]{1,0:T(8,128)} %copy.61, f32[2048,1]{1,0:T(8,128)} %copy.57, f32[2048,128]{1,0:T(8,128)S(1)} %shard_map.86), kind=kLoop, calls=%fused_computation.15 | loop fusion | flops 30720 | bytes 73728 | tf_op jit(solution)/shard_map/add | solution.py:202
  109.2 11.5 %shard_map.87 = (f32[2048,256]{1,0:T(8,128)S(1)}, f32[2048,256]{1,0:T(8,128)}) custom-call(bf16[2048,256]{1,0:T(8,128)(2,1)S(1)} %copy-done.2, bf16[2048,256]{1,0:T(8,128)(2,1)S(1)} %pad_maximum_fusion.1.items_ref, f32[2048,128]{1,0:T(8,128)S(1)} %broadcast_in_dim.73.totals_ref), custom_call_target="tpu_custom_call" | custom-call | tf_op jit(solution)/shard_map/pallas_call | solution.py:78
  120.7 2.7 %fusion = f32[256,256]{1,0:T(8,128)S(1)} fusion(f32[256,256]{1,0:T(8,128)S(1)} %copy-done.9, f32[2048,256]{1,0:T(8,128)S(1)} %get-tuple-element.11, bf16[512,256]{1,0:T(8,128)(2,1)S(1)} %copy-done.13, bf16[512,256]{1,0:T(8,128)(2,1)} %collective-permute-done.1, bf16[512,256]{1,0:T(8,128)(2,1)} %collective-permute-done, bf16[512,256]{1,0:T(8,128)(2,1)S(1)} %copy-done.6), kind=kOutput, calls=%fused_computation.10 | convolution fusion | flops 1614938112 | bytes 3670016 | tf_op jit(solution)/shard_map/dot_general | solution.py:205
  123.4 3.6 %collective-permute-start.12 = (f32[128,256]{1,0:T(8,128)S(1)}, f32[128,256]{1,0:T(8,128)}, u32[]{:S(2)}, u32[]{:S(2)}) collective-permute-start(f32[128,256]{1,0:T(8,128)S(1)} %slice_select_fusion), channel_id=1, source_target_pairs={{0,1},{1,0},{2,3},{3,2},{4,5},{5,4},{6,7},{7,6},{8,9},{9,8},{10,11... | collective-permute-start | bytes 393224 | tf_op jit(solution)/shard_map/ppermute | solution.py:131
  127.0 1.1 collective-permute-done.12
  128.1 0.9 select_add_fusion
  129.1 1.4 collective-permute-start.13
  130.5 1.8 collective-permute-done.13
  132.3 3.2 %collective-permute-start.14 = (f32[32,256]{1,0:T(8,128)S(1)}, f32[32,256]{1,0:T(8,128)S(1)}, u32[]{:S(2)}, u32[]{:S(2)}) collective-permute-start(f32[32,256]{1,0:T(8,128)S(1)} %slice_select_fusion.2), channel_id=1, source_target_pairs={{0,4},{1,5},{2,6},{3,7},{4,0},{5,1},{6,2},{7,3},{8,12},{9,13},{10,... | collective-permute-start | bytes 98312 | tf_op jit(solution)/shard_map/ppermute | solution.py:131
  135.6 1.5 collective-permute-start.11
  137.5 0.6 collective-permute-start.9
  138.3 3.0 %collective-permute-done.15 = f32[32,256]{1,0:T(8,128)S(1)} collective-permute-done((f32[32,256]{1,0:T(8,128)S(1)}, f32[32,256]{1,0:T(8,128)S(1)}, u32[]{:S(2)}, u32[]{:S(2)}) %collective-permute-start.15) | collective-permute-done | bytes 32800 | tf_op jit(solution)/shard_map/ppermute | solution.py:135
  141.3 4.6 %collective-permute-done.16 = f32[32,256]{1,0:T(8,128)S(1)} collective-permute-done((f32[32,256]{1,0:T(8,128)S(1)}, f32[32,256]{1,0:T(8,128)S(1)}, u32[]{:S(2)}, u32[]{:S(2)}) %collective-permute-start.16) | collective-permute-done | bytes 32800 | tf_op jit(solution)/shard_map/ppermute | solution.py:135
  145.9 1.3 collective-permute-start.17
  147.2 12.2 %collective-permute-done.17 = f32[32,256]{1,0:T(8,128)S(1)} collective-permute-done((f32[32,256]{1,0:T(8,128)S(1)}, f32[32,256]{1,0:T(8,128)S(1)}, u32[]{:S(2)}, u32[]{:S(2)}) %collective-permute-start.17) | collective-permute-done | bytes 32800 | tf_op jit(solution)/shard_map/ppermute | solution.py:135
  159.4 1.9 collective-permute-start.18
  161.3 2.7 %collective-permute-done.18 = f32[32,256]{1,0:T(8,128)S(1)} collective-permute-done((f32[32,256]{1,0:T(8,128)S(1)}, f32[32,256]{1,0:T(8,128)S(1)}, u32[]{:S(2)}, u32[]{:S(2)}) %collective-permute-start.18) | collective-permute-done | bytes 32800 | tf_op jit(solution)/shard_map/ppermute | solution.py:135
  164.2 4.1 %collective-permute-done.19 = f32[32,256]{1,0:T(8,128)S(1)} collective-permute-done((f32[32,256]{1,0:T(8,128)S(1)}, f32[32,256]{1,0:T(8,128)S(1)}, u32[]{:S(2)}, u32[]{:S(2)}) %collective-permute-start.19) | collective-permute-done | bytes 32800 | tf_op jit(solution)/shard_map/ppermute | solution.py:139
  168.3 0.6 collective-permute-start.20
  168.9 2.9 %collective-permute-done.20 = f32[64,256]{1,0:T(8,128)S(1)} collective-permute-done((f32[64,256]{1,0:T(8,128)S(1)}, f32[64,256]{1,0:T(8,128)S(1)}, u32[]{:S(2)}, u32[]{:S(2)}) %collective-permute-start.20) | collective-permute-done | bytes 65568 | tf_op jit(solution)/shard_map/ppermute | solution.py:139
  171.8 5.8 %collective-permute-start.21 = (f32[128,256]{1,0:T(8,128)S(1)}, f32[128,256]{1,0:T(8,128)S(1)}, u32[]{:S(2)}, u32[]{:S(2)}) collective-permute-start(f32[128,256]{1,0:T(8,128)S(1)} %maximum_select_fusion.1), channel_id=1, source_target_pairs={{0,1},{1,0},{2,3},{3,2},{4,5},{5,4},{6,7},{7,6},{8,9},{9,8},{10,11... | collective-permute-start | bytes 393224 | tf_op jit(solution)/shard_map/ppermute | solution.py:139
  177.6 1.9 subtract_multiply_fusion
  179.5 0.7 maximum_select_fusion
  180.2 4.8 %scatter_custom_fusion = f32[1024,256]{1,0:T(8,128)} fusion(s32[512]{0:T(512)S(1)} %get-tuple-element.17, f32[512,256]{1,0:T(8,128)} %subtract_multiply_fusion, f32[]{:T(128)} %constant.43.clone.1), kind=kCustom, calls=%fused_computation.22 | custom fusion | flops 131072 | bytes 1049088 | tf_op jit(solution)/shard_map/scatter-add | solution.py:263
  185.0 5.5 %all-to-all-start.2 = ((f32[128,8,256]{2,1,0:T(8,128)}), f32[128,8,256]{2,1,0:T(8,128)S(1)}, u32[]{:S(2)}, u32[]{:S(2)}) async-start(f32[128,8,256]{2,1,0:T(8,128)} %bitcast.17), calls=%async_computation.2 | async-start | bytes 2097152 | tf_op jit(solution)/shard_map/all_to_all | solution.py:265
  190.5 0.5 broadcast.93
  191.0 0.7 reduce.10
  191.8 17.7 %all-to-all-done.2 = f32[128,8,256]{2,1,0:T(8,128)S(1)} async-done(((f32[128,8,256]{2,1,0:T(8,128)}), f32[128,8,256]{2,1,0:T(8,128)S(1)}, u32[]{:S(2)}, u32[]{:S(2)}) %all-to-all-start.2) | async-done | bytes 1048608 | tf_op jit(solution)/shard_map/all_to_all | solution.py:265
  209.5 7.5 %scatter_custom_fusion.1 = f32[2048,256]{1,0:T(8,128)} fusion(s32[1024]{0:T(1024)S(1)} %bitcast.47, f32[128,8,256]{2,1,0:T(8,128)S(1)} %all-to-all-done.2, f32[]{:T(128)} %constant.43.clone.1), kind=kCustom, calls=%fused_computation.13 | custom fusion | flops 262144 | bytes 3145732 | tf_op jit(solution)/shard_map/scatter-add | solution.py:271
  (88 shorter events, 2.7 us)
Async XLA Ops:
  0.6 23.0 %copy-start = (bf16[2048,256]{1,0:T(8,128)(2,1)S(1)}, bf16[2048,256]{1,0:T(8,128)(2,1)}, u32[]{:S(2)}) copy-start(bf16[2048,256]{1,0:T(8,128)(2,1)} %param.7) | copy-start | bytes 3145732
  0.6 19.0 %copy-start.11 = (s32[512]{0:T(512)S(1)}, s32[512]{0:T(512)}, u32[]{:S(2)}) copy-start(s32[512]{0:T(512)} %param.13) | copy-start | bytes 6148
  2.2 20.9 %all-to-all-start = ((s32[128,1,8]{2,1,0:T(1,128)}), s32[128,1,8]{2,1,0:T(1,128)S(1)}, u32[]{:S(2)}, u32[]{:S(2)}) async-start(s32[128,1,8]{2,1,0:T(1,128)} %bitcast), calls=%async_computation | async-start | bytes 131072 | tf_op jit(solution)/shard_map/all_to_all | solution.py:222
  23.0 0.6 copy-start.7
  23.7 5.0 %copy-start.10 = (s32[512,8]{0,1:T(8,128)S(1)}, s32[512,8]{0,1:T(8,128)}, u32[]{:S(2)}) copy-start(s32[512,8]{0,1:T(8,128)} %param.10) | copy-start | bytes 49156
  29.1 33.1 %all-to-all-start.1 = ((bf16[128,8,256]{2,1,0:T(8,128)(2,1)}), bf16[128,8,256]{2,1,0:T(8,128)(2,1)S(1)}, u32[]{:S(2)}, u32[]{:S(2)}) async-start(bf16[128,8,256]{2,1,0:T(8,128)(2,1)} %bitcast_select_fusion.1), calls=%async_computation.1 | async-start | bytes 1048576 | tf_op jit(solution)/shard_map/all_to_all | solution.py:225
  58.4 19.6 %copy-start.4 = (bf16[512,256]{1,0:T(8,128)(2,1)}, bf16[512,256]{1,0:T(8,128)(2,1)S(1)}, u32[]{:S(2)}) copy-start(bf16[512,256]{1,0:T(8,128)(2,1)S(1)} %multiply_convert_fusion) | copy-start | bytes 786436
  58.4 13.4 %collective-permute-start.2 = (bf16[512,256]{1,0:T(8,128)(2,1)S(1)}, bf16[512,256]{1,0:T(8,128)(2,1)S(1)}, u32[]{:S(2)}, u32[]{:S(2)}) collective-permute-start(bf16[512,256]{1,0:T(8,128)(2,1)S(1)} %multiply_convert_fusion), channel_id=1, source_target_pairs={{0,24},{8,0},{16,8},{24,16},{32,56},{40,32},{48,40},{56,48},{64,88... | collective-permute-start | bytes 786440 | tf_op jit(solution)/shard_map/ppermute | solution.py:167
  61.1 10.8 %collective-permute-start.1 = (bf16[512,256]{1,0:T(8,128)(2,1)S(1)}, bf16[512,256]{1,0:T(8,128)(2,1)}, u32[]{:S(2)}, u32[]{:S(2)}) collective-permute-start(bf16[512,256]{1,0:T(8,128)(2,1)S(1)} %multiply_convert_fusion), channel_id=1, source_target_pairs={{0,16},{8,24},{16,0},{24,8},{32,48},{40,56},{48,32},{56,40},{64,80... | collective-permute-start | bytes 786440 | tf_op jit(solution)/shard_map/ppermute | solution.py:167
  61.6 14.9 %collective-permute-start = (bf16[512,256]{1,0:T(8,128)(2,1)S(1)}, bf16[512,256]{1,0:T(8,128)(2,1)}, u32[]{:S(2)}, u32[]{:S(2)}) collective-permute-start(bf16[512,256]{1,0:T(8,128)(2,1)S(1)} %multiply_convert_fusion), channel_id=1, source_target_pairs={{0,8},{8,16},{16,24},{24,0},{32,40},{40,48},{48,56},{56,32},{64,72... | collective-permute-start | bytes 786440 | tf_op jit(solution)/shard_map/ppermute | solution.py:167
  64.3 13.7 %collective-permute-start.5 = (bf16[512,256]{1,0:T(8,128)(2,1)S(1)}, bf16[512,256]{1,0:T(8,128)(2,1)S(1)}, u32[]{:S(2)}, u32[]{:S(2)}) collective-permute-start(bf16[512,256]{1,0:T(8,128)(2,1)S(1)} %broadcast_select_fusion), channel_id=1, source_target_pairs={{0,96},{8,104},{16,112},{24,120},{32,0},{40,8},{48,16},{56,24},{64... | collective-permute-start | bytes 786440 | tf_op jit(solution)/shard_map/ppermute | solution.py:167
  66.9 11.2 %collective-permute-start.4 = (bf16[512,256]{1,0:T(8,128)(2,1)S(1)}, bf16[512,256]{1,0:T(8,128)(2,1)S(1)}, u32[]{:S(2)}, u32[]{:S(2)}) collective-permute-start(bf16[512,256]{1,0:T(8,128)(2,1)S(1)} %broadcast_select_fusion), channel_id=1, source_target_pairs={{0,64},{8,72},{16,80},{24,88},{32,96},{40,104},{48,112},{56,120},{... | collective-permute-start | bytes 786440 | tf_op jit(solution)/shard_map/ppermute | solution.py:167
  71.8 6.2 %copy-start.12 = (bf16[512,256]{1,0:T(8,128)(2,1)}, bf16[512,256]{1,0:T(8,128)(2,1)S(1)}, u32[]{:S(2)}) copy-start(bf16[512,256]{1,0:T(8,128)(2,1)S(1)} %collective-permute-done.2) | copy-start | bytes 786436
  71.8 10.1 %collective-permute-start.3 = (bf16[512,256]{1,0:T(8,128)(2,1)S(1)}, bf16[512,256]{1,0:T(8,128)(2,1)S(1)}, u32[]{:S(2)}, u32[]{:S(2)}) collective-permute-start(bf16[512,256]{1,0:T(8,128)(2,1)S(1)} %broadcast_select_fusion), channel_id=1, source_target_pairs={{0,32},{8,40},{16,48},{24,56},{32,64},{40,72},{48,80},{56,88},{64,... | collective-permute-start | bytes 786440 | tf_op jit(solution)/shard_map/ppermute | solution.py:167
  78.0 11.2 %copy-start.1 = (bf16[2048,256]{1,0:T(8,128)(2,1)}, bf16[2048,256]{1,0:T(8,128)(2,1)S(1)}, u32[]{:S(2)}) copy-start(bf16[2048,256]{1,0:T(8,128)(2,1)S(1)} %convolution_convert_fusion.q_ref) | copy-start | bytes 3145732
  82.0 9.6 %copy-start.5 = (bf16[512,256]{1,0:T(8,128)(2,1)S(1)}, bf16[512,256]{1,0:T(8,128)(2,1)}, u32[]{:S(2)}) copy-start(bf16[512,256]{1,0:T(8,128)(2,1)} %copy-done.4) | copy-start | bytes 786436
  90.2 4.7 %collective-permute-start.8 = (f32[2,2048]{1,0:T(2,128)S(1)}, f32[2,2048]{1,0:T(2,128)S(1)}, u32[]{:S(2)}, u32[]{:S(2)}) collective-permute-start(f32[2,2048]{1,0:T(2,128)S(1)} %pad_maximum_fusion.4), channel_id=1, source_target_pairs={{0,24},{8,0},{16,8},{24,16},{32,56},{40,32},{48,40},{56,48},{64,88... | collective-permute-start | bytes 49160 | tf_op jit(solution)/shard_map/ppermute | solution.py:167
  92.5 4.1 %collective-permute-start.7 = (f32[2,2048]{1,0:T(2,128)S(1)}, f32[2,2048]{1,0:T(2,128)S(1)}, u32[]{:S(2)}, u32[]{:S(2)}) collective-permute-start(f32[2,2048]{1,0:T(2,128)S(1)} %pad_maximum_fusion.4), channel_id=1, source_target_pairs={{0,16},{8,24},{16,0},{24,8},{32,48},{40,56},{48,32},{56,40},{64,80... | collective-permute-start | bytes 49160 | tf_op jit(solution)/shard_map/ppermute | solution.py:167
  94.9 7.2 %collective-permute-start.6 = (f32[2,2048]{1,0:T(2,128)S(1)}, f32[2,2048]{1,0:T(2,128)S(1)}, u32[]{:S(2)}, u32[]{:S(2)}) collective-permute-start(f32[2,2048]{1,0:T(2,128)S(1)} %pad_maximum_fusion.4), channel_id=1, source_target_pairs={{0,8},{8,16},{16,24},{24,0},{32,40},{40,48},{48,56},{56,32},{64,72... | collective-permute-start | bytes 49160 | tf_op jit(solution)/shard_map/ppermute | solution.py:167
  104.8 4.3 %copy-start.2 = (bf16[2048,256]{1,0:T(8,128)(2,1)S(1)}, bf16[2048,256]{1,0:T(8,128)(2,1)}, u32[]{:S(2)}) copy-start(bf16[2048,256]{1,0:T(8,128)(2,1)} %copy-done.1) | copy-start | bytes 3145732
  108.8 11.8 %copy-start.6 = (bf16[512,256]{1,0:T(8,128)(2,1)S(1)}, bf16[512,256]{1,0:T(8,128)(2,1)}, u32[]{:S(2)}) copy-start(bf16[512,256]{1,0:T(8,128)(2,1)} %copy-done.4) | copy-start | bytes 786436
  108.8 11.8 %copy-start.9 = (f32[256,256]{1,0:T(8,128)S(1)}, f32[256,256]{1,0:T(8,128)}, u32[]{:S(2)}) copy-start(f32[256,256]{1,0:T(8,128)} %fusion.19) | copy-start | bytes 786436
  108.8 11.8 %copy-start.13 = (bf16[512,256]{1,0:T(8,128)(2,1)S(1)}, bf16[512,256]{1,0:T(8,128)(2,1)}, u32[]{:S(2)}) copy-start(bf16[512,256]{1,0:T(8,128)(2,1)} %copy-done.12) | copy-start | bytes 786436
  120.7 14.8 %copy-start.3 = (f32[2048,256]{1,0:T(8,128)S(1)}, f32[2048,256]{1,0:T(8,128)}, u32[]{:S(2)}) copy-start(f32[2048,256]{1,0:T(8,128)} %get-tuple-element.10) | copy-start | bytes 6291460
  123.4 4.7 %collective-permute-start.12 = (f32[128,256]{1,0:T(8,128)S(1)}, f32[128,256]{1,0:T(8,128)}, u32[]{:S(2)}, u32[]{:S(2)}) collective-permute-start(f32[128,256]{1,0:T(8,128)S(1)} %slice_select_fusion), channel_id=1, source_target_pairs={{0,1},{1,0},{2,3},{3,2},{4,5},{5,4},{6,7},{7,6},{8,9},{9,8},{10,11... | collective-permute-start | bytes 393224 | tf_op jit(solution)/shard_map/ppermute | solution.py:131
  129.1 3.2 %collective-permute-start.13 = (f32[64,256]{1,0:T(8,128)S(1)}, f32[64,256]{1,0:T(8,128)S(1)}, u32[]{:S(2)}, u32[]{:S(2)}) collective-permute-start(f32[64,256]{1,0:T(8,128)S(1)} %slice_select_fusion.1), channel_id=1, source_target_pairs={{0,2},{1,3},{2,0},{3,1},{4,6},{5,7},{6,4},{7,5},{8,10},{9,11},{10,... | collective-permute-start | bytes 196616 | tf_op jit(solution)/shard_map/ppermute | solution.py:131
  132.3 5.9 %collective-permute-start.14 = (f32[32,256]{1,0:T(8,128)S(1)}, f32[32,256]{1,0:T(8,128)S(1)}, u32[]{:S(2)}, u32[]{:S(2)}) collective-permute-start(f32[32,256]{1,0:T(8,128)S(1)} %slice_select_fusion.2), channel_id=1, source_target_pairs={{0,4},{1,5},{2,6},{3,7},{4,0},{5,1},{6,2},{7,3},{8,12},{9,13},{10,... | collective-permute-start | bytes 98312 | tf_op jit(solution)/shard_map/ppermute | solution.py:131
  135.6 41.9 %collective-permute-start.11 = (f32[512,256]{1,0:T(8,128)S(1)}, f32[512,256]{1,0:T(8,128)S(1)}, u32[]{:S(2)}, u32[]{:S(2)}) collective-permute-start(f32[512,256]{1,0:T(8,128)S(1)} %get-tuple-element.19), channel_id=1, source_target_pairs={{0,96},{8,104},{16,112},{24,120},{32,0},{40,8},{48,16},{56,24},{64... | collective-permute-start | bytes 1572872 | tf_op jit(solution)/shard_map/ppermute | solution.py:167
  137.1 40.5 %collective-permute-start.10 = (f32[512,256]{1,0:T(8,128)S(1)}, f32[512,256]{1,0:T(8,128)S(1)}, u32[]{:S(2)}, u32[]{:S(2)}) collective-permute-start(f32[512,256]{1,0:T(8,128)S(1)} %get-tuple-element.20), channel_id=1, source_target_pairs={{0,64},{8,72},{16,80},{24,88},{32,96},{40,104},{48,112},{56,120},{... | collective-permute-start | bytes 1572872 | tf_op jit(solution)/shard_map/ppermute | solution.py:167
  137.5 40.0 %collective-permute-start.9 = (f32[512,256]{1,0:T(8,128)S(1)}, f32[512,256]{1,0:T(8,128)S(1)}, u32[]{:S(2)}, u32[]{:S(2)}) collective-permute-start(f32[512,256]{1,0:T(8,128)S(1)} %get-tuple-element.18), channel_id=1, source_target_pairs={{0,32},{8,40},{16,48},{24,56},{32,64},{40,72},{48,80},{56,88},{64,... | collective-permute-start | bytes 1572872 | tf_op jit(solution)/shard_map/ppermute | solution.py:167
  138.2 3.1 %collective-permute-start.15 = (f32[32,256]{1,0:T(8,128)S(1)}, f32[32,256]{1,0:T(8,128)S(1)}, u32[]{:S(2)}, u32[]{:S(2)}) collective-permute-start(f32[32,256]{1,0:T(8,128)S(1)} %select_add_fusion.2), channel_id=1, source_target_pairs={{0,8},{1,9},{2,10},{3,11},{4,12},{5,13},{6,14},{7,15},{8,0},{9,1},... | collective-permute-start | bytes 98312 | tf_op jit(solution)/shard_map/ppermute | solution.py:135
  141.3 4.6 %collective-permute-start.16 = (f32[32,256]{1,0:T(8,128)S(1)}, f32[32,256]{1,0:T(8,128)S(1)}, u32[]{:S(2)}, u32[]{:S(2)}) collective-permute-start(f32[32,256]{1,0:T(8,128)S(1)} %add.153), channel_id=1, source_target_pairs={{0,16},{1,17},{2,18},{3,19},{4,20},{5,21},{6,22},{7,23},{8,24},{9,... | collective-permute-start | bytes 98312 | tf_op jit(solution)/shard_map/ppermute | solution.py:135
  145.9 13.5 %collective-permute-start.17 = (f32[32,256]{1,0:T(8,128)S(1)}, f32[32,256]{1,0:T(8,128)S(1)}, u32[]{:S(2)}, u32[]{:S(2)}) collective-permute-start(f32[32,256]{1,0:T(8,128)S(1)} %add.154), channel_id=1, source_target_pairs={{0,32},{1,33},{2,34},{3,35},{4,36},{5,37},{6,38},{7,39},{8,40},{9,... | collective-permute-start | bytes 98312 | tf_op jit(solution)/shard_map/ppermute | solution.py:135
  159.4 4.6 %collective-permute-start.18 = (f32[32,256]{1,0:T(8,128)S(1)}, f32[32,256]{1,0:T(8,128)S(1)}, u32[]{:S(2)}, u32[]{:S(2)}) collective-permute-start(f32[32,256]{1,0:T(8,128)S(1)} %add.155), channel_id=1, source_target_pairs={{0,64},{1,65},{2,66},{3,67},{4,68},{5,69},{6,70},{7,71},{8,72},{9,... | collective-permute-start | bytes 98312 | tf_op jit(solution)/shard_map/ppermute | solution.py:135
  164.0 4.3 %collective-permute-start.19 = (f32[32,256]{1,0:T(8,128)S(1)}, f32[32,256]{1,0:T(8,128)S(1)}, u32[]{:S(2)}, u32[]{:S(2)}) collective-permute-start(f32[32,256]{1,0:T(8,128)S(1)} %add.156), channel_id=1, source_target_pairs={{0,4},{1,5},{2,6},{3,7},{4,0},{5,1},{6,2},{7,3},{8,12},{9,13},{10,... | collective-permute-start | bytes 98312 | tf_op jit(solution)/shard_map/ppermute | solution.py:139
  168.3 3.5 %collective-permute-start.20 = (f32[64,256]{1,0:T(8,128)S(1)}, f32[64,256]{1,0:T(8,128)S(1)}, u32[]{:S(2)}, u32[]{:S(2)}) collective-permute-start(f32[64,256]{1,0:T(8,128)S(1)} %maximum_select_fusion.2), channel_id=1, source_target_pairs={{0,2},{1,3},{2,0},{3,1},{4,6},{5,7},{6,4},{7,5},{8,10},{9,11},{10,... | collective-permute-start | bytes 196616 | tf_op jit(solution)/shard_map/ppermute | solution.py:139
  171.8 7.7 %collective-permute-start.21 = (f32[128,256]{1,0:T(8,128)S(1)}, f32[128,256]{1,0:T(8,128)S(1)}, u32[]{:S(2)}, u32[]{:S(2)}) collective-permute-start(f32[128,256]{1,0:T(8,128)S(1)} %maximum_select_fusion.1), channel_id=1, source_target_pairs={{0,1},{1,0},{2,3},{3,2},{4,5},{5,4},{6,7},{7,6},{8,9},{9,8},{10,11... | collective-permute-start | bytes 393224 | tf_op jit(solution)/shard_map/ppermute | solution.py:139
  179.5 11.5 %copy-start.8 = (s32[128,1,8]{2,1,0:T(1,128)S(1)}, s32[128,1,8]{2,1,0:T(1,128)}, u32[]{:S(2)}) copy-start(s32[128,1,8]{2,1,0:T(1,128)} %copy-done.7) | copy-start | bytes 12292
  185.0 24.5 %all-to-all-start.2 = ((f32[128,8,256]{2,1,0:T(8,128)}), f32[128,8,256]{2,1,0:T(8,128)S(1)}, u32[]{:S(2)}, u32[]{:S(2)}) async-start(f32[128,8,256]{2,1,0:T(8,128)} %bitcast.17), calls=%async_computation.2 | async-start | bytes 2097152 | tf_op jit(solution)/shard_map/all_to_all | solution.py:265

commit v10 on v9

--- a/solution.py
+++ b/solution.py
@@ -44,11 +44,13 @@
 
 
 def stats_block(q_ref, items_ref, stats_ref, *, scaling):
-    scores = scaling * lax.dot_general(q_ref[...], items_ref[...], (((1,), (1,)), ((), ())), preferred_element_type=jnp.float32)
-    highest = jnp.max(scores, axis=1, keepdims=True)
-    mass = jnp.sum(jnp.exp(scores - highest), axis=1, keepdims=True)
-    lane = lax.broadcasted_iota(jnp.int32, stats_ref.shape, 1)
-    stats_ref[...] = jnp.where(lane == 0, highest, mass)
+    scores = scaling * lax.dot_general(
+        items_ref[...], q_ref[...], (((1,), (1,)), ((), ())), preferred_element_type=jnp.float32
+    )
+    highest = jnp.max(scores, axis=0, keepdims=True)
+    stats_ref[0:1, :] = highest
+    stats_ref[1:2, :] = jnp.sum(jnp.exp(scores - highest), axis=0, keepdims=True)
+
 
 def block_stats(queries, items, scaling, tile=256):
     rows, width = queries.shape
@@ -56,34 +58,54 @@
         functools.partial(stats_block, scaling=scaling),
         grid=(rows // tile,),
         in_specs=[pl.BlockSpec((tile, width), lambda i: (i, 0)), pl.BlockSpec(items.shape, lambda i: (0, 0))],
-        out_specs=pl.BlockSpec((tile, 128), lambda i: (i, 0)),
-        out_shape=jax.ShapeDtypeStruct((rows, 128), jnp.float32),
+        out_specs=pl.BlockSpec((2, tile), lambda i: (0, i)),
+        out_shape=jax.ShapeDtypeStruct((2, rows), jnp.float32),
         compiler_params=pltpu.CompilerParams(vmem_limit_bytes=48 * 1024 * 1024),
     )(queries, items)
 
+
 def grads_block(q_ref, items_ref, totals_ref, pulled_ref, pushed_ref, *, scaling):
-    scores = scaling * lax.dot_general(q_ref[...], items_ref[...], (((1,), (1,)), ((), ())), preferred_element_type=jnp.float32)
-    soft = jnp.exp(scores - totals_ref[:, :1]).astype(jnp.bfloat16)
-    pulled_ref[...] = jnp.dot(soft, items_ref[...], preferred_element_type=jnp.float32)
-    part = lax.dot_general(soft, q_ref[...], (((0,), (0,)), ((), ())), preferred_element_type=jnp.float32)
+    scores = scaling * lax.dot_general(
+        items_ref[...], q_ref[...], (((1,), (1,)), ((), ())), preferred_element_type=jnp.float32
+    )
+    soft = jnp.exp(scores - totals_ref[...]).astype(jnp.bfloat16)
+    pulled_ref[...] = lax.dot_general(
+        soft, items_ref[...], (((0,), (0,)), ((), ())), preferred_element_type=jnp.float32
+    )
+    part = jnp.dot(soft, q_ref[...], preferred_element_type=jnp.float32)
+
     @pl.when(pl.program_id(0) == 0)
     def _():
         pushed_ref[...] = part
+
     @pl.when(pl.program_id(0) != 0)
     def _():
         pushed_ref[...] += part
+
 
 def block_grads_k(queries, items, totals, scaling, tile=256):
     rows, width = queries.shape
     return pl.pallas_call(
         functools.partial(grads_block, scaling=scaling),
         grid=(rows // tile,),
-        in_specs=[pl.BlockSpec((tile, width), lambda i: (i, 0)), pl.BlockSpec(items.shape, lambda i: (0, 0)),
-                  pl.BlockSpec((tile, 128), lambda i: (i, 0))],
-        out_specs=[pl.BlockSpec((tile, width), lambda i: (i, 0)), pl.BlockSpec((items.shape[0], width), lambda i: (0, 0))],
-        out_shape=[jax.ShapeDtypeStruct((rows, width), jnp.float32), jax.ShapeDtypeStruct((items.shape[0], width), jnp.float32)],
-        compiler_params=pltpu.CompilerParams(vmem_limit_bytes=48 * 1024 * 1024, dimension_semantics=("arbitrary",)),
+        in_specs=[
+            pl.BlockSpec((tile, width), lambda i: (i, 0)),
+            pl.BlockSpec(items.shape, lambda i: (0, 0)),
+            pl.BlockSpec((1, tile), lambda i: (0, i)),
+        ],
+        out_specs=[
+            pl.BlockSpec((tile, width), lambda i: (i, 0)),
+            pl.BlockSpec((items.shape[0], width), lambda i: (0, 0)),
+        ],
+        out_shape=[
+            jax.ShapeDtypeStruct((rows, width), jnp.float32),
+            jax.ShapeDtypeStruct((items.shape[0], width), jnp.float32),
+        ],
+        compiler_params=pltpu.CompilerParams(
+            vmem_limit_bytes=48 * 1024 * 1024, dimension_semantics=("arbitrary",)
+        ),
     )(queries, items, totals)
+
 
 def plane_gather(value, axis, side):
     size = side * side
@@ -186,9 +208,6 @@
     column_items = plane_gather_rows(item_vectors, axis, side, False)
     row_queries = jnp.dot(row_hidden, query_weight, preferred_element_type=jnp.float32).astype(jnp.bfloat16)
     stats = block_stats(row_queries, column_items, scaling)
-    local_max = stats[:, 0]
-    local_sum = stats[:, 1]
-    stats = jnp.stack([local_max, local_sum])
     block = hidden.shape[0]
     gathered = [stats] + [
         jnp.roll(plane_shift(stats, axis, side, step, True), step * block, axis=1) for step in range(1, side)
@@ -200,8 +219,7 @@
     for other in gathered[1:]:
         mass = mass + other[1] * jnp.exp(other[0] - highest)
     totals = highest + jnp.log(mass)
-    lanes = jnp.broadcast_to(totals[:, None], (totals.shape[0], 128))
-    pulled, pushed = block_grads_k(row_queries, column_items, lanes, scaling)
+    pulled, pushed = block_grads_k(row_queries, column_items, totals.reshape(1, -1), scaling)
     weight_part = lax.dot_general(
         row_hidden, pulled, (((0,), (0,)), ((), ())),
         preferred_element_type=jnp.float32, precision=lax.Precision.HIGHEST,

time: 217 us -> 204 us (0.940)
  local copies, waits for them, and re-layouts: 41.4 us -> 32.8 us
  other arithmetic: 28 us -> 22.1 us
    squeeze x6 -> x0, local copies, waits for them, and re-layouts: 8.16 us -> none  [the longest x3 4.1 us: block_grads(): highest = jnp.maximum(highest, other[0])]
    add x1, other arithmetic: 3.97 us -> 0.1 us  [block_grads(): totals = highest + jnp.log(mass)]
  transfers between devices with their start and end apart: 25 -> 25, of which waited for: 14 -> 14; matrix products, arithmetic and copies ran while one was open for 19% -> 18% of each run, Pallas kernels for 0% -> 0%
where the time goes in v10:
time: 204 us
  waiting for transfers between devices  67.8 us (33%)
  starting transfers between devices  54.6 us (27%)
  local copies, waits for them, and re-layouts  32.8 us (16%)
  other arithmetic  22.1 us (11%)
  Pallas kernels  20.8 us (10%)
  matrix products  4.44 us (2%)
    ppermute x4, waiting for transfers between devices, tree_sum(): lax.ppermute(value, axes, [(i, i ^ step) for i in range(total)])  20.9 us
    gather x1, local copies, waits for them, and re-layouts, local(): looked = jnp.take(query_table, query_ids, axis=0).astype(jnp.float32)  18.7 us
    all_to_all x1, waiting for transfers between devices, local(): lax.all_to_all(slot_grads, ('batch', 'table'), split_axis=0, concat_axis=...  17.6 us
    ppermute x12, waiting for transfers between devices, plane_shift(): return lax.ppermute(value, axis, pairs)  16.4 us
    ppermute x12, starting transfers between devices, plane_shift(): return lax.ppermute(value, axis, pairs)  13.3 us
    pallas_call x1, Pallas kernels, block_grads_k(): pl.pallas_call(functools.partial(grads_block, scaling=scaling), grid=(row...  12.9 us
    all_to_all x1, starting transfers between devices, local(): lax.all_to_all(requests, ('batch', 'table'), split_axis=0, concat_axis=0,...  11.5 us
    pallas_call x1, Pallas kernels, block_stats(): pl.pallas_call(functools.partial(stats_block, scaling=scaling), grid=(row...  7.89 us
  transfers between devices with their start and end apart: 25, of which 14 were waited for; matrix products, arithmetic and copies ran while one was open for 18% of the time, Pallas kernels for 0%

profile of v10, /device:TPU:1, one launch (start us, length us, event | category | flops | bytes accessed | tf_op | source)
XLA Modules:
  0.0 203.5 jit_solution(6618812913684234177)
XLA Ops:
  0.7 1.5 copy.22
  2.2 11.5 %all-to-all-start = ((s32[128,1,8]{2,1,0:T(1,128)}), s32[128,1,8]{2,1,0:T(1,128)S(1)}, u32[]{:S(2)}, u32[]{:S(2)}) async-start(s32[128,1,8]{2,1,0:T(1,128)} %bitcast), calls=%async_computation | async-start | bytes 131072 | tf_op jit(solution)/shard_map/all_to_all | solution.py:240
  13.7 0.8 copy.23
  14.4 0.2 reduce-window.8
  14.6 0.1 reduce.1
  14.7 0.7 bitcast_subtract_fusion
  15.4 0.9 convert_reduce_fusion.1
  16.3 3.3 %gather_fusion = s32[512]{0:T(512)S(1)} fusion(s32[128]{0:T(128)S(1)} %bitcast_subtract_fusion, s32[1024]{0:T(1024)S(1)} %pad_clamp_fusion.1), kind=kCustom, calls=%fused_computation | custom fusion | bytes 6144 | tf_op jit(solution)/shard_map/jit(_take)/gather | solution.py:137
  19.7 3.3 %all-to-all-done = s32[128,1,8]{2,1,0:T(1,128)S(1)} async-done(((s32[128,1,8]{2,1,0:T(1,128)}), s32[128,1,8]{2,1,0:T(1,128)S(1)}, u32[]{:S(2)}, u32[]{:S(2)}) %all-to-all-start) | async-done | bytes 4128 | tf_op jit(solution)/shard_map/all_to_all | solution.py:240
  23.2 3.9 %gather_fusion.1 = bf16[1024,256]{1,0:T(8,128)(2,1)S(1)} fusion(bf16[2048,256]{1,0:T(8,128)(2,1)S(1)} %copy-done, s32[1024]{0:T(1024)S(1)} %broadcast_clamp_fusion.1), kind=kCustom, calls=%fused_computation.1 | custom fusion | bytes 1052672 | tf_op jit(solution)/shard_map/jit(_take)/gather | solution.py:241
  27.1 1.0 bitcast_select_fusion.1
  28.2 6.5 %all-to-all-start.1 = ((bf16[128,8,256]{2,1,0:T(8,128)(2,1)}), bf16[128,8,256]{2,1,0:T(8,128)(2,1)S(1)}, u32[]{:S(2)}, u32[]{:S(2)}) async-start(bf16[128,8,256]{2,1,0:T(8,128)(2,1)} %bitcast_select_fusion.1), calls=%async_computation.1 | async-start | bytes 1048576 | tf_op jit(solution)/shard_map/all_to_all | solution.py:243
  34.6 0.2 copy.24
  34.8 0.1 copy.25
  34.9 0.2 reshape.165
  35.1 18.7 %gather_fusion.2 = bf16[4096,256]{1,0:T(8,128)(2,1)} fusion(bf16[8192,256]{1,0:T(8,128)(2,1)} %param.8, s32[4096]{0:T(1024)S(1)} %broadcast_clamp_fusion), kind=kCustom, calls=%fused_computation.2 | custom fusion | bytes 4210688 | tf_op jit(solution)/shard_map/jit(_take)/gather | solution.py:248
  53.8 4.1 %convert_reduce_fusion = f32[512,256]{1,0:T(8,128)S(1)} fusion(bf16[4096,256]{1,0:T(8,128)(2,1)} %gather_fusion.2, pred[512,8]{1,0:T(8,128)(4,1)S(1)} %copy.24), kind=kLoop, calls=%fused_computation.6 | loop fusion | flops 3014656 | bytes 2625536 | tf_op jit(solution)/shard_map/reduce_sum | solution.py:249
  57.9 2.6 %collective-permute-start.2 = (bf16[512,256]{1,0:T(8,128)(2,1)S(1)}, bf16[512,256]{1,0:T(8,128)(2,1)}, u32[]{:S(2)}, u32[]{:S(2)}) collective-permute-start(bf16[512,256]{1,0:T(8,128)(2,1)S(1)} %multiply_convert_fusion), channel_id=1, source_target_pairs={{0,24},{8,0},{16,8},{24,16},{32,56},{40,32},{48,40},{56,48},{64,88... | collective-permute-start | bytes 786440 | tf_op jit(solution)/shard_map/ppermute | solution.py:189
  60.5 0.6 collective-permute-start.1
  61.1 0.6 collective-permute-start
  61.7 2.0 gather_fusion.3
  63.7 0.1 broadcast_select_fusion
  63.8 2.6 %collective-permute-start.5 = (bf16[512,256]{1,0:T(8,128)(2,1)S(1)}, bf16[512,256]{1,0:T(8,128)(2,1)S(1)}, u32[]{:S(2)}, u32[]{:S(2)}) collective-permute-start(bf16[512,256]{1,0:T(8,128)(2,1)S(1)} %broadcast_select_fusion), channel_id=1, source_target_pairs={{0,96},{8,104},{16,112},{24,120},{32,0},{40,8},{48,16},{56,24},{64... | collective-permute-start | bytes 786440 | tf_op jit(solution)/shard_map/ppermute | solution.py:189
  66.4 0.5 collective-permute-start.4
  66.9 4.4 %collective-permute-done.2 = bf16[512,256]{1,0:T(8,128)(2,1)} collective-permute-done((bf16[512,256]{1,0:T(8,128)(2,1)S(1)}, bf16[512,256]{1,0:T(8,128)(2,1)}, u32[]{:S(2)}, u32[]{:S(2)}) %collective-permute-start.2) | collective-permute-done | bytes 262176 | tf_op jit(solution)/shard_map/ppermute | solution.py:189
  71.3 4.7 %collective-permute-done = bf16[512,256]{1,0:T(8,128)(2,1)} collective-permute-done((bf16[512,256]{1,0:T(8,128)(2,1)S(1)}, bf16[512,256]{1,0:T(8,128)(2,1)}, u32[]{:S(2)}, u32[]{:S(2)}) %collective-permute-start) | collective-permute-done | bytes 262176 | tf_op jit(solution)/shard_map/ppermute | solution.py:189
  76.0 1.6 convolution_convert_fusion.q_ref
  77.6 3.8 %collective-permute-done.3 = bf16[512,256]{1,0:T(8,128)(2,1)S(1)} collective-permute-done((bf16[512,256]{1,0:T(8,128)(2,1)S(1)}, bf16[512,256]{1,0:T(8,128)(2,1)S(1)}, u32[]{:S(2)}, u32[]{:S(2)}) %collective-permute-start.3) | collective-permute-done | bytes 262176 | tf_op jit(solution)/shard_map/ppermute | solution.py:189
  81.5 7.9 %shard_map.86 = f32[2,2048]{1,0:T(2,128)S(1)} custom-call(bf16[2048,256]{1,0:T(8,128)(2,1)S(1)} %convolution_convert_fusion.q_ref, bf16[2048,256]{1,0:T(8,128)(2,1)S(1)} %pad_maximum_fusion.1.items_ref), custom_call_target="tpu_custom_call" | custom-call | tf_op jit(solution)/shard_map/pallas_call | solution.py:57
  89.4 1.5 collective-permute-start.8
  90.8 2.2 %collective-permute-start.7 = (f32[2,2048]{1,0:T(2,128)S(1)}, f32[2,2048]{1,0:T(2,128)S(1)}, u32[]{:S(2)}, u32[]{:S(2)}) collective-permute-start(f32[2,2048]{1,0:T(2,128)S(1)} %shard_map.86), channel_id=1, source_target_pairs={{0,16},{8,24},{16,0},{24,8},{32,48},{40,56},{48,32},{56,40},{64,80... | collective-permute-start | bytes 49160 | tf_op jit(solution)/shard_map/ppermute | solution.py:189
  93.1 0.3 fusion.19
  93.4 3.5 %collective-permute-done.6 = f32[2,2048]{1,0:T(2,128)S(1)} collective-permute-done((f32[2,2048]{1,0:T(2,128)S(1)}, f32[2,2048]{1,0:T(2,128)S(1)}, u32[]{:S(2)}, u32[]{:S(2)}) %collective-permute-start.6) | collective-permute-done | bytes 16416 | tf_op jit(solution)/shard_map/ppermute | solution.py:189
  96.9 0.1 log_add_fusion.totals_ref
  97.0 12.9 %shard_map.87 = (f32[2048,256]{1,0:T(8,128)S(1)}, f32[2048,256]{1,0:T(8,128)}) custom-call(bf16[2048,256]{1,0:T(8,128)(2,1)S(1)} %convolution_convert_fusion.q_ref, bf16[2048,256]{1,0:T(8,128)(2,1)S(1)} %pad_maximum_fusion.1.items_ref, f32[1,2048]{1,0:T(1,128)S(1)} %log_add_fusion.totals_ref), custom_call_target="tpu_custom_call" | custom-call | tf_op jit(solution)/shard_map/pallas_call | solution.py:88
  109.9 2.6 %fusion = f32[256,256]{1,0:T(8,128)S(1)} fusion(f32[256,256]{1,0:T(8,128)S(1)} %fusion.19, f32[2048,256]{1,0:T(8,128)S(1)} %get-tuple-element.11, bf16[512,256]{1,0:T(8,128)(2,1)} %collective-permute-done.2, bf16[512,256]{1,0:T(8,128)(2,1)} %collective-permute-done.1, bf16[512,256]{1,0:T(8,128)(2,1)} %collective-permute-done, ...), kind=kOutput, calls=%fused_computation.10 | convolution fusion | flops 1614938112 | bytes 3670016 | tf_op jit(solution)/shard_map/dot_general | solution.py:223
  112.6 2.3 %collective-permute-start.12 = (f32[128,256]{1,0:T(8,128)S(1)}, f32[128,256]{1,0:T(8,128)S(1)}, u32[]{:S(2)}, u32[]{:S(2)}) collective-permute-start(f32[128,256]{1,0:T(8,128)S(1)} %slice_select_fusion), channel_id=1, source_target_pairs={{0,1},{1,0},{2,3},{3,2},{4,5},{5,4},{6,7},{7,6},{8,9},{9,8},{10,11... | collective-permute-start | bytes 393224 | tf_op jit(solution)/shard_map/ppermute | solution.py:153
  114.8 1.0 collective-permute-done.12
  115.9 1.5 collective-permute-start.13
  117.4 1.7 collective-permute-done.13
  119.1 3.3 %collective-permute-start.14 = (f32[32,256]{1,0:T(8,128)S(1)}, f32[32,256]{1,0:T(8,128)S(1)}, u32[]{:S(2)}, u32[]{:S(2)}) collective-permute-start(f32[32,256]{1,0:T(8,128)S(1)} %slice_select_fusion.2), channel_id=1, source_target_pairs={{0,4},{1,5},{2,6},{3,7},{4,0},{5,1},{6,2},{7,3},{8,12},{9,13},{10,... | collective-permute-start | bytes 98312 | tf_op jit(solution)/shard_map/ppermute | solution.py:153
  122.4 1.5 fusion.17
  124.0 2.7 %collective-permute-start.11 = (f32[512,256]{1,0:T(8,128)S(1)}, f32[512,256]{1,0:T(8,128)S(1)}, u32[]{:S(2)}, u32[]{:S(2)}) collective-permute-start(f32[512,256]{1,0:T(8,128)S(1)} %get-tuple-element.17), channel_id=1, source_target_pairs={{0,96},{8,104},{16,112},{24,120},{32,0},{40,8},{48,16},{56,24},{64... | collective-permute-start | bytes 1572872 | tf_op jit(solution)/shard_map/ppermute | solution.py:189
  126.7 3.0 %collective-permute-done.15 = f32[32,256]{1,0:T(8,128)S(1)} collective-permute-done((f32[32,256]{1,0:T(8,128)S(1)}, f32[32,256]{1,0:T(8,128)S(1)}, u32[]{:S(2)}, u32[]{:S(2)}) %collective-permute-start.15) | collective-permute-done | bytes 32800 | tf_op jit(solution)/shard_map/ppermute | solution.py:157
  129.8 1.4 collective-permute-start.16
  131.2 2.8 %collective-permute-done.16 = f32[32,256]{1,0:T(8,128)S(1)} collective-permute-done((f32[32,256]{1,0:T(8,128)S(1)}, f32[32,256]{1,0:T(8,128)S(1)}, u32[]{:S(2)}, u32[]{:S(2)}) %collective-permute-start.16) | collective-permute-done | bytes 32800 | tf_op jit(solution)/shard_map/ppermute | solution.py:157
  134.1 0.6 collective-permute-start.17
  134.6 13.1 %collective-permute-done.17 = f32[32,256]{1,0:T(8,128)S(1)} collective-permute-done((f32[32,256]{1,0:T(8,128)S(1)}, f32[32,256]{1,0:T(8,128)S(1)}, u32[]{:S(2)}, u32[]{:S(2)}) %collective-permute-start.17) | collective-permute-done | bytes 32800 | tf_op jit(solution)/shard_map/ppermute | solution.py:157
  147.7 2.3 %collective-permute-start.18 = (f32[32,256]{1,0:T(8,128)S(1)}, f32[32,256]{1,0:T(8,128)S(1)}, u32[]{:S(2)}, u32[]{:S(2)}) collective-permute-start(f32[32,256]{1,0:T(8,128)S(1)} %add.155), channel_id=1, source_target_pairs={{0,64},{1,65},{2,66},{3,67},{4,68},{5,69},{6,70},{7,71},{8,72},{9,... | collective-permute-start | bytes 98312 | tf_op jit(solution)/shard_map/ppermute | solution.py:157
  150.0 2.0 collective-permute-done.18
  152.0 0.3 collective-permute-start.19
  152.3 4.0 %collective-permute-done.19 = f32[32,256]{1,0:T(8,128)S(1)} collective-permute-done((f32[32,256]{1,0:T(8,128)S(1)}, f32[32,256]{1,0:T(8,128)S(1)}, u32[]{:S(2)}, u32[]{:S(2)}) %collective-permute-start.19) | collective-permute-done | bytes 32800 | tf_op jit(solution)/shard_map/ppermute | solution.py:161
  156.3 0.6 collective-permute-start.20
  156.9 2.9 %collective-permute-done.20 = f32[64,256]{1,0:T(8,128)S(1)} collective-permute-done((f32[64,256]{1,0:T(8,128)S(1)}, f32[64,256]{1,0:T(8,128)S(1)}, u32[]{:S(2)}, u32[]{:S(2)}) %collective-permute-start.20) | collective-permute-done | bytes 65568 | tf_op jit(solution)/shard_map/ppermute | solution.py:161
  159.8 5.9 %collective-permute-start.21 = (f32[128,256]{1,0:T(8,128)S(1)}, f32[128,256]{1,0:T(8,128)S(1)}, u32[]{:S(2)}, u32[]{:S(2)}) collective-permute-start(f32[128,256]{1,0:T(8,128)S(1)} %maximum_select_fusion.1), channel_id=1, source_target_pairs={{0,1},{1,0},{2,3},{3,2},{4,5},{5,4},{6,7},{7,6},{8,9},{9,8},{10,11... | collective-permute-start | bytes 393224 | tf_op jit(solution)/shard_map/ppermute | solution.py:161
  165.7 1.2 subtract_multiply_fusion
  166.9 0.7 maximum_select_fusion
  167.6 4.3 %scatter_custom_fusion = f32[1024,256]{1,0:T(8,128)} fusion(s32[512]{0:T(512)S(1)} %get-tuple-element.15, f32[512,256]{1,0:T(8,128)S(1)} %subtract_multiply_fusion, f32[]{:T(128)} %constant.43.clone.1), kind=kCustom, calls=%fused_computation.19 | custom fusion | flops 131072 | bytes 1048580 | tf_op jit(solution)/shard_map/scatter-add | solution.py:281
  171.9 5.1 %all-to-all-start.2 = ((f32[128,8,256]{2,1,0:T(8,128)}), f32[128,8,256]{2,1,0:T(8,128)S(1)}, u32[]{:S(2)}, u32[]{:S(2)}) async-start(f32[128,8,256]{2,1,0:T(8,128)} %bitcast.11), calls=%async_computation.2 | async-start | bytes 2097152 | tf_op jit(solution)/shard_map/all_to_all | solution.py:283
  177.0 0.5 broadcast.90
  177.5 0.8 reduce.4
  178.3 0.1 reshape.140
  178.5 17.6 %all-to-all-done.2 = f32[128,8,256]{2,1,0:T(8,128)S(1)} async-done(((f32[128,8,256]{2,1,0:T(8,128)}), f32[128,8,256]{2,1,0:T(8,128)S(1)}, u32[]{:S(2)}, u32[]{:S(2)}) %all-to-all-start.2) | async-done | bytes 1048608 | tf_op jit(solution)/shard_map/all_to_all | solution.py:283
  196.0 7.5 %scatter_custom_fusion.1 = f32[2048,256]{1,0:T(8,128)} fusion(s32[1024]{0:T(1024)S(1)} %bitcast.31, f32[128,8,256]{2,1,0:T(8,128)S(1)} %all-to-all-done.2, f32[]{:T(128)} %constant.43.clone.1), kind=kCustom, calls=%fused_computation.13 | custom fusion | flops 262144 | bytes 3145732 | tf_op jit(solution)/shard_map/scatter-add | solution.py:289
  (54 shorter events, 0.7 us)
Async XLA Ops:
  0.6 22.5 %copy-start = (bf16[2048,256]{1,0:T(8,128)(2,1)S(1)}, bf16[2048,256]{1,0:T(8,128)(2,1)}, u32[]{:S(2)}) copy-start(bf16[2048,256]{1,0:T(8,128)(2,1)} %param.7) | copy-start | bytes 3145732
  0.6 19.0 %copy-start.2 = (s32[512]{0:T(512)S(1)}, s32[512]{0:T(512)}, u32[]{:S(2)}) copy-start(s32[512]{0:T(512)} %param.13) | copy-start | bytes 6148
  2.2 20.9 %all-to-all-start = ((s32[128,1,8]{2,1,0:T(1,128)}), s32[128,1,8]{2,1,0:T(1,128)S(1)}, u32[]{:S(2)}, u32[]{:S(2)}) async-start(s32[128,1,8]{2,1,0:T(1,128)} %bitcast), calls=%async_computation | async-start | bytes 131072 | tf_op jit(solution)/shard_map/all_to_all | solution.py:240
  23.2 5.0 %copy-start.1 = (s32[512,8]{0,1:T(8,128)S(1)}, s32[512,8]{0,1:T(8,128)}, u32[]{:S(2)}) copy-start(s32[512,8]{0,1:T(8,128)} %param.10) | copy-start | bytes 49156
  28.2 33.5 %all-to-all-start.1 = ((bf16[128,8,256]{2,1,0:T(8,128)(2,1)}), bf16[128,8,256]{2,1,0:T(8,128)(2,1)S(1)}, u32[]{:S(2)}, u32[]{:S(2)}) async-start(bf16[128,8,256]{2,1,0:T(8,128)(2,1)} %bitcast_select_fusion.1), calls=%async_computation.1 | async-start | bytes 1048576 | tf_op jit(solution)/shard_map/all_to_all | solution.py:243
  57.9 13.4 %collective-permute-start.2 = (bf16[512,256]{1,0:T(8,128)(2,1)S(1)}, bf16[512,256]{1,0:T(8,128)(2,1)}, u32[]{:S(2)}, u32[]{:S(2)}) collective-permute-start(bf16[512,256]{1,0:T(8,128)(2,1)S(1)} %multiply_convert_fusion), channel_id=1, source_target_pairs={{0,24},{8,0},{16,8},{24,16},{32,56},{40,32},{48,40},{56,48},{64,88... | collective-permute-start | bytes 786440 | tf_op jit(solution)/shard_map/ppermute | solution.py:189
  60.5 10.8 %collective-permute-start.1 = (bf16[512,256]{1,0:T(8,128)(2,1)S(1)}, bf16[512,256]{1,0:T(8,128)(2,1)}, u32[]{:S(2)}, u32[]{:S(2)}) collective-permute-start(bf16[512,256]{1,0:T(8,128)(2,1)S(1)} %multiply_convert_fusion), channel_id=1, source_target_pairs={{0,16},{8,24},{16,0},{24,8},{32,48},{40,56},{48,32},{56,40},{64,80... | collective-permute-start | bytes 786440 | tf_op jit(solution)/shard_map/ppermute | solution.py:189
  61.1 14.9 %collective-permute-start = (bf16[512,256]{1,0:T(8,128)(2,1)S(1)}, bf16[512,256]{1,0:T(8,128)(2,1)}, u32[]{:S(2)}, u32[]{:S(2)}) collective-permute-start(bf16[512,256]{1,0:T(8,128)(2,1)S(1)} %multiply_convert_fusion), channel_id=1, source_target_pairs={{0,8},{8,16},{16,24},{24,0},{32,40},{40,48},{48,56},{56,32},{64,72... | collective-permute-start | bytes 786440 | tf_op jit(solution)/shard_map/ppermute | solution.py:189
  63.8 13.8 %collective-permute-start.5 = (bf16[512,256]{1,0:T(8,128)(2,1)S(1)}, bf16[512,256]{1,0:T(8,128)(2,1)S(1)}, u32[]{:S(2)}, u32[]{:S(2)}) collective-permute-start(bf16[512,256]{1,0:T(8,128)(2,1)S(1)} %broadcast_select_fusion), channel_id=1, source_target_pairs={{0,96},{8,104},{16,112},{24,120},{32,0},{40,8},{48,16},{56,24},{64... | collective-permute-start | bytes 786440 | tf_op jit(solution)/shard_map/ppermute | solution.py:189
  66.4 11.2 %collective-permute-start.4 = (bf16[512,256]{1,0:T(8,128)(2,1)S(1)}, bf16[512,256]{1,0:T(8,128)(2,1)S(1)}, u32[]{:S(2)}, u32[]{:S(2)}) collective-permute-start(bf16[512,256]{1,0:T(8,128)(2,1)S(1)} %broadcast_select_fusion), channel_id=1, source_target_pairs={{0,64},{8,72},{16,80},{24,88},{32,96},{40,104},{48,112},{56,120},{... | collective-permute-start | bytes 786440 | tf_op jit(solution)/shard_map/ppermute | solution.py:189
  71.3 10.1 %collective-permute-start.3 = (bf16[512,256]{1,0:T(8,128)(2,1)S(1)}, bf16[512,256]{1,0:T(8,128)(2,1)S(1)}, u32[]{:S(2)}, u32[]{:S(2)}) collective-permute-start(bf16[512,256]{1,0:T(8,128)(2,1)S(1)} %broadcast_select_fusion), channel_id=1, source_target_pairs={{0,32},{8,40},{16,48},{24,56},{32,64},{40,72},{48,80},{56,88},{64,... | collective-permute-start | bytes 786440 | tf_op jit(solution)/shard_map/ppermute | solution.py:189
  89.4 4.0 %collective-permute-start.8 = (f32[2,2048]{1,0:T(2,128)S(1)}, f32[2,2048]{1,0:T(2,128)S(1)}, u32[]{:S(2)}, u32[]{:S(2)}) collective-permute-start(f32[2,2048]{1,0:T(2,128)S(1)} %shard_map.86), channel_id=1, source_target_pairs={{0,24},{8,0},{16,8},{24,16},{32,56},{40,32},{48,40},{56,48},{64,88... | collective-permute-start | bytes 49160 | tf_op jit(solution)/shard_map/ppermute | solution.py:189
  90.8 6.1 %collective-permute-start.7 = (f32[2,2048]{1,0:T(2,128)S(1)}, f32[2,2048]{1,0:T(2,128)S(1)}, u32[]{:S(2)}, u32[]{:S(2)}) collective-permute-start(f32[2,2048]{1,0:T(2,128)S(1)} %shard_map.86), channel_id=1, source_target_pairs={{0,16},{8,24},{16,0},{24,8},{32,48},{40,56},{48,32},{56,40},{64,80... | collective-permute-start | bytes 49160 | tf_op jit(solution)/shard_map/ppermute | solution.py:189
  93.1 3.8 %collective-permute-start.6 = (f32[2,2048]{1,0:T(2,128)S(1)}, f32[2,2048]{1,0:T(2,128)S(1)}, u32[]{:S(2)}, u32[]{:S(2)}) collective-permute-start(f32[2,2048]{1,0:T(2,128)S(1)} %shard_map.86), channel_id=1, source_target_pairs={{0,8},{8,16},{16,24},{24,0},{32,40},{40,48},{48,56},{56,32},{64,72... | collective-permute-start | bytes 49160 | tf_op jit(solution)/shard_map/ppermute | solution.py:189
  112.6 3.3 %collective-permute-start.12 = (f32[128,256]{1,0:T(8,128)S(1)}, f32[128,256]{1,0:T(8,128)S(1)}, u32[]{:S(2)}, u32[]{:S(2)}) collective-permute-start(f32[128,256]{1,0:T(8,128)S(1)} %slice_select_fusion), channel_id=1, source_target_pairs={{0,1},{1,0},{2,3},{3,2},{4,5},{5,4},{6,7},{7,6},{8,9},{9,8},{10,11... | collective-permute-start | bytes 393224 | tf_op jit(solution)/shard_map/ppermute | solution.py:153
  115.9 3.2 %collective-permute-start.13 = (f32[64,256]{1,0:T(8,128)S(1)}, f32[64,256]{1,0:T(8,128)S(1)}, u32[]{:S(2)}, u32[]{:S(2)}) collective-permute-start(f32[64,256]{1,0:T(8,128)S(1)} %slice_select_fusion.1), channel_id=1, source_target_pairs={{0,2},{1,3},{2,0},{3,1},{4,6},{5,7},{6,4},{7,5},{8,10},{9,11},{10,... | collective-permute-start | bytes 196616 | tf_op jit(solution)/shard_map/ppermute | solution.py:153
  119.1 7.5 %collective-permute-start.14 = (f32[32,256]{1,0:T(8,128)S(1)}, f32[32,256]{1,0:T(8,128)S(1)}, u32[]{:S(2)}, u32[]{:S(2)}) collective-permute-start(f32[32,256]{1,0:T(8,128)S(1)} %slice_select_fusion.2), channel_id=1, source_target_pairs={{0,4},{1,5},{2,6},{3,7},{4,0},{5,1},{6,2},{7,3},{8,12},{9,13},{10,... | collective-permute-start | bytes 98312 | tf_op jit(solution)/shard_map/ppermute | solution.py:153
  123.9 41.8 %collective-permute-start.9 = (f32[512,256]{1,0:T(8,128)S(1)}, f32[512,256]{1,0:T(8,128)S(1)}, u32[]{:S(2)}, u32[]{:S(2)}) collective-permute-start(f32[512,256]{1,0:T(8,128)S(1)} %get-tuple-element.16), channel_id=1, source_target_pairs={{0,32},{8,40},{16,48},{24,56},{32,64},{40,72},{48,80},{56,88},{64,... | collective-permute-start | bytes 1572872 | tf_op jit(solution)/shard_map/ppermute | solution.py:189
  124.0 41.7 %collective-permute-start.11 = (f32[512,256]{1,0:T(8,128)S(1)}, f32[512,256]{1,0:T(8,128)S(1)}, u32[]{:S(2)}, u32[]{:S(2)}) collective-permute-start(f32[512,256]{1,0:T(8,128)S(1)} %get-tuple-element.17), channel_id=1, source_target_pairs={{0,96},{8,104},{16,112},{24,120},{32,0},{40,8},{48,16},{56,24},{64... | collective-permute-start | bytes 1572872 | tf_op jit(solution)/shard_map/ppermute | solution.py:189
  126.6 39.0 %collective-permute-start.10 = (f32[512,256]{1,0:T(8,128)S(1)}, f32[512,256]{1,0:T(8,128)S(1)}, u32[]{:S(2)}, u32[]{:S(2)}) collective-permute-start(f32[512,256]{1,0:T(8,128)S(1)} %get-tuple-element.18), channel_id=1, source_target_pairs={{0,64},{8,72},{16,80},{24,88},{32,96},{40,104},{48,112},{56,120},{... | collective-permute-start | bytes 1572872 | tf_op jit(solution)/shard_map/ppermute | solution.py:189
  126.6 3.1 %collective-permute-start.15 = (f32[32,256]{1,0:T(8,128)S(1)}, f32[32,256]{1,0:T(8,128)S(1)}, u32[]{:S(2)}, u32[]{:S(2)}) collective-permute-start(f32[32,256]{1,0:T(8,128)S(1)} %select_add_fusion.2), channel_id=1, source_target_pairs={{0,8},{1,9},{2,10},{3,11},{4,12},{5,13},{6,14},{7,15},{8,0},{9,1},... | collective-permute-start | bytes 98312 | tf_op jit(solution)/shard_map/ppermute | solution.py:157
  129.8 4.3 %collective-permute-start.16 = (f32[32,256]{1,0:T(8,128)S(1)}, f32[32,256]{1,0:T(8,128)S(1)}, u32[]{:S(2)}, u32[]{:S(2)}) collective-permute-start(f32[32,256]{1,0:T(8,128)S(1)} %add.153), channel_id=1, source_target_pairs={{0,16},{1,17},{2,18},{3,19},{4,20},{5,21},{6,22},{7,23},{8,24},{9,... | collective-permute-start | bytes 98312 | tf_op jit(solution)/shard_map/ppermute | solution.py:157
  134.1 13.6 %collective-permute-start.17 = (f32[32,256]{1,0:T(8,128)S(1)}, f32[32,256]{1,0:T(8,128)S(1)}, u32[]{:S(2)}, u32[]{:S(2)}) collective-permute-start(f32[32,256]{1,0:T(8,128)S(1)} %add.154), channel_id=1, source_target_pairs={{0,32},{1,33},{2,34},{3,35},{4,36},{5,37},{6,38},{7,39},{8,40},{9,... | collective-permute-start | bytes 98312 | tf_op jit(solution)/shard_map/ppermute | solution.py:157
  147.7 4.3 %collective-permute-start.18 = (f32[32,256]{1,0:T(8,128)S(1)}, f32[32,256]{1,0:T(8,128)S(1)}, u32[]{:S(2)}, u32[]{:S(2)}) collective-permute-start(f32[32,256]{1,0:T(8,128)S(1)} %add.155), channel_id=1, source_target_pairs={{0,64},{1,65},{2,66},{3,67},{4,68},{5,69},{6,70},{7,71},{8,72},{9,... | collective-permute-start | bytes 98312 | tf_op jit(solution)/shard_map/ppermute | solution.py:157
  152.0 4.3 %collective-permute-start.19 = (f32[32,256]{1,0:T(8,128)S(1)}, f32[32,256]{1,0:T(8,128)S(1)}, u32[]{:S(2)}, u32[]{:S(2)}) collective-permute-start(f32[32,256]{1,0:T(8,128)S(1)} %add.156), channel_id=1, source_target_pairs={{0,4},{1,5},{2,6},{3,7},{4,0},{5,1},{6,2},{7,3},{8,12},{9,13},{10,... | collective-permute-start | bytes 98312 | tf_op jit(solution)/shard_map/ppermute | solution.py:161
  156.3 3.5 %collective-permute-start.20 = (f32[64,256]{1,0:T(8,128)S(1)}, f32[64,256]{1,0:T(8,128)S(1)}, u32[]{:S(2)}, u32[]{:S(2)}) collective-permute-start(f32[64,256]{1,0:T(8,128)S(1)} %maximum_select_fusion.2), channel_id=1, source_target_pairs={{0,2},{1,3},{2,0},{3,1},{4,6},{5,7},{6,4},{7,5},{8,10},{9,11},{10,... | collective-permute-start | bytes 196616 | tf_op jit(solution)/shard_map/ppermute | solution.py:161
  159.8 7.1 %collective-permute-start.21 = (f32[128,256]{1,0:T(8,128)S(1)}, f32[128,256]{1,0:T(8,128)S(1)}, u32[]{:S(2)}, u32[]{:S(2)}) collective-permute-start(f32[128,256]{1,0:T(8,128)S(1)} %maximum_select_fusion.1), channel_id=1, source_target_pairs={{0,1},{1,0},{2,3},{3,2},{4,5},{5,4},{6,7},{7,6},{8,9},{9,8},{10,11... | collective-permute-start | bytes 393224 | tf_op jit(solution)/shard_map/ppermute | solution.py:161
  171.9 24.1 %all-to-all-start.2 = ((f32[128,8,256]{2,1,0:T(8,128)}), f32[128,8,256]{2,1,0:T(8,128)S(1)}, u32[]{:S(2)}, u32[]{:S(2)}) async-start(f32[128,8,256]{2,1,0:T(8,128)} %bitcast.11), calls=%async_computation.2 | async-start | bytes 2097152 | tf_op jit(solution)/shard_map/all_to_all | solution.py:283

commit v11 on v10

--- a/solution.py
+++ b/solution.py
@@ -137,13 +137,17 @@
     return holder * slot_cap + positions - jnp.take(opening, holder)
 
 
-def tree_sum(value, axes, inner):
+def flat_index(axes):
     total = 1
+    index = 0
     for axis in axes:
         total *= lax.axis_size(axis)
-    index = 0
-    for axis in axes:
         index = index * lax.axis_size(axis) + lax.axis_index(axis)
+    return total, index
+
+
+def tree_halve(value, axes, inner):
+    total, index = flat_index(axes)
     step = 1
     while step < inner and step < total and value.shape[0] % 2 == 0:
         half = value.shape[0] // 2
@@ -152,7 +156,12 @@
         send = jnp.where(upper, value[:half], value[half:])
         value = keep + lax.ppermute(send, axes, [(i, i ^ step) for i in range(total)])
         step *= 2
-    halved = step
+    return value, step
+
+
+def tree_finish(value, axes, halved):
+    total, index = flat_index(axes)
+    step = halved
     while step < total:
         value = value + lax.ppermute(value, axes, [(i, i ^ step) for i in range(total)])
         step *= 2
@@ -274,10 +283,11 @@
         )
     total = lax.axis_size("batch") * lax.axis_size("table")
     if total & (total - 1) == 0:
-        weight_grad = tree_sum(partial_value, ("batch", "table"), min(8, lax.axis_size("table")))
+        shard, halved = tree_halve(partial_value, ("batch", "table"), min(8, lax.axis_size("table")))
+        item_grad, shard = lax.optimization_barrier((item_grad, shard))
+        weight_grad = tree_finish(shard, ("batch", "table"), halved)
     else:
         weight_grad = lax.psum(partial_value, ("batch", "table"))
-    item_grad, weight_grad = lax.optimization_barrier((item_grad, weight_grad))
     slot_grads = jax.ops.segment_sum(item_grad, slot_ids, num_segments=sources * slot_cap)
     slot_grads = slot_grads.reshape(sources, slot_cap, model_width)
     returned = lax.all_to_all(

time: 204 us -> 207 us (1.015)
  starting transfers between devices: 54.6 us -> 65.7 us
  waiting for transfers between devices: 67.8 us -> 60 us
    all_to_all x1, waiting for transfers between devices: 17.6 us -> 0.01 us  [local(): lax.all_to_all(slot_grads, ('batch', 'table'), split_axis=0, concat_axis=...]
    ppermute x12, waiting for transfers between devices: 16.4 us -> 33.9 us  [plane_shift(): return lax.ppermute(value, axis, pairs)]
    ppermute x10, waiting for transfers between devices: 30.5 us -> 22.8 us  [the longest x4 17.5 us: tree_finish(): lax.ppermute(value, axes, [(i, i ^ step) for i in range(total)])]
    ppermute x10, starting transfers between devices: 18.3 us -> 24.9 us  [the longest x3 10.5 us: tree_finish(): got = lax.ppermute(value, axes, [(i, i ^ step) for i in range(total)])]
    all_to_all x1, starting transfers between devices: 5.07 us -> 9.51 us  [local(): lax.all_to_all(slot_grads, ('batch', 'table'), split_axis=0, concat_axis=...]
  transfers between devices with their start and end apart: 25 -> 25, of which waited for: 14 -> 16; matrix products, arithmetic and copies ran while one was open for 18% -> 18% of each run, Pallas kernels for 0% -> 0%
where the time goes in v11:
time: 207 us
  starting transfers between devices  65.7 us (32%)
  waiting for transfers between devices  60 us (29%)
  local copies, waits for them, and re-layouts  32.8 us (16%)
  other arithmetic  22.1 us (11%)
  Pallas kernels  20.8 us (10%)
  matrix products  4.44 us (2%)
    ppermute x12, waiting for transfers between devices, plane_shift(): return lax.ppermute(value, axis, pairs)  33.9 us
    gather x1, local copies, waits for them, and re-layouts, local(): looked = jnp.take(query_table, query_ids, axis=0).astype(jnp.float32)  18.7 us
    ppermute x4, waiting for transfers between devices, tree_finish(): lax.ppermute(value, axes, [(i, i ^ step) for i in range(total)])  17.5 us
    ppermute x12, starting transfers between devices, plane_shift(): return lax.ppermute(value, axis, pairs)  13.3 us
    pallas_call x1, Pallas kernels, block_grads_k(): pl.pallas_call(functools.partial(grads_block, scaling=scaling), grid=(row...  12.9 us
    all_to_all x1, starting transfers between devices, local(): lax.all_to_all(requests, ('batch', 'table'), split_axis=0, concat_axis=0,...  11.5 us
    ppermute x3, starting transfers between devices, tree_finish(): got = lax.ppermute(value, axes, [(i, i ^ step) for i in range(total)])  10.5 us
    all_to_all x1, starting transfers between devices, local(): lax.all_to_all(slot_grads, ('batch', 'table'), split_axis=0, concat_axis=...  9.51 us
  transfers between devices with their start and end apart: 25, of which 16 were waited for; matrix products, arithmetic and copies ran while one was open for 18% of the time, Pallas kernels for 0%

profile of v11, /device:TPU:1, one launch (start us, length us, event | category | flops | bytes accessed | tf_op | source)
XLA Modules:
  0.0 206.8 jit_solution(8004377515542905752)
XLA Ops:
  0.7 1.5 copy.22
  2.2 11.5 %all-to-all-start = ((s32[128,1,8]{2,1,0:T(1,128)}), s32[128,1,8]{2,1,0:T(1,128)S(1)}, u32[]{:S(2)}, u32[]{:S(2)}) async-start(s32[128,1,8]{2,1,0:T(1,128)} %bitcast), calls=%async_computation | async-start | bytes 131072 | tf_op jit(solution)/shard_map/all_to_all | solution.py:249
  13.7 0.8 copy.23
  14.4 0.2 reduce-window.8
  14.7 0.7 bitcast_subtract_fusion
  15.4 0.9 convert_reduce_fusion.1
  16.3 3.3 %gather_fusion = s32[512]{0:T(512)S(1)} fusion(s32[128]{0:T(128)S(1)} %bitcast_subtract_fusion, s32[1024]{0:T(1024)S(1)} %pad_clamp_fusion.1), kind=kCustom, calls=%fused_computation | custom fusion | bytes 6144 | tf_op jit(solution)/shard_map/jit(_take)/gather | solution.py:137
  19.7 3.3 %all-to-all-done = s32[128,1,8]{2,1,0:T(1,128)S(1)} async-done(((s32[128,1,8]{2,1,0:T(1,128)}), s32[128,1,8]{2,1,0:T(1,128)S(1)}, u32[]{:S(2)}, u32[]{:S(2)}) %all-to-all-start) | async-done | bytes 4128 | tf_op jit(solution)/shard_map/all_to_all | solution.py:249
  23.2 3.9 %gather_fusion.1 = bf16[1024,256]{1,0:T(8,128)(2,1)S(1)} fusion(bf16[2048,256]{1,0:T(8,128)(2,1)S(1)} %copy-done, s32[1024]{0:T(1024)S(1)} %broadcast_clamp_fusion.1), kind=kCustom, calls=%fused_computation.1 | custom fusion | bytes 1052672 | tf_op jit(solution)/shard_map/jit(_take)/gather | solution.py:250
  27.1 1.0 bitcast_select_fusion.1
  28.2 6.5 %all-to-all-start.1 = ((bf16[128,8,256]{2,1,0:T(8,128)(2,1)}), bf16[128,8,256]{2,1,0:T(8,128)(2,1)S(1)}, u32[]{:S(2)}, u32[]{:S(2)}) async-start(bf16[128,8,256]{2,1,0:T(8,128)(2,1)} %bitcast_select_fusion.1), calls=%async_computation.1 | async-start | bytes 1048576 | tf_op jit(solution)/shard_map/all_to_all | solution.py:252
  34.6 0.2 copy.24
  34.8 0.1 copy.25
  34.9 0.2 reshape.165
  35.1 18.7 %gather_fusion.2 = bf16[4096,256]{1,0:T(8,128)(2,1)} fusion(bf16[8192,256]{1,0:T(8,128)(2,1)} %param.8, s32[4096]{0:T(1024)S(1)} %broadcast_clamp_fusion), kind=kCustom, calls=%fused_computation.2 | custom fusion | bytes 4210688 | tf_op jit(solution)/shard_map/jit(_take)/gather | solution.py:257
  53.8 4.1 %convert_reduce_fusion = f32[512,256]{1,0:T(8,128)S(1)} fusion(bf16[4096,256]{1,0:T(8,128)(2,1)} %gather_fusion.2, pred[512,8]{1,0:T(8,128)(4,1)S(1)} %copy.24), kind=kLoop, calls=%fused_computation.6 | loop fusion | flops 3014656 | bytes 2625536 | tf_op jit(solution)/shard_map/reduce_sum | solution.py:258
  57.9 2.6 %collective-permute-start.2 = (bf16[512,256]{1,0:T(8,128)(2,1)S(1)}, bf16[512,256]{1,0:T(8,128)(2,1)}, u32[]{:S(2)}, u32[]{:S(2)}) collective-permute-start(bf16[512,256]{1,0:T(8,128)(2,1)S(1)} %multiply_convert_fusion), channel_id=1, source_target_pairs={{0,24},{8,0},{16,8},{24,16},{32,56},{40,32},{48,40},{56,48},{64,88... | collective-permute-start | bytes 786440 | tf_op jit(solution)/shard_map/ppermute | solution.py:198
  60.5 0.6 collective-permute-start.1
  61.1 0.6 collective-permute-start
  61.7 2.0 gather_fusion.3
  63.7 0.1 broadcast_select_fusion
  63.8 2.6 %collective-permute-start.5 = (bf16[512,256]{1,0:T(8,128)(2,1)S(1)}, bf16[512,256]{1,0:T(8,128)(2,1)S(1)}, u32[]{:S(2)}, u32[]{:S(2)}) collective-permute-start(bf16[512,256]{1,0:T(8,128)(2,1)S(1)} %broadcast_select_fusion), channel_id=1, source_target_pairs={{0,96},{8,104},{16,112},{24,120},{32,0},{40,8},{48,16},{56,24},{64... | collective-permute-start | bytes 786440 | tf_op jit(solution)/shard_map/ppermute | solution.py:198
  66.4 0.5 collective-permute-start.4
  66.9 4.4 %collective-permute-done.2 = bf16[512,256]{1,0:T(8,128)(2,1)} collective-permute-done((bf16[512,256]{1,0:T(8,128)(2,1)S(1)}, bf16[512,256]{1,0:T(8,128)(2,1)}, u32[]{:S(2)}, u32[]{:S(2)}) %collective-permute-start.2) | collective-permute-done | bytes 262176 | tf_op jit(solution)/shard_map/ppermute | solution.py:198
  71.3 4.7 %collective-permute-done = bf16[512,256]{1,0:T(8,128)(2,1)} collective-permute-done((bf16[512,256]{1,0:T(8,128)(2,1)S(1)}, bf16[512,256]{1,0:T(8,128)(2,1)}, u32[]{:S(2)}, u32[]{:S(2)}) %collective-permute-start) | collective-permute-done | bytes 262176 | tf_op jit(solution)/shard_map/ppermute | solution.py:198
  76.0 1.6 convolution_convert_fusion.q_ref
  77.6 3.8 %collective-permute-done.3 = bf16[512,256]{1,0:T(8,128)(2,1)S(1)} collective-permute-done((bf16[512,256]{1,0:T(8,128)(2,1)S(1)}, bf16[512,256]{1,0:T(8,128)(2,1)S(1)}, u32[]{:S(2)}, u32[]{:S(2)}) %collective-permute-start.3) | collective-permute-done | bytes 262176 | tf_op jit(solution)/shard_map/ppermute | solution.py:198
  81.5 7.9 %shard_map.86 = f32[2,2048]{1,0:T(2,128)S(1)} custom-call(bf16[2048,256]{1,0:T(8,128)(2,1)S(1)} %convolution_convert_fusion.q_ref, bf16[2048,256]{1,0:T(8,128)(2,1)S(1)} %pad_maximum_fusion.1.items_ref), custom_call_target="tpu_custom_call" | custom-call | tf_op jit(solution)/shard_map/pallas_call | solution.py:57
  89.4 1.5 collective-permute-start.8
  90.8 2.2 %collective-permute-start.7 = (f32[2,2048]{1,0:T(2,128)S(1)}, f32[2,2048]{1,0:T(2,128)S(1)}, u32[]{:S(2)}, u32[]{:S(2)}) collective-permute-start(f32[2,2048]{1,0:T(2,128)S(1)} %shard_map.86), channel_id=1, source_target_pairs={{0,16},{8,24},{16,0},{24,8},{32,48},{40,56},{48,32},{56,40},{64,80... | collective-permute-start | bytes 49160 | tf_op jit(solution)/shard_map/ppermute | solution.py:198
  93.1 0.3 fusion.19
  93.4 3.5 %collective-permute-done.6 = f32[2,2048]{1,0:T(2,128)S(1)} collective-permute-done((f32[2,2048]{1,0:T(2,128)S(1)}, f32[2,2048]{1,0:T(2,128)S(1)}, u32[]{:S(2)}, u32[]{:S(2)}) %collective-permute-start.6) | collective-permute-done | bytes 16416 | tf_op jit(solution)/shard_map/ppermute | solution.py:198
  97.0 12.9 %shard_map.87 = (f32[2048,256]{1,0:T(8,128)S(1)}, f32[2048,256]{1,0:T(8,128)}) custom-call(bf16[2048,256]{1,0:T(8,128)(2,1)S(1)} %convolution_convert_fusion.q_ref, bf16[2048,256]{1,0:T(8,128)(2,1)S(1)} %pad_maximum_fusion.1.items_ref, f32[1,2048]{1,0:T(1,128)S(1)} %log_add_fusion.totals_ref), custom_call_target="tpu_custom_call" | custom-call | tf_op jit(solution)/shard_map/pallas_call | solution.py:88
  109.9 2.6 %fusion = f32[256,256]{1,0:T(8,128)S(1)} fusion(f32[256,256]{1,0:T(8,128)S(1)} %fusion.19, f32[2048,256]{1,0:T(8,128)S(1)} %get-tuple-element.11, bf16[512,256]{1,0:T(8,128)(2,1)} %collective-permute-done.2, bf16[512,256]{1,0:T(8,128)(2,1)} %collective-permute-done.1, bf16[512,256]{1,0:T(8,128)(2,1)} %collective-permute-done, ...), kind=kOutput, calls=%fused_computation.10 | convolution fusion | flops 1614938112 | bytes 3670016 | tf_op jit(solution)/shard_map/dot_general | solution.py:232
  112.6 2.3 %collective-permute-start.12 = (f32[128,256]{1,0:T(8,128)S(1)}, f32[128,256]{1,0:T(8,128)S(1)}, u32[]{:S(2)}, u32[]{:S(2)}) collective-permute-start(f32[128,256]{1,0:T(8,128)S(1)} %slice_select_fusion), channel_id=1, source_target_pairs={{0,1},{1,0},{2,3},{3,2},{4,5},{5,4},{6,7},{7,6},{8,9},{9,8},{10,11... | collective-permute-start | bytes 393224 | tf_op jit(solution)/shard_map/ppermute | solution.py:157
  114.8 1.0 collective-permute-done.12
  115.9 1.5 collective-permute-start.13
  117.4 1.5 fusion.17
  118.9 2.7 %collective-permute-start.11 = (f32[512,256]{1,0:T(8,128)S(1)}, f32[512,256]{1,0:T(8,128)S(1)}, u32[]{:S(2)}, u32[]{:S(2)}) collective-permute-start(f32[512,256]{1,0:T(8,128)S(1)} %get-tuple-element.17), channel_id=1, source_target_pairs={{0,96},{8,104},{16,112},{24,120},{32,0},{40,8},{48,16},{56,24},{64... | collective-permute-start | bytes 1572872 | tf_op jit(solution)/shard_map/ppermute | solution.py:198
  121.6 3.0 %collective-permute-start.14 = (f32[32,256]{1,0:T(8,128)S(1)}, f32[32,256]{1,0:T(8,128)S(1)}, u32[]{:S(2)}, u32[]{:S(2)}) collective-permute-start(f32[32,256]{1,0:T(8,128)S(1)} %slice_select_fusion.2), channel_id=1, source_target_pairs={{0,4},{1,5},{2,6},{3,7},{4,0},{5,1},{6,2},{7,3},{8,12},{9,13},{10,... | collective-permute-start | bytes 98312 | tf_op jit(solution)/shard_map/ppermute | solution.py:157
  124.7 1.3 collective-permute-done.14
  126.0 7.8 %collective-permute-done.9 = f32[512,256]{1,0:T(8,128)S(1)} collective-permute-done((f32[512,256]{1,0:T(8,128)S(1)}, f32[512,256]{1,0:T(8,128)S(1)}, u32[]{:S(2)}, u32[]{:S(2)}) %collective-permute-start.9) | collective-permute-done | bytes 524320 | tf_op jit(solution)/shard_map/ppermute | solution.py:198
  133.8 9.6 %collective-permute-done.10 = f32[512,256]{1,0:T(8,128)S(1)} collective-permute-done((f32[512,256]{1,0:T(8,128)S(1)}, f32[512,256]{1,0:T(8,128)S(1)}, u32[]{:S(2)}, u32[]{:S(2)}) %collective-permute-start.10) | collective-permute-done | bytes 524320 | tf_op jit(solution)/shard_map/ppermute | solution.py:198
  143.4 1.2 subtract_multiply_fusion
  144.7 4.3 %scatter_custom_fusion = f32[1024,256]{1,0:T(8,128)} fusion(s32[512]{0:T(512)S(1)} %get-tuple-element.15, f32[512,256]{1,0:T(8,128)S(1)} %subtract_multiply_fusion, f32[]{:T(128)} %constant.43.clone.1), kind=kCustom, calls=%fused_computation.19 | custom fusion | flops 131072 | bytes 1048580 | tf_op jit(solution)/shard_map/scatter-add | solution.py:291
  149.0 9.5 %all-to-all-start.2 = ((f32[128,8,256]{2,1,0:T(8,128)}), f32[128,8,256]{2,1,0:T(8,128)S(1)}, u32[]{:S(2)}, u32[]{:S(2)}) async-start(f32[128,8,256]{2,1,0:T(8,128)} %bitcast.11), calls=%async_computation.2 | async-start | bytes 2097152 | tf_op jit(solution)/shard_map/all_to_all | solution.py:293
  158.5 1.4 collective-permute-start.15
  159.9 11.9 %collective-permute-done.15 = f32[32,256]{1,0:T(8,128)S(1)} collective-permute-done((f32[32,256]{1,0:T(8,128)S(1)}, f32[32,256]{1,0:T(8,128)S(1)}, u32[]{:S(2)}, u32[]{:S(2)}) %collective-permute-start.15) | collective-permute-done | bytes 32800 | tf_op jit(solution)/shard_map/ppermute | solution.py:166
  171.8 2.4 %collective-permute-start.16 = (f32[32,256]{1,0:T(8,128)S(1)}, f32[32,256]{1,0:T(8,128)S(1)}, u32[]{:S(2)}, u32[]{:S(2)}) collective-permute-start(f32[32,256]{1,0:T(8,128)S(1)} %add.154), channel_id=1, source_target_pairs={{0,16},{1,17},{2,18},{3,19},{4,20},{5,21},{6,22},{7,23},{8,24},{9,... | collective-permute-start | bytes 98312 | tf_op jit(solution)/shard_map/ppermute | solution.py:166
  174.2 2.2 %collective-permute-done.16 = f32[32,256]{1,0:T(8,128)S(1)} collective-permute-done((f32[32,256]{1,0:T(8,128)S(1)}, f32[32,256]{1,0:T(8,128)S(1)}, u32[]{:S(2)}, u32[]{:S(2)}) %collective-permute-start.16) | collective-permute-done | bytes 32800 | tf_op jit(solution)/shard_map/ppermute | solution.py:166
  176.4 1.2 collective-permute-start.17
  177.5 1.6 collective-permute-done.17
  179.1 2.6 %collective-permute-start.18 = (f32[32,256]{1,0:T(8,128)S(1)}, f32[32,256]{1,0:T(8,128)S(1)}, u32[]{:S(2)}, u32[]{:S(2)}) collective-permute-start(f32[32,256]{1,0:T(8,128)S(1)} %add.156), channel_id=1, source_target_pairs={{0,64},{1,65},{2,66},{3,67},{4,68},{5,69},{6,70},{7,71},{8,72},{9,... | collective-permute-start | bytes 98312 | tf_op jit(solution)/shard_map/ppermute | solution.py:166
  181.7 1.8 collective-permute-done.18
  183.5 2.7 %collective-permute-start.19 = (f32[32,256]{1,0:T(8,128)S(1)}, f32[32,256]{1,0:T(8,128)S(1)}, u32[]{:S(2)}, u32[]{:S(2)}) collective-permute-start(f32[32,256]{1,0:T(8,128)S(1)} %add.157), channel_id=1, source_target_pairs={{0,4},{1,5},{2,6},{3,7},{4,0},{5,1},{6,2},{7,3},{8,12},{9,13},{10,... | collective-permute-start | bytes 98312 | tf_op jit(solution)/shard_map/ppermute | solution.py:170
  186.2 1.6 collective-permute-done.19
  187.8 1.3 collective-permute-start.20
  189.1 0.5 broadcast.90
  189.6 0.8 reduce.4
  190.6 0.5 collective-permute-done.20
  191.0 6.6 %collective-permute-start.21 = (f32[128,256]{1,0:T(8,128)S(1)}, f32[128,256]{1,0:T(8,128)S(1)}, u32[]{:S(2)}, u32[]{:S(2)}) collective-permute-start(f32[128,256]{1,0:T(8,128)S(1)} %maximum_select_fusion.1), channel_id=1, source_target_pairs={{0,1},{1,0},{2,3},{3,2},{4,5},{5,4},{6,7},{7,6},{8,9},{9,8},{10,11... | collective-permute-start | bytes 393224 | tf_op jit(solution)/shard_map/ppermute | solution.py:170
  197.6 1.0 collective-permute-done.21
  198.6 0.7 maximum_select_fusion
  199.3 7.5 %scatter_custom_fusion.1 = f32[2048,256]{1,0:T(8,128)} fusion(s32[1024]{0:T(1024)S(1)} %bitcast.31, f32[128,8,256]{2,1,0:T(8,128)S(1)} %all-to-all-done.2, f32[]{:T(128)} %constant.43.clone.1), kind=kCustom, calls=%fused_computation.13 | custom fusion | flops 262144 | bytes 3145732 | tf_op jit(solution)/shard_map/scatter-add | solution.py:299
  (54 shorter events, 0.9 us)
Async XLA Ops:
  0.6 22.5 %copy-start = (bf16[2048,256]{1,0:T(8,128)(2,1)S(1)}, bf16[2048,256]{1,0:T(8,128)(2,1)}, u32[]{:S(2)}) copy-start(bf16[2048,256]{1,0:T(8,128)(2,1)} %param.7) | copy-start | bytes 3145732
  0.6 19.0 %copy-start.2 = (s32[512]{0:T(512)S(1)}, s32[512]{0:T(512)}, u32[]{:S(2)}) copy-start(s32[512]{0:T(512)} %param.13) | copy-start | bytes 6148
  2.2 20.9 %all-to-all-start = ((s32[128,1,8]{2,1,0:T(1,128)}), s32[128,1,8]{2,1,0:T(1,128)S(1)}, u32[]{:S(2)}, u32[]{:S(2)}) async-start(s32[128,1,8]{2,1,0:T(1,128)} %bitcast), calls=%async_computation | async-start | bytes 131072 | tf_op jit(solution)/shard_map/all_to_all | solution.py:249
  23.2 5.0 %copy-start.1 = (s32[512,8]{0,1:T(8,128)S(1)}, s32[512,8]{0,1:T(8,128)}, u32[]{:S(2)}) copy-start(s32[512,8]{0,1:T(8,128)} %param.10) | copy-start | bytes 49156
  28.2 33.5 %all-to-all-start.1 = ((bf16[128,8,256]{2,1,0:T(8,128)(2,1)}), bf16[128,8,256]{2,1,0:T(8,128)(2,1)S(1)}, u32[]{:S(2)}, u32[]{:S(2)}) async-start(bf16[128,8,256]{2,1,0:T(8,128)(2,1)} %bitcast_select_fusion.1), calls=%async_computation.1 | async-start | bytes 1048576 | tf_op jit(solution)/shard_map/all_to_all | solution.py:252
  57.9 13.4 %collective-permute-start.2 = (bf16[512,256]{1,0:T(8,128)(2,1)S(1)}, bf16[512,256]{1,0:T(8,128)(2,1)}, u32[]{:S(2)}, u32[]{:S(2)}) collective-permute-start(bf16[512,256]{1,0:T(8,128)(2,1)S(1)} %multiply_convert_fusion), channel_id=1, source_target_pairs={{0,24},{8,0},{16,8},{24,16},{32,56},{40,32},{48,40},{56,48},{64,88... | collective-permute-start | bytes 786440 | tf_op jit(solution)/shard_map/ppermute | solution.py:198
  60.5 10.8 %collective-permute-start.1 = (bf16[512,256]{1,0:T(8,128)(2,1)S(1)}, bf16[512,256]{1,0:T(8,128)(2,1)}, u32[]{:S(2)}, u32[]{:S(2)}) collective-permute-start(bf16[512,256]{1,0:T(8,128)(2,1)S(1)} %multiply_convert_fusion), channel_id=1, source_target_pairs={{0,16},{8,24},{16,0},{24,8},{32,48},{40,56},{48,32},{56,40},{64,80... | collective-permute-start | bytes 786440 | tf_op jit(solution)/shard_map/ppermute | solution.py:198
  61.1 14.9 %collective-permute-start = (bf16[512,256]{1,0:T(8,128)(2,1)S(1)}, bf16[512,256]{1,0:T(8,128)(2,1)}, u32[]{:S(2)}, u32[]{:S(2)}) collective-permute-start(bf16[512,256]{1,0:T(8,128)(2,1)S(1)} %multiply_convert_fusion), channel_id=1, source_target_pairs={{0,8},{8,16},{16,24},{24,0},{32,40},{40,48},{48,56},{56,32},{64,72... | collective-permute-start | bytes 786440 | tf_op jit(solution)/shard_map/ppermute | solution.py:198
  63.8 13.8 %collective-permute-start.5 = (bf16[512,256]{1,0:T(8,128)(2,1)S(1)}, bf16[512,256]{1,0:T(8,128)(2,1)S(1)}, u32[]{:S(2)}, u32[]{:S(2)}) collective-permute-start(bf16[512,256]{1,0:T(8,128)(2,1)S(1)} %broadcast_select_fusion), channel_id=1, source_target_pairs={{0,96},{8,104},{16,112},{24,120},{32,0},{40,8},{48,16},{56,24},{64... | collective-permute-start | bytes 786440 | tf_op jit(solution)/shard_map/ppermute | solution.py:198
  66.4 11.2 %collective-permute-start.4 = (bf16[512,256]{1,0:T(8,128)(2,1)S(1)}, bf16[512,256]{1,0:T(8,128)(2,1)S(1)}, u32[]{:S(2)}, u32[]{:S(2)}) collective-permute-start(bf16[512,256]{1,0:T(8,128)(2,1)S(1)} %broadcast_select_fusion), channel_id=1, source_target_pairs={{0,64},{8,72},{16,80},{24,88},{32,96},{40,104},{48,112},{56,120},{... | collective-permute-start | bytes 786440 | tf_op jit(solution)/shard_map/ppermute | solution.py:198
  71.3 10.1 %collective-permute-start.3 = (bf16[512,256]{1,0:T(8,128)(2,1)S(1)}, bf16[512,256]{1,0:T(8,128)(2,1)S(1)}, u32[]{:S(2)}, u32[]{:S(2)}) collective-permute-start(bf16[512,256]{1,0:T(8,128)(2,1)S(1)} %broadcast_select_fusion), channel_id=1, source_target_pairs={{0,32},{8,40},{16,48},{24,56},{32,64},{40,72},{48,80},{56,88},{64,... | collective-permute-start | bytes 786440 | tf_op jit(solution)/shard_map/ppermute | solution.py:198
  89.4 4.0 %collective-permute-start.8 = (f32[2,2048]{1,0:T(2,128)S(1)}, f32[2,2048]{1,0:T(2,128)S(1)}, u32[]{:S(2)}, u32[]{:S(2)}) collective-permute-start(f32[2,2048]{1,0:T(2,128)S(1)} %shard_map.86), channel_id=1, source_target_pairs={{0,24},{8,0},{16,8},{24,16},{32,56},{40,32},{48,40},{56,48},{64,88... | collective-permute-start | bytes 49160 | tf_op jit(solution)/shard_map/ppermute | solution.py:198
  90.8 6.1 %collective-permute-start.7 = (f32[2,2048]{1,0:T(2,128)S(1)}, f32[2,2048]{1,0:T(2,128)S(1)}, u32[]{:S(2)}, u32[]{:S(2)}) collective-permute-start(f32[2,2048]{1,0:T(2,128)S(1)} %shard_map.86), channel_id=1, source_target_pairs={{0,16},{8,24},{16,0},{24,8},{32,48},{40,56},{48,32},{56,40},{64,80... | collective-permute-start | bytes 49160 | tf_op jit(solution)/shard_map/ppermute | solution.py:198
  93.1 3.8 %collective-permute-start.6 = (f32[2,2048]{1,0:T(2,128)S(1)}, f32[2,2048]{1,0:T(2,128)S(1)}, u32[]{:S(2)}, u32[]{:S(2)}) collective-permute-start(f32[2,2048]{1,0:T(2,128)S(1)} %shard_map.86), channel_id=1, source_target_pairs={{0,8},{8,16},{16,24},{24,0},{32,40},{40,48},{48,56},{56,32},{64,72... | collective-permute-start | bytes 49160 | tf_op jit(solution)/shard_map/ppermute | solution.py:198
  112.6 3.3 %collective-permute-start.12 = (f32[128,256]{1,0:T(8,128)S(1)}, f32[128,256]{1,0:T(8,128)S(1)}, u32[]{:S(2)}, u32[]{:S(2)}) collective-permute-start(f32[128,256]{1,0:T(8,128)S(1)} %slice_select_fusion), channel_id=1, source_target_pairs={{0,1},{1,0},{2,3},{3,2},{4,5},{5,4},{6,7},{7,6},{8,9},{9,8},{10,11... | collective-permute-start | bytes 393224 | tf_op jit(solution)/shard_map/ppermute | solution.py:157
  115.9 5.7 %collective-permute-start.13 = (f32[64,256]{1,0:T(8,128)S(1)}, f32[64,256]{1,0:T(8,128)S(1)}, u32[]{:S(2)}, u32[]{:S(2)}) collective-permute-start(f32[64,256]{1,0:T(8,128)S(1)} %slice_select_fusion.1), channel_id=1, source_target_pairs={{0,2},{1,3},{2,0},{3,1},{4,6},{5,7},{6,4},{7,5},{8,10},{9,11},{10,... | collective-permute-start | bytes 196616 | tf_op jit(solution)/shard_map/ppermute | solution.py:157
  118.9 14.9 %collective-permute-start.9 = (f32[512,256]{1,0:T(8,128)S(1)}, f32[512,256]{1,0:T(8,128)S(1)}, u32[]{:S(2)}, u32[]{:S(2)}) collective-permute-start(f32[512,256]{1,0:T(8,128)S(1)} %get-tuple-element.16), channel_id=1, source_target_pairs={{0,32},{8,40},{16,48},{24,56},{32,64},{40,72},{48,80},{56,88},{64,... | collective-permute-start | bytes 1572872 | tf_op jit(solution)/shard_map/ppermute | solution.py:198
  118.9 14.9 %collective-permute-start.11 = (f32[512,256]{1,0:T(8,128)S(1)}, f32[512,256]{1,0:T(8,128)S(1)}, u32[]{:S(2)}, u32[]{:S(2)}) collective-permute-start(f32[512,256]{1,0:T(8,128)S(1)} %get-tuple-element.17), channel_id=1, source_target_pairs={{0,96},{8,104},{16,112},{24,120},{32,0},{40,8},{48,16},{56,24},{64... | collective-permute-start | bytes 1572872 | tf_op jit(solution)/shard_map/ppermute | solution.py:198
  121.6 21.8 %collective-permute-start.10 = (f32[512,256]{1,0:T(8,128)S(1)}, f32[512,256]{1,0:T(8,128)S(1)}, u32[]{:S(2)}, u32[]{:S(2)}) collective-permute-start(f32[512,256]{1,0:T(8,128)S(1)} %get-tuple-element.18), channel_id=1, source_target_pairs={{0,64},{8,72},{16,80},{24,88},{32,96},{40,104},{48,112},{56,120},{... | collective-permute-start | bytes 1572872 | tf_op jit(solution)/shard_map/ppermute | solution.py:198
  121.6 4.3 %collective-permute-start.14 = (f32[32,256]{1,0:T(8,128)S(1)}, f32[32,256]{1,0:T(8,128)S(1)}, u32[]{:S(2)}, u32[]{:S(2)}) collective-permute-start(f32[32,256]{1,0:T(8,128)S(1)} %slice_select_fusion.2), channel_id=1, source_target_pairs={{0,4},{1,5},{2,6},{3,7},{4,0},{5,1},{6,2},{7,3},{8,12},{9,13},{10,... | collective-permute-start | bytes 98312 | tf_op jit(solution)/shard_map/ppermute | solution.py:157
  149.0 50.4 %all-to-all-start.2 = ((f32[128,8,256]{2,1,0:T(8,128)}), f32[128,8,256]{2,1,0:T(8,128)S(1)}, u32[]{:S(2)}, u32[]{:S(2)}) async-start(f32[128,8,256]{2,1,0:T(8,128)} %bitcast.11), calls=%async_computation.2 | async-start | bytes 2097152 | tf_op jit(solution)/shard_map/all_to_all | solution.py:293
  158.5 13.3 %collective-permute-start.15 = (f32[32,256]{1,0:T(8,128)S(1)}, f32[32,256]{1,0:T(8,128)S(1)}, u32[]{:S(2)}, u32[]{:S(2)}) collective-permute-start(f32[32,256]{1,0:T(8,128)S(1)} %select_add_fusion.2), channel_id=1, source_target_pairs={{0,8},{1,9},{2,10},{3,11},{4,12},{5,13},{6,14},{7,15},{8,0},{9,1},... | collective-permute-start | bytes 98312 | tf_op jit(solution)/shard_map/ppermute | solution.py:166
  171.8 4.6 %collective-permute-start.16 = (f32[32,256]{1,0:T(8,128)S(1)}, f32[32,256]{1,0:T(8,128)S(1)}, u32[]{:S(2)}, u32[]{:S(2)}) collective-permute-start(f32[32,256]{1,0:T(8,128)S(1)} %add.154), channel_id=1, source_target_pairs={{0,16},{1,17},{2,18},{3,19},{4,20},{5,21},{6,22},{7,23},{8,24},{9,... | collective-permute-start | bytes 98312 | tf_op jit(solution)/shard_map/ppermute | solution.py:166
  176.4 2.8 %collective-permute-start.17 = (f32[32,256]{1,0:T(8,128)S(1)}, f32[32,256]{1,0:T(8,128)S(1)}, u32[]{:S(2)}, u32[]{:S(2)}) collective-permute-start(f32[32,256]{1,0:T(8,128)S(1)} %add.155), channel_id=1, source_target_pairs={{0,32},{1,33},{2,34},{3,35},{4,36},{5,37},{6,38},{7,39},{8,40},{9,... | collective-permute-start | bytes 98312 | tf_op jit(solution)/shard_map/ppermute | solution.py:166
  179.1 4.4 %collective-permute-start.18 = (f32[32,256]{1,0:T(8,128)S(1)}, f32[32,256]{1,0:T(8,128)S(1)}, u32[]{:S(2)}, u32[]{:S(2)}) collective-permute-start(f32[32,256]{1,0:T(8,128)S(1)} %add.156), channel_id=1, source_target_pairs={{0,64},{1,65},{2,66},{3,67},{4,68},{5,69},{6,70},{7,71},{8,72},{9,... | collective-permute-start | bytes 98312 | tf_op jit(solution)/shard_map/ppermute | solution.py:166
  183.5 4.3 %collective-permute-start.19 = (f32[32,256]{1,0:T(8,128)S(1)}, f32[32,256]{1,0:T(8,128)S(1)}, u32[]{:S(2)}, u32[]{:S(2)}) collective-permute-start(f32[32,256]{1,0:T(8,128)S(1)} %add.157), channel_id=1, source_target_pairs={{0,4},{1,5},{2,6},{3,7},{4,0},{5,1},{6,2},{7,3},{8,12},{9,13},{10,... | collective-permute-start | bytes 98312 | tf_op jit(solution)/shard_map/ppermute | solution.py:170
  187.8 3.2 %collective-permute-start.20 = (f32[64,256]{1,0:T(8,128)S(1)}, f32[64,256]{1,0:T(8,128)S(1)}, u32[]{:S(2)}, u32[]{:S(2)}) collective-permute-start(f32[64,256]{1,0:T(8,128)S(1)} %maximum_select_fusion.2), channel_id=1, source_target_pairs={{0,2},{1,3},{2,0},{3,1},{4,6},{5,7},{6,4},{7,5},{8,10},{9,11},{10,... | collective-permute-start | bytes 196616 | tf_op jit(solution)/shard_map/ppermute | solution.py:170
  191.0 7.6 %collective-permute-start.21 = (f32[128,256]{1,0:T(8,128)S(1)}, f32[128,256]{1,0:T(8,128)S(1)}, u32[]{:S(2)}, u32[]{:S(2)}) collective-permute-start(f32[128,256]{1,0:T(8,128)S(1)} %maximum_select_fusion.1), channel_id=1, source_target_pairs={{0,1},{1,0},{2,3},{3,2},{4,5},{5,4},{6,7},{7,6},{8,9},{9,8},{10,11... | collective-permute-start | bytes 393224 | tf_op jit(solution)/shard_map/ppermute | solution.py:170

commit v12 on v10

--- a/solution.py
+++ b/solution.py
@@ -52,8 +52,9 @@
     stats_ref[1:2, :] = jnp.sum(jnp.exp(scores - highest), axis=0, keepdims=True)
 
 
-def block_stats(queries, items, scaling, tile=256):
+def block_stats(queries, items, scaling, tile=1024):
     rows, width = queries.shape
+    tile = tile if rows % tile == 0 else rows
     return pl.pallas_call(
         functools.partial(stats_block, scaling=scaling),
         grid=(rows // tile,),
@@ -83,8 +84,9 @@
         pushed_ref[...] += part
 
 
-def block_grads_k(queries, items, totals, scaling, tile=256):
+def block_grads_k(queries, items, totals, scaling, tile=1024):
     rows, width = queries.shape
+    tile = tile if rows % tile == 0 else rows
     return pl.pallas_call(
         functools.partial(grads_block, scaling=scaling),
         grid=(rows // tile,),

time: 204 us -> 199 us (0.975)
  Pallas kernels: 20.8 us -> 15.2 us
    pallas_call x1, Pallas kernels: 12.9 us -> 9.35 us  [block_grads_k(): pl.pallas_call(functools.partial(grads_block, scaling=scaling), grid=(row...]
  transfers between devices with their start and end apart: 25 -> 25, of which waited for: 14 -> 14; matrix products, arithmetic and copies ran while one was open for 18% -> 19% of each run, Pallas kernels for 0% -> 0%
where the time goes in v12:
time: 199 us; the launch traced here: 198 us
  waiting for transfers between devices  67.8 us (34%)
  starting transfers between devices  55 us (28%)
  local copies, waits for them, and re-layouts  32.8 us (16%)
  other arithmetic  22.1 us (11%)
  Pallas kernels  15.2 us (8%)
  matrix products  4.43 us (2%)
    ppermute x4, waiting for transfers between devices, tree_sum(): lax.ppermute(value, axes, [(i, i ^ step) for i in range(total)])  20.9 us
    gather x1, local copies, waits for them, and re-layouts, local(): looked = jnp.take(query_table, query_ids, axis=0).astype(jnp.float32)  18.7 us
    all_to_all x1, waiting for transfers between devices, local(): lax.all_to_all(slot_grads, ('batch', 'table'), split_axis=0, concat_axis=...  17.6 us
    ppermute x12, waiting for transfers between devices, plane_shift(): return lax.ppermute(value, axis, pairs)  16.4 us
    ppermute x12, starting transfers between devices, plane_shift(): return lax.ppermute(value, axis, pairs)  13.5 us
    all_to_all x1, starting transfers between devices, local(): lax.all_to_all(requests, ('batch', 'table'), split_axis=0, concat_axis=0,...  11.5 us
    pallas_call x1, Pallas kernels, block_grads_k(): pl.pallas_call(functools.partial(grads_block, scaling=scaling), grid=(row...  9.35 us
    scatter-add x1, other arithmetic, local(): table_grad = jnp.zeros((table_rows, model_width), jnp.float32).at[wanted....  7.51 us
  transfers between devices with their start and end apart: 25, of which 14 were waited for; matrix products, arithmetic and copies ran while one was open for 19% of the time, Pallas kernels for 0%

profile of v12, /device:TPU:1, one launch (start us, length us, event | category | flops | bytes accessed | tf_op | source)
XLA Modules:
  0.0 198.3 jit_solution(3592990750838262033)
XLA Ops:
  0.7 1.5 copy.22
  2.2 11.5 %all-to-all-start = ((s32[128,1,8]{2,1,0:T(1,128)}), s32[128,1,8]{2,1,0:T(1,128)S(1)}, u32[]{:S(2)}, u32[]{:S(2)}) async-start(s32[128,1,8]{2,1,0:T(1,128)} %bitcast), calls=%async_computation | async-start | bytes 131072 | tf_op jit(solution)/shard_map/all_to_all | solution.py:242
  13.7 0.8 copy.23
  14.4 0.2 reduce-window.8
  14.6 0.1 reduce.1
  14.7 0.7 bitcast_subtract_fusion
  15.4 0.9 convert_reduce_fusion.1
  16.3 3.3 %gather_fusion = s32[512]{0:T(512)S(1)} fusion(s32[128]{0:T(128)S(1)} %bitcast_subtract_fusion, s32[1024]{0:T(1024)S(1)} %pad_clamp_fusion.1), kind=kCustom, calls=%fused_computation | custom fusion | bytes 6144 | tf_op jit(solution)/shard_map/jit(_take)/gather | solution.py:139
  19.7 3.3 %all-to-all-done = s32[128,1,8]{2,1,0:T(1,128)S(1)} async-done(((s32[128,1,8]{2,1,0:T(1,128)}), s32[128,1,8]{2,1,0:T(1,128)S(1)}, u32[]{:S(2)}, u32[]{:S(2)}) %all-to-all-start) | async-done | bytes 4128 | tf_op jit(solution)/shard_map/all_to_all | solution.py:242
  23.2 3.9 %gather_fusion.1 = bf16[1024,256]{1,0:T(8,128)(2,1)S(1)} fusion(bf16[2048,256]{1,0:T(8,128)(2,1)S(1)} %copy-done, s32[1024]{0:T(1024)S(1)} %broadcast_clamp_fusion.1), kind=kCustom, calls=%fused_computation.1 | custom fusion | bytes 1052672 | tf_op jit(solution)/shard_map/jit(_take)/gather | solution.py:243
  27.1 1.0 bitcast_select_fusion.1
  28.2 6.5 %all-to-all-start.1 = ((bf16[128,8,256]{2,1,0:T(8,128)(2,1)}), bf16[128,8,256]{2,1,0:T(8,128)(2,1)S(1)}, u32[]{:S(2)}, u32[]{:S(2)}) async-start(bf16[128,8,256]{2,1,0:T(8,128)(2,1)} %bitcast_select_fusion.1), calls=%async_computation.1 | async-start | bytes 1048576 | tf_op jit(solution)/shard_map/all_to_all | solution.py:245
  34.6 0.2 copy.24
  34.8 0.1 copy.25
  34.9 0.2 reshape.165
  35.1 18.7 %gather_fusion.2 = bf16[4096,256]{1,0:T(8,128)(2,1)} fusion(bf16[8192,256]{1,0:T(8,128)(2,1)} %param.8, s32[4096]{0:T(1024)S(1)} %broadcast_clamp_fusion), kind=kCustom, calls=%fused_computation.2 | custom fusion | bytes 4210688 | tf_op jit(solution)/shard_map/jit(_take)/gather | solution.py:250
  53.8 4.1 %convert_reduce_fusion = f32[512,256]{1,0:T(8,128)S(1)} fusion(bf16[4096,256]{1,0:T(8,128)(2,1)} %gather_fusion.2, pred[512,8]{1,0:T(8,128)(4,1)S(1)} %copy.24), kind=kLoop, calls=%fused_computation.6 | loop fusion | flops 3014656 | bytes 2625536 | tf_op jit(solution)/shard_map/reduce_sum | solution.py:251
  57.9 2.6 %collective-permute-start.2 = (bf16[512,256]{1,0:T(8,128)(2,1)S(1)}, bf16[512,256]{1,0:T(8,128)(2,1)}, u32[]{:S(2)}, u32[]{:S(2)}) collective-permute-start(bf16[512,256]{1,0:T(8,128)(2,1)S(1)} %multiply_convert_fusion), channel_id=1, source_target_pairs={{0,24},{8,0},{16,8},{24,16},{32,56},{40,32},{48,40},{56,48},{64,88... | collective-permute-start | bytes 786440 | tf_op jit(solution)/shard_map/ppermute | solution.py:191
  60.5 0.6 collective-permute-start.1
  61.1 0.6 collective-permute-start
  61.7 2.0 gather_fusion.3
  63.7 0.1 broadcast_select_fusion
  63.8 2.6 %collective-permute-start.5 = (bf16[512,256]{1,0:T(8,128)(2,1)S(1)}, bf16[512,256]{1,0:T(8,128)(2,1)S(1)}, u32[]{:S(2)}, u32[]{:S(2)}) collective-permute-start(bf16[512,256]{1,0:T(8,128)(2,1)S(1)} %broadcast_select_fusion), channel_id=1, source_target_pairs={{0,96},{8,104},{16,112},{24,120},{32,0},{40,8},{48,16},{56,24},{64... | collective-permute-start | bytes 786440 | tf_op jit(solution)/shard_map/ppermute | solution.py:191
  66.4 0.5 collective-permute-start.4
  66.9 4.4 %collective-permute-done.2 = bf16[512,256]{1,0:T(8,128)(2,1)} collective-permute-done((bf16[512,256]{1,0:T(8,128)(2,1)S(1)}, bf16[512,256]{1,0:T(8,128)(2,1)}, u32[]{:S(2)}, u32[]{:S(2)}) %collective-permute-start.2) | collective-permute-done | bytes 262176 | tf_op jit(solution)/shard_map/ppermute | solution.py:191
  71.3 4.7 %collective-permute-done = bf16[512,256]{1,0:T(8,128)(2,1)} collective-permute-done((bf16[512,256]{1,0:T(8,128)(2,1)S(1)}, bf16[512,256]{1,0:T(8,128)(2,1)}, u32[]{:S(2)}, u32[]{:S(2)}) %collective-permute-start) | collective-permute-done | bytes 262176 | tf_op jit(solution)/shard_map/ppermute | solution.py:191
  76.0 1.6 convolution_convert_fusion.q_ref
  77.6 3.8 %collective-permute-done.3 = bf16[512,256]{1,0:T(8,128)(2,1)S(1)} collective-permute-done((bf16[512,256]{1,0:T(8,128)(2,1)S(1)}, bf16[512,256]{1,0:T(8,128)(2,1)S(1)}, u32[]{:S(2)}, u32[]{:S(2)}) %collective-permute-start.3) | collective-permute-done | bytes 262176 | tf_op jit(solution)/shard_map/ppermute | solution.py:191
  81.5 5.9 %shard_map.86 = f32[2,2048]{1,0:T(2,128)S(1)} custom-call(bf16[2048,256]{1,0:T(8,128)(2,1)S(1)} %convolution_convert_fusion.q_ref, bf16[2048,256]{1,0:T(8,128)(2,1)S(1)} %pad_maximum_fusion.1.items_ref), custom_call_target="tpu_custom_call" | custom-call | tf_op jit(solution)/shard_map/pallas_call | solution.py:58
  87.3 1.6 collective-permute-start.8
  89.0 2.2 %collective-permute-start.7 = (f32[2,2048]{1,0:T(2,128)S(1)}, f32[2,2048]{1,0:T(2,128)S(1)}, u32[]{:S(2)}, u32[]{:S(2)}) collective-permute-start(f32[2,2048]{1,0:T(2,128)S(1)} %shard_map.86), channel_id=1, source_target_pairs={{0,16},{8,24},{16,0},{24,8},{32,48},{40,56},{48,32},{56,40},{64,80... | collective-permute-start | bytes 49160 | tf_op jit(solution)/shard_map/ppermute | solution.py:191
  91.2 0.3 fusion.19
  91.5 3.5 %collective-permute-done.6 = f32[2,2048]{1,0:T(2,128)S(1)} collective-permute-done((f32[2,2048]{1,0:T(2,128)S(1)}, f32[2,2048]{1,0:T(2,128)S(1)}, u32[]{:S(2)}, u32[]{:S(2)}) %collective-permute-start.6) | collective-permute-done | bytes 16416 | tf_op jit(solution)/shard_map/ppermute | solution.py:191
  95.1 0.1 log_add_fusion.totals_ref
  95.1 9.4 %shard_map.87 = (f32[2048,256]{1,0:T(8,128)S(1)}, f32[2048,256]{1,0:T(8,128)}) custom-call(bf16[2048,256]{1,0:T(8,128)(2,1)S(1)} %convolution_convert_fusion.q_ref, bf16[2048,256]{1,0:T(8,128)(2,1)S(1)} %pad_maximum_fusion.1.items_ref, f32[1,2048]{1,0:T(1,128)S(1)} %log_add_fusion.totals_ref), custom_call_target="tpu_custom_call" | custom-call | tf_op jit(solution)/shard_map/pallas_call | solution.py:90
  104.5 2.6 %fusion = f32[256,256]{1,0:T(8,128)S(1)} fusion(f32[256,256]{1,0:T(8,128)S(1)} %fusion.19, f32[2048,256]{1,0:T(8,128)S(1)} %get-tuple-element.11, bf16[512,256]{1,0:T(8,128)(2,1)} %collective-permute-done.2, bf16[512,256]{1,0:T(8,128)(2,1)} %collective-permute-done.1, bf16[512,256]{1,0:T(8,128)(2,1)} %collective-permute-done, ...), kind=kOutput, calls=%fused_computation.10 | convolution fusion | flops 1614938112 | bytes 3670016 | tf_op jit(solution)/shard_map/dot_general | solution.py:225
  107.1 2.3 %collective-permute-start.12 = (f32[128,256]{1,0:T(8,128)S(1)}, f32[128,256]{1,0:T(8,128)S(1)}, u32[]{:S(2)}, u32[]{:S(2)}) collective-permute-start(f32[128,256]{1,0:T(8,128)S(1)} %slice_select_fusion), channel_id=1, source_target_pairs={{0,1},{1,0},{2,3},{3,2},{4,5},{5,4},{6,7},{7,6},{8,9},{9,8},{10,11... | collective-permute-start | bytes 393224 | tf_op jit(solution)/shard_map/ppermute | solution.py:155
  109.4 1.0 collective-permute-done.12
  110.5 1.5 collective-permute-start.13
  112.0 1.7 collective-permute-done.13
  113.7 3.3 %collective-permute-start.14 = (f32[32,256]{1,0:T(8,128)S(1)}, f32[32,256]{1,0:T(8,128)S(1)}, u32[]{:S(2)}, u32[]{:S(2)}) collective-permute-start(f32[32,256]{1,0:T(8,128)S(1)} %slice_select_fusion.2), channel_id=1, source_target_pairs={{0,4},{1,5},{2,6},{3,7},{4,0},{5,1},{6,2},{7,3},{8,12},{9,13},{10,... | collective-permute-start | bytes 98312 | tf_op jit(solution)/shard_map/ppermute | solution.py:155
  117.0 1.5 fusion.17
  118.5 2.7 %collective-permute-start.11 = (f32[512,256]{1,0:T(8,128)S(1)}, f32[512,256]{1,0:T(8,128)S(1)}, u32[]{:S(2)}, u32[]{:S(2)}) collective-permute-start(f32[512,256]{1,0:T(8,128)S(1)} %get-tuple-element.17), channel_id=1, source_target_pairs={{0,96},{8,104},{16,112},{24,120},{32,0},{40,8},{48,16},{56,24},{64... | collective-permute-start | bytes 1572872 | tf_op jit(solution)/shard_map/ppermute | solution.py:191
  121.3 3.0 %collective-permute-done.15 = f32[32,256]{1,0:T(8,128)S(1)} collective-permute-done((f32[32,256]{1,0:T(8,128)S(1)}, f32[32,256]{1,0:T(8,128)S(1)}, u32[]{:S(2)}, u32[]{:S(2)}) %collective-permute-start.15) | collective-permute-done | bytes 32800 | tf_op jit(solution)/shard_map/ppermute | solution.py:159
  124.4 1.4 collective-permute-start.16
  125.8 2.8 %collective-permute-done.16 = f32[32,256]{1,0:T(8,128)S(1)} collective-permute-done((f32[32,256]{1,0:T(8,128)S(1)}, f32[32,256]{1,0:T(8,128)S(1)}, u32[]{:S(2)}, u32[]{:S(2)}) %collective-permute-start.16) | collective-permute-done | bytes 32800 | tf_op jit(solution)/shard_map/ppermute | solution.py:159
  128.6 0.6 collective-permute-start.17
  129.2 13.1 %collective-permute-done.17 = f32[32,256]{1,0:T(8,128)S(1)} collective-permute-done((f32[32,256]{1,0:T(8,128)S(1)}, f32[32,256]{1,0:T(8,128)S(1)}, u32[]{:S(2)}, u32[]{:S(2)}) %collective-permute-start.17) | collective-permute-done | bytes 32800 | tf_op jit(solution)/shard_map/ppermute | solution.py:159
  142.3 2.3 %collective-permute-start.18 = (f32[32,256]{1,0:T(8,128)S(1)}, f32[32,256]{1,0:T(8,128)S(1)}, u32[]{:S(2)}, u32[]{:S(2)}) collective-permute-start(f32[32,256]{1,0:T(8,128)S(1)} %add.155), channel_id=1, source_target_pairs={{0,64},{1,65},{2,66},{3,67},{4,68},{5,69},{6,70},{7,71},{8,72},{9,... | collective-permute-start | bytes 98312 | tf_op jit(solution)/shard_map/ppermute | solution.py:159
  144.6 2.0 %collective-permute-done.18 = f32[32,256]{1,0:T(8,128)S(1)} collective-permute-done((f32[32,256]{1,0:T(8,128)S(1)}, f32[32,256]{1,0:T(8,128)S(1)}, u32[]{:S(2)}, u32[]{:S(2)}) %collective-permute-start.18) | collective-permute-done | bytes 32800 | tf_op jit(solution)/shard_map/ppermute | solution.py:159
  146.6 0.3 collective-permute-start.19
  146.9 4.0 %collective-permute-done.19 = f32[32,256]{1,0:T(8,128)S(1)} collective-permute-done((f32[32,256]{1,0:T(8,128)S(1)}, f32[32,256]{1,0:T(8,128)S(1)}, u32[]{:S(2)}, u32[]{:S(2)}) %collective-permute-start.19) | collective-permute-done | bytes 32800 | tf_op jit(solution)/shard_map/ppermute | solution.py:163
  150.8 0.6 collective-permute-start.20
  151.5 2.9 %collective-permute-done.20 = f32[64,256]{1,0:T(8,128)S(1)} collective-permute-done((f32[64,256]{1,0:T(8,128)S(1)}, f32[64,256]{1,0:T(8,128)S(1)}, u32[]{:S(2)}, u32[]{:S(2)}) %collective-permute-start.20) | collective-permute-done | bytes 65568 | tf_op jit(solution)/shard_map/ppermute | solution.py:163
  154.3 6.1 %collective-permute-start.21 = (f32[128,256]{1,0:T(8,128)S(1)}, f32[128,256]{1,0:T(8,128)S(1)}, u32[]{:S(2)}, u32[]{:S(2)}) collective-permute-start(f32[128,256]{1,0:T(8,128)S(1)} %maximum_select_fusion.1), channel_id=1, source_target_pairs={{0,1},{1,0},{2,3},{3,2},{4,5},{5,4},{6,7},{7,6},{8,9},{9,8},{10,11... | collective-permute-start | bytes 393224 | tf_op jit(solution)/shard_map/ppermute | solution.py:163
  160.5 1.2 subtract_multiply_fusion
  161.7 0.7 maximum_select_fusion
  162.4 4.3 %scatter_custom_fusion = f32[1024,256]{1,0:T(8,128)} fusion(s32[512]{0:T(512)S(1)} %get-tuple-element.15, f32[512,256]{1,0:T(8,128)S(1)} %subtract_multiply_fusion, f32[]{:T(128)} %constant.43.clone.1), kind=kCustom, calls=%fused_computation.19 | custom fusion | flops 131072 | bytes 1048580 | tf_op jit(solution)/shard_map/scatter-add | solution.py:283
  166.7 5.0 %all-to-all-start.2 = ((f32[128,8,256]{2,1,0:T(8,128)}), f32[128,8,256]{2,1,0:T(8,128)S(1)}, u32[]{:S(2)}, u32[]{:S(2)}) async-start(f32[128,8,256]{2,1,0:T(8,128)} %bitcast.11), calls=%async_computation.2 | async-start | bytes 2097152 | tf_op jit(solution)/shard_map/all_to_all | solution.py:285
  171.8 0.5 broadcast.90
  172.3 0.8 reduce.4
  173.1 0.1 reshape.140
  173.2 17.6 %all-to-all-done.2 = f32[128,8,256]{2,1,0:T(8,128)S(1)} async-done(((f32[128,8,256]{2,1,0:T(8,128)}), f32[128,8,256]{2,1,0:T(8,128)S(1)}, u32[]{:S(2)}, u32[]{:S(2)}) %all-to-all-start.2) | async-done | bytes 1048608 | tf_op jit(solution)/shard_map/all_to_all | solution.py:285
  190.8 7.5 %scatter_custom_fusion.1 = f32[2048,256]{1,0:T(8,128)} fusion(s32[1024]{0:T(1024)S(1)} %bitcast.31, f32[128,8,256]{2,1,0:T(8,128)S(1)} %all-to-all-done.2, f32[]{:T(128)} %constant.43.clone.1), kind=kCustom, calls=%fused_computation.13 | custom fusion | flops 262144 | bytes 3145732 | tf_op jit(solution)/shard_map/scatter-add | solution.py:291
  (54 shorter events, 0.7 us)
Async XLA Ops:
  0.6 22.5 %copy-start = (bf16[2048,256]{1,0:T(8,128)(2,1)S(1)}, bf16[2048,256]{1,0:T(8,128)(2,1)}, u32[]{:S(2)}) copy-start(bf16[2048,256]{1,0:T(8,128)(2,1)} %param.7) | copy-start | bytes 3145732
  0.6 19.0 %copy-start.2 = (s32[512]{0:T(512)S(1)}, s32[512]{0:T(512)}, u32[]{:S(2)}) copy-start(s32[512]{0:T(512)} %param.13) | copy-start | bytes 6148
  2.2 20.9 %all-to-all-start = ((s32[128,1,8]{2,1,0:T(1,128)}), s32[128,1,8]{2,1,0:T(1,128)S(1)}, u32[]{:S(2)}, u32[]{:S(2)}) async-start(s32[128,1,8]{2,1,0:T(1,128)} %bitcast), calls=%async_computation | async-start | bytes 131072 | tf_op jit(solution)/shard_map/all_to_all | solution.py:242
  23.2 5.0 %copy-start.1 = (s32[512,8]{0,1:T(8,128)S(1)}, s32[512,8]{0,1:T(8,128)}, u32[]{:S(2)}) copy-start(s32[512,8]{0,1:T(8,128)} %param.10) | copy-start | bytes 49156
  28.2 33.5 %all-to-all-start.1 = ((bf16[128,8,256]{2,1,0:T(8,128)(2,1)}), bf16[128,8,256]{2,1,0:T(8,128)(2,1)S(1)}, u32[]{:S(2)}, u32[]{:S(2)}) async-start(bf16[128,8,256]{2,1,0:T(8,128)(2,1)} %bitcast_select_fusion.1), calls=%async_computation.1 | async-start | bytes 1048576 | tf_op jit(solution)/shard_map/all_to_all | solution.py:245
  57.9 13.4 %collective-permute-start.2 = (bf16[512,256]{1,0:T(8,128)(2,1)S(1)}, bf16[512,256]{1,0:T(8,128)(2,1)}, u32[]{:S(2)}, u32[]{:S(2)}) collective-permute-start(bf16[512,256]{1,0:T(8,128)(2,1)S(1)} %multiply_convert_fusion), channel_id=1, source_target_pairs={{0,24},{8,0},{16,8},{24,16},{32,56},{40,32},{48,40},{56,48},{64,88... | collective-permute-start | bytes 786440 | tf_op jit(solution)/shard_map/ppermute | solution.py:191
  60.5 10.8 %collective-permute-start.1 = (bf16[512,256]{1,0:T(8,128)(2,1)S(1)}, bf16[512,256]{1,0:T(8,128)(2,1)}, u32[]{:S(2)}, u32[]{:S(2)}) collective-permute-start(bf16[512,256]{1,0:T(8,128)(2,1)S(1)} %multiply_convert_fusion), channel_id=1, source_target_pairs={{0,16},{8,24},{16,0},{24,8},{32,48},{40,56},{48,32},{56,40},{64,80... | collective-permute-start | bytes 786440 | tf_op jit(solution)/shard_map/ppermute | solution.py:191
  61.1 14.9 %collective-permute-start = (bf16[512,256]{1,0:T(8,128)(2,1)S(1)}, bf16[512,256]{1,0:T(8,128)(2,1)}, u32[]{:S(2)}, u32[]{:S(2)}) collective-permute-start(bf16[512,256]{1,0:T(8,128)(2,1)S(1)} %multiply_convert_fusion), channel_id=1, source_target_pairs={{0,8},{8,16},{16,24},{24,0},{32,40},{40,48},{48,56},{56,32},{64,72... | collective-permute-start | bytes 786440 | tf_op jit(solution)/shard_map/ppermute | solution.py:191
  63.8 13.8 %collective-permute-start.5 = (bf16[512,256]{1,0:T(8,128)(2,1)S(1)}, bf16[512,256]{1,0:T(8,128)(2,1)S(1)}, u32[]{:S(2)}, u32[]{:S(2)}) collective-permute-start(bf16[512,256]{1,0:T(8,128)(2,1)S(1)} %broadcast_select_fusion), channel_id=1, source_target_pairs={{0,96},{8,104},{16,112},{24,120},{32,0},{40,8},{48,16},{56,24},{64... | collective-permute-start | bytes 786440 | tf_op jit(solution)/shard_map/ppermute | solution.py:191
  66.4 11.2 %collective-permute-start.4 = (bf16[512,256]{1,0:T(8,128)(2,1)S(1)}, bf16[512,256]{1,0:T(8,128)(2,1)S(1)}, u32[]{:S(2)}, u32[]{:S(2)}) collective-permute-start(bf16[512,256]{1,0:T(8,128)(2,1)S(1)} %broadcast_select_fusion), channel_id=1, source_target_pairs={{0,64},{8,72},{16,80},{24,88},{32,96},{40,104},{48,112},{56,120},{... | collective-permute-start | bytes 786440 | tf_op jit(solution)/shard_map/ppermute | solution.py:191
  71.3 10.1 %collective-permute-start.3 = (bf16[512,256]{1,0:T(8,128)(2,1)S(1)}, bf16[512,256]{1,0:T(8,128)(2,1)S(1)}, u32[]{:S(2)}, u32[]{:S(2)}) collective-permute-start(bf16[512,256]{1,0:T(8,128)(2,1)S(1)} %broadcast_select_fusion), channel_id=1, source_target_pairs={{0,32},{8,40},{16,48},{24,56},{32,64},{40,72},{48,80},{56,88},{64,... | collective-permute-start | bytes 786440 | tf_op jit(solution)/shard_map/ppermute | solution.py:191
  87.3 4.2 %collective-permute-start.8 = (f32[2,2048]{1,0:T(2,128)S(1)}, f32[2,2048]{1,0:T(2,128)S(1)}, u32[]{:S(2)}, u32[]{:S(2)}) collective-permute-start(f32[2,2048]{1,0:T(2,128)S(1)} %shard_map.86), channel_id=1, source_target_pairs={{0,24},{8,0},{16,8},{24,16},{32,56},{40,32},{48,40},{56,48},{64,88... | collective-permute-start | bytes 49160 | tf_op jit(solution)/shard_map/ppermute | solution.py:191
  89.0 6.1 %collective-permute-start.7 = (f32[2,2048]{1,0:T(2,128)S(1)}, f32[2,2048]{1,0:T(2,128)S(1)}, u32[]{:S(2)}, u32[]{:S(2)}) collective-permute-start(f32[2,2048]{1,0:T(2,128)S(1)} %shard_map.86), channel_id=1, source_target_pairs={{0,16},{8,24},{16,0},{24,8},{32,48},{40,56},{48,32},{56,40},{64,80... | collective-permute-start | bytes 49160 | tf_op jit(solution)/shard_map/ppermute | solution.py:191
  91.2 3.8 %collective-permute-start.6 = (f32[2,2048]{1,0:T(2,128)S(1)}, f32[2,2048]{1,0:T(2,128)S(1)}, u32[]{:S(2)}, u32[]{:S(2)}) collective-permute-start(f32[2,2048]{1,0:T(2,128)S(1)} %shard_map.86), channel_id=1, source_target_pairs={{0,8},{8,16},{16,24},{24,0},{32,40},{40,48},{48,56},{56,32},{64,72... | collective-permute-start | bytes 49160 | tf_op jit(solution)/shard_map/ppermute | solution.py:191
  107.1 3.3 %collective-permute-start.12 = (f32[128,256]{1,0:T(8,128)S(1)}, f32[128,256]{1,0:T(8,128)S(1)}, u32[]{:S(2)}, u32[]{:S(2)}) collective-permute-start(f32[128,256]{1,0:T(8,128)S(1)} %slice_select_fusion), channel_id=1, source_target_pairs={{0,1},{1,0},{2,3},{3,2},{4,5},{5,4},{6,7},{7,6},{8,9},{9,8},{10,11... | collective-permute-start | bytes 393224 | tf_op jit(solution)/shard_map/ppermute | solution.py:155
  110.5 3.2 %collective-permute-start.13 = (f32[64,256]{1,0:T(8,128)S(1)}, f32[64,256]{1,0:T(8,128)S(1)}, u32[]{:S(2)}, u32[]{:S(2)}) collective-permute-start(f32[64,256]{1,0:T(8,128)S(1)} %slice_select_fusion.1), channel_id=1, source_target_pairs={{0,2},{1,3},{2,0},{3,1},{4,6},{5,7},{6,4},{7,5},{8,10},{9,11},{10,... | collective-permute-start | bytes 196616 | tf_op jit(solution)/shard_map/ppermute | solution.py:155
  113.7 7.5 %collective-permute-start.14 = (f32[32,256]{1,0:T(8,128)S(1)}, f32[32,256]{1,0:T(8,128)S(1)}, u32[]{:S(2)}, u32[]{:S(2)}) collective-permute-start(f32[32,256]{1,0:T(8,128)S(1)} %slice_select_fusion.2), channel_id=1, source_target_pairs={{0,4},{1,5},{2,6},{3,7},{4,0},{5,1},{6,2},{7,3},{8,12},{9,13},{10,... | collective-permute-start | bytes 98312 | tf_op jit(solution)/shard_map/ppermute | solution.py:155
  118.5 42.0 %collective-permute-start.9 = (f32[512,256]{1,0:T(8,128)S(1)}, f32[512,256]{1,0:T(8,128)S(1)}, u32[]{:S(2)}, u32[]{:S(2)}) collective-permute-start(f32[512,256]{1,0:T(8,128)S(1)} %get-tuple-element.16), channel_id=1, source_target_pairs={{0,32},{8,40},{16,48},{24,56},{32,64},{40,72},{48,80},{56,88},{64,... | collective-permute-start | bytes 1572872 | tf_op jit(solution)/shard_map/ppermute | solution.py:191
  118.5 41.9 %collective-permute-start.11 = (f32[512,256]{1,0:T(8,128)S(1)}, f32[512,256]{1,0:T(8,128)S(1)}, u32[]{:S(2)}, u32[]{:S(2)}) collective-permute-start(f32[512,256]{1,0:T(8,128)S(1)} %get-tuple-element.17), channel_id=1, source_target_pairs={{0,96},{8,104},{16,112},{24,120},{32,0},{40,8},{48,16},{56,24},{64... | collective-permute-start | bytes 1572872 | tf_op jit(solution)/shard_map/ppermute | solution.py:191
  121.2 39.3 %collective-permute-start.10 = (f32[512,256]{1,0:T(8,128)S(1)}, f32[512,256]{1,0:T(8,128)S(1)}, u32[]{:S(2)}, u32[]{:S(2)}) collective-permute-start(f32[512,256]{1,0:T(8,128)S(1)} %get-tuple-element.18), channel_id=1, source_target_pairs={{0,64},{8,72},{16,80},{24,88},{32,96},{40,104},{48,112},{56,120},{... | collective-permute-start | bytes 1572872 | tf_op jit(solution)/shard_map/ppermute | solution.py:191
  121.2 3.1 %collective-permute-start.15 = (f32[32,256]{1,0:T(8,128)S(1)}, f32[32,256]{1,0:T(8,128)S(1)}, u32[]{:S(2)}, u32[]{:S(2)}) collective-permute-start(f32[32,256]{1,0:T(8,128)S(1)} %select_add_fusion.2), channel_id=1, source_target_pairs={{0,8},{1,9},{2,10},{3,11},{4,12},{5,13},{6,14},{7,15},{8,0},{9,1},... | collective-permute-start | bytes 98312 | tf_op jit(solution)/shard_map/ppermute | solution.py:159
  124.4 4.3 %collective-permute-start.16 = (f32[32,256]{1,0:T(8,128)S(1)}, f32[32,256]{1,0:T(8,128)S(1)}, u32[]{:S(2)}, u32[]{:S(2)}) collective-permute-start(f32[32,256]{1,0:T(8,128)S(1)} %add.153), channel_id=1, source_target_pairs={{0,16},{1,17},{2,18},{3,19},{4,20},{5,21},{6,22},{7,23},{8,24},{9,... | collective-permute-start | bytes 98312 | tf_op jit(solution)/shard_map/ppermute | solution.py:159
  128.6 13.6 %collective-permute-start.17 = (f32[32,256]{1,0:T(8,128)S(1)}, f32[32,256]{1,0:T(8,128)S(1)}, u32[]{:S(2)}, u32[]{:S(2)}) collective-permute-start(f32[32,256]{1,0:T(8,128)S(1)} %add.154), channel_id=1, source_target_pairs={{0,32},{1,33},{2,34},{3,35},{4,36},{5,37},{6,38},{7,39},{8,40},{9,... | collective-permute-start | bytes 98312 | tf_op jit(solution)/shard_map/ppermute | solution.py:159
  142.3 4.3 %collective-permute-start.18 = (f32[32,256]{1,0:T(8,128)S(1)}, f32[32,256]{1,0:T(8,128)S(1)}, u32[]{:S(2)}, u32[]{:S(2)}) collective-permute-start(f32[32,256]{1,0:T(8,128)S(1)} %add.155), channel_id=1, source_target_pairs={{0,64},{1,65},{2,66},{3,67},{4,68},{5,69},{6,70},{7,71},{8,72},{9,... | collective-permute-start | bytes 98312 | tf_op jit(solution)/shard_map/ppermute | solution.py:159
  146.6 4.3 %collective-permute-start.19 = (f32[32,256]{1,0:T(8,128)S(1)}, f32[32,256]{1,0:T(8,128)S(1)}, u32[]{:S(2)}, u32[]{:S(2)}) collective-permute-start(f32[32,256]{1,0:T(8,128)S(1)} %add.156), channel_id=1, source_target_pairs={{0,4},{1,5},{2,6},{3,7},{4,0},{5,1},{6,2},{7,3},{8,12},{9,13},{10,... | collective-permute-start | bytes 98312 | tf_op jit(solution)/shard_map/ppermute | solution.py:163
  150.8 3.5 %collective-permute-start.20 = (f32[64,256]{1,0:T(8,128)S(1)}, f32[64,256]{1,0:T(8,128)S(1)}, u32[]{:S(2)}, u32[]{:S(2)}) collective-permute-start(f32[64,256]{1,0:T(8,128)S(1)} %maximum_select_fusion.2), channel_id=1, source_target_pairs={{0,2},{1,3},{2,0},{3,1},{4,6},{5,7},{6,4},{7,5},{8,10},{9,11},{10,... | collective-permute-start | bytes 196616 | tf_op jit(solution)/shard_map/ppermute | solution.py:163
  154.3 7.4 %collective-permute-start.21 = (f32[128,256]{1,0:T(8,128)S(1)}, f32[128,256]{1,0:T(8,128)S(1)}, u32[]{:S(2)}, u32[]{:S(2)}) collective-permute-start(f32[128,256]{1,0:T(8,128)S(1)} %maximum_select_fusion.1), channel_id=1, source_target_pairs={{0,1},{1,0},{2,3},{3,2},{4,5},{5,4},{6,7},{7,6},{8,9},{9,8},{10,11... | collective-permute-start | bytes 393224 | tf_op jit(solution)/shard_map/ppermute | solution.py:163
  166.7 24.1 %all-to-all-start.2 = ((f32[128,8,256]{2,1,0:T(8,128)}), f32[128,8,256]{2,1,0:T(8,128)S(1)}, u32[]{:S(2)}, u32[]{:S(2)}) async-start(f32[128,8,256]{2,1,0:T(8,128)} %bitcast.11), calls=%async_computation.2 | async-start | bytes 2097152 | tf_op jit(solution)/shard_map/all_to_all | solution.py:285

commit v13 on v12

--- a/solution.py
+++ b/solution.py
@@ -167,18 +167,6 @@
     return value
 
 
-def butterfly_sum(value, axes):
-    total = 1
-    for axis in axes:
-        total *= lax.axis_size(axis)
-    step = 1
-    while step < total:
-        pairs = [(i, i ^ step) for i in range(total)]
-        value = value + lax.ppermute(value, axes, pairs)
-        step *= 2
-    return value
-
-
 def plane_shift(value, axis, side, step, along_row):
     pairs = []
     for source in range(side * side):
@@ -233,7 +221,7 @@
     return item_grad, scaling * weight_part
 
 
-def local(item_table, query_table, query_weight, query_ids, fetch_rows, counts, example_pos):
+def step_body(item_table, query_table, query_weight, query_ids, fetch_rows, counts, example_pos):
     table_rows, model_width = item_table.shape
     sources = fetch_rows.shape[1]
     slot_cap = fetch_rows.shape[2]
@@ -304,4 +292,4 @@
         P(("batch", "table")),
     )
     out_specs = (P(("batch", "table"), None), P())
-    return jax.shard_map(local, mesh=mesh, in_specs=in_specs, out_specs=out_specs, check_vma=False)
+    return jax.shard_map(step_body, mesh=mesh, in_specs=in_specs, out_specs=out_specs, check_vma=False)

time: 199 us -> 199 us (level)
  no operation moved by 1% of the time
where the time goes in v13:
time: 199 us; the launch traced here: 198 us
  waiting for transfers between devices  67.8 us (34%)
  starting transfers between devices  55 us (28%)
  local copies, waits for them, and re-layouts  32.8 us (16%)
  other arithmetic  22.1 us (11%)
  Pallas kernels  15.2 us (8%)
  matrix products  4.43 us (2%)
    ppermute x4, waiting for transfers between devices, tree_sum(): lax.ppermute(value, axes, [(i, i ^ step) for i in range(total)])  20.9 us
    gather x1, local copies, waits for them, and re-layouts, step_body(): looked = jnp.take(query_table, query_ids, axis=0).astype(jnp.float32)  18.7 us
    all_to_all x1, waiting for transfers between devices, step_body(): lax.all_to_all(slot_grads, ('batch', 'table'), split_axis=0, concat_axis=...  17.6 us
    ppermute x12, waiting for transfers between devices, plane_shift(): return lax.ppermute(value, axis, pairs)  16.4 us
    ppermute x12, starting transfers between devices, plane_shift(): return lax.ppermute(value, axis, pairs)  13.5 us
    all_to_all x1, starting transfers between devices, step_body(): lax.all_to_all(requests, ('batch', 'table'), split_axis=0, concat_axis=0,...  11.5 us
    pallas_call x1, Pallas kernels, block_grads_k(): pl.pallas_call(functools.partial(grads_block, scaling=scaling), grid=(row...  9.35 us
    scatter-add x1, other arithmetic, step_body(): table_grad = jnp.zeros((table_rows, model_width), jnp.float32).at[wanted....  7.51 us
  transfers between devices with their start and end apart: 25, of which 14 were waited for; matrix products, arithmetic and copies ran while one was open for 19% of the time, Pallas kernels for 0%

profile of v13, /device:TPU:1, one launch (start us, length us, event | category | flops | bytes accessed | tf_op | source)
XLA Modules:
  0.0 198.3 jit_solution(3592990750838262033)
XLA Ops:
  0.7 1.5 copy.22
  2.2 11.5 %all-to-all-start = ((s32[128,1,8]{2,1,0:T(1,128)}), s32[128,1,8]{2,1,0:T(1,128)S(1)}, u32[]{:S(2)}, u32[]{:S(2)}) async-start(s32[128,1,8]{2,1,0:T(1,128)} %bitcast), calls=%async_computation | async-start | bytes 131072 | tf_op jit(solution)/shard_map/all_to_all | solution.py:230
  13.7 0.8 copy.23
  14.4 0.2 reduce-window.8
  14.6 0.1 reduce.1
  14.7 0.7 bitcast_subtract_fusion
  15.4 0.9 convert_reduce_fusion.1
  16.3 3.3 %gather_fusion = s32[512]{0:T(512)S(1)} fusion(s32[128]{0:T(128)S(1)} %bitcast_subtract_fusion, s32[1024]{0:T(1024)S(1)} %pad_clamp_fusion.1), kind=kCustom, calls=%fused_computation | custom fusion | bytes 6144 | tf_op jit(solution)/shard_map/jit(_take)/gather | solution.py:139
  19.7 3.3 %all-to-all-done = s32[128,1,8]{2,1,0:T(1,128)S(1)} async-done(((s32[128,1,8]{2,1,0:T(1,128)}), s32[128,1,8]{2,1,0:T(1,128)S(1)}, u32[]{:S(2)}, u32[]{:S(2)}) %all-to-all-start) | async-done | bytes 4128 | tf_op jit(solution)/shard_map/all_to_all | solution.py:230
  23.2 3.9 %gather_fusion.1 = bf16[1024,256]{1,0:T(8,128)(2,1)S(1)} fusion(bf16[2048,256]{1,0:T(8,128)(2,1)S(1)} %copy-done, s32[1024]{0:T(1024)S(1)} %broadcast_clamp_fusion.1), kind=kCustom, calls=%fused_computation.1 | custom fusion | bytes 1052672 | tf_op jit(solution)/shard_map/jit(_take)/gather | solution.py:231
  27.1 1.0 bitcast_select_fusion.1
  28.2 6.5 %all-to-all-start.1 = ((bf16[128,8,256]{2,1,0:T(8,128)(2,1)}), bf16[128,8,256]{2,1,0:T(8,128)(2,1)S(1)}, u32[]{:S(2)}, u32[]{:S(2)}) async-start(bf16[128,8,256]{2,1,0:T(8,128)(2,1)} %bitcast_select_fusion.1), calls=%async_computation.1 | async-start | bytes 1048576 | tf_op jit(solution)/shard_map/all_to_all | solution.py:233
  34.6 0.2 copy.24
  34.8 0.1 copy.25
  34.9 0.2 reshape.165
  35.1 18.7 %gather_fusion.2 = bf16[4096,256]{1,0:T(8,128)(2,1)} fusion(bf16[8192,256]{1,0:T(8,128)(2,1)} %param.8, s32[4096]{0:T(1024)S(1)} %broadcast_clamp_fusion), kind=kCustom, calls=%fused_computation.2 | custom fusion | bytes 4210688 | tf_op jit(solution)/shard_map/jit(_take)/gather | solution.py:238
  53.8 4.1 %convert_reduce_fusion = f32[512,256]{1,0:T(8,128)S(1)} fusion(bf16[4096,256]{1,0:T(8,128)(2,1)} %gather_fusion.2, pred[512,8]{1,0:T(8,128)(4,1)S(1)} %copy.24), kind=kLoop, calls=%fused_computation.6 | loop fusion | flops 3014656 | bytes 2625536 | tf_op jit(solution)/shard_map/reduce_sum | solution.py:239
  57.9 2.6 %collective-permute-start.2 = (bf16[512,256]{1,0:T(8,128)(2,1)S(1)}, bf16[512,256]{1,0:T(8,128)(2,1)}, u32[]{:S(2)}, u32[]{:S(2)}) collective-permute-start(bf16[512,256]{1,0:T(8,128)(2,1)S(1)} %multiply_convert_fusion), channel_id=1, source_target_pairs={{0,24},{8,0},{16,8},{24,16},{32,56},{40,32},{48,40},{56,48},{64,88... | collective-permute-start | bytes 786440 | tf_op jit(solution)/shard_map/ppermute | solution.py:179
  60.5 0.6 collective-permute-start.1
  61.1 0.6 collective-permute-start
  61.7 2.0 gather_fusion.3
  63.7 0.1 broadcast_select_fusion
  63.8 2.6 %collective-permute-start.5 = (bf16[512,256]{1,0:T(8,128)(2,1)S(1)}, bf16[512,256]{1,0:T(8,128)(2,1)S(1)}, u32[]{:S(2)}, u32[]{:S(2)}) collective-permute-start(bf16[512,256]{1,0:T(8,128)(2,1)S(1)} %broadcast_select_fusion), channel_id=1, source_target_pairs={{0,96},{8,104},{16,112},{24,120},{32,0},{40,8},{48,16},{56,24},{64... | collective-permute-start | bytes 786440 | tf_op jit(solution)/shard_map/ppermute | solution.py:179
  66.4 0.5 collective-permute-start.4
  66.9 4.4 %collective-permute-done.2 = bf16[512,256]{1,0:T(8,128)(2,1)} collective-permute-done((bf16[512,256]{1,0:T(8,128)(2,1)S(1)}, bf16[512,256]{1,0:T(8,128)(2,1)}, u32[]{:S(2)}, u32[]{:S(2)}) %collective-permute-start.2) | collective-permute-done | bytes 262176 | tf_op jit(solution)/shard_map/ppermute | solution.py:179
  71.3 4.7 %collective-permute-done = bf16[512,256]{1,0:T(8,128)(2,1)} collective-permute-done((bf16[512,256]{1,0:T(8,128)(2,1)S(1)}, bf16[512,256]{1,0:T(8,128)(2,1)}, u32[]{:S(2)}, u32[]{:S(2)}) %collective-permute-start) | collective-permute-done | bytes 262176 | tf_op jit(solution)/shard_map/ppermute | solution.py:179
  76.0 1.6 convolution_convert_fusion.q_ref
  77.6 3.8 %collective-permute-done.3 = bf16[512,256]{1,0:T(8,128)(2,1)S(1)} collective-permute-done((bf16[512,256]{1,0:T(8,128)(2,1)S(1)}, bf16[512,256]{1,0:T(8,128)(2,1)S(1)}, u32[]{:S(2)}, u32[]{:S(2)}) %collective-permute-start.3) | collective-permute-done | bytes 262176 | tf_op jit(solution)/shard_map/ppermute | solution.py:179
  81.5 5.9 %shard_map.86 = f32[2,2048]{1,0:T(2,128)S(1)} custom-call(bf16[2048,256]{1,0:T(8,128)(2,1)S(1)} %convolution_convert_fusion.q_ref, bf16[2048,256]{1,0:T(8,128)(2,1)S(1)} %pad_maximum_fusion.1.items_ref), custom_call_target="tpu_custom_call" | custom-call | tf_op jit(solution)/shard_map/pallas_call | solution.py:58
  87.3 1.6 collective-permute-start.8
  89.0 2.2 %collective-permute-start.7 = (f32[2,2048]{1,0:T(2,128)S(1)}, f32[2,2048]{1,0:T(2,128)S(1)}, u32[]{:S(2)}, u32[]{:S(2)}) collective-permute-start(f32[2,2048]{1,0:T(2,128)S(1)} %shard_map.86), channel_id=1, source_target_pairs={{0,16},{8,24},{16,0},{24,8},{32,48},{40,56},{48,32},{56,40},{64,80... | collective-permute-start | bytes 49160 | tf_op jit(solution)/shard_map/ppermute | solution.py:179
  91.2 0.3 fusion.19
  91.5 3.5 %collective-permute-done.6 = f32[2,2048]{1,0:T(2,128)S(1)} collective-permute-done((f32[2,2048]{1,0:T(2,128)S(1)}, f32[2,2048]{1,0:T(2,128)S(1)}, u32[]{:S(2)}, u32[]{:S(2)}) %collective-permute-start.6) | collective-permute-done | bytes 16416 | tf_op jit(solution)/shard_map/ppermute | solution.py:179
  95.1 0.1 log_add_fusion.totals_ref
  95.1 9.4 %shard_map.87 = (f32[2048,256]{1,0:T(8,128)S(1)}, f32[2048,256]{1,0:T(8,128)}) custom-call(bf16[2048,256]{1,0:T(8,128)(2,1)S(1)} %convolution_convert_fusion.q_ref, bf16[2048,256]{1,0:T(8,128)(2,1)S(1)} %pad_maximum_fusion.1.items_ref, f32[1,2048]{1,0:T(1,128)S(1)} %log_add_fusion.totals_ref), custom_call_target="tpu_custom_call" | custom-call | tf_op jit(solution)/shard_map/pallas_call | solution.py:90
  104.5 2.6 %fusion = f32[256,256]{1,0:T(8,128)S(1)} fusion(f32[256,256]{1,0:T(8,128)S(1)} %fusion.19, f32[2048,256]{1,0:T(8,128)S(1)} %get-tuple-element.11, bf16[512,256]{1,0:T(8,128)(2,1)} %collective-permute-done.2, bf16[512,256]{1,0:T(8,128)(2,1)} %collective-permute-done.1, bf16[512,256]{1,0:T(8,128)(2,1)} %collective-permute-done, ...), kind=kOutput, calls=%fused_computation.10 | convolution fusion | flops 1614938112 | bytes 3670016 | tf_op jit(solution)/shard_map/dot_general | solution.py:213
  107.1 2.3 %collective-permute-start.12 = (f32[128,256]{1,0:T(8,128)S(1)}, f32[128,256]{1,0:T(8,128)S(1)}, u32[]{:S(2)}, u32[]{:S(2)}) collective-permute-start(f32[128,256]{1,0:T(8,128)S(1)} %slice_select_fusion), channel_id=1, source_target_pairs={{0,1},{1,0},{2,3},{3,2},{4,5},{5,4},{6,7},{7,6},{8,9},{9,8},{10,11... | collective-permute-start | bytes 393224 | tf_op jit(solution)/shard_map/ppermute | solution.py:155
  109.4 1.0 collective-permute-done.12
  110.5 1.5 collective-permute-start.13
  112.0 1.7 collective-permute-done.13
  113.7 3.3 %collective-permute-start.14 = (f32[32,256]{1,0:T(8,128)S(1)}, f32[32,256]{1,0:T(8,128)S(1)}, u32[]{:S(2)}, u32[]{:S(2)}) collective-permute-start(f32[32,256]{1,0:T(8,128)S(1)} %slice_select_fusion.2), channel_id=1, source_target_pairs={{0,4},{1,5},{2,6},{3,7},{4,0},{5,1},{6,2},{7,3},{8,12},{9,13},{10,... | collective-permute-start | bytes 98312 | tf_op jit(solution)/shard_map/ppermute | solution.py:155
  117.0 1.5 fusion.17
  118.5 2.7 %collective-permute-start.11 = (f32[512,256]{1,0:T(8,128)S(1)}, f32[512,256]{1,0:T(8,128)S(1)}, u32[]{:S(2)}, u32[]{:S(2)}) collective-permute-start(f32[512,256]{1,0:T(8,128)S(1)} %get-tuple-element.17), channel_id=1, source_target_pairs={{0,96},{8,104},{16,112},{24,120},{32,0},{40,8},{48,16},{56,24},{64... | collective-permute-start | bytes 1572872 | tf_op jit(solution)/shard_map/ppermute | solution.py:179
  121.3 3.0 %collective-permute-done.15 = f32[32,256]{1,0:T(8,128)S(1)} collective-permute-done((f32[32,256]{1,0:T(8,128)S(1)}, f32[32,256]{1,0:T(8,128)S(1)}, u32[]{:S(2)}, u32[]{:S(2)}) %collective-permute-start.15) | collective-permute-done | bytes 32800 | tf_op jit(solution)/shard_map/ppermute | solution.py:159
  124.4 1.4 collective-permute-start.16
  125.8 2.8 %collective-permute-done.16 = f32[32,256]{1,0:T(8,128)S(1)} collective-permute-done((f32[32,256]{1,0:T(8,128)S(1)}, f32[32,256]{1,0:T(8,128)S(1)}, u32[]{:S(2)}, u32[]{:S(2)}) %collective-permute-start.16) | collective-permute-done | bytes 32800 | tf_op jit(solution)/shard_map/ppermute | solution.py:159
  128.6 0.6 collective-permute-start.17
  129.2 13.1 %collective-permute-done.17 = f32[32,256]{1,0:T(8,128)S(1)} collective-permute-done((f32[32,256]{1,0:T(8,128)S(1)}, f32[32,256]{1,0:T(8,128)S(1)}, u32[]{:S(2)}, u32[]{:S(2)}) %collective-permute-start.17) | collective-permute-done | bytes 32800 | tf_op jit(solution)/shard_map/ppermute | solution.py:159
  142.3 2.3 %collective-permute-start.18 = (f32[32,256]{1,0:T(8,128)S(1)}, f32[32,256]{1,0:T(8,128)S(1)}, u32[]{:S(2)}, u32[]{:S(2)}) collective-permute-start(f32[32,256]{1,0:T(8,128)S(1)} %add.155), channel_id=1, source_target_pairs={{0,64},{1,65},{2,66},{3,67},{4,68},{5,69},{6,70},{7,71},{8,72},{9,... | collective-permute-start | bytes 98312 | tf_op jit(solution)/shard_map/ppermute | solution.py:159
  144.6 2.0 %collective-permute-done.18 = f32[32,256]{1,0:T(8,128)S(1)} collective-permute-done((f32[32,256]{1,0:T(8,128)S(1)}, f32[32,256]{1,0:T(8,128)S(1)}, u32[]{:S(2)}, u32[]{:S(2)}) %collective-permute-start.18) | collective-permute-done | bytes 32800 | tf_op jit(solution)/shard_map/ppermute | solution.py:159
  146.6 0.3 collective-permute-start.19
  146.9 4.0 %collective-permute-done.19 = f32[32,256]{1,0:T(8,128)S(1)} collective-permute-done((f32[32,256]{1,0:T(8,128)S(1)}, f32[32,256]{1,0:T(8,128)S(1)}, u32[]{:S(2)}, u32[]{:S(2)}) %collective-permute-start.19) | collective-permute-done | bytes 32800 | tf_op jit(solution)/shard_map/ppermute | solution.py:163
  150.8 0.6 collective-permute-start.20
  151.5 2.9 %collective-permute-done.20 = f32[64,256]{1,0:T(8,128)S(1)} collective-permute-done((f32[64,256]{1,0:T(8,128)S(1)}, f32[64,256]{1,0:T(8,128)S(1)}, u32[]{:S(2)}, u32[]{:S(2)}) %collective-permute-start.20) | collective-permute-done | bytes 65568 | tf_op jit(solution)/shard_map/ppermute | solution.py:163
  154.3 6.1 %collective-permute-start.21 = (f32[128,256]{1,0:T(8,128)S(1)}, f32[128,256]{1,0:T(8,128)S(1)}, u32[]{:S(2)}, u32[]{:S(2)}) collective-permute-start(f32[128,256]{1,0:T(8,128)S(1)} %maximum_select_fusion.1), channel_id=1, source_target_pairs={{0,1},{1,0},{2,3},{3,2},{4,5},{5,4},{6,7},{7,6},{8,9},{9,8},{10,11... | collective-permute-start | bytes 393224 | tf_op jit(solution)/shard_map/ppermute | solution.py:163
  160.5 1.2 subtract_multiply_fusion
  161.7 0.7 maximum_select_fusion
  162.4 4.3 %scatter_custom_fusion = f32[1024,256]{1,0:T(8,128)} fusion(s32[512]{0:T(512)S(1)} %get-tuple-element.15, f32[512,256]{1,0:T(8,128)S(1)} %subtract_multiply_fusion, f32[]{:T(128)} %constant.43.clone.1), kind=kCustom, calls=%fused_computation.19 | custom fusion | flops 131072 | bytes 1048580 | tf_op jit(solution)/shard_map/scatter-add | solution.py:271
  166.7 5.0 %all-to-all-start.2 = ((f32[128,8,256]{2,1,0:T(8,128)}), f32[128,8,256]{2,1,0:T(8,128)S(1)}, u32[]{:S(2)}, u32[]{:S(2)}) async-start(f32[128,8,256]{2,1,0:T(8,128)} %bitcast.11), calls=%async_computation.2 | async-start | bytes 2097152 | tf_op jit(solution)/shard_map/all_to_all | solution.py:273
  171.8 0.5 broadcast.90
  172.3 0.8 reduce.4
  173.1 0.1 reshape.140
  173.2 17.6 %all-to-all-done.2 = f32[128,8,256]{2,1,0:T(8,128)S(1)} async-done(((f32[128,8,256]{2,1,0:T(8,128)}), f32[128,8,256]{2,1,0:T(8,128)S(1)}, u32[]{:S(2)}, u32[]{:S(2)}) %all-to-all-start.2) | async-done | bytes 1048608 | tf_op jit(solution)/shard_map/all_to_all | solution.py:273
  190.8 7.5 %scatter_custom_fusion.1 = f32[2048,256]{1,0:T(8,128)} fusion(s32[1024]{0:T(1024)S(1)} %bitcast.31, f32[128,8,256]{2,1,0:T(8,128)S(1)} %all-to-all-done.2, f32[]{:T(128)} %constant.43.clone.1), kind=kCustom, calls=%fused_computation.13 | custom fusion | flops 262144 | bytes 3145732 | tf_op jit(solution)/shard_map/scatter-add | solution.py:279
  (54 shorter events, 0.7 us)
Async XLA Ops:
  0.6 22.5 %copy-start = (bf16[2048,256]{1,0:T(8,128)(2,1)S(1)}, bf16[2048,256]{1,0:T(8,128)(2,1)}, u32[]{:S(2)}) copy-start(bf16[2048,256]{1,0:T(8,128)(2,1)} %param.7) | copy-start | bytes 3145732
  0.6 19.0 %copy-start.2 = (s32[512]{0:T(512)S(1)}, s32[512]{0:T(512)}, u32[]{:S(2)}) copy-start(s32[512]{0:T(512)} %param.13) | copy-start | bytes 6148
  2.2 20.9 %all-to-all-start = ((s32[128,1,8]{2,1,0:T(1,128)}), s32[128,1,8]{2,1,0:T(1,128)S(1)}, u32[]{:S(2)}, u32[]{:S(2)}) async-start(s32[128,1,8]{2,1,0:T(1,128)} %bitcast), calls=%async_computation | async-start | bytes 131072 | tf_op jit(solution)/shard_map/all_to_all | solution.py:230
  23.2 5.0 %copy-start.1 = (s32[512,8]{0,1:T(8,128)S(1)}, s32[512,8]{0,1:T(8,128)}, u32[]{:S(2)}) copy-start(s32[512,8]{0,1:T(8,128)} %param.10) | copy-start | bytes 49156
  28.2 33.5 %all-to-all-start.1 = ((bf16[128,8,256]{2,1,0:T(8,128)(2,1)}), bf16[128,8,256]{2,1,0:T(8,128)(2,1)S(1)}, u32[]{:S(2)}, u32[]{:S(2)}) async-start(bf16[128,8,256]{2,1,0:T(8,128)(2,1)} %bitcast_select_fusion.1), calls=%async_computation.1 | async-start | bytes 1048576 | tf_op jit(solution)/shard_map/all_to_all | solution.py:233
  57.9 13.4 %collective-permute-start.2 = (bf16[512,256]{1,0:T(8,128)(2,1)S(1)}, bf16[512,256]{1,0:T(8,128)(2,1)}, u32[]{:S(2)}, u32[]{:S(2)}) collective-permute-start(bf16[512,256]{1,0:T(8,128)(2,1)S(1)} %multiply_convert_fusion), channel_id=1, source_target_pairs={{0,24},{8,0},{16,8},{24,16},{32,56},{40,32},{48,40},{56,48},{64,88... | collective-permute-start | bytes 786440 | tf_op jit(solution)/shard_map/ppermute | solution.py:179
  60.5 10.8 %collective-permute-start.1 = (bf16[512,256]{1,0:T(8,128)(2,1)S(1)}, bf16[512,256]{1,0:T(8,128)(2,1)}, u32[]{:S(2)}, u32[]{:S(2)}) collective-permute-start(bf16[512,256]{1,0:T(8,128)(2,1)S(1)} %multiply_convert_fusion), channel_id=1, source_target_pairs={{0,16},{8,24},{16,0},{24,8},{32,48},{40,56},{48,32},{56,40},{64,80... | collective-permute-start | bytes 786440 | tf_op jit(solution)/shard_map/ppermute | solution.py:179
  61.1 14.9 %collective-permute-start = (bf16[512,256]{1,0:T(8,128)(2,1)S(1)}, bf16[512,256]{1,0:T(8,128)(2,1)}, u32[]{:S(2)}, u32[]{:S(2)}) collective-permute-start(bf16[512,256]{1,0:T(8,128)(2,1)S(1)} %multiply_convert_fusion), channel_id=1, source_target_pairs={{0,8},{8,16},{16,24},{24,0},{32,40},{40,48},{48,56},{56,32},{64,72... | collective-permute-start | bytes 786440 | tf_op jit(solution)/shard_map/ppermute | solution.py:179
  63.8 13.8 %collective-permute-start.5 = (bf16[512,256]{1,0:T(8,128)(2,1)S(1)}, bf16[512,256]{1,0:T(8,128)(2,1)S(1)}, u32[]{:S(2)}, u32[]{:S(2)}) collective-permute-start(bf16[512,256]{1,0:T(8,128)(2,1)S(1)} %broadcast_select_fusion), channel_id=1, source_target_pairs={{0,96},{8,104},{16,112},{24,120},{32,0},{40,8},{48,16},{56,24},{64... | collective-permute-start | bytes 786440 | tf_op jit(solution)/shard_map/ppermute | solution.py:179
  66.4 11.2 %collective-permute-start.4 = (bf16[512,256]{1,0:T(8,128)(2,1)S(1)}, bf16[512,256]{1,0:T(8,128)(2,1)S(1)}, u32[]{:S(2)}, u32[]{:S(2)}) collective-permute-start(bf16[512,256]{1,0:T(8,128)(2,1)S(1)} %broadcast_select_fusion), channel_id=1, source_target_pairs={{0,64},{8,72},{16,80},{24,88},{32,96},{40,104},{48,112},{56,120},{... | collective-permute-start | bytes 786440 | tf_op jit(solution)/shard_map/ppermute | solution.py:179
  71.3 10.1 %collective-permute-start.3 = (bf16[512,256]{1,0:T(8,128)(2,1)S(1)}, bf16[512,256]{1,0:T(8,128)(2,1)S(1)}, u32[]{:S(2)}, u32[]{:S(2)}) collective-permute-start(bf16[512,256]{1,0:T(8,128)(2,1)S(1)} %broadcast_select_fusion), channel_id=1, source_target_pairs={{0,32},{8,40},{16,48},{24,56},{32,64},{40,72},{48,80},{56,88},{64,... | collective-permute-start | bytes 786440 | tf_op jit(solution)/shard_map/ppermute | solution.py:179
  87.3 4.2 %collective-permute-start.8 = (f32[2,2048]{1,0:T(2,128)S(1)}, f32[2,2048]{1,0:T(2,128)S(1)}, u32[]{:S(2)}, u32[]{:S(2)}) collective-permute-start(f32[2,2048]{1,0:T(2,128)S(1)} %shard_map.86), channel_id=1, source_target_pairs={{0,24},{8,0},{16,8},{24,16},{32,56},{40,32},{48,40},{56,48},{64,88... | collective-permute-start | bytes 49160 | tf_op jit(solution)/shard_map/ppermute | solution.py:179
  89.0 6.1 %collective-permute-start.7 = (f32[2,2048]{1,0:T(2,128)S(1)}, f32[2,2048]{1,0:T(2,128)S(1)}, u32[]{:S(2)}, u32[]{:S(2)}) collective-permute-start(f32[2,2048]{1,0:T(2,128)S(1)} %shard_map.86), channel_id=1, source_target_pairs={{0,16},{8,24},{16,0},{24,8},{32,48},{40,56},{48,32},{56,40},{64,80... | collective-permute-start | bytes 49160 | tf_op jit(solution)/shard_map/ppermute | solution.py:179
  91.2 3.8 %collective-permute-start.6 = (f32[2,2048]{1,0:T(2,128)S(1)}, f32[2,2048]{1,0:T(2,128)S(1)}, u32[]{:S(2)}, u32[]{:S(2)}) collective-permute-start(f32[2,2048]{1,0:T(2,128)S(1)} %shard_map.86), channel_id=1, source_target_pairs={{0,8},{8,16},{16,24},{24,0},{32,40},{40,48},{48,56},{56,32},{64,72... | collective-permute-start | bytes 49160 | tf_op jit(solution)/shard_map/ppermute | solution.py:179
  107.1 3.3 %collective-permute-start.12 = (f32[128,256]{1,0:T(8,128)S(1)}, f32[128,256]{1,0:T(8,128)S(1)}, u32[]{:S(2)}, u32[]{:S(2)}) collective-permute-start(f32[128,256]{1,0:T(8,128)S(1)} %slice_select_fusion), channel_id=1, source_target_pairs={{0,1},{1,0},{2,3},{3,2},{4,5},{5,4},{6,7},{7,6},{8,9},{9,8},{10,11... | collective-permute-start | bytes 393224 | tf_op jit(solution)/shard_map/ppermute | solution.py:155
  110.5 3.2 %collective-permute-start.13 = (f32[64,256]{1,0:T(8,128)S(1)}, f32[64,256]{1,0:T(8,128)S(1)}, u32[]{:S(2)}, u32[]{:S(2)}) collective-permute-start(f32[64,256]{1,0:T(8,128)S(1)} %slice_select_fusion.1), channel_id=1, source_target_pairs={{0,2},{1,3},{2,0},{3,1},{4,6},{5,7},{6,4},{7,5},{8,10},{9,11},{10,... | collective-permute-start | bytes 196616 | tf_op jit(solution)/shard_map/ppermute | solution.py:155
  113.7 7.5 %collective-permute-start.14 = (f32[32,256]{1,0:T(8,128)S(1)}, f32[32,256]{1,0:T(8,128)S(1)}, u32[]{:S(2)}, u32[]{:S(2)}) collective-permute-start(f32[32,256]{1,0:T(8,128)S(1)} %slice_select_fusion.2), channel_id=1, source_target_pairs={{0,4},{1,5},{2,6},{3,7},{4,0},{5,1},{6,2},{7,3},{8,12},{9,13},{10,... | collective-permute-start | bytes 98312 | tf_op jit(solution)/shard_map/ppermute | solution.py:155
  118.5 42.0 %collective-permute-start.9 = (f32[512,256]{1,0:T(8,128)S(1)}, f32[512,256]{1,0:T(8,128)S(1)}, u32[]{:S(2)}, u32[]{:S(2)}) collective-permute-start(f32[512,256]{1,0:T(8,128)S(1)} %get-tuple-element.16), channel_id=1, source_target_pairs={{0,32},{8,40},{16,48},{24,56},{32,64},{40,72},{48,80},{56,88},{64,... | collective-permute-start | bytes 1572872 | tf_op jit(solution)/shard_map/ppermute | solution.py:179
  118.5 41.9 %collective-permute-start.11 = (f32[512,256]{1,0:T(8,128)S(1)}, f32[512,256]{1,0:T(8,128)S(1)}, u32[]{:S(2)}, u32[]{:S(2)}) collective-permute-start(f32[512,256]{1,0:T(8,128)S(1)} %get-tuple-element.17), channel_id=1, source_target_pairs={{0,96},{8,104},{16,112},{24,120},{32,0},{40,8},{48,16},{56,24},{64... | collective-permute-start | bytes 1572872 | tf_op jit(solution)/shard_map/ppermute | solution.py:179
  121.2 39.3 %collective-permute-start.10 = (f32[512,256]{1,0:T(8,128)S(1)}, f32[512,256]{1,0:T(8,128)S(1)}, u32[]{:S(2)}, u32[]{:S(2)}) collective-permute-start(f32[512,256]{1,0:T(8,128)S(1)} %get-tuple-element.18), channel_id=1, source_target_pairs={{0,64},{8,72},{16,80},{24,88},{32,96},{40,104},{48,112},{56,120},{... | collective-permute-start | bytes 1572872 | tf_op jit(solution)/shard_map/ppermute | solution.py:179
  121.2 3.1 %collective-permute-start.15 = (f32[32,256]{1,0:T(8,128)S(1)}, f32[32,256]{1,0:T(8,128)S(1)}, u32[]{:S(2)}, u32[]{:S(2)}) collective-permute-start(f32[32,256]{1,0:T(8,128)S(1)} %select_add_fusion.2), channel_id=1, source_target_pairs={{0,8},{1,9},{2,10},{3,11},{4,12},{5,13},{6,14},{7,15},{8,0},{9,1},... | collective-permute-start | bytes 98312 | tf_op jit(solution)/shard_map/ppermute | solution.py:159
  124.4 4.3 %collective-permute-start.16 = (f32[32,256]{1,0:T(8,128)S(1)}, f32[32,256]{1,0:T(8,128)S(1)}, u32[]{:S(2)}, u32[]{:S(2)}) collective-permute-start(f32[32,256]{1,0:T(8,128)S(1)} %add.153), channel_id=1, source_target_pairs={{0,16},{1,17},{2,18},{3,19},{4,20},{5,21},{6,22},{7,23},{8,24},{9,... | collective-permute-start | bytes 98312 | tf_op jit(solution)/shard_map/ppermute | solution.py:159
  128.6 13.6 %collective-permute-start.17 = (f32[32,256]{1,0:T(8,128)S(1)}, f32[32,256]{1,0:T(8,128)S(1)}, u32[]{:S(2)}, u32[]{:S(2)}) collective-permute-start(f32[32,256]{1,0:T(8,128)S(1)} %add.154), channel_id=1, source_target_pairs={{0,32},{1,33},{2,34},{3,35},{4,36},{5,37},{6,38},{7,39},{8,40},{9,... | collective-permute-start | bytes 98312 | tf_op jit(solution)/shard_map/ppermute | solution.py:159
  142.3 4.3 %collective-permute-start.18 = (f32[32,256]{1,0:T(8,128)S(1)}, f32[32,256]{1,0:T(8,128)S(1)}, u32[]{:S(2)}, u32[]{:S(2)}) collective-permute-start(f32[32,256]{1,0:T(8,128)S(1)} %add.155), channel_id=1, source_target_pairs={{0,64},{1,65},{2,66},{3,67},{4,68},{5,69},{6,70},{7,71},{8,72},{9,... | collective-permute-start | bytes 98312 | tf_op jit(solution)/shard_map/ppermute | solution.py:159
  146.6 4.3 %collective-permute-start.19 = (f32[32,256]{1,0:T(8,128)S(1)}, f32[32,256]{1,0:T(8,128)S(1)}, u32[]{:S(2)}, u32[]{:S(2)}) collective-permute-start(f32[32,256]{1,0:T(8,128)S(1)} %add.156), channel_id=1, source_target_pairs={{0,4},{1,5},{2,6},{3,7},{4,0},{5,1},{6,2},{7,3},{8,12},{9,13},{10,... | collective-permute-start | bytes 98312 | tf_op jit(solution)/shard_map/ppermute | solution.py:163
  150.8 3.5 %collective-permute-start.20 = (f32[64,256]{1,0:T(8,128)S(1)}, f32[64,256]{1,0:T(8,128)S(1)}, u32[]{:S(2)}, u32[]{:S(2)}) collective-permute-start(f32[64,256]{1,0:T(8,128)S(1)} %maximum_select_fusion.2), channel_id=1, source_target_pairs={{0,2},{1,3},{2,0},{3,1},{4,6},{5,7},{6,4},{7,5},{8,10},{9,11},{10,... | collective-permute-start | bytes 196616 | tf_op jit(solution)/shard_map/ppermute | solution.py:163
  154.3 7.4 %collective-permute-start.21 = (f32[128,256]{1,0:T(8,128)S(1)}, f32[128,256]{1,0:T(8,128)S(1)}, u32[]{:S(2)}, u32[]{:S(2)}) collective-permute-start(f32[128,256]{1,0:T(8,128)S(1)} %maximum_select_fusion.1), channel_id=1, source_target_pairs={{0,1},{1,0},{2,3},{3,2},{4,5},{5,4},{6,7},{7,6},{8,9},{9,8},{10,11... | collective-permute-start | bytes 393224 | tf_op jit(solution)/shard_map/ppermute | solution.py:163
  166.7 24.1 %all-to-all-start.2 = ((f32[128,8,256]{2,1,0:T(8,128)}), f32[128,8,256]{2,1,0:T(8,128)S(1)}, u32[]{:S(2)}, u32[]{:S(2)}) async-start(f32[128,8,256]{2,1,0:T(8,128)} %bitcast.11), calls=%async_computation.2 | async-start | bytes 2097152 | tf_op jit(solution)/shard_map/all_to_all | solution.py:273

commit v14 on v13

--- a/solution.py
+++ b/solution.py
@@ -268,7 +268,11 @@
     else:
         weight_grad = lax.psum(partial_value, ("batch", "table"))
     item_grad, weight_grad = lax.optimization_barrier((item_grad, weight_grad))
-    slot_grads = jax.ops.segment_sum(item_grad, slot_ids, num_segments=sources * slot_cap)
+    chosen = (lax.broadcasted_iota(jnp.int32, (sources * slot_cap, slot_ids.shape[0]), 0) == slot_ids[None, :])
+    slot_grads = jnp.dot(
+        chosen.astype(jnp.bfloat16), item_grad,
+        preferred_element_type=jnp.float32, precision=lax.Precision.HIGHEST,
+    )
     slot_grads = slot_grads.reshape(sources, slot_cap, model_width)
     returned = lax.all_to_all(
         slot_grads, ("batch", "table"), split_axis=0, concat_axis=0, tiled=True

time: 199 us -> 196 us (0.985)
  other arithmetic: 22.1 us -> 17.7 us
  matrix products: 4.43 us -> 6.5 us
    scatter-add x1 -> x0, other arithmetic: 4.29 us -> none  [step_body(): jax.ops.segment_sum(item_grad, slot_ids, num_segments=sources * slot_cap)]
    dot_general x0 -> x1, matrix products: none -> 2.07 us  [step_body(): jnp.dot(chosen.astype(jnp.bfloat16), item_grad, preferred_element_type=jn...]
where the time goes in v14:
time: 196 us
  waiting for transfers between devices  67.9 us (35%)
  starting transfers between devices  54.7 us (28%)
  local copies, waits for them, and re-layouts  32.8 us (17%)
  other arithmetic  17.7 us (9%)
  Pallas kernels  15.2 us (8%)
  matrix products  6.5 us (3%)
    ppermute x4, waiting for transfers between devices, tree_sum(): lax.ppermute(value, axes, [(i, i ^ step) for i in range(total)])  20.9 us
    gather x1, local copies, waits for them, and re-layouts, step_body(): looked = jnp.take(query_table, query_ids, axis=0).astype(jnp.float32)  18.7 us
    all_to_all x1, waiting for transfers between devices, step_body(): lax.all_to_all(slot_grads, ('batch', 'table'), split_axis=0, concat_axis=...  17.7 us
    ppermute x12, waiting for transfers between devices, plane_shift(): return lax.ppermute(value, axis, pairs)  16.4 us
    ppermute x12, starting transfers between devices, plane_shift(): return lax.ppermute(value, axis, pairs)  13.5 us
    all_to_all x1, starting transfers between devices, step_body(): lax.all_to_all(requests, ('batch', 'table'), split_axis=0, concat_axis=0,...  11.5 us
    pallas_call x1, Pallas kernels, block_grads_k(): pl.pallas_call(functools.partial(grads_block, scaling=scaling), grid=(row...  9.35 us
    scatter-add x1, other arithmetic, step_body(): table_grad = jnp.zeros((table_rows, model_width), jnp.float32).at[wanted....  7.51 us
  transfers between devices with their start and end apart: 25, of which 14 were waited for; matrix products, arithmetic and copies ran while one was open for 19% of the time, Pallas kernels for 0%

profile of v14, /device:TPU:1, one launch (start us, length us, event | category | flops | bytes accessed | tf_op | source)
XLA Modules:
  0.0 195.9 jit_solution(13814832604428832048)
XLA Ops:
  0.7 1.5 copy.22
  2.2 11.5 %all-to-all-start = ((s32[128,1,8]{2,1,0:T(1,128)}), s32[128,1,8]{2,1,0:T(1,128)S(1)}, u32[]{:S(2)}, u32[]{:S(2)}) async-start(s32[128,1,8]{2,1,0:T(1,128)} %bitcast), calls=%async_computation | async-start | bytes 131072 | tf_op jit(solution)/shard_map/all_to_all | solution.py:230
  13.7 0.8 copy.23
  14.4 0.2 reduce-window.8
  14.6 0.1 reduce.1
  14.7 0.7 bitcast_subtract_fusion
  15.4 0.9 convert_reduce_fusion.1
  16.3 3.3 %gather_fusion = s32[512]{0:T(512)S(1)} fusion(s32[128]{0:T(128)S(1)} %bitcast_subtract_fusion, s32[1024]{0:T(1024)S(1)} %pad_clamp_fusion.1), kind=kCustom, calls=%fused_computation | custom fusion | bytes 6144 | tf_op jit(solution)/shard_map/jit(_take)/gather | solution.py:139
  19.7 3.3 %all-to-all-done = s32[128,1,8]{2,1,0:T(1,128)S(1)} async-done(((s32[128,1,8]{2,1,0:T(1,128)}), s32[128,1,8]{2,1,0:T(1,128)S(1)}, u32[]{:S(2)}, u32[]{:S(2)}) %all-to-all-start) | async-done | bytes 4128 | tf_op jit(solution)/shard_map/all_to_all | solution.py:230
  23.2 3.9 %gather_fusion.1 = bf16[1024,256]{1,0:T(8,128)(2,1)S(1)} fusion(bf16[2048,256]{1,0:T(8,128)(2,1)S(1)} %copy-done, s32[1024]{0:T(1024)S(1)} %broadcast_clamp_fusion.1), kind=kCustom, calls=%fused_computation.1 | custom fusion | bytes 1052672 | tf_op jit(solution)/shard_map/jit(_take)/gather | solution.py:231
  27.1 1.0 bitcast_select_fusion.1
  28.2 6.5 %all-to-all-start.1 = ((bf16[128,8,256]{2,1,0:T(8,128)(2,1)}), bf16[128,8,256]{2,1,0:T(8,128)(2,1)S(1)}, u32[]{:S(2)}, u32[]{:S(2)}) async-start(bf16[128,8,256]{2,1,0:T(8,128)(2,1)} %bitcast_select_fusion.1), calls=%async_computation.1 | async-start | bytes 1048576 | tf_op jit(solution)/shard_map/all_to_all | solution.py:233
  34.6 0.2 copy.24
  34.8 0.1 copy.25
  34.9 0.2 reshape.166
  35.1 18.7 %gather_fusion.2 = bf16[4096,256]{1,0:T(8,128)(2,1)} fusion(bf16[8192,256]{1,0:T(8,128)(2,1)} %param.8, s32[4096]{0:T(1024)S(1)} %broadcast_clamp_fusion), kind=kCustom, calls=%fused_computation.2 | custom fusion | bytes 4210688 | tf_op jit(solution)/shard_map/jit(_take)/gather | solution.py:238
  53.8 4.1 %convert_reduce_fusion = f32[512,256]{1,0:T(8,128)S(1)} fusion(bf16[4096,256]{1,0:T(8,128)(2,1)} %gather_fusion.2, pred[512,8]{1,0:T(8,128)(4,1)S(1)} %copy.24), kind=kLoop, calls=%fused_computation.5 | loop fusion | flops 3014656 | bytes 2625536 | tf_op jit(solution)/shard_map/reduce_sum | solution.py:239
  57.9 2.6 %collective-permute-start.2 = (bf16[512,256]{1,0:T(8,128)(2,1)S(1)}, bf16[512,256]{1,0:T(8,128)(2,1)}, u32[]{:S(2)}, u32[]{:S(2)}) collective-permute-start(bf16[512,256]{1,0:T(8,128)(2,1)S(1)} %multiply_convert_fusion), channel_id=1, source_target_pairs={{0,24},{8,0},{16,8},{24,16},{32,56},{40,32},{48,40},{56,48},{64,88... | collective-permute-start | bytes 786440 | tf_op jit(solution)/shard_map/ppermute | solution.py:179
  60.5 0.6 collective-permute-start.1
  61.1 0.6 collective-permute-start
  61.7 2.0 gather_fusion.3
  63.7 0.1 broadcast_select_fusion
  63.8 2.6 %collective-permute-start.5 = (bf16[512,256]{1,0:T(8,128)(2,1)S(1)}, bf16[512,256]{1,0:T(8,128)(2,1)S(1)}, u32[]{:S(2)}, u32[]{:S(2)}) collective-permute-start(bf16[512,256]{1,0:T(8,128)(2,1)S(1)} %broadcast_select_fusion), channel_id=1, source_target_pairs={{0,96},{8,104},{16,112},{24,120},{32,0},{40,8},{48,16},{56,24},{64... | collective-permute-start | bytes 786440 | tf_op jit(solution)/shard_map/ppermute | solution.py:179
  66.4 0.5 collective-permute-start.4
  66.9 4.4 %collective-permute-done.2 = bf16[512,256]{1,0:T(8,128)(2,1)} collective-permute-done((bf16[512,256]{1,0:T(8,128)(2,1)S(1)}, bf16[512,256]{1,0:T(8,128)(2,1)}, u32[]{:S(2)}, u32[]{:S(2)}) %collective-permute-start.2) | collective-permute-done | bytes 262176 | tf_op jit(solution)/shard_map/ppermute | solution.py:179
  71.3 4.7 %collective-permute-done = bf16[512,256]{1,0:T(8,128)(2,1)} collective-permute-done((bf16[512,256]{1,0:T(8,128)(2,1)S(1)}, bf16[512,256]{1,0:T(8,128)(2,1)}, u32[]{:S(2)}, u32[]{:S(2)}) %collective-permute-start) | collective-permute-done | bytes 262176 | tf_op jit(solution)/shard_map/ppermute | solution.py:179
  76.0 1.6 convolution_convert_fusion.q_ref
  77.6 3.8 %collective-permute-done.3 = bf16[512,256]{1,0:T(8,128)(2,1)S(1)} collective-permute-done((bf16[512,256]{1,0:T(8,128)(2,1)S(1)}, bf16[512,256]{1,0:T(8,128)(2,1)S(1)}, u32[]{:S(2)}, u32[]{:S(2)}) %collective-permute-start.3) | collective-permute-done | bytes 262176 | tf_op jit(solution)/shard_map/ppermute | solution.py:179
  81.5 5.9 %shard_map.86 = f32[2,2048]{1,0:T(2,128)S(1)} custom-call(bf16[2048,256]{1,0:T(8,128)(2,1)S(1)} %convolution_convert_fusion.q_ref, bf16[2048,256]{1,0:T(8,128)(2,1)S(1)} %pad_maximum_fusion.1.items_ref), custom_call_target="tpu_custom_call" | custom-call | tf_op jit(solution)/shard_map/pallas_call | solution.py:58
  87.3 1.6 collective-permute-start.8
  89.0 2.2 %collective-permute-start.7 = (f32[2,2048]{1,0:T(2,128)S(1)}, f32[2,2048]{1,0:T(2,128)S(1)}, u32[]{:S(2)}, u32[]{:S(2)}) collective-permute-start(f32[2,2048]{1,0:T(2,128)S(1)} %shard_map.86), channel_id=1, source_target_pairs={{0,16},{8,24},{16,0},{24,8},{32,48},{40,56},{48,32},{56,40},{64,80... | collective-permute-start | bytes 49160 | tf_op jit(solution)/shard_map/ppermute | solution.py:179
  91.2 0.3 fusion.20
  91.5 3.5 %collective-permute-done.6 = f32[2,2048]{1,0:T(2,128)S(1)} collective-permute-done((f32[2,2048]{1,0:T(2,128)S(1)}, f32[2,2048]{1,0:T(2,128)S(1)}, u32[]{:S(2)}, u32[]{:S(2)}) %collective-permute-start.6) | collective-permute-done | bytes 16416 | tf_op jit(solution)/shard_map/ppermute | solution.py:179
  95.1 0.1 log_add_fusion.totals_ref
  95.1 9.4 %shard_map.87 = (f32[2048,256]{1,0:T(8,128)S(1)}, f32[2048,256]{1,0:T(8,128)}) custom-call(bf16[2048,256]{1,0:T(8,128)(2,1)S(1)} %convolution_convert_fusion.q_ref, bf16[2048,256]{1,0:T(8,128)(2,1)S(1)} %pad_maximum_fusion.1.items_ref, f32[1,2048]{1,0:T(1,128)S(1)} %log_add_fusion.totals_ref), custom_call_target="tpu_custom_call" | custom-call | tf_op jit(solution)/shard_map/pallas_call | solution.py:90
  104.5 2.6 %fusion.2 = f32[256,256]{1,0:T(8,128)S(1)} fusion(f32[256,256]{1,0:T(8,128)S(1)} %fusion.20, f32[2048,256]{1,0:T(8,128)S(1)} %get-tuple-element.11, bf16[512,256]{1,0:T(8,128)(2,1)} %collective-permute-done.2, bf16[512,256]{1,0:T(8,128)(2,1)} %collective-permute-done.1, bf16[512,256]{1,0:T(8,128)(2,1)} %collective-permute-done, ...), kind=kOutput, calls=%fused_computation.12 | convolution fusion | flops 1614938112 | bytes 3670016 | tf_op jit(solution)/shard_map/dot_general | solution.py:213
  107.1 2.3 %collective-permute-start.12 = (f32[128,256]{1,0:T(8,128)S(1)}, f32[128,256]{1,0:T(8,128)S(1)}, u32[]{:S(2)}, u32[]{:S(2)}) collective-permute-start(f32[128,256]{1,0:T(8,128)S(1)} %slice_select_fusion), channel_id=1, source_target_pairs={{0,1},{1,0},{2,3},{3,2},{4,5},{5,4},{6,7},{7,6},{8,9},{9,8},{10,11... | collective-permute-start | bytes 393224 | tf_op jit(solution)/shard_map/ppermute | solution.py:155
  109.4 1.0 collective-permute-done.12
  110.5 1.5 collective-permute-start.13
  112.0 1.7 collective-permute-done.13
  113.7 3.3 %collective-permute-start.14 = (f32[32,256]{1,0:T(8,128)S(1)}, f32[32,256]{1,0:T(8,128)S(1)}, u32[]{:S(2)}, u32[]{:S(2)}) collective-permute-start(f32[32,256]{1,0:T(8,128)S(1)} %slice_select_fusion.2), channel_id=1, source_target_pairs={{0,4},{1,5},{2,6},{3,7},{4,0},{5,1},{6,2},{7,3},{8,12},{9,13},{10,... | collective-permute-start | bytes 98312 | tf_op jit(solution)/shard_map/ppermute | solution.py:155
  117.0 1.5 fusion.18
  118.5 2.7 %collective-permute-start.11 = (f32[512,256]{1,0:T(8,128)S(1)}, f32[512,256]{1,0:T(8,128)S(1)}, u32[]{:S(2)}, u32[]{:S(2)}) collective-permute-start(f32[512,256]{1,0:T(8,128)S(1)} %get-tuple-element.17), channel_id=1, source_target_pairs={{0,96},{8,104},{16,112},{24,120},{32,0},{40,8},{48,16},{56,24},{64... | collective-permute-start | bytes 1572872 | tf_op jit(solution)/shard_map/ppermute | solution.py:179
  121.3 3.0 %collective-permute-done.15 = f32[32,256]{1,0:T(8,128)S(1)} collective-permute-done((f32[32,256]{1,0:T(8,128)S(1)}, f32[32,256]{1,0:T(8,128)S(1)}, u32[]{:S(2)}, u32[]{:S(2)}) %collective-permute-start.15) | collective-permute-done | bytes 32800 | tf_op jit(solution)/shard_map/ppermute | solution.py:159
  124.4 1.4 collective-permute-start.16
  125.8 2.8 %collective-permute-done.16 = f32[32,256]{1,0:T(8,128)S(1)} collective-permute-done((f32[32,256]{1,0:T(8,128)S(1)}, f32[32,256]{1,0:T(8,128)S(1)}, u32[]{:S(2)}, u32[]{:S(2)}) %collective-permute-start.16) | collective-permute-done | bytes 32800 | tf_op jit(solution)/shard_map/ppermute | solution.py:159
  128.6 0.6 collective-permute-start.17
  129.2 13.1 %collective-permute-done.17 = f32[32,256]{1,0:T(8,128)S(1)} collective-permute-done((f32[32,256]{1,0:T(8,128)S(1)}, f32[32,256]{1,0:T(8,128)S(1)}, u32[]{:S(2)}, u32[]{:S(2)}) %collective-permute-start.17) | collective-permute-done | bytes 32800 | tf_op jit(solution)/shard_map/ppermute | solution.py:159
  142.3 2.3 %collective-permute-start.18 = (f32[32,256]{1,0:T(8,128)S(1)}, f32[32,256]{1,0:T(8,128)S(1)}, u32[]{:S(2)}, u32[]{:S(2)}) collective-permute-start(f32[32,256]{1,0:T(8,128)S(1)} %add.153), channel_id=1, source_target_pairs={{0,64},{1,65},{2,66},{3,67},{4,68},{5,69},{6,70},{7,71},{8,72},{9,... | collective-permute-start | bytes 98312 | tf_op jit(solution)/shard_map/ppermute | solution.py:159
  144.6 2.0 %collective-permute-done.18 = f32[32,256]{1,0:T(8,128)S(1)} collective-permute-done((f32[32,256]{1,0:T(8,128)S(1)}, f32[32,256]{1,0:T(8,128)S(1)}, u32[]{:S(2)}, u32[]{:S(2)}) %collective-permute-start.18) | collective-permute-done | bytes 32800 | tf_op jit(solution)/shard_map/ppermute | solution.py:159
  146.6 0.3 collective-permute-start.19
  146.9 4.0 %collective-permute-done.19 = f32[32,256]{1,0:T(8,128)S(1)} collective-permute-done((f32[32,256]{1,0:T(8,128)S(1)}, f32[32,256]{1,0:T(8,128)S(1)}, u32[]{:S(2)}, u32[]{:S(2)}) %collective-permute-start.19) | collective-permute-done | bytes 32800 | tf_op jit(solution)/shard_map/ppermute | solution.py:163
  150.8 0.6 collective-permute-start.20
  151.5 2.9 %collective-permute-done.20 = f32[64,256]{1,0:T(8,128)S(1)} collective-permute-done((f32[64,256]{1,0:T(8,128)S(1)}, f32[64,256]{1,0:T(8,128)S(1)}, u32[]{:S(2)}, u32[]{:S(2)}) %collective-permute-start.20) | collective-permute-done | bytes 65568 | tf_op jit(solution)/shard_map/ppermute | solution.py:163
  154.3 5.9 %collective-permute-start.21 = (f32[128,256]{1,0:T(8,128)S(1)}, f32[128,256]{1,0:T(8,128)S(1)}, u32[]{:S(2)}, u32[]{:S(2)}) collective-permute-start(f32[128,256]{1,0:T(8,128)S(1)} %maximum_select_fusion.1), channel_id=1, source_target_pairs={{0,1},{1,0},{2,3},{3,2},{4,5},{5,4},{6,7},{7,6},{8,9},{9,8},{10,11... | collective-permute-start | bytes 393224 | tf_op jit(solution)/shard_map/ppermute | solution.py:163
  160.2 1.2 subtract_multiply_fusion
  161.5 0.7 maximum_select_fusion
  162.2 2.1 %fusion.1 = f32[128,8,256]{2,1,0:T(8,128)} fusion(f32[512,256]{1,0:T(8,128)S(1)} %subtract_multiply_fusion, s32[512]{0:T(512)S(1)} %get-tuple-element.15), kind=kOutput, calls=%fused_computation.10 | convolution fusion | flops 1611137024 | bytes 1574912 | tf_op jit(solution)/shard_map/dot_general | solution.py:272
  164.3 5.0 %all-to-all-start.2 = ((f32[128,8,256]{2,1,0:T(8,128)}), f32[128,8,256]{2,1,0:T(8,128)S(1)}, u32[]{:S(2)}, u32[]{:S(2)}) async-start(f32[128,8,256]{2,1,0:T(8,128)} %fusion.1), calls=%async_computation.2 | async-start | bytes 2097152 | tf_op jit(solution)/shard_map/all_to_all | solution.py:277
  169.3 0.5 broadcast.91
  169.8 0.7 reduce.4
  170.5 0.1 reshape.141
  170.6 17.7 %all-to-all-done.2 = f32[128,8,256]{2,1,0:T(8,128)S(1)} async-done(((f32[128,8,256]{2,1,0:T(8,128)}), f32[128,8,256]{2,1,0:T(8,128)S(1)}, u32[]{:S(2)}, u32[]{:S(2)}) %all-to-all-start.2) | async-done | bytes 1048608 | tf_op jit(solution)/shard_map/all_to_all | solution.py:277
  188.4 7.5 %scatter_custom_fusion = f32[2048,256]{1,0:T(8,128)} fusion(s32[1024]{0:T(1024)S(1)} %bitcast.33, f32[128,8,256]{2,1,0:T(8,128)S(1)} %all-to-all-done.2, f32[]{:T(128)} %constant.43.clone.1), kind=kCustom, calls=%fused_computation.15 | custom fusion | flops 262144 | bytes 3145732 | tf_op jit(solution)/shard_map/scatter-add | solution.py:283
  (54 shorter events, 0.7 us)
Async XLA Ops:
  0.6 22.5 %copy-start = (bf16[2048,256]{1,0:T(8,128)(2,1)S(1)}, bf16[2048,256]{1,0:T(8,128)(2,1)}, u32[]{:S(2)}) copy-start(bf16[2048,256]{1,0:T(8,128)(2,1)} %param.7) | copy-start | bytes 3145732
  0.6 19.0 %copy-start.2 = (s32[512]{0:T(512)S(1)}, s32[512]{0:T(512)}, u32[]{:S(2)}) copy-start(s32[512]{0:T(512)} %param.13) | copy-start | bytes 6148
  2.2 20.9 %all-to-all-start = ((s32[128,1,8]{2,1,0:T(1,128)}), s32[128,1,8]{2,1,0:T(1,128)S(1)}, u32[]{:S(2)}, u32[]{:S(2)}) async-start(s32[128,1,8]{2,1,0:T(1,128)} %bitcast), calls=%async_computation | async-start | bytes 131072 | tf_op jit(solution)/shard_map/all_to_all | solution.py:230
  23.2 5.0 %copy-start.1 = (s32[512,8]{0,1:T(8,128)S(1)}, s32[512,8]{0,1:T(8,128)}, u32[]{:S(2)}) copy-start(s32[512,8]{0,1:T(8,128)} %param.10) | copy-start | bytes 49156
  28.2 33.5 %all-to-all-start.1 = ((bf16[128,8,256]{2,1,0:T(8,128)(2,1)}), bf16[128,8,256]{2,1,0:T(8,128)(2,1)S(1)}, u32[]{:S(2)}, u32[]{:S(2)}) async-start(bf16[128,8,256]{2,1,0:T(8,128)(2,1)} %bitcast_select_fusion.1), calls=%async_computation.1 | async-start | bytes 1048576 | tf_op jit(solution)/shard_map/all_to_all | solution.py:233
  57.9 13.4 %collective-permute-start.2 = (bf16[512,256]{1,0:T(8,128)(2,1)S(1)}, bf16[512,256]{1,0:T(8,128)(2,1)}, u32[]{:S(2)}, u32[]{:S(2)}) collective-permute-start(bf16[512,256]{1,0:T(8,128)(2,1)S(1)} %multiply_convert_fusion), channel_id=1, source_target_pairs={{0,24},{8,0},{16,8},{24,16},{32,56},{40,32},{48,40},{56,48},{64,88... | collective-permute-start | bytes 786440 | tf_op jit(solution)/shard_map/ppermute | solution.py:179
  60.5 10.8 %collective-permute-start.1 = (bf16[512,256]{1,0:T(8,128)(2,1)S(1)}, bf16[512,256]{1,0:T(8,128)(2,1)}, u32[]{:S(2)}, u32[]{:S(2)}) collective-permute-start(bf16[512,256]{1,0:T(8,128)(2,1)S(1)} %multiply_convert_fusion), channel_id=1, source_target_pairs={{0,16},{8,24},{16,0},{24,8},{32,48},{40,56},{48,32},{56,40},{64,80... | collective-permute-start | bytes 786440 | tf_op jit(solution)/shard_map/ppermute | solution.py:179
  61.1 14.9 %collective-permute-start = (bf16[512,256]{1,0:T(8,128)(2,1)S(1)}, bf16[512,256]{1,0:T(8,128)(2,1)}, u32[]{:S(2)}, u32[]{:S(2)}) collective-permute-start(bf16[512,256]{1,0:T(8,128)(2,1)S(1)} %multiply_convert_fusion), channel_id=1, source_target_pairs={{0,8},{8,16},{16,24},{24,0},{32,40},{40,48},{48,56},{56,32},{64,72... | collective-permute-start | bytes 786440 | tf_op jit(solution)/shard_map/ppermute | solution.py:179
  63.8 13.8 %collective-permute-start.5 = (bf16[512,256]{1,0:T(8,128)(2,1)S(1)}, bf16[512,256]{1,0:T(8,128)(2,1)S(1)}, u32[]{:S(2)}, u32[]{:S(2)}) collective-permute-start(bf16[512,256]{1,0:T(8,128)(2,1)S(1)} %broadcast_select_fusion), channel_id=1, source_target_pairs={{0,96},{8,104},{16,112},{24,120},{32,0},{40,8},{48,16},{56,24},{64... | collective-permute-start | bytes 786440 | tf_op jit(solution)/shard_map/ppermute | solution.py:179
  66.4 11.2 %collective-permute-start.4 = (bf16[512,256]{1,0:T(8,128)(2,1)S(1)}, bf16[512,256]{1,0:T(8,128)(2,1)S(1)}, u32[]{:S(2)}, u32[]{:S(2)}) collective-permute-start(bf16[512,256]{1,0:T(8,128)(2,1)S(1)} %broadcast_select_fusion), channel_id=1, source_target_pairs={{0,64},{8,72},{16,80},{24,88},{32,96},{40,104},{48,112},{56,120},{... | collective-permute-start | bytes 786440 | tf_op jit(solution)/shard_map/ppermute | solution.py:179
  71.3 10.1 %collective-permute-start.3 = (bf16[512,256]{1,0:T(8,128)(2,1)S(1)}, bf16[512,256]{1,0:T(8,128)(2,1)S(1)}, u32[]{:S(2)}, u32[]{:S(2)}) collective-permute-start(bf16[512,256]{1,0:T(8,128)(2,1)S(1)} %broadcast_select_fusion), channel_id=1, source_target_pairs={{0,32},{8,40},{16,48},{24,56},{32,64},{40,72},{48,80},{56,88},{64,... | collective-permute-start | bytes 786440 | tf_op jit(solution)/shard_map/ppermute | solution.py:179
  87.3 4.2 %collective-permute-start.8 = (f32[2,2048]{1,0:T(2,128)S(1)}, f32[2,2048]{1,0:T(2,128)S(1)}, u32[]{:S(2)}, u32[]{:S(2)}) collective-permute-start(f32[2,2048]{1,0:T(2,128)S(1)} %shard_map.86), channel_id=1, source_target_pairs={{0,24},{8,0},{16,8},{24,16},{32,56},{40,32},{48,40},{56,48},{64,88... | collective-permute-start | bytes 49160 | tf_op jit(solution)/shard_map/ppermute | solution.py:179
  89.0 6.1 %collective-permute-start.7 = (f32[2,2048]{1,0:T(2,128)S(1)}, f32[2,2048]{1,0:T(2,128)S(1)}, u32[]{:S(2)}, u32[]{:S(2)}) collective-permute-start(f32[2,2048]{1,0:T(2,128)S(1)} %shard_map.86), channel_id=1, source_target_pairs={{0,16},{8,24},{16,0},{24,8},{32,48},{40,56},{48,32},{56,40},{64,80... | collective-permute-start | bytes 49160 | tf_op jit(solution)/shard_map/ppermute | solution.py:179
  91.2 3.8 %collective-permute-start.6 = (f32[2,2048]{1,0:T(2,128)S(1)}, f32[2,2048]{1,0:T(2,128)S(1)}, u32[]{:S(2)}, u32[]{:S(2)}) collective-permute-start(f32[2,2048]{1,0:T(2,128)S(1)} %shard_map.86), channel_id=1, source_target_pairs={{0,8},{8,16},{16,24},{24,0},{32,40},{40,48},{48,56},{56,32},{64,72... | collective-permute-start | bytes 49160 | tf_op jit(solution)/shard_map/ppermute | solution.py:179
  107.1 3.3 %collective-permute-start.12 = (f32[128,256]{1,0:T(8,128)S(1)}, f32[128,256]{1,0:T(8,128)S(1)}, u32[]{:S(2)}, u32[]{:S(2)}) collective-permute-start(f32[128,256]{1,0:T(8,128)S(1)} %slice_select_fusion), channel_id=1, source_target_pairs={{0,1},{1,0},{2,3},{3,2},{4,5},{5,4},{6,7},{7,6},{8,9},{9,8},{10,11... | collective-permute-start | bytes 393224 | tf_op jit(solution)/shard_map/ppermute | solution.py:155
  110.5 3.2 %collective-permute-start.13 = (f32[64,256]{1,0:T(8,128)S(1)}, f32[64,256]{1,0:T(8,128)S(1)}, u32[]{:S(2)}, u32[]{:S(2)}) collective-permute-start(f32[64,256]{1,0:T(8,128)S(1)} %slice_select_fusion.1), channel_id=1, source_target_pairs={{0,2},{1,3},{2,0},{3,1},{4,6},{5,7},{6,4},{7,5},{8,10},{9,11},{10,... | collective-permute-start | bytes 196616 | tf_op jit(solution)/shard_map/ppermute | solution.py:155
  113.7 7.5 %collective-permute-start.14 = (f32[32,256]{1,0:T(8,128)S(1)}, f32[32,256]{1,0:T(8,128)S(1)}, u32[]{:S(2)}, u32[]{:S(2)}) collective-permute-start(f32[32,256]{1,0:T(8,128)S(1)} %slice_select_fusion.2), channel_id=1, source_target_pairs={{0,4},{1,5},{2,6},{3,7},{4,0},{5,1},{6,2},{7,3},{8,12},{9,13},{10,... | collective-permute-start | bytes 98312 | tf_op jit(solution)/shard_map/ppermute | solution.py:155
  118.5 41.8 %collective-permute-start.9 = (f32[512,256]{1,0:T(8,128)S(1)}, f32[512,256]{1,0:T(8,128)S(1)}, u32[]{:S(2)}, u32[]{:S(2)}) collective-permute-start(f32[512,256]{1,0:T(8,128)S(1)} %get-tuple-element.16), channel_id=1, source_target_pairs={{0,32},{8,40},{16,48},{24,56},{32,64},{40,72},{48,80},{56,88},{64,... | collective-permute-start | bytes 1572872 | tf_op jit(solution)/shard_map/ppermute | solution.py:179
  118.5 41.7 %collective-permute-start.11 = (f32[512,256]{1,0:T(8,128)S(1)}, f32[512,256]{1,0:T(8,128)S(1)}, u32[]{:S(2)}, u32[]{:S(2)}) collective-permute-start(f32[512,256]{1,0:T(8,128)S(1)} %get-tuple-element.17), channel_id=1, source_target_pairs={{0,96},{8,104},{16,112},{24,120},{32,0},{40,8},{48,16},{56,24},{64... | collective-permute-start | bytes 1572872 | tf_op jit(solution)/shard_map/ppermute | solution.py:179
  121.2 39.0 %collective-permute-start.10 = (f32[512,256]{1,0:T(8,128)S(1)}, f32[512,256]{1,0:T(8,128)S(1)}, u32[]{:S(2)}, u32[]{:S(2)}) collective-permute-start(f32[512,256]{1,0:T(8,128)S(1)} %get-tuple-element.18), channel_id=1, source_target_pairs={{0,64},{8,72},{16,80},{24,88},{32,96},{40,104},{48,112},{56,120},{... | collective-permute-start | bytes 1572872 | tf_op jit(solution)/shard_map/ppermute | solution.py:179
  121.2 3.1 %collective-permute-start.15 = (f32[32,256]{1,0:T(8,128)S(1)}, f32[32,256]{1,0:T(8,128)S(1)}, u32[]{:S(2)}, u32[]{:S(2)}) collective-permute-start(f32[32,256]{1,0:T(8,128)S(1)} %select_add_fusion.2), channel_id=1, source_target_pairs={{0,8},{1,9},{2,10},{3,11},{4,12},{5,13},{6,14},{7,15},{8,0},{9,1},... | collective-permute-start | bytes 98312 | tf_op jit(solution)/shard_map/ppermute | solution.py:159
  124.4 4.3 %collective-permute-start.16 = (f32[32,256]{1,0:T(8,128)S(1)}, f32[32,256]{1,0:T(8,128)S(1)}, u32[]{:S(2)}, u32[]{:S(2)}) collective-permute-start(f32[32,256]{1,0:T(8,128)S(1)} %add.151), channel_id=1, source_target_pairs={{0,16},{1,17},{2,18},{3,19},{4,20},{5,21},{6,22},{7,23},{8,24},{9,... | collective-permute-start | bytes 98312 | tf_op jit(solution)/shard_map/ppermute | solution.py:159
  128.6 13.6 %collective-permute-start.17 = (f32[32,256]{1,0:T(8,128)S(1)}, f32[32,256]{1,0:T(8,128)S(1)}, u32[]{:S(2)}, u32[]{:S(2)}) collective-permute-start(f32[32,256]{1,0:T(8,128)S(1)} %add.152), channel_id=1, source_target_pairs={{0,32},{1,33},{2,34},{3,35},{4,36},{5,37},{6,38},{7,39},{8,40},{9,... | collective-permute-start | bytes 98312 | tf_op jit(solution)/shard_map/ppermute | solution.py:159
  142.3 4.3 %collective-permute-start.18 = (f32[32,256]{1,0:T(8,128)S(1)}, f32[32,256]{1,0:T(8,128)S(1)}, u32[]{:S(2)}, u32[]{:S(2)}) collective-permute-start(f32[32,256]{1,0:T(8,128)S(1)} %add.153), channel_id=1, source_target_pairs={{0,64},{1,65},{2,66},{3,67},{4,68},{5,69},{6,70},{7,71},{8,72},{9,... | collective-permute-start | bytes 98312 | tf_op jit(solution)/shard_map/ppermute | solution.py:159
  146.6 4.3 %collective-permute-start.19 = (f32[32,256]{1,0:T(8,128)S(1)}, f32[32,256]{1,0:T(8,128)S(1)}, u32[]{:S(2)}, u32[]{:S(2)}) collective-permute-start(f32[32,256]{1,0:T(8,128)S(1)} %add.154), channel_id=1, source_target_pairs={{0,4},{1,5},{2,6},{3,7},{4,0},{5,1},{6,2},{7,3},{8,12},{9,13},{10,... | collective-permute-start | bytes 98312 | tf_op jit(solution)/shard_map/ppermute | solution.py:163
  150.8 3.5 %collective-permute-start.20 = (f32[64,256]{1,0:T(8,128)S(1)}, f32[64,256]{1,0:T(8,128)S(1)}, u32[]{:S(2)}, u32[]{:S(2)}) collective-permute-start(f32[64,256]{1,0:T(8,128)S(1)} %maximum_select_fusion.2), channel_id=1, source_target_pairs={{0,2},{1,3},{2,0},{3,1},{4,6},{5,7},{6,4},{7,5},{8,10},{9,11},{10,... | collective-permute-start | bytes 196616 | tf_op jit(solution)/shard_map/ppermute | solution.py:163
  154.3 7.1 %collective-permute-start.21 = (f32[128,256]{1,0:T(8,128)S(1)}, f32[128,256]{1,0:T(8,128)S(1)}, u32[]{:S(2)}, u32[]{:S(2)}) collective-permute-start(f32[128,256]{1,0:T(8,128)S(1)} %maximum_select_fusion.1), channel_id=1, source_target_pairs={{0,1},{1,0},{2,3},{3,2},{4,5},{5,4},{6,7},{7,6},{8,9},{9,8},{10,11... | collective-permute-start | bytes 393224 | tf_op jit(solution)/shard_map/ppermute | solution.py:163
  164.3 24.1 %all-to-all-start.2 = ((f32[128,8,256]{2,1,0:T(8,128)}), f32[128,8,256]{2,1,0:T(8,128)S(1)}, u32[]{:S(2)}, u32[]{:S(2)}) async-start(f32[128,8,256]{2,1,0:T(8,128)} %fusion.1), calls=%async_computation.2 | async-start | bytes 2097152 | tf_op jit(solution)/shard_map/all_to_all | solution.py:277

commit v15 on v14

--- a/solution.py
+++ b/solution.py
@@ -264,7 +264,7 @@
         )
     total = lax.axis_size("batch") * lax.axis_size("table")
     if total & (total - 1) == 0:
-        weight_grad = tree_sum(partial_value, ("batch", "table"), min(8, lax.axis_size("table")))
+        weight_grad = tree_sum(partial_value, ("batch", "table"), min(4, lax.axis_size("table")))
     else:
         weight_grad = lax.psum(partial_value, ("batch", "table"))
     item_grad, weight_grad = lax.optimization_barrier((item_grad, weight_grad))
@@ -277,10 +277,12 @@
     returned = lax.all_to_all(
         slot_grads, ("batch", "table"), split_axis=0, concat_axis=0, tiled=True
     )
-    table_grad = (
-        jnp.zeros((table_rows, model_width), jnp.float32)
-        .at[wanted.reshape(-1)]
-        .add(returned.reshape(-1, model_width))
+    landing = (
+        lax.broadcasted_iota(jnp.int32, (table_rows, wanted.size), 0) == wanted.reshape(1, -1)
+    )
+    table_grad = jnp.dot(
+        landing.astype(jnp.bfloat16), returned.reshape(-1, model_width),
+        preferred_element_type=jnp.float32, precision=lax.Precision.HIGHEST,
     )
     return (table_grad, weight_grad)
 

time: 196 us -> 187 us (0.954)
  other arithmetic: 17.7 us -> 10.3 us
  waiting for transfers between devices: 67.9 us -> 61.9 us
  matrix products: 6.5 us -> 11.8 us
    scatter-add x1 -> x0, other arithmetic: 7.51 us -> none  [step_body(): table_grad = jnp.zeros((table_rows, model_width), jnp.float32).at[wanted....]
    dot_general x0 -> x1, matrix products: none -> 5.31 us  [step_body(): jnp.dot(landing.astype(jnp.bfloat16), returned.reshape(-1, model_width),...]
    ppermute x3 -> x2, waiting for transfers between devices: 6.84 us -> 3.09 us  [tree_sum(): got = lax.ppermute(value, axes, [(i, i ^ step) for i in range(total)])]
    ppermute x3 -> x2, starting transfers between devices: 7.12 us -> 3.81 us  [tree_sum(): lax.ppermute(send, axes, [(i, i ^ step) for i in range(total)])]
    ppermute x3 -> x2, starting transfers between devices: 6.8 us -> 3.98 us  [tree_sum(): got = lax.ppermute(value, axes, [(i, i ^ step) for i in range(total)])]
    ppermute x4 -> x5, starting transfers between devices: 4.37 us -> 7.02 us  [tree_sum(): lax.ppermute(value, axes, [(i, i ^ step) for i in range(total)])]
    all_to_all x1, starting transfers between devices: 5.04 us -> 7.1 us  [step_body(): lax.all_to_all(slot_grads, ('batch', 'table'), split_axis=0, concat_axis=...]
    ppermute x4 -> x5, waiting for transfers between devices: 20.9 us -> 20.5 us  [tree_sum(): lax.ppermute(value, axes, [(i, i ^ step) for i in range(total)])]
  transfers between devices with their start and end apart: 25 -> 24, of which waited for: 14 -> 13; matrix products, arithmetic and copies ran while one was open for 19% -> 20% of each run, Pallas kernels for 0% -> 0%
where the time goes in v15:
time: 187 us; the launch traced here: 186 us
  waiting for transfers between devices  61.9 us (33%)
  starting transfers between devices  53.3 us (29%)
  local copies, waits for them, and re-layouts  32.9 us (18%)
  Pallas kernels  15.2 us (8%)
  matrix products  11.8 us (6%)
  other arithmetic  10.3 us (6%)
    ppermute x5, waiting for transfers between devices, tree_sum(): lax.ppermute(value, axes, [(i, i ^ step) for i in range(total)])  20.5 us
    gather x1, local copies, waits for them, and re-layouts, step_body(): looked = jnp.take(query_table, query_ids, axis=0).astype(jnp.float32)  18.7 us
    all_to_all x1, waiting for transfers between devices, step_body(): lax.all_to_all(slot_grads, ('batch', 'table'), split_axis=0, concat_axis=...  17.5 us
    ppermute x12, waiting for transfers between devices, plane_shift(): return lax.ppermute(value, axis, pairs)  16.4 us
    ppermute x12, starting transfers between devices, plane_shift(): return lax.ppermute(value, axis, pairs)  13.5 us
    all_to_all x1, starting transfers between devices, step_body(): lax.all_to_all(requests, ('batch', 'table'), split_axis=0, concat_axis=0,...  11.5 us
    pallas_call x1, Pallas kernels, block_grads_k(): pl.pallas_call(functools.partial(grads_block, scaling=scaling), grid=(row...  9.35 us
    all_to_all x1, starting transfers between devices, step_body(): lax.all_to_all(slot_grads, ('batch', 'table'), split_axis=0, concat_axis=...  7.1 us
  transfers between devices with their start and end apart: 24, of which 13 were waited for; matrix products, arithmetic and copies ran while one was open for 20% of the time, Pallas kernels for 0%

profile of v15, /device:TPU:1, one launch (start us, length us, event | category | flops | bytes accessed | tf_op | source)
XLA Modules:
  0.0 186.5 jit_solution(16111691209022836456)
XLA Ops:
  0.7 1.5 copy.22
  2.2 11.5 %all-to-all-start = ((s32[128,1,8]{2,1,0:T(1,128)}), s32[128,1,8]{2,1,0:T(1,128)S(1)}, u32[]{:S(2)}, u32[]{:S(2)}) async-start(s32[128,1,8]{2,1,0:T(1,128)} %bitcast), calls=%async_computation | async-start | bytes 131072 | tf_op jit(solution)/shard_map/all_to_all | solution.py:230
  13.7 0.8 copy.23
  14.4 0.2 reduce-window.8
  14.6 0.1 reduce.1
  14.7 0.7 bitcast_subtract_fusion
  15.4 0.9 convert_reduce_fusion.1
  16.3 3.3 %gather_fusion = s32[512]{0:T(512)S(1)} fusion(s32[128]{0:T(128)S(1)} %bitcast_subtract_fusion, s32[1024]{0:T(1024)S(1)} %pad_clamp_fusion.1), kind=kCustom, calls=%fused_computation | custom fusion | bytes 6144 | tf_op jit(solution)/shard_map/jit(_take)/gather | solution.py:139
  19.7 3.3 %all-to-all-done = s32[128,1,8]{2,1,0:T(1,128)S(1)} async-done(((s32[128,1,8]{2,1,0:T(1,128)}), s32[128,1,8]{2,1,0:T(1,128)S(1)}, u32[]{:S(2)}, u32[]{:S(2)}) %all-to-all-start) | async-done | bytes 4128 | tf_op jit(solution)/shard_map/all_to_all | solution.py:230
  23.1 0.1 reshape.128
  23.2 3.9 %gather_fusion.1 = bf16[1024,256]{1,0:T(8,128)(2,1)S(1)} fusion(bf16[2048,256]{1,0:T(8,128)(2,1)S(1)} %copy-done, s32[1024]{0:T(1024)S(1)} %broadcast_clamp_fusion.1), kind=kCustom, calls=%fused_computation.1 | custom fusion | bytes 1052672 | tf_op jit(solution)/shard_map/jit(_take)/gather | solution.py:231
  27.1 1.0 bitcast_select_fusion.1
  28.2 6.5 %all-to-all-start.1 = ((bf16[128,8,256]{2,1,0:T(8,128)(2,1)}), bf16[128,8,256]{2,1,0:T(8,128)(2,1)S(1)}, u32[]{:S(2)}, u32[]{:S(2)}) async-start(bf16[128,8,256]{2,1,0:T(8,128)(2,1)} %bitcast_select_fusion.1), calls=%async_computation.1 | async-start | bytes 1048576 | tf_op jit(solution)/shard_map/all_to_all | solution.py:233
  34.6 0.2 copy.24
  34.8 0.1 copy.25
  34.9 0.2 reshape.136
  35.1 18.7 %gather_fusion.2 = bf16[4096,256]{1,0:T(8,128)(2,1)} fusion(bf16[8192,256]{1,0:T(8,128)(2,1)} %param.8, s32[4096]{0:T(1024)S(1)} %broadcast_clamp_fusion), kind=kCustom, calls=%fused_computation.2 | custom fusion | bytes 4210688 | tf_op jit(solution)/shard_map/jit(_take)/gather | solution.py:238
  53.8 4.1 %convert_reduce_fusion = f32[512,256]{1,0:T(8,128)S(1)} fusion(bf16[4096,256]{1,0:T(8,128)(2,1)} %gather_fusion.2, pred[512,8]{1,0:T(8,128)(4,1)S(1)} %copy.24), kind=kLoop, calls=%fused_computation.6 | loop fusion | flops 3014656 | bytes 2625536 | tf_op jit(solution)/shard_map/reduce_sum | solution.py:239
  57.9 2.6 %collective-permute-start.2 = (bf16[512,256]{1,0:T(8,128)(2,1)S(1)}, bf16[512,256]{1,0:T(8,128)(2,1)}, u32[]{:S(2)}, u32[]{:S(2)}) collective-permute-start(bf16[512,256]{1,0:T(8,128)(2,1)S(1)} %multiply_convert_fusion), channel_id=1, source_target_pairs={{0,24},{8,0},{16,8},{24,16},{32,56},{40,32},{48,40},{56,48},{64,88... | collective-permute-start | bytes 786440 | tf_op jit(solution)/shard_map/ppermute | solution.py:179
  60.6 0.6 collective-permute-start.1
  61.1 0.6 collective-permute-start
  61.7 2.0 %gather_fusion.3 = bf16[512,256]{1,0:T(8,128)(2,1)S(1)} fusion(bf16[1024,256]{1,0:T(8,128)(2,1)S(1)} %bitcast.27, s32[1024]{0:T(1024)S(1)} %pad_clamp_fusion), kind=kCustom, calls=%fused_computation.3 | custom fusion | bytes 526336 | tf_op jit(solution)/shard_map/jit(_take)/gather | solution.py:237
  63.7 0.1 broadcast_select_fusion
  63.8 2.6 %collective-permute-start.5 = (bf16[512,256]{1,0:T(8,128)(2,1)S(1)}, bf16[512,256]{1,0:T(8,128)(2,1)S(1)}, u32[]{:S(2)}, u32[]{:S(2)}) collective-permute-start(bf16[512,256]{1,0:T(8,128)(2,1)S(1)} %broadcast_select_fusion), channel_id=1, source_target_pairs={{0,96},{8,104},{16,112},{24,120},{32,0},{40,8},{48,16},{56,24},{64... | collective-permute-start | bytes 786440 | tf_op jit(solution)/shard_map/ppermute | solution.py:179
  66.4 0.5 collective-permute-start.4
  66.9 4.4 %collective-permute-done.2 = bf16[512,256]{1,0:T(8,128)(2,1)} collective-permute-done((bf16[512,256]{1,0:T(8,128)(2,1)S(1)}, bf16[512,256]{1,0:T(8,128)(2,1)}, u32[]{:S(2)}, u32[]{:S(2)}) %collective-permute-start.2) | collective-permute-done | bytes 262176 | tf_op jit(solution)/shard_map/ppermute | solution.py:179
  71.3 4.7 %collective-permute-done = bf16[512,256]{1,0:T(8,128)(2,1)} collective-permute-done((bf16[512,256]{1,0:T(8,128)(2,1)S(1)}, bf16[512,256]{1,0:T(8,128)(2,1)}, u32[]{:S(2)}, u32[]{:S(2)}) %collective-permute-start) | collective-permute-done | bytes 262176 | tf_op jit(solution)/shard_map/ppermute | solution.py:179
  76.0 1.6 convolution_convert_fusion.q_ref
  77.6 3.8 %collective-permute-done.3 = bf16[512,256]{1,0:T(8,128)(2,1)S(1)} collective-permute-done((bf16[512,256]{1,0:T(8,128)(2,1)S(1)}, bf16[512,256]{1,0:T(8,128)(2,1)S(1)}, u32[]{:S(2)}, u32[]{:S(2)}) %collective-permute-start.3) | collective-permute-done | bytes 262176 | tf_op jit(solution)/shard_map/ppermute | solution.py:179
  81.5 5.9 %shard_map.86 = f32[2,2048]{1,0:T(2,128)S(1)} custom-call(bf16[2048,256]{1,0:T(8,128)(2,1)S(1)} %convolution_convert_fusion.q_ref, bf16[2048,256]{1,0:T(8,128)(2,1)S(1)} %pad_maximum_fusion.1.items_ref), custom_call_target="tpu_custom_call" | custom-call | tf_op jit(solution)/shard_map/pallas_call | solution.py:58
  87.3 1.6 collective-permute-start.8
  89.0 2.2 %collective-permute-start.7 = (f32[2,2048]{1,0:T(2,128)S(1)}, f32[2,2048]{1,0:T(2,128)S(1)}, u32[]{:S(2)}, u32[]{:S(2)}) collective-permute-start(f32[2,2048]{1,0:T(2,128)S(1)} %shard_map.86), channel_id=1, source_target_pairs={{0,16},{8,24},{16,0},{24,8},{32,48},{40,56},{48,32},{56,40},{64,80... | collective-permute-start | bytes 49160 | tf_op jit(solution)/shard_map/ppermute | solution.py:179
  91.2 0.3 fusion.20
  91.5 3.5 %collective-permute-done.6 = f32[2,2048]{1,0:T(2,128)S(1)} collective-permute-done((f32[2,2048]{1,0:T(2,128)S(1)}, f32[2,2048]{1,0:T(2,128)S(1)}, u32[]{:S(2)}, u32[]{:S(2)}) %collective-permute-start.6) | collective-permute-done | bytes 16416 | tf_op jit(solution)/shard_map/ppermute | solution.py:179
  95.1 0.1 log_add_fusion.totals_ref
  95.2 9.4 %shard_map.87 = (f32[2048,256]{1,0:T(8,128)S(1)}, f32[2048,256]{1,0:T(8,128)}) custom-call(bf16[2048,256]{1,0:T(8,128)(2,1)S(1)} %convolution_convert_fusion.q_ref, bf16[2048,256]{1,0:T(8,128)(2,1)S(1)} %pad_maximum_fusion.1.items_ref, f32[1,2048]{1,0:T(1,128)S(1)} %log_add_fusion.totals_ref), custom_call_target="tpu_custom_call" | custom-call | tf_op jit(solution)/shard_map/pallas_call | solution.py:90
  104.5 2.6 %fusion.4 = f32[256,256]{1,0:T(8,128)S(1)} fusion(f32[256,256]{1,0:T(8,128)S(1)} %fusion.20, f32[2048,256]{1,0:T(8,128)S(1)} %get-tuple-element.11, bf16[512,256]{1,0:T(8,128)(2,1)} %collective-permute-done.2, bf16[512,256]{1,0:T(8,128)(2,1)} %collective-permute-done.1, bf16[512,256]{1,0:T(8,128)(2,1)} %collective-permute-done, ...), kind=kOutput, calls=%fused_computation.14 | convolution fusion | flops 1614938112 | bytes 3670016 | tf_op jit(solution)/shard_map/dot_general | solution.py:213
  107.2 2.3 %collective-permute-start.12 = (f32[128,256]{1,0:T(8,128)S(1)}, f32[128,256]{1,0:T(8,128)S(1)}, u32[]{:S(2)}, u32[]{:S(2)}) collective-permute-start(f32[128,256]{1,0:T(8,128)S(1)} %slice_select_fusion), channel_id=1, source_target_pairs={{0,1},{1,0},{2,3},{3,2},{4,5},{5,4},{6,7},{7,6},{8,9},{9,8},{10,11... | collective-permute-start | bytes 393224 | tf_op jit(solution)/shard_map/ppermute | solution.py:155
  109.4 1.0 collective-permute-done.12
  110.5 1.5 collective-permute-start.13
  112.0 1.5 fusion.18
  113.5 2.7 %collective-permute-start.11 = (f32[512,256]{1,0:T(8,128)S(1)}, f32[512,256]{1,0:T(8,128)S(1)}, u32[]{:S(2)}, u32[]{:S(2)}) collective-permute-start(f32[512,256]{1,0:T(8,128)S(1)} %get-tuple-element.17), channel_id=1, source_target_pairs={{0,96},{8,104},{16,112},{24,120},{32,0},{40,8},{48,16},{56,24},{64... | collective-permute-start | bytes 1572872 | tf_op jit(solution)/shard_map/ppermute | solution.py:179
  116.2 3.0 %collective-permute-start.14 = (f32[64,256]{1,0:T(8,128)S(1)}, f32[64,256]{1,0:T(8,128)S(1)}, u32[]{:S(2)}, u32[]{:S(2)}) collective-permute-start(f32[64,256]{1,0:T(8,128)S(1)} %select_add_fusion.1), channel_id=1, source_target_pairs={{0,4},{1,5},{2,6},{3,7},{4,0},{5,1},{6,2},{7,3},{8,12},{9,13},{10,... | collective-permute-start | bytes 196616 | tf_op jit(solution)/shard_map/ppermute | solution.py:159
  119.2 1.7 collective-permute-done.14
  120.9 0.1 collective-permute-start.15
  121.0 3.4 %collective-permute-done.15 = f32[64,256]{1,0:T(8,128)S(1)} collective-permute-done((f32[64,256]{1,0:T(8,128)S(1)}, f32[64,256]{1,0:T(8,128)S(1)}, u32[]{:S(2)}, u32[]{:S(2)}) %collective-permute-start.15) | collective-permute-done | bytes 65568 | tf_op jit(solution)/shard_map/ppermute | solution.py:159
  124.4 1.5 collective-permute-start.16
  126.0 3.5 %collective-permute-done.16 = f32[64,256]{1,0:T(8,128)S(1)} collective-permute-done((f32[64,256]{1,0:T(8,128)S(1)}, f32[64,256]{1,0:T(8,128)S(1)}, u32[]{:S(2)}, u32[]{:S(2)}) %collective-permute-start.16) | collective-permute-done | bytes 65568 | tf_op jit(solution)/shard_map/ppermute | solution.py:159
  129.5 0.4 collective-permute-start.17
  129.8 9.3 %collective-permute-done.17 = f32[64,256]{1,0:T(8,128)S(1)} collective-permute-done((f32[64,256]{1,0:T(8,128)S(1)}, f32[64,256]{1,0:T(8,128)S(1)}, u32[]{:S(2)}, u32[]{:S(2)}) %collective-permute-start.17) | collective-permute-done | bytes 65568 | tf_op jit(solution)/shard_map/ppermute | solution.py:159
  139.2 2.1 %collective-permute-start.18 = (f32[64,256]{1,0:T(8,128)S(1)}, f32[64,256]{1,0:T(8,128)S(1)}, u32[]{:S(2)}, u32[]{:S(2)}) collective-permute-start(f32[64,256]{1,0:T(8,128)S(1)} %add.136), channel_id=1, source_target_pairs={{0,64},{1,65},{2,66},{3,67},{4,68},{5,69},{6,70},{7,71},{8,72},{9,... | collective-permute-start | bytes 196616 | tf_op jit(solution)/shard_map/ppermute | solution.py:159
  141.2 2.6 %collective-permute-done.18 = f32[64,256]{1,0:T(8,128)S(1)} collective-permute-done((f32[64,256]{1,0:T(8,128)S(1)}, f32[64,256]{1,0:T(8,128)S(1)}, u32[]{:S(2)}, u32[]{:S(2)}) %collective-permute-start.18) | collective-permute-done | bytes 65568 | tf_op jit(solution)/shard_map/ppermute | solution.py:159
  143.9 0.1 collective-permute-start.19
  144.0 3.1 %collective-permute-done.19 = f32[64,256]{1,0:T(8,128)S(1)} collective-permute-done((f32[64,256]{1,0:T(8,128)S(1)}, f32[64,256]{1,0:T(8,128)S(1)}, u32[]{:S(2)}, u32[]{:S(2)}) %collective-permute-start.19) | collective-permute-done | bytes 65568 | tf_op jit(solution)/shard_map/ppermute | solution.py:163
  147.1 3.9 %collective-permute-start.20 = (f32[128,256]{1,0:T(8,128)S(1)}, f32[128,256]{1,0:T(8,128)S(1)}, u32[]{:S(2)}, u32[]{:S(2)}) collective-permute-start(f32[128,256]{1,0:T(8,128)S(1)} %maximum_select_fusion.1), channel_id=1, source_target_pairs={{0,1},{1,0},{2,3},{3,2},{4,5},{5,4},{6,7},{7,6},{8,9},{9,8},{10,11... | collective-permute-start | bytes 393224 | tf_op jit(solution)/shard_map/ppermute | solution.py:163
  151.0 1.2 subtract_multiply_fusion
  152.2 0.7 maximum_select_fusion
  152.9 2.1 %fusion.3 = f32[128,8,256]{2,1,0:T(8,128)} fusion(f32[512,256]{1,0:T(8,128)S(1)} %subtract_multiply_fusion, s32[512]{0:T(512)S(1)} %get-tuple-element.15), kind=kOutput, calls=%fused_computation.12 | convolution fusion | flops 1611137024 | bytes 1574912 | tf_op jit(solution)/shard_map/dot_general | solution.py:272
  155.0 7.1 %all-to-all-start.2 = ((f32[128,8,256]{2,1,0:T(8,128)}), f32[128,8,256]{2,1,0:T(8,128)S(1)}, u32[]{:S(2)}, u32[]{:S(2)}) async-start(f32[128,8,256]{2,1,0:T(8,128)} %fusion.3), calls=%async_computation.2 | async-start | bytes 2097152 | tf_op jit(solution)/shard_map/all_to_all | solution.py:277
  162.1 0.6 broadcast.77
  162.7 0.9 reduce.4
  163.6 0.1 eq.18
  163.7 17.5 %all-to-all-done.2 = f32[128,8,256]{2,1,0:T(8,128)S(1)} async-done(((f32[128,8,256]{2,1,0:T(8,128)}), f32[128,8,256]{2,1,0:T(8,128)S(1)}, u32[]{:S(2)}, u32[]{:S(2)}) %all-to-all-start.2) | async-done | bytes 1048608 | tf_op jit(solution)/shard_map/all_to_all | solution.py:277
  181.1 5.3 %fusion = f32[2048,256]{1,0:T(8,128)} fusion(s32[1024]{0:T(1024)S(1)} %eq.18, f32[128,8,256]{2,1,0:T(8,128)S(1)} %all-to-all-done.2), kind=kOutput, calls=%fused_computation.5 | convolution fusion | flops 6444548096 | bytes 3149824 | tf_op jit(solution)/shard_map/dot_general | solution.py:283
  (49 shorter events, 0.5 us)
Async XLA Ops:
  0.6 22.5 %copy-start = (bf16[2048,256]{1,0:T(8,128)(2,1)S(1)}, bf16[2048,256]{1,0:T(8,128)(2,1)}, u32[]{:S(2)}) copy-start(bf16[2048,256]{1,0:T(8,128)(2,1)} %param.7) | copy-start | bytes 3145732
  0.6 19.0 %copy-start.2 = (s32[512]{0:T(512)S(1)}, s32[512]{0:T(512)}, u32[]{:S(2)}) copy-start(s32[512]{0:T(512)} %param.13) | copy-start | bytes 6148
  2.2 20.9 %all-to-all-start = ((s32[128,1,8]{2,1,0:T(1,128)}), s32[128,1,8]{2,1,0:T(1,128)S(1)}, u32[]{:S(2)}, u32[]{:S(2)}) async-start(s32[128,1,8]{2,1,0:T(1,128)} %bitcast), calls=%async_computation | async-start | bytes 131072 | tf_op jit(solution)/shard_map/all_to_all | solution.py:230
  23.2 5.0 %copy-start.1 = (s32[512,8]{0,1:T(8,128)S(1)}, s32[512,8]{0,1:T(8,128)}, u32[]{:S(2)}) copy-start(s32[512,8]{0,1:T(8,128)} %param.10) | copy-start | bytes 49156
  28.2 33.5 %all-to-all-start.1 = ((bf16[128,8,256]{2,1,0:T(8,128)(2,1)}), bf16[128,8,256]{2,1,0:T(8,128)(2,1)S(1)}, u32[]{:S(2)}, u32[]{:S(2)}) async-start(bf16[128,8,256]{2,1,0:T(8,128)(2,1)} %bitcast_select_fusion.1), calls=%async_computation.1 | async-start | bytes 1048576 | tf_op jit(solution)/shard_map/all_to_all | solution.py:233
  57.9 13.4 %collective-permute-start.2 = (bf16[512,256]{1,0:T(8,128)(2,1)S(1)}, bf16[512,256]{1,0:T(8,128)(2,1)}, u32[]{:S(2)}, u32[]{:S(2)}) collective-permute-start(bf16[512,256]{1,0:T(8,128)(2,1)S(1)} %multiply_convert_fusion), channel_id=1, source_target_pairs={{0,24},{8,0},{16,8},{24,16},{32,56},{40,32},{48,40},{56,48},{64,88... | collective-permute-start | bytes 786440 | tf_op jit(solution)/shard_map/ppermute | solution.py:179
  60.6 10.8 %collective-permute-start.1 = (bf16[512,256]{1,0:T(8,128)(2,1)S(1)}, bf16[512,256]{1,0:T(8,128)(2,1)}, u32[]{:S(2)}, u32[]{:S(2)}) collective-permute-start(bf16[512,256]{1,0:T(8,128)(2,1)S(1)} %multiply_convert_fusion), channel_id=1, source_target_pairs={{0,16},{8,24},{16,0},{24,8},{32,48},{40,56},{48,32},{56,40},{64,80... | collective-permute-start | bytes 786440 | tf_op jit(solution)/shard_map/ppermute | solution.py:179
  61.1 14.9 %collective-permute-start = (bf16[512,256]{1,0:T(8,128)(2,1)S(1)}, bf16[512,256]{1,0:T(8,128)(2,1)}, u32[]{:S(2)}, u32[]{:S(2)}) collective-permute-start(bf16[512,256]{1,0:T(8,128)(2,1)S(1)} %multiply_convert_fusion), channel_id=1, source_target_pairs={{0,8},{8,16},{16,24},{24,0},{32,40},{40,48},{48,56},{56,32},{64,72... | collective-permute-start | bytes 786440 | tf_op jit(solution)/shard_map/ppermute | solution.py:179
  63.8 13.8 %collective-permute-start.5 = (bf16[512,256]{1,0:T(8,128)(2,1)S(1)}, bf16[512,256]{1,0:T(8,128)(2,1)S(1)}, u32[]{:S(2)}, u32[]{:S(2)}) collective-permute-start(bf16[512,256]{1,0:T(8,128)(2,1)S(1)} %broadcast_select_fusion), channel_id=1, source_target_pairs={{0,96},{8,104},{16,112},{24,120},{32,0},{40,8},{48,16},{56,24},{64... | collective-permute-start | bytes 786440 | tf_op jit(solution)/shard_map/ppermute | solution.py:179
  66.4 11.2 %collective-permute-start.4 = (bf16[512,256]{1,0:T(8,128)(2,1)S(1)}, bf16[512,256]{1,0:T(8,128)(2,1)S(1)}, u32[]{:S(2)}, u32[]{:S(2)}) collective-permute-start(bf16[512,256]{1,0:T(8,128)(2,1)S(1)} %broadcast_select_fusion), channel_id=1, source_target_pairs={{0,64},{8,72},{16,80},{24,88},{32,96},{40,104},{48,112},{56,120},{... | collective-permute-start | bytes 786440 | tf_op jit(solution)/shard_map/ppermute | solution.py:179
  71.3 10.1 %collective-permute-start.3 = (bf16[512,256]{1,0:T(8,128)(2,1)S(1)}, bf16[512,256]{1,0:T(8,128)(2,1)S(1)}, u32[]{:S(2)}, u32[]{:S(2)}) collective-permute-start(bf16[512,256]{1,0:T(8,128)(2,1)S(1)} %broadcast_select_fusion), channel_id=1, source_target_pairs={{0,32},{8,40},{16,48},{24,56},{32,64},{40,72},{48,80},{56,88},{64,... | collective-permute-start | bytes 786440 | tf_op jit(solution)/shard_map/ppermute | solution.py:179
  87.3 4.2 %collective-permute-start.8 = (f32[2,2048]{1,0:T(2,128)S(1)}, f32[2,2048]{1,0:T(2,128)S(1)}, u32[]{:S(2)}, u32[]{:S(2)}) collective-permute-start(f32[2,2048]{1,0:T(2,128)S(1)} %shard_map.86), channel_id=1, source_target_pairs={{0,24},{8,0},{16,8},{24,16},{32,56},{40,32},{48,40},{56,48},{64,88... | collective-permute-start | bytes 49160 | tf_op jit(solution)/shard_map/ppermute | solution.py:179
  89.0 6.1 %collective-permute-start.7 = (f32[2,2048]{1,0:T(2,128)S(1)}, f32[2,2048]{1,0:T(2,128)S(1)}, u32[]{:S(2)}, u32[]{:S(2)}) collective-permute-start(f32[2,2048]{1,0:T(2,128)S(1)} %shard_map.86), channel_id=1, source_target_pairs={{0,16},{8,24},{16,0},{24,8},{32,48},{40,56},{48,32},{56,40},{64,80... | collective-permute-start | bytes 49160 | tf_op jit(solution)/shard_map/ppermute | solution.py:179
  91.2 3.8 %collective-permute-start.6 = (f32[2,2048]{1,0:T(2,128)S(1)}, f32[2,2048]{1,0:T(2,128)S(1)}, u32[]{:S(2)}, u32[]{:S(2)}) collective-permute-start(f32[2,2048]{1,0:T(2,128)S(1)} %shard_map.86), channel_id=1, source_target_pairs={{0,8},{8,16},{16,24},{24,0},{32,40},{40,48},{48,56},{56,32},{64,72... | collective-permute-start | bytes 49160 | tf_op jit(solution)/shard_map/ppermute | solution.py:179
  107.2 3.3 %collective-permute-start.12 = (f32[128,256]{1,0:T(8,128)S(1)}, f32[128,256]{1,0:T(8,128)S(1)}, u32[]{:S(2)}, u32[]{:S(2)}) collective-permute-start(f32[128,256]{1,0:T(8,128)S(1)} %slice_select_fusion), channel_id=1, source_target_pairs={{0,1},{1,0},{2,3},{3,2},{4,5},{5,4},{6,7},{7,6},{8,9},{9,8},{10,11... | collective-permute-start | bytes 393224 | tf_op jit(solution)/shard_map/ppermute | solution.py:155
  110.5 5.7 %collective-permute-start.13 = (f32[64,256]{1,0:T(8,128)S(1)}, f32[64,256]{1,0:T(8,128)S(1)}, u32[]{:S(2)}, u32[]{:S(2)}) collective-permute-start(f32[64,256]{1,0:T(8,128)S(1)} %slice_select_fusion.1), channel_id=1, source_target_pairs={{0,2},{1,3},{2,0},{3,1},{4,6},{5,7},{6,4},{7,5},{8,10},{9,11},{10,... | collective-permute-start | bytes 196616 | tf_op jit(solution)/shard_map/ppermute | solution.py:155
  113.5 37.5 %collective-permute-start.9 = (f32[512,256]{1,0:T(8,128)S(1)}, f32[512,256]{1,0:T(8,128)S(1)}, u32[]{:S(2)}, u32[]{:S(2)}) collective-permute-start(f32[512,256]{1,0:T(8,128)S(1)} %get-tuple-element.16), channel_id=1, source_target_pairs={{0,32},{8,40},{16,48},{24,56},{32,64},{40,72},{48,80},{56,88},{64,... | collective-permute-start | bytes 1572872 | tf_op jit(solution)/shard_map/ppermute | solution.py:179
  113.5 37.4 %collective-permute-start.11 = (f32[512,256]{1,0:T(8,128)S(1)}, f32[512,256]{1,0:T(8,128)S(1)}, u32[]{:S(2)}, u32[]{:S(2)}) collective-permute-start(f32[512,256]{1,0:T(8,128)S(1)} %get-tuple-element.17), channel_id=1, source_target_pairs={{0,96},{8,104},{16,112},{24,120},{32,0},{40,8},{48,16},{56,24},{64... | collective-permute-start | bytes 1572872 | tf_op jit(solution)/shard_map/ppermute | solution.py:179
  116.2 34.8 %collective-permute-start.10 = (f32[512,256]{1,0:T(8,128)S(1)}, f32[512,256]{1,0:T(8,128)S(1)}, u32[]{:S(2)}, u32[]{:S(2)}) collective-permute-start(f32[512,256]{1,0:T(8,128)S(1)} %get-tuple-element.18), channel_id=1, source_target_pairs={{0,64},{8,72},{16,80},{24,88},{32,96},{40,104},{48,112},{56,120},{... | collective-permute-start | bytes 1572872 | tf_op jit(solution)/shard_map/ppermute | solution.py:179
  116.2 4.7 %collective-permute-start.14 = (f32[64,256]{1,0:T(8,128)S(1)}, f32[64,256]{1,0:T(8,128)S(1)}, u32[]{:S(2)}, u32[]{:S(2)}) collective-permute-start(f32[64,256]{1,0:T(8,128)S(1)} %select_add_fusion.1), channel_id=1, source_target_pairs={{0,4},{1,5},{2,6},{3,7},{4,0},{5,1},{6,2},{7,3},{8,12},{9,13},{10,... | collective-permute-start | bytes 196616 | tf_op jit(solution)/shard_map/ppermute | solution.py:159
  120.9 3.5 %collective-permute-start.15 = (f32[64,256]{1,0:T(8,128)S(1)}, f32[64,256]{1,0:T(8,128)S(1)}, u32[]{:S(2)}, u32[]{:S(2)}) collective-permute-start(f32[64,256]{1,0:T(8,128)S(1)} %add.133), channel_id=1, source_target_pairs={{0,8},{1,9},{2,10},{3,11},{4,12},{5,13},{6,14},{7,15},{8,0},{9,1},... | collective-permute-start | bytes 196616 | tf_op jit(solution)/shard_map/ppermute | solution.py:159
  124.4 5.0 %collective-permute-start.16 = (f32[64,256]{1,0:T(8,128)S(1)}, f32[64,256]{1,0:T(8,128)S(1)}, u32[]{:S(2)}, u32[]{:S(2)}) collective-permute-start(f32[64,256]{1,0:T(8,128)S(1)} %add.134), channel_id=1, source_target_pairs={{0,16},{1,17},{2,18},{3,19},{4,20},{5,21},{6,22},{7,23},{8,24},{9,... | collective-permute-start | bytes 196616 | tf_op jit(solution)/shard_map/ppermute | solution.py:159
  129.5 9.7 %collective-permute-start.17 = (f32[64,256]{1,0:T(8,128)S(1)}, f32[64,256]{1,0:T(8,128)S(1)}, u32[]{:S(2)}, u32[]{:S(2)}) collective-permute-start(f32[64,256]{1,0:T(8,128)S(1)} %add.135), channel_id=1, source_target_pairs={{0,32},{1,33},{2,34},{3,35},{4,36},{5,37},{6,38},{7,39},{8,40},{9,... | collective-permute-start | bytes 196616 | tf_op jit(solution)/shard_map/ppermute | solution.py:159
  139.2 4.7 %collective-permute-start.18 = (f32[64,256]{1,0:T(8,128)S(1)}, f32[64,256]{1,0:T(8,128)S(1)}, u32[]{:S(2)}, u32[]{:S(2)}) collective-permute-start(f32[64,256]{1,0:T(8,128)S(1)} %add.136), channel_id=1, source_target_pairs={{0,64},{1,65},{2,66},{3,67},{4,68},{5,69},{6,70},{7,71},{8,72},{9,... | collective-permute-start | bytes 196616 | tf_op jit(solution)/shard_map/ppermute | solution.py:159
  143.9 3.2 %collective-permute-start.19 = (f32[64,256]{1,0:T(8,128)S(1)}, f32[64,256]{1,0:T(8,128)S(1)}, u32[]{:S(2)}, u32[]{:S(2)}) collective-permute-start(f32[64,256]{1,0:T(8,128)S(1)} %add.137), channel_id=1, source_target_pairs={{0,2},{1,3},{2,0},{3,1},{4,6},{5,7},{6,4},{7,5},{8,10},{9,11},{10,... | collective-permute-start | bytes 196616 | tf_op jit(solution)/shard_map/ppermute | solution.py:163
  147.1 5.1 %collective-permute-start.20 = (f32[128,256]{1,0:T(8,128)S(1)}, f32[128,256]{1,0:T(8,128)S(1)}, u32[]{:S(2)}, u32[]{:S(2)}) collective-permute-start(f32[128,256]{1,0:T(8,128)S(1)} %maximum_select_fusion.1), channel_id=1, source_target_pairs={{0,1},{1,0},{2,3},{3,2},{4,5},{5,4},{6,7},{7,6},{8,9},{9,8},{10,11... | collective-permute-start | bytes 393224 | tf_op jit(solution)/shard_map/ppermute | solution.py:163
  155.0 26.1 %all-to-all-start.2 = ((f32[128,8,256]{2,1,0:T(8,128)}), f32[128,8,256]{2,1,0:T(8,128)S(1)}, u32[]{:S(2)}, u32[]{:S(2)}) async-start(f32[128,8,256]{2,1,0:T(8,128)} %fusion.3), calls=%async_computation.2 | async-start | bytes 2097152 | tf_op jit(solution)/shard_map/all_to_all | solution.py:277

commit v16 on v15

--- a/solution.py
+++ b/solution.py
@@ -52,7 +52,7 @@
     stats_ref[1:2, :] = jnp.sum(jnp.exp(scores - highest), axis=0, keepdims=True)
 
 
-def block_stats(queries, items, scaling, tile=1024):
+def block_stats(queries, items, scaling, tile=2048):
     rows, width = queries.shape
     tile = tile if rows % tile == 0 else rows
     return pl.pallas_call(
@@ -84,7 +84,7 @@
         pushed_ref[...] += part
 
 
-def block_grads_k(queries, items, totals, scaling, tile=1024):
+def block_grads_k(queries, items, totals, scaling, tile=2048):
     rows, width = queries.shape
     tile = tile if rows % tile == 0 else rows
     return pl.pallas_call(
@@ -264,7 +264,7 @@
         )
     total = lax.axis_size("batch") * lax.axis_size("table")
     if total & (total - 1) == 0:
-        weight_grad = tree_sum(partial_value, ("batch", "table"), min(4, lax.axis_size("table")))
+        weight_grad = tree_sum(partial_value, ("batch", "table"), min(2, lax.axis_size("table")))
     else:
         weight_grad = lax.psum(partial_value, ("batch", "table"))
     item_grad, weight_grad = lax.optimization_barrier((item_grad, weight_grad))

time: 187 us -> 191 us (1.021)
  waiting for transfers between devices: 61.9 us -> 70.5 us
  matrix products: 11.8 us -> 9.57 us
    ppermute x5 -> x6, waiting for transfers between devices: 20.5 us -> 30.1 us  [tree_sum(): lax.ppermute(value, axes, [(i, i ^ step) for i in range(total)])]
    ppermute x2 -> x1, waiting for transfers between devices: 3.09 us -> 0.81 us  [tree_sum(): got = lax.ppermute(value, axes, [(i, i ^ step) for i in range(total)])]
    ppermute x5 -> x6, starting transfers between devices: 7.02 us -> 8.62 us  [tree_sum(): lax.ppermute(value, axes, [(i, i ^ step) for i in range(total)])]
    ppermute x2 -> x1, starting transfers between devices: 3.98 us -> 4.19 us  [tree_sum(): got = lax.ppermute(value, axes, [(i, i ^ step) for i in range(total)])]
  transfers between devices with their start and end apart: 24 -> 23, of which waited for: 13 -> 14; matrix products, arithmetic and copies ran while one was open for 20% -> 18% of each run, Pallas kernels for 0% -> 0%
where the time goes in v16:
time: 191 us; the launch traced here: 190 us
  waiting for transfers between devices  70.5 us (37%)
  starting transfers between devices  54.6 us (29%)
  local copies, waits for them, and re-layouts  31.5 us (16%)
  Pallas kernels  14.2 us (7%)
  matrix products  9.57 us (5%)
  other arithmetic  9.11 us (5%)
    ppermute x6, waiting for transfers between devices, tree_sum(): lax.ppermute(value, axes, [(i, i ^ step) for i in range(total)])  30.1 us
    gather x1, local copies, waits for them, and re-layouts, step_body(): looked = jnp.take(query_table, query_ids, axis=0).astype(jnp.float32)  18.7 us
    all_to_all x1, waiting for transfers between devices, step_body(): lax.all_to_all(slot_grads, ('batch', 'table'), split_axis=0, concat_axis=...  17.7 us
    ppermute x12, waiting for transfers between devices, plane_shift(): return lax.ppermute(value, axis, pairs)  17.6 us
    ppermute x12, starting transfers between devices, plane_shift(): return lax.ppermute(value, axis, pairs)  13.3 us
    all_to_all x1, starting transfers between devices, step_body(): lax.all_to_all(requests, ('batch', 'table'), split_axis=0, concat_axis=0,...  11.5 us
    pallas_call x1, Pallas kernels, block_grads_k(): pl.pallas_call(functools.partial(grads_block, scaling=scaling), grid=(row...  8.89 us
    ppermute x6, starting transfers between devices, tree_sum(): lax.ppermute(value, axes, [(i, i ^ step) for i in range(total)])  8.62 us
  transfers between devices with their start and end apart: 23, of which 14 were waited for; matrix products, arithmetic and copies ran while one was open for 18% of the time, Pallas kernels for 0%

profile of v16, /device:TPU:1, one launch (start us, length us, event | category | flops | bytes accessed | tf_op | source)
XLA Modules:
  0.0 190.5 jit_solution(18323236474002179913)
XLA Ops:
  0.7 1.5 copy.22
  2.2 11.5 %all-to-all-start = ((s32[128,1,8]{2,1,0:T(1,128)}), s32[128,1,8]{2,1,0:T(1,128)S(1)}, u32[]{:S(2)}, u32[]{:S(2)}) async-start(s32[128,1,8]{2,1,0:T(1,128)} %bitcast), calls=%async_computation | async-start | bytes 131072 | tf_op jit(solution)/shard_map/all_to_all | solution.py:230
  13.7 0.8 copy.23
  14.4 0.2 reduce-window.8
  14.6 0.1 reduce.1
  14.7 0.7 bitcast_subtract_fusion
  15.4 0.9 convert_reduce_fusion.1
  16.3 3.3 %gather_fusion = s32[512]{0:T(512)S(1)} fusion(s32[128]{0:T(128)S(1)} %bitcast_subtract_fusion, s32[1024]{0:T(1024)S(1)} %pad_clamp_fusion.1), kind=kCustom, calls=%fused_computation | custom fusion | bytes 6144 | tf_op jit(solution)/shard_map/jit(_take)/gather | solution.py:139
  19.7 3.3 %all-to-all-done = s32[128,1,8]{2,1,0:T(1,128)S(1)} async-done(((s32[128,1,8]{2,1,0:T(1,128)}), s32[128,1,8]{2,1,0:T(1,128)S(1)}, u32[]{:S(2)}, u32[]{:S(2)}) %all-to-all-start) | async-done | bytes 4128 | tf_op jit(solution)/shard_map/all_to_all | solution.py:230
  23.1 0.1 reshape.128
  23.2 3.9 %gather_fusion.1 = bf16[1024,256]{1,0:T(8,128)(2,1)S(1)} fusion(bf16[2048,256]{1,0:T(8,128)(2,1)S(1)} %copy-done, s32[1024]{0:T(1024)S(1)} %broadcast_clamp_fusion.1), kind=kCustom, calls=%fused_computation.1 | custom fusion | bytes 1052672 | tf_op jit(solution)/shard_map/jit(_take)/gather | solution.py:231
  27.1 1.0 bitcast_select_fusion.1
  28.2 6.5 %all-to-all-start.1 = ((bf16[128,8,256]{2,1,0:T(8,128)(2,1)}), bf16[128,8,256]{2,1,0:T(8,128)(2,1)S(1)}, u32[]{:S(2)}, u32[]{:S(2)}) async-start(bf16[128,8,256]{2,1,0:T(8,128)(2,1)} %bitcast_select_fusion.1), calls=%async_computation.1 | async-start | bytes 1048576 | tf_op jit(solution)/shard_map/all_to_all | solution.py:233
  34.6 0.2 copy.24
  34.8 0.1 copy.25
  34.9 0.2 reshape.136
  35.1 18.7 %gather_fusion.2 = bf16[4096,256]{1,0:T(8,128)(2,1)} fusion(bf16[8192,256]{1,0:T(8,128)(2,1)} %param.8, s32[4096]{0:T(1024)S(1)} %broadcast_clamp_fusion), kind=kCustom, calls=%fused_computation.2 | custom fusion | bytes 4210688 | tf_op jit(solution)/shard_map/jit(_take)/gather | solution.py:238
  53.8 4.1 %convert_reduce_fusion = f32[512,256]{1,0:T(8,128)S(1)} fusion(bf16[4096,256]{1,0:T(8,128)(2,1)} %gather_fusion.2, pred[512,8]{1,0:T(8,128)(4,1)S(1)} %copy.24), kind=kLoop, calls=%fused_computation.6 | loop fusion | flops 3014656 | bytes 2625536 | tf_op jit(solution)/shard_map/reduce_sum | solution.py:239
  57.9 2.6 %collective-permute-start.2 = (bf16[512,256]{1,0:T(8,128)(2,1)S(1)}, bf16[512,256]{1,0:T(8,128)(2,1)S(1)}, u32[]{:S(2)}, u32[]{:S(2)}) collective-permute-start(bf16[512,256]{1,0:T(8,128)(2,1)S(1)} %multiply_convert_fusion), channel_id=1, source_target_pairs={{0,24},{8,0},{16,8},{24,16},{32,56},{40,32},{48,40},{56,48},{64,88... | collective-permute-start | bytes 786440 | tf_op jit(solution)/shard_map/ppermute | solution.py:179
  60.6 0.6 collective-permute-start.1
  61.1 0.6 collective-permute-start
  61.7 2.0 %gather_fusion.3 = bf16[512,256]{1,0:T(8,128)(2,1)S(1)} fusion(bf16[1024,256]{1,0:T(8,128)(2,1)S(1)} %bitcast.27, s32[1024]{0:T(1024)S(1)} %pad_clamp_fusion), kind=kCustom, calls=%fused_computation.3 | custom fusion | bytes 526336 | tf_op jit(solution)/shard_map/jit(_take)/gather | solution.py:237
  63.7 0.1 broadcast_select_fusion
  63.8 2.6 %collective-permute-start.5 = (bf16[512,256]{1,0:T(8,128)(2,1)S(1)}, bf16[512,256]{1,0:T(8,128)(2,1)S(1)}, u32[]{:S(2)}, u32[]{:S(2)}) collective-permute-start(bf16[512,256]{1,0:T(8,128)(2,1)S(1)} %broadcast_select_fusion), channel_id=1, source_target_pairs={{0,96},{8,104},{16,112},{24,120},{32,0},{40,8},{48,16},{56,24},{64... | collective-permute-start | bytes 786440 | tf_op jit(solution)/shard_map/ppermute | solution.py:179
  66.4 0.5 collective-permute-start.4
  66.9 4.4 %collective-permute-done.2 = bf16[512,256]{1,0:T(8,128)(2,1)S(1)} collective-permute-done((bf16[512,256]{1,0:T(8,128)(2,1)S(1)}, bf16[512,256]{1,0:T(8,128)(2,1)S(1)}, u32[]{:S(2)}, u32[]{:S(2)}) %collective-permute-start.2) | collective-permute-done | bytes 262176 | tf_op jit(solution)/shard_map/ppermute | solution.py:179
  71.3 4.6 %collective-permute-done = bf16[512,256]{1,0:T(8,128)(2,1)S(1)} collective-permute-done((bf16[512,256]{1,0:T(8,128)(2,1)S(1)}, bf16[512,256]{1,0:T(8,128)(2,1)S(1)}, u32[]{:S(2)}, u32[]{:S(2)}) %collective-permute-start) | collective-permute-done | bytes 262176 | tf_op jit(solution)/shard_map/ppermute | solution.py:179
  75.9 0.4 convolution_convert_fusion.q_ref
  76.4 5.0 %collective-permute-done.3 = bf16[512,256]{1,0:T(8,128)(2,1)S(1)} collective-permute-done((bf16[512,256]{1,0:T(8,128)(2,1)S(1)}, bf16[512,256]{1,0:T(8,128)(2,1)S(1)}, u32[]{:S(2)}, u32[]{:S(2)}) %collective-permute-start.3) | collective-permute-done | bytes 262176 | tf_op jit(solution)/shard_map/ppermute | solution.py:179
  81.5 5.3 %shard_map.86 = f32[2,2048]{1,0:T(2,128)S(1)} custom-call(bf16[2048,256]{1,0:T(8,128)(2,1)S(1)} %convolution_convert_fusion.q_ref, bf16[2048,256]{1,0:T(8,128)(2,1)S(1)} %pad_maximum_fusion.1.items_ref), custom_call_target="tpu_custom_call" | custom-call | tf_op jit(solution)/shard_map/pallas_call | solution.py:58
  86.8 1.4 collective-permute-start.8
  88.1 2.4 %collective-permute-start.7 = (f32[2,2048]{1,0:T(2,128)S(1)}, f32[2,2048]{1,0:T(2,128)S(1)}, u32[]{:S(2)}, u32[]{:S(2)}) collective-permute-start(f32[2,2048]{1,0:T(2,128)S(1)} %shard_map.86), channel_id=1, source_target_pairs={{0,16},{8,24},{16,0},{24,8},{32,48},{40,56},{48,32},{56,40},{64,80... | collective-permute-start | bytes 49160 | tf_op jit(solution)/shard_map/ppermute | solution.py:179
  90.5 0.3 fusion.20
  90.8 3.5 %collective-permute-done.6 = f32[2,2048]{1,0:T(2,128)S(1)} collective-permute-done((f32[2,2048]{1,0:T(2,128)S(1)}, f32[2,2048]{1,0:T(2,128)S(1)}, u32[]{:S(2)}, u32[]{:S(2)}) %collective-permute-start.6) | collective-permute-done | bytes 16416 | tf_op jit(solution)/shard_map/ppermute | solution.py:179
  94.3 0.1 log_add_fusion.totals_ref
  94.4 8.9 %shard_map.87 = (f32[2048,256]{1,0:T(8,128)S(1)}, f32[2048,256]{1,0:T(8,128)}) custom-call(bf16[2048,256]{1,0:T(8,128)(2,1)S(1)} %convolution_convert_fusion.q_ref, bf16[2048,256]{1,0:T(8,128)(2,1)S(1)} %pad_maximum_fusion.1.items_ref, f32[1,2048]{1,0:T(1,128)S(1)} %log_add_fusion.totals_ref), custom_call_target="tpu_custom_call" | custom-call | tf_op jit(solution)/shard_map/pallas_call | solution.py:90
  103.3 1.5 fusion.4
  104.8 2.3 %collective-permute-start.12 = (f32[128,256]{1,0:T(8,128)S(1)}, f32[128,256]{1,0:T(8,128)S(1)}, u32[]{:S(2)}, u32[]{:S(2)}) collective-permute-start(f32[128,256]{1,0:T(8,128)S(1)} %slice_select_fusion), channel_id=1, source_target_pairs={{0,1},{1,0},{2,3},{3,2},{4,5},{5,4},{6,7},{7,6},{8,9},{9,8},{10,11... | collective-permute-start | bytes 393224 | tf_op jit(solution)/shard_map/ppermute | solution.py:155
  107.1 1.0 collective-permute-done.12
  108.1 1.5 collective-permute-start.13
  109.7 3.2 %collective-permute-done.13 = f32[128,256]{1,0:T(8,128)S(1)} collective-permute-done((f32[128,256]{1,0:T(8,128)S(1)}, f32[128,256]{1,0:T(8,128)S(1)}, u32[]{:S(2)}, u32[]{:S(2)}) %collective-permute-start.13) | collective-permute-done | bytes 131104 | tf_op jit(solution)/shard_map/ppermute | solution.py:159
  112.9 3.3 %collective-permute-start.14 = (f32[128,256]{1,0:T(8,128)S(1)}, f32[128,256]{1,0:T(8,128)S(1)}, u32[]{:S(2)}, u32[]{:S(2)}) collective-permute-start(f32[128,256]{1,0:T(8,128)S(1)} %add.132), channel_id=1, source_target_pairs={{0,4},{1,5},{2,6},{3,7},{4,0},{5,1},{6,2},{7,3},{8,12},{9,13},{10,... | collective-permute-start | bytes 393224 | tf_op jit(solution)/shard_map/ppermute | solution.py:159
  116.2 2.4 %collective-permute-done.14 = f32[128,256]{1,0:T(8,128)S(1)} collective-permute-done((f32[128,256]{1,0:T(8,128)S(1)}, f32[128,256]{1,0:T(8,128)S(1)}, u32[]{:S(2)}, u32[]{:S(2)}) %collective-permute-start.14) | collective-permute-done | bytes 131104 | tf_op jit(solution)/shard_map/ppermute | solution.py:159
  118.6 0.1 collective-permute-start.15
  118.7 0.1 fusion.18
  118.9 2.7 %collective-permute-start.11 = (f32[512,256]{1,0:T(8,128)S(1)}, f32[512,256]{1,0:T(8,128)S(1)}, u32[]{:S(2)}, u32[]{:S(2)}) collective-permute-start(f32[512,256]{1,0:T(8,128)S(1)} %get-tuple-element.17), channel_id=1, source_target_pairs={{0,96},{8,104},{16,112},{24,120},{32,0},{40,8},{48,16},{56,24},{64... | collective-permute-start | bytes 1572872 | tf_op jit(solution)/shard_map/ppermute | solution.py:179
  121.6 0.9 collective-permute-done.15
  122.5 1.0 collective-permute-start.16
  123.5 4.4 %collective-permute-done.16 = f32[128,256]{1,0:T(8,128)S(1)} collective-permute-done((f32[128,256]{1,0:T(8,128)S(1)}, f32[128,256]{1,0:T(8,128)S(1)}, u32[]{:S(2)}, u32[]{:S(2)}) %collective-permute-start.16) | collective-permute-done | bytes 131104 | tf_op jit(solution)/shard_map/ppermute | solution.py:159
  128.0 0.3 collective-permute-start.17
  128.3 16.1 %collective-permute-done.17 = f32[128,256]{1,0:T(8,128)S(1)} collective-permute-done((f32[128,256]{1,0:T(8,128)S(1)}, f32[128,256]{1,0:T(8,128)S(1)}, u32[]{:S(2)}, u32[]{:S(2)}) %collective-permute-start.17) | collective-permute-done | bytes 131104 | tf_op jit(solution)/shard_map/ppermute | solution.py:159
  144.5 2.3 %collective-permute-start.18 = (f32[128,256]{1,0:T(8,128)S(1)}, f32[128,256]{1,0:T(8,128)S(1)}, u32[]{:S(2)}, u32[]{:S(2)}) collective-permute-start(f32[128,256]{1,0:T(8,128)S(1)} %add.136), channel_id=1, source_target_pairs={{0,64},{1,65},{2,66},{3,67},{4,68},{5,69},{6,70},{7,71},{8,72},{9,... | collective-permute-start | bytes 393224 | tf_op jit(solution)/shard_map/ppermute | solution.py:159
  146.8 3.1 %collective-permute-done.18 = f32[128,256]{1,0:T(8,128)S(1)} collective-permute-done((f32[128,256]{1,0:T(8,128)S(1)}, f32[128,256]{1,0:T(8,128)S(1)}, u32[]{:S(2)}, u32[]{:S(2)}) %collective-permute-start.18) | collective-permute-done | bytes 131104 | tf_op jit(solution)/shard_map/ppermute | solution.py:159
  149.9 4.2 %collective-permute-start.19 = (f32[128,256]{1,0:T(8,128)S(1)}, f32[128,256]{1,0:T(8,128)S(1)}, u32[]{:S(2)}, u32[]{:S(2)}) collective-permute-start(f32[128,256]{1,0:T(8,128)S(1)} %add.137), channel_id=1, source_target_pairs={{0,1},{1,0},{2,3},{3,2},{4,5},{5,4},{6,7},{7,6},{8,9},{9,8},{10,11... | collective-permute-start | bytes 393224 | tf_op jit(solution)/shard_map/ppermute | solution.py:163
  154.1 0.2 subtract_multiply_fusion
  154.3 0.8 collective-permute-done.19
  155.1 0.7 maximum_select_fusion
  155.8 2.1 %fusion.3 = f32[128,8,256]{2,1,0:T(8,128)} fusion(f32[512,256]{1,0:T(8,128)S(1)} %subtract_multiply_fusion, s32[512]{0:T(512)S(1)} %get-tuple-element.15), kind=kOutput, calls=%fused_computation.12 | convolution fusion | flops 1611137024 | bytes 1574912 | tf_op jit(solution)/shard_map/dot_general | solution.py:272
  157.9 8.2 %all-to-all-start.2 = ((f32[128,8,256]{2,1,0:T(8,128)}), f32[128,8,256]{2,1,0:T(8,128)S(1)}, u32[]{:S(2)}, u32[]{:S(2)}) async-start(f32[128,8,256]{2,1,0:T(8,128)} %fusion.3), calls=%async_computation.2 | async-start | bytes 2097152 | tf_op jit(solution)/shard_map/all_to_all | solution.py:277
  166.1 0.5 broadcast.77
  166.6 0.7 reduce.4
  167.4 0.1 eq.18
  167.5 17.7 %all-to-all-done.2 = f32[128,8,256]{2,1,0:T(8,128)S(1)} async-done(((f32[128,8,256]{2,1,0:T(8,128)}), f32[128,8,256]{2,1,0:T(8,128)S(1)}, u32[]{:S(2)}, u32[]{:S(2)}) %all-to-all-start.2) | async-done | bytes 1048608 | tf_op jit(solution)/shard_map/all_to_all | solution.py:277
  185.1 5.3 %fusion = f32[2048,256]{1,0:T(8,128)} fusion(s32[1024]{0:T(1024)S(1)} %eq.18, f32[128,8,256]{2,1,0:T(8,128)S(1)} %all-to-all-done.2), kind=kOutput, calls=%fused_computation.5 | convolution fusion | flops 6444548096 | bytes 3149824 | tf_op jit(solution)/shard_map/dot_general | solution.py:283
  (49 shorter events, 0.5 us)
Async XLA Ops:
  0.6 22.5 %copy-start = (bf16[2048,256]{1,0:T(8,128)(2,1)S(1)}, bf16[2048,256]{1,0:T(8,128)(2,1)}, u32[]{:S(2)}) copy-start(bf16[2048,256]{1,0:T(8,128)(2,1)} %param.7) | copy-start | bytes 3145732
  0.6 19.0 %copy-start.3 = (s32[512]{0:T(512)S(1)}, s32[512]{0:T(512)}, u32[]{:S(2)}) copy-start(s32[512]{0:T(512)} %param.13) | copy-start | bytes 6148
  2.2 20.9 %all-to-all-start = ((s32[128,1,8]{2,1,0:T(1,128)}), s32[128,1,8]{2,1,0:T(1,128)S(1)}, u32[]{:S(2)}, u32[]{:S(2)}) async-start(s32[128,1,8]{2,1,0:T(1,128)} %bitcast), calls=%async_computation | async-start | bytes 131072 | tf_op jit(solution)/shard_map/all_to_all | solution.py:230
  23.2 5.0 %copy-start.2 = (s32[512,8]{0,1:T(8,128)S(1)}, s32[512,8]{0,1:T(8,128)}, u32[]{:S(2)}) copy-start(s32[512,8]{0,1:T(8,128)} %param.10) | copy-start | bytes 49156
  28.2 33.6 %all-to-all-start.1 = ((bf16[128,8,256]{2,1,0:T(8,128)(2,1)}), bf16[128,8,256]{2,1,0:T(8,128)(2,1)S(1)}, u32[]{:S(2)}, u32[]{:S(2)}) async-start(bf16[128,8,256]{2,1,0:T(8,128)(2,1)} %bitcast_select_fusion.1), calls=%async_computation.1 | async-start | bytes 1048576 | tf_op jit(solution)/shard_map/all_to_all | solution.py:233
  57.9 18.0 %copy-start.4 = (bf16[256,256]{1,0:T(8,128)(2,1)S(1)}, bf16[256,256]{1,0:T(8,128)(2,1)}, u32[]{:S(2)}) copy-start(bf16[256,256]{1,0:T(8,128)(2,1)} %param.9) | copy-start | bytes 393220
  57.9 13.4 %collective-permute-start.2 = (bf16[512,256]{1,0:T(8,128)(2,1)S(1)}, bf16[512,256]{1,0:T(8,128)(2,1)S(1)}, u32[]{:S(2)}, u32[]{:S(2)}) collective-permute-start(bf16[512,256]{1,0:T(8,128)(2,1)S(1)} %multiply_convert_fusion), channel_id=1, source_target_pairs={{0,24},{8,0},{16,8},{24,16},{32,56},{40,32},{48,40},{56,48},{64,88... | collective-permute-start | bytes 786440 | tf_op jit(solution)/shard_map/ppermute | solution.py:179
  60.6 10.8 %collective-permute-start.1 = (bf16[512,256]{1,0:T(8,128)(2,1)S(1)}, bf16[512,256]{1,0:T(8,128)(2,1)S(1)}, u32[]{:S(2)}, u32[]{:S(2)}) collective-permute-start(bf16[512,256]{1,0:T(8,128)(2,1)S(1)} %multiply_convert_fusion), channel_id=1, source_target_pairs={{0,16},{8,24},{16,0},{24,8},{32,48},{40,56},{48,32},{56,40},{64,80... | collective-permute-start | bytes 786440 | tf_op jit(solution)/shard_map/ppermute | solution.py:179
  61.1 14.8 %collective-permute-start = (bf16[512,256]{1,0:T(8,128)(2,1)S(1)}, bf16[512,256]{1,0:T(8,128)(2,1)S(1)}, u32[]{:S(2)}, u32[]{:S(2)}) collective-permute-start(bf16[512,256]{1,0:T(8,128)(2,1)S(1)} %multiply_convert_fusion), channel_id=1, source_target_pairs={{0,8},{8,16},{16,24},{24,0},{32,40},{40,48},{48,56},{56,32},{64,72... | collective-permute-start | bytes 786440 | tf_op jit(solution)/shard_map/ppermute | solution.py:179
  63.8 12.5 %collective-permute-start.5 = (bf16[512,256]{1,0:T(8,128)(2,1)S(1)}, bf16[512,256]{1,0:T(8,128)(2,1)S(1)}, u32[]{:S(2)}, u32[]{:S(2)}) collective-permute-start(bf16[512,256]{1,0:T(8,128)(2,1)S(1)} %broadcast_select_fusion), channel_id=1, source_target_pairs={{0,96},{8,104},{16,112},{24,120},{32,0},{40,8},{48,16},{56,24},{64... | collective-permute-start | bytes 786440 | tf_op jit(solution)/shard_map/ppermute | solution.py:179
  66.4 10.0 %collective-permute-start.4 = (bf16[512,256]{1,0:T(8,128)(2,1)S(1)}, bf16[512,256]{1,0:T(8,128)(2,1)S(1)}, u32[]{:S(2)}, u32[]{:S(2)}) collective-permute-start(bf16[512,256]{1,0:T(8,128)(2,1)S(1)} %broadcast_select_fusion), channel_id=1, source_target_pairs={{0,64},{8,72},{16,80},{24,88},{32,96},{40,104},{48,112},{56,120},{... | collective-permute-start | bytes 786440 | tf_op jit(solution)/shard_map/ppermute | solution.py:179
  71.3 10.1 %collective-permute-start.3 = (bf16[512,256]{1,0:T(8,128)(2,1)S(1)}, bf16[512,256]{1,0:T(8,128)(2,1)S(1)}, u32[]{:S(2)}, u32[]{:S(2)}) collective-permute-start(bf16[512,256]{1,0:T(8,128)(2,1)S(1)} %broadcast_select_fusion), channel_id=1, source_target_pairs={{0,32},{8,40},{16,48},{24,56},{32,64},{40,72},{48,80},{56,88},{64,... | collective-permute-start | bytes 786440 | tf_op jit(solution)/shard_map/ppermute | solution.py:179
  86.8 4.0 %collective-permute-start.8 = (f32[2,2048]{1,0:T(2,128)S(1)}, f32[2,2048]{1,0:T(2,128)S(1)}, u32[]{:S(2)}, u32[]{:S(2)}) collective-permute-start(f32[2,2048]{1,0:T(2,128)S(1)} %shard_map.86), channel_id=1, source_target_pairs={{0,24},{8,0},{16,8},{24,16},{32,56},{40,32},{48,40},{56,48},{64,88... | collective-permute-start | bytes 49160 | tf_op jit(solution)/shard_map/ppermute | solution.py:179
  88.1 6.2 %collective-permute-start.7 = (f32[2,2048]{1,0:T(2,128)S(1)}, f32[2,2048]{1,0:T(2,128)S(1)}, u32[]{:S(2)}, u32[]{:S(2)}) collective-permute-start(f32[2,2048]{1,0:T(2,128)S(1)} %shard_map.86), channel_id=1, source_target_pairs={{0,16},{8,24},{16,0},{24,8},{32,48},{40,56},{48,32},{56,40},{64,80... | collective-permute-start | bytes 49160 | tf_op jit(solution)/shard_map/ppermute | solution.py:179
  90.5 3.8 %collective-permute-start.6 = (f32[2,2048]{1,0:T(2,128)S(1)}, f32[2,2048]{1,0:T(2,128)S(1)}, u32[]{:S(2)}, u32[]{:S(2)}) collective-permute-start(f32[2,2048]{1,0:T(2,128)S(1)} %shard_map.86), channel_id=1, source_target_pairs={{0,8},{8,16},{16,24},{24,0},{32,40},{40,48},{48,56},{56,32},{64,72... | collective-permute-start | bytes 49160 | tf_op jit(solution)/shard_map/ppermute | solution.py:179
  103.3 15.4 %copy-start.1 = (f32[2048,256]{1,0:T(8,128)S(1)}, f32[2048,256]{1,0:T(8,128)}, u32[]{:S(2)}) copy-start(f32[2048,256]{1,0:T(8,128)} %get-tuple-element.10) | copy-start | bytes 6291460
  104.8 3.3 %collective-permute-start.12 = (f32[128,256]{1,0:T(8,128)S(1)}, f32[128,256]{1,0:T(8,128)S(1)}, u32[]{:S(2)}, u32[]{:S(2)}) collective-permute-start(f32[128,256]{1,0:T(8,128)S(1)} %slice_select_fusion), channel_id=1, source_target_pairs={{0,1},{1,0},{2,3},{3,2},{4,5},{5,4},{6,7},{7,6},{8,9},{9,8},{10,11... | collective-permute-start | bytes 393224 | tf_op jit(solution)/shard_map/ppermute | solution.py:155
  108.1 4.8 %collective-permute-start.13 = (f32[128,256]{1,0:T(8,128)S(1)}, f32[128,256]{1,0:T(8,128)S(1)}, u32[]{:S(2)}, u32[]{:S(2)}) collective-permute-start(f32[128,256]{1,0:T(8,128)S(1)} %select_add_fusion), channel_id=1, source_target_pairs={{0,2},{1,3},{2,0},{3,1},{4,6},{5,7},{6,4},{7,5},{8,10},{9,11},{10,... | collective-permute-start | bytes 393224 | tf_op jit(solution)/shard_map/ppermute | solution.py:159
  112.9 5.7 %collective-permute-start.14 = (f32[128,256]{1,0:T(8,128)S(1)}, f32[128,256]{1,0:T(8,128)S(1)}, u32[]{:S(2)}, u32[]{:S(2)}) collective-permute-start(f32[128,256]{1,0:T(8,128)S(1)} %add.132), channel_id=1, source_target_pairs={{0,4},{1,5},{2,6},{3,7},{4,0},{5,1},{6,2},{7,3},{8,12},{9,13},{10,... | collective-permute-start | bytes 393224 | tf_op jit(solution)/shard_map/ppermute | solution.py:159
  118.6 3.9 %collective-permute-start.15 = (f32[128,256]{1,0:T(8,128)S(1)}, f32[128,256]{1,0:T(8,128)S(1)}, u32[]{:S(2)}, u32[]{:S(2)}) collective-permute-start(f32[128,256]{1,0:T(8,128)S(1)} %add.133), channel_id=1, source_target_pairs={{0,8},{1,9},{2,10},{3,11},{4,12},{5,13},{6,14},{7,15},{8,0},{9,1},... | collective-permute-start | bytes 393224 | tf_op jit(solution)/shard_map/ppermute | solution.py:159
  118.8 35.3 %collective-permute-start.9 = (f32[512,256]{1,0:T(8,128)S(1)}, f32[512,256]{1,0:T(8,128)S(1)}, u32[]{:S(2)}, u32[]{:S(2)}) collective-permute-start(f32[512,256]{1,0:T(8,128)S(1)} %get-tuple-element.16), channel_id=1, source_target_pairs={{0,32},{8,40},{16,48},{24,56},{32,64},{40,72},{48,80},{56,88},{64,... | collective-permute-start | bytes 1572872 | tf_op jit(solution)/shard_map/ppermute | solution.py:179
  118.9 35.2 %collective-permute-start.11 = (f32[512,256]{1,0:T(8,128)S(1)}, f32[512,256]{1,0:T(8,128)S(1)}, u32[]{:S(2)}, u32[]{:S(2)}) collective-permute-start(f32[512,256]{1,0:T(8,128)S(1)} %get-tuple-element.17), channel_id=1, source_target_pairs={{0,96},{8,104},{16,112},{24,120},{32,0},{40,8},{48,16},{56,24},{64... | collective-permute-start | bytes 1572872 | tf_op jit(solution)/shard_map/ppermute | solution.py:179
  121.6 32.5 %collective-permute-start.10 = (f32[512,256]{1,0:T(8,128)S(1)}, f32[512,256]{1,0:T(8,128)S(1)}, u32[]{:S(2)}, u32[]{:S(2)}) collective-permute-start(f32[512,256]{1,0:T(8,128)S(1)} %get-tuple-element.18), channel_id=1, source_target_pairs={{0,64},{8,72},{16,80},{24,88},{32,96},{40,104},{48,112},{56,120},{... | collective-permute-start | bytes 1572872 | tf_op jit(solution)/shard_map/ppermute | solution.py:179
  122.5 5.4 %collective-permute-start.16 = (f32[128,256]{1,0:T(8,128)S(1)}, f32[128,256]{1,0:T(8,128)S(1)}, u32[]{:S(2)}, u32[]{:S(2)}) collective-permute-start(f32[128,256]{1,0:T(8,128)S(1)} %add.134), channel_id=1, source_target_pairs={{0,16},{1,17},{2,18},{3,19},{4,20},{5,21},{6,22},{7,23},{8,24},{9,... | collective-permute-start | bytes 393224 | tf_op jit(solution)/shard_map/ppermute | solution.py:159
  128.0 16.5 %collective-permute-start.17 = (f32[128,256]{1,0:T(8,128)S(1)}, f32[128,256]{1,0:T(8,128)S(1)}, u32[]{:S(2)}, u32[]{:S(2)}) collective-permute-start(f32[128,256]{1,0:T(8,128)S(1)} %add.135), channel_id=1, source_target_pairs={{0,32},{1,33},{2,34},{3,35},{4,36},{5,37},{6,38},{7,39},{8,40},{9,... | collective-permute-start | bytes 393224 | tf_op jit(solution)/shard_map/ppermute | solution.py:159
  144.5 5.4 %collective-permute-start.18 = (f32[128,256]{1,0:T(8,128)S(1)}, f32[128,256]{1,0:T(8,128)S(1)}, u32[]{:S(2)}, u32[]{:S(2)}) collective-permute-start(f32[128,256]{1,0:T(8,128)S(1)} %add.136), channel_id=1, source_target_pairs={{0,64},{1,65},{2,66},{3,67},{4,68},{5,69},{6,70},{7,71},{8,72},{9,... | collective-permute-start | bytes 393224 | tf_op jit(solution)/shard_map/ppermute | solution.py:159
  149.9 5.2 %collective-permute-start.19 = (f32[128,256]{1,0:T(8,128)S(1)}, f32[128,256]{1,0:T(8,128)S(1)}, u32[]{:S(2)}, u32[]{:S(2)}) collective-permute-start(f32[128,256]{1,0:T(8,128)S(1)} %add.137), channel_id=1, source_target_pairs={{0,1},{1,0},{2,3},{3,2},{4,5},{5,4},{6,7},{7,6},{8,9},{9,8},{10,11... | collective-permute-start | bytes 393224 | tf_op jit(solution)/shard_map/ppermute | solution.py:163
  157.9 27.3 %all-to-all-start.2 = ((f32[128,8,256]{2,1,0:T(8,128)}), f32[128,8,256]{2,1,0:T(8,128)S(1)}, u32[]{:S(2)}, u32[]{:S(2)}) async-start(f32[128,8,256]{2,1,0:T(8,128)} %fusion.3), calls=%async_computation.2 | async-start | bytes 2097152 | tf_op jit(solution)/shard_map/all_to_all | solution.py:277
